TPU v7x, 32 devices: a whole 2x2x4 slice. The times are simulated.
32 devices in a mesh: det: 2 (over x), harm: 16 (over z, y, core).
Axes of the slice: x: 2, y: 2, z: 4, core: 2. Of those that a mesh axis runs over, the one named last changes fastest.
Arguments:
- perturbation: bfloat16 [32, 2, 2, 256, 512], P(('det', 'harm')), parts along dimension 0, may hold values from -16 to 16, as said below
- coupling: bfloat16 [4, 2, 512, 512], replicated, may hold values from -0.1875 to 0.1875
- y_operator: bfloat16 [128, 128], replicated, may hold values from -0.5 to 0.5
- x_operator: bfloat16 [256, 256], replicated, may hold values from -0.5 to 0.5
- tile_mask: int32 [2, 2], replicated, may hold values 0 or 1
- slot_offsets: int32 [4], replicated, may hold values from 0 to 3, each once
- detuning: float32 [2], P('det'), parts along dimension 0, may hold values from -0.5 to 0.5
Outputs:
- image: bfloat16 [32, 2, 2, 256, 512], P(('det', 'harm')), parts along dimension 0
- projected: bfloat16 [32, 2, 2, 256, 512], P(('det', 'harm')), parts along dimension 0
There are 2 independent parts, one for each index of `det`. A program takes and returns all parts, laid end to end along the dimension named above; an argument that names none is the same for every part. Nothing has to cross between parts.
Inputs may be any that keep to these rules, and one draw needn't show every extreme that they name: `perturbation`: real-valued entries with scales that vary over harmonics and streamwise points.
All inputs are finite; a program needn't handle non-finite values.
Results may differ from a plain program's by a relative error of at most 0.0004.
Values may be sent and summed in bfloat16 or wider, within the bound.
No kernel may reach another device: no remote copies, remote signals or barrier semaphores. Data moves between devices by JAX's collectives and lax.ppermute only.
A program may use at most 64 MiB of HBM per device.

v0:
```python
import jax
import jax.numpy as jnp
from jax import lax
from jax.sharding import PartitionSpec as P


def passed_along(value, axis, steps):
    count = lax.axis_size(axis)
    pairs = [(source, (source + steps) % count) for source in range(count)]
    return lax.ppermute(value, axis, pairs)


def body(perturbation, coupling, y_operator, x_operator, tile_mask, slot_offsets, detuning):
    block = perturbation[0]
    vecs = block.shape[1]
    width_x = block.shape[2]
    width_fy = block.shape[3]
    ny = y_operator.shape[0]
    harmonics = lax.axis_size("harm")
    position = lax.axis_index("harm")
    tile = width_x // tile_mask.shape[0]
    below_one = passed_along(block, "harm", 1)
    above_one = passed_along(block, "harm", -1)
    below_two = passed_along(below_one, "harm", 1)
    above_two = passed_along(above_one, "harm", -1)
    rows = block.reshape(-1, ny)
    along_y = jnp.dot(rows, y_operator, preferred_element_type=jnp.float32).reshape(block.shape)
    full_mask = jnp.repeat(jnp.repeat(tile_mask, tile, axis=0), tile, axis=1).astype(jnp.bfloat16)
    masked = x_operator * full_mask
    along_x = jnp.einsum("ab,cvbf->cvaf", masked, block, preferred_element_type=jnp.float32)
    centered = (position - harmonics // 2).astype(jnp.float32) + detuning[0]
    lam = -(centered * centered) / (4.0 * harmonics)
    image = along_y + along_x + lam * block.astype(jnp.float32)
    sources = (above_two, above_one, below_one, below_two)
    counter = jnp.arange(4, dtype=jnp.int32)
    for place in range(4):
        slot = jnp.sum(jnp.where(slot_offsets == place, counter, 0))
        matrix = lax.dynamic_index_in_dim(coupling, slot, 0, keepdims=False)
        other = sources[place].reshape(2, vecs * width_x, width_fy)
        prod = jnp.einsum("cri,kio->ckro", other, matrix, preferred_element_type=jnp.float32)
        real_part = prod[0, 0] - prod[1, 1]
        imag_part = prod[0, 1] + prod[1, 0]
        image = image + jnp.stack([real_part, imag_part]).reshape(block.shape)
    hp = lax.Precision.HIGHEST
    qfull = block.astype(jnp.float32)
    qr = qfull[0]
    qi = qfull[1]
    wr = image[0]
    wi = image[1]
    num_re = jnp.einsum("vxf,uxf->vu", qr, wr, precision=hp) + jnp.einsum(
        "vxf,uxf->vu", qi, wi, precision=hp
    )
    num_im = jnp.einsum("vxf,uxf->vu", qr, wi, precision=hp) - jnp.einsum(
        "vxf,uxf->vu", qi, wr, precision=hp
    )
    norms = jnp.sum(qr * qr + qi * qi, axis=(1, 2))
    total_re, total_im, total_norms = lax.psum((num_re, num_im, norms), "harm")
    h_re = total_re / (total_norms + 1e-06)[:, None]
    h_im = total_im / (total_norms + 1e-06)[:, None]
    proj_re = (
        wr
        - jnp.einsum("vu,vxf->uxf", h_re, qr, precision=hp)
        + jnp.einsum("vu,vxf->uxf", h_im, qi, precision=hp)
    )
    proj_im = (
        wi
        - jnp.einsum("vu,vxf->uxf", h_re, qi, precision=hp)
        - jnp.einsum("vu,vxf->uxf", h_im, qr, precision=hp)
    )
    projected = jnp.stack([proj_re, proj_im])
    return (image.astype(jnp.bfloat16)[None], projected.astype(jnp.bfloat16)[None])


def solution(mesh):
    in_specs = (P(("det", "harm"), None, None, None, None), P(), P(), P(), P(), P(), P("det"))
    out_specs = (
        P(("det", "harm"), None, None, None, None),
        P(("det", "harm"), None, None, None, None),
    )
    return jax.shard_map(body, mesh=mesh, in_specs=in_specs, out_specs=out_specs, check_vma=False)
```

profile of v0, /device:TPU:0, one launch (start us, length us, event | category | flops | bytes accessed | tf_op | source)
XLA Modules:
  0.0 127.1 jit_solution(13211541068705902138)
XLA Ops:
  0.6 0.0 copy-start
  0.6 0.5 collective-permute-start.2
  1.1 5.1 %collective-permute-start = (bf16[2,2,256,512]{3,2,1,0:T(8,128)(2,1)}, bf16[2,2,256,512]{3,2,1,0:T(8,128)(2,1)}, u32[]{:S(2)}, u32[]{:S(2)}) collective-permute-start(bf16[2,2,256,512]{3,2,1,0:T(8,128)(2,1)} %bitcast.149), channel_id=1, source_target_pairs={{0,15},{1,0},{2,1},{3,2},{4,3},{5,4},{6,5},{7,6},{8,7},{9,8},{10,9... | collective-permute-start | bytes 3145736 | tf_op jit(solution)/shard_map/ppermute | solution.py:10
  6.2 1.4 %fusion.40 = (s32[]{:T(128)}, s32[]{:T(128)}, s32[]{:T(128)}, s32[]{:T(128)}) fusion(s32[4]{0:T(128)} %param.12), kind=kLoop, calls=%fused_computation.76 | loop fusion | flops 44 | bytes 32 | tf_op jit(solution)/shard_map/reduce_sum | solution.py:37
  12.7 1.7 %reshape_squeeze.3 = bf16[4096,128]{1,0:T(8,128)(2,1)S(1)} reshape(bf16[1,2,2,256,512]{4,3,2,1,0:T(8,128)(2,1)} %param.7) | data formatting | bytes 2097152 | tf_op jit(solution)/shard_map/reshape;squeeze | solution.py:26
  14.4 0.0 copy-done
  14.4 0.4 fusion.43
  14.8 0.0 copy-start.13
  14.8 0.0 copy-start.1
  14.8 1.5 %reshape.236 = f32[2,2,256,512]{3,2,1,0:T(8,128)} reshape(f32[4096,128]{1,0:T(8,128)S(1)} %fusion.43) | data formatting | bytes 4194304 | tf_op jit(solution)/shard_map/reshape | solution.py:27
  16.4 0.0 copy-done.13
  17.0 0.0 copy-done.1
  17.0 0.1 fusion.42
  17.1 0.0 copy-start.4
  17.1 0.0 copy-start.6
  17.1 1.2 copy.29
  18.3 1.1 copy.28
  21.9 0.0 copy-start.3
  22.0 0.3 bitcast_convert_fusion
  22.2 0.0 copy-done.4
  22.3 0.0 copy-done.6
  22.3 0.3 fusion.9
  22.5 0.0 collective-permute-done.2
  22.5 4.5 %collective-permute-start.3 = (bf16[2,2,256,512]{3,2,1,0:T(8,128)(2,1)}, bf16[2,2,256,512]{3,2,1,0:T(8,128)(2,1)S(1)}, u32[]{:S(2)}, u32[]{:S(2)}) collective-permute-start(bf16[2,2,256,512]{3,2,1,0:T(8,128)(2,1)} %collective-permute-done.2), channel_id=1, source_target_pairs={{0,1},{1,2},{2,3},{3,4},{4,5},{5,6},{6,7},{7,8},{8,9},{9,10},{10,1... | collective-permute-start | bytes 3145736 | tf_op jit(solution)/shard_map/ppermute | solution.py:10
  27.1 0.0 collective-permute-done
  27.1 0.0 copy-done.3
  27.1 2.5 %convolution_bitcast_fusion.2 = f32[2,2,512,512]{3,2,0,1:T(8,128)S(1)} fusion(bf16[2,512,512,1]{2,1,0,3:T(8,128)(2,1)} %bitcast.18, bf16[4,2,512,512]{3,2,1,0:T(8,128)(2,1)S(1)} %copy-done.3, s32[]{:T(128)S(6)} %select_n.29), kind=kOutput, calls=%fused_computation.2 | convolution fusion | flops 1073741824 | bytes 6291460 | tf_op jit(solution)/shard_map/cri,kio->ckro/dot_general | solution.py:40
  29.6 0.1 collective-permute-start.1
  29.6 2.5 %convolution_bitcast_fusion.1 = f32[2,2,512,512]{3,2,0,1:T(8,128)S(1)} fusion(bf16[2,512,512,1]{2,1,0,3:T(8,128)(2,1)} %bitcast.26, bf16[4,2,512,512]{3,2,1,0:T(8,128)(2,1)S(1)} %copy-done.3, s32[]{:T(128)S(6)} %select_n.31), kind=kOutput, calls=%fused_computation.1 | convolution fusion | flops 1073741824 | bytes 6291460 | tf_op jit(solution)/shard_map/cri,kio->ckro/dot_general | solution.py:40
  32.2 0.5 slice_subtract_fusion.2
  32.7 0.5 slice_subtract_fusion.1
  33.1 6.6 %collective-permute-done.3 = bf16[2,2,256,512]{3,2,1,0:T(8,128)(2,1)S(1)} collective-permute-done((bf16[2,2,256,512]{3,2,1,0:T(8,128)(2,1)}, bf16[2,2,256,512]{3,2,1,0:T(8,128)(2,1)S(1)}, u32[]{:S(2)}, u32[]{:S(2)}) %collective-permute-start.3) | collective-permute-done | bytes 1048608 | tf_op jit(solution)/shard_map/ppermute | solution.py:10
  39.8 1.3 %convolution_bitcast_fusion = f32[2,2,512,512]{3,2,0,1:T(8,128)S(1)} fusion(bf16[2,512,512,1]{2,1,0,3:T(8,128)(2,1)S(1)} %bitcast.159, bf16[4,2,512,512]{3,2,1,0:T(8,128)(2,1)S(1)} %copy-done.3, s32[]{:T(128)S(6)} %select_n.33), kind=kOutput, calls=%fused_computation | convolution fusion | flops 1073741824 | bytes 6291460 | tf_op jit(solution)/shard_map/cri,kio->ckro/dot_general | solution.py:40
  41.1 0.5 slice_subtract_fusion
  41.5 4.2 %collective-permute-done.1 = bf16[2,2,256,512]{3,2,1,0:T(8,128)(2,1)S(1)} collective-permute-done((bf16[2,2,256,512]{3,2,1,0:T(8,128)(2,1)}, bf16[2,2,256,512]{3,2,1,0:T(8,128)(2,1)S(1)}, u32[]{:S(2)}, u32[]{:S(2)}) %collective-permute-start.1) | collective-permute-done | bytes 1048608 | tf_op jit(solution)/shard_map/ppermute | solution.py:10
  45.7 1.3 %convolution_bitcast_fusion.3 = f32[2,2,512,512]{3,2,0,1:T(8,128)S(1)} fusion(bf16[2,512,512,1]{2,1,0,3:T(8,128)(2,1)S(1)} %bitcast.158, bf16[4,2,512,512]{3,2,1,0:T(8,128)(2,1)S(1)} %copy-done.3, s32[]{:T(128)S(6)} %select_n.27), kind=kOutput, calls=%fused_computation.3 | convolution fusion | flops 1073741824 | bytes 6291460 | tf_op jit(solution)/shard_map/cri,kio->ckro/dot_general | solution.py:40
  47.0 0.0 copy-start.2
  47.0 0.0 copy-start.12
  47.0 0.5 slice_subtract_fusion.3
  47.5 0.3 broadcast_in_dim.18
  47.9 0.7 copy-done.2
  48.6 0.0 copy-done.12
  48.6 1.0 fusion.2
  49.6 1.1 slice_bitcast_fusion
  50.7 2.2 %copy.12 = f32[2,256,512]{1,0,2:T(2,128)} copy(f32[2,256,512]{2,1,0:T(8,128)} %get-tuple-element.19) | data formatting | bytes 2097152 | tf_op jit(solution)/shard_map/squeeze | solution.py:49
  53.0 1.3 %copy.10 = f32[2,256,512]{1,0,2:T(2,128)} copy(f32[2,256,512]{2,1,0:T(8,128)S(1)} %get-tuple-element.20) | data formatting | bytes 2097152 | tf_op jit(solution)/shard_map/squeeze | solution.py:48
  54.3 6.0 %convolution_bitcast_fusion.6 = f32[2,2]{1,0:T(2,128)S(1)} fusion(f32[2,256,512]{1,0,2:T(2,128)} %copy.12, bf16[1,1,2,256,512]{3,2,4,1,0:T(2,128)(2,1)} %copy.29), kind=kOutput, calls=%fused_computation.12 | convolution fusion | flops 6291456 | bytes 1572880 | tf_op jit(solution)/shard_map/vxf,uxf->vu/dot_general | solution.py:50
  60.3 0.0 copy-done.9
  60.3 0.0 copy-done.11
  60.3 0.0 copy-start.10
  60.3 4.6 %convolution_bitcast_fusion.4 = f32[2,2]{1,0:T(2,128)S(1)} fusion(f32[2,256,512]{1,0,2:T(2,128)S(1)} %copy-done.9, bf16[1,1,2,256,512]{3,2,4,1,0:T(2,128)(2,1)S(1)} %copy-done.11), kind=kOutput, calls=%fused_computation.10 | convolution fusion | flops 6291456 | bytes 1572880 | tf_op jit(solution)/shard_map/vxf,uxf->vu/dot_general | solution.py:53
  64.9 0.0 copy-done.10
  64.9 5.5 %fusion.5 = f32[2,2]{0,1:T(2,128)S(1)} fusion(f32[2,2]{1,0:T(2,128)S(1)} %convolution_bitcast_fusion.6, f32[2,256,512]{1,0,2:T(2,128)S(1)} %copy-done.9, bf16[1,1,2,256,512]{3,2,4,1,0:T(2,128)(2,1)S(1)} %copy-done.10), kind=kOutput, calls=%fused_computation.15 | convolution fusion | flops 6291460 | bytes 1572896 | tf_op jit(solution)/shard_map/vxf,uxf->vu/dot_general | solution.py:50
  70.4 0.0 copy-done.8
  70.4 4.8 %fusion.7 = f32[2,2]{0,1:T(2,128)S(1)} fusion(f32[2,2]{1,0:T(2,128)S(1)} %convolution_bitcast_fusion.4, f32[2,256,512]{1,0,2:T(2,128)S(1)} %copy-done.8, bf16[1,1,2,256,512]{3,2,4,1,0:T(2,128)(2,1)S(1)} %copy-done.10), kind=kOutput, calls=%fused_computation.17 | convolution fusion | flops 6291460 | bytes 1572896 | tf_op jit(solution)/shard_map/vxf,uxf->vu/dot_general | solution.py:53
  75.3 41.6 %all-reduce = (f32[2,2]{0,1:T(2,128)S(1)}, f32[2]{0:T(128)S(1)}, f32[2,2]{0,1:T(2,128)S(1)}) all-reduce(f32[2,2]{0,1:T(2,128)S(1)} %fusion.7, f32[2]{0:T(128)S(1)} %fusion.9, f32[2,2]{0,1:T(2,128)S(1)} %fusion.5), channel_id=1, replica_groups=mesh['det'=2,'harm'=16] {'harm'}, use_global_device_ids=true, to_apply=%region_7.8 | all-reduce | flops 10 | bytes 80 | tf_op jit(solution)/shard_map/psum | solution.py:57
  116.8 0.0 copy-done.5
  116.8 1.8 %fusion.28 = f32[2,256,512]{2,0,1:T(2,128)S(1)} fusion(bf16[1,1,2,256,512]{4,3,2,1,0:T(8,128)(2,1)S(1)} %copy-done.5, f32[2,2]{0,1:T(2,128)S(1)} %get-tuple-element.8, f32[2]{0:T(128)S(1)} %broadcast_add_fusion), kind=kOutput, calls=%fused_computation.58 | convolution fusion | flops 6291460 | bytes 1572888 | tf_op jit(solution)/shard_map/vu,vxf->uxf/dot_general | solution.py:67
  118.7 1.8 %fusion.27 = f32[2,256,512]{2,0,1:T(2,128)S(1)} fusion(bf16[1,1,2,256,512]{4,3,2,1,0:T(8,128)(2,1)S(1)} %copy-done.7, f32[2,2]{0,1:T(2,128)S(1)} %get-tuple-element.8, f32[2]{0:T(128)S(1)} %broadcast_add_fusion), kind=kOutput, calls=%fused_computation.57 | convolution fusion | flops 6291460 | bytes 1572888 | tf_op jit(solution)/shard_map/vu,vxf->uxf/dot_general | solution.py:62
  120.4 1.8 %fusion.26 = f32[2,256,512]{2,0,1:T(2,128)S(1)} fusion(bf16[1,1,2,256,512]{4,3,2,1,0:T(8,128)(2,1)S(1)} %copy-done.7, f32[2,2]{0,1:T(2,128)S(1)} %get-tuple-element.6, f32[2]{0:T(128)S(1)} %broadcast_add_fusion), kind=kOutput, calls=%fused_computation.56 | convolution fusion | flops 6291460 | bytes 1572888 | tf_op jit(solution)/shard_map/vu,vxf->uxf/dot_general | solution.py:68
  122.2 1.8 %fusion.29 = f32[2,256,512]{2,0,1:T(2,128)S(1)} fusion(bf16[1,1,2,256,512]{4,3,2,1,0:T(8,128)(2,1)S(1)} %copy-done.5, f32[2,2]{0,1:T(2,128)S(1)} %get-tuple-element.6, f32[2]{0:T(128)S(1)} %broadcast_add_fusion), kind=kOutput, calls=%fused_computation.59 | convolution fusion | flops 6291460 | bytes 1572888 | tf_op jit(solution)/shard_map/vu,vxf->uxf/dot_general | solution.py:63
  124.0 1.1 convert_bitcast_fusion
  125.1 0.9 fusion.20
  126.1 1.1 pad_maximum_fusion
  (9 shorter events, 0.0 us)
Async XLA Ops:
  0.6 13.8 %copy-start = (bf16[128,128]{1,0:T(8,128)(2,1)S(1)}, bf16[128,128]{1,0:T(8,128)(2,1)}, u32[]{:S(2)}) copy-start(bf16[128,128]{1,0:T(8,128)(2,1)} %param.9) | copy-start | bytes 98308
  0.6 21.9 %collective-permute-start.2 = (bf16[2,2,256,512]{3,2,1,0:T(8,128)(2,1)}, bf16[2,2,256,512]{3,2,1,0:T(8,128)(2,1)}, u32[]{:S(2)}, u32[]{:S(2)}) collective-permute-start(bf16[2,2,256,512]{3,2,1,0:T(8,128)(2,1)} %bitcast.148), channel_id=1, source_target_pairs={{0,1},{1,2},{2,3},{3,4},{4,5},{5,6},{6,7},{7,8},{8,9},{9,10},{10,1... | collective-permute-start | bytes 3145736 | tf_op jit(solution)/shard_map/ppermute | solution.py:10
  1.1 25.9 %collective-permute-start = (bf16[2,2,256,512]{3,2,1,0:T(8,128)(2,1)}, bf16[2,2,256,512]{3,2,1,0:T(8,128)(2,1)}, u32[]{:S(2)}, u32[]{:S(2)}) collective-permute-start(bf16[2,2,256,512]{3,2,1,0:T(8,128)(2,1)} %bitcast.149), channel_id=1, source_target_pairs={{0,15},{1,0},{2,1},{3,2},{4,3},{5,4},{6,5},{7,6},{8,7},{9,8},{10,9... | collective-permute-start | bytes 3145736 | tf_op jit(solution)/shard_map/ppermute | solution.py:10
  14.8 1.5 %copy-start.13 = (s32[2,2]{1,0:T(2,128)S(1)}, s32[2,2]{1,0:T(2,128)}, u32[]{:S(2)}) copy-start(s32[2,2]{1,0:T(2,128)} %param.11) | copy-start | bytes 52
  14.8 2.2 %copy-start.1 = (bf16[1,2,2,256,512]{4,3,2,1,0:T(8,128)(2,1)S(1)}, bf16[1,2,2,256,512]{4,3,2,1,0:T(8,128)(2,1)}, u32[]{:S(2)}) copy-start(bf16[1,2,2,256,512]{4,3,2,1,0:T(8,128)(2,1)} %param.7) | copy-start | bytes 3145732
  17.1 5.1 %copy-start.4 = (bf16[1,1,2,256,512]{4,3,2,1,0:T(8,128)(2,1)}, bf16[1,1,2,256,512]{4,3,2,1,0:T(8,128)(2,1)S(1)}, u32[]{:S(2)}) copy-start(bf16[1,1,2,256,512]{4,3,2,1,0:T(8,128)(2,1)S(1)} %get-tuple-element.21) | copy-start | bytes 1572868
  17.1 5.1 %copy-start.6 = (bf16[1,1,2,256,512]{4,3,2,1,0:T(8,128)(2,1)}, bf16[1,1,2,256,512]{4,3,2,1,0:T(8,128)(2,1)S(1)}, u32[]{:S(2)}) copy-start(bf16[1,1,2,256,512]{4,3,2,1,0:T(8,128)(2,1)S(1)} %get-tuple-element.22) | copy-start | bytes 1572868
  21.9 5.1 %copy-start.3 = (bf16[4,2,512,512]{3,2,1,0:T(8,128)(2,1)S(1)}, bf16[4,2,512,512]{3,2,1,0:T(8,128)(2,1)}, u32[]{:S(2)}) copy-start(bf16[4,2,512,512]{3,2,1,0:T(8,128)(2,1)} %param.8) | copy-start | bytes 12582916
  22.5 17.2 %collective-permute-start.3 = (bf16[2,2,256,512]{3,2,1,0:T(8,128)(2,1)}, bf16[2,2,256,512]{3,2,1,0:T(8,128)(2,1)S(1)}, u32[]{:S(2)}, u32[]{:S(2)}) collective-permute-start(bf16[2,2,256,512]{3,2,1,0:T(8,128)(2,1)} %collective-permute-done.2), channel_id=1, source_target_pairs={{0,1},{1,2},{2,3},{3,4},{4,5},{5,6},{6,7},{7,8},{8,9},{9,10},{10,1... | collective-permute-start | bytes 3145736 | tf_op jit(solution)/shard_map/ppermute | solution.py:10
  29.6 16.1 %collective-permute-start.1 = (bf16[2,2,256,512]{3,2,1,0:T(8,128)(2,1)}, bf16[2,2,256,512]{3,2,1,0:T(8,128)(2,1)S(1)}, u32[]{:S(2)}, u32[]{:S(2)}) collective-permute-start(bf16[2,2,256,512]{3,2,1,0:T(8,128)(2,1)} %collective-permute-done), channel_id=1, source_target_pairs={{0,15},{1,0},{2,1},{3,2},{4,3},{5,4},{6,5},{7,6},{8,7},{9,8},{10,9... | collective-permute-start | bytes 3145736 | tf_op jit(solution)/shard_map/ppermute | solution.py:10
  47.0 1.6 %copy-start.2 = (f32[2,2,256,512]{3,2,1,0:T(8,128)S(1)}, f32[2,2,256,512]{3,2,1,0:T(8,128)}, u32[]{:S(2)}) copy-start(f32[2,2,256,512]{3,2,1,0:T(8,128)} %reshape.236) | copy-start | bytes 6291460
  47.0 1.6 %copy-start.12 = (bf16[256,256]{1,0:T(8,128)(2,1)S(1)}, bf16[256,256]{1,0:T(8,128)(2,1)}, u32[]{:S(2)}) copy-start(bf16[256,256]{1,0:T(8,128)(2,1)} %param.10) | copy-start | bytes 393220
  54.2 6.0 %copy-start.9 = (f32[2,256,512]{1,0,2:T(2,128)S(1)}, f32[2,256,512]{1,0,2:T(2,128)}, u32[]{:S(2)}) copy-start(f32[2,256,512]{1,0,2:T(2,128)} %copy.10) | copy-start | bytes 3145732
  54.3 6.0 %copy-start.11 = (bf16[1,1,2,256,512]{3,2,4,1,0:T(2,128)(2,1)S(1)}, bf16[1,1,2,256,512]{3,2,4,1,0:T(2,128)(2,1)}, u32[]{:S(2)}) copy-start(bf16[1,1,2,256,512]{3,2,4,1,0:T(2,128)(2,1)} %copy.29) | copy-start | bytes 1572868
  60.3 4.6 %copy-start.10 = (bf16[1,1,2,256,512]{3,2,4,1,0:T(2,128)(2,1)S(1)}, bf16[1,1,2,256,512]{3,2,4,1,0:T(2,128)(2,1)}, u32[]{:S(2)}) copy-start(bf16[1,1,2,256,512]{3,2,4,1,0:T(2,128)(2,1)} %copy.28) | copy-start | bytes 1572868
  64.9 5.5 %copy-start.8 = (f32[2,256,512]{1,0,2:T(2,128)S(1)}, f32[2,256,512]{1,0,2:T(2,128)}, u32[]{:S(2)}) copy-start(f32[2,256,512]{1,0,2:T(2,128)} %copy.12) | copy-start | bytes 3145732
  70.4 46.4 %copy-start.5 = (bf16[1,1,2,256,512]{4,3,2,1,0:T(8,128)(2,1)S(1)}, bf16[1,1,2,256,512]{4,3,2,1,0:T(8,128)(2,1)}, u32[]{:S(2)}) copy-start(bf16[1,1,2,256,512]{4,3,2,1,0:T(8,128)(2,1)} %copy-done.4) | copy-start | bytes 1572868
  70.4 48.2 %copy-start.7 = (bf16[1,1,2,256,512]{4,3,2,1,0:T(8,128)(2,1)S(1)}, bf16[1,1,2,256,512]{4,3,2,1,0:T(8,128)(2,1)}, u32[]{:S(2)}) copy-start(bf16[1,1,2,256,512]{4,3,2,1,0:T(8,128)(2,1)} %copy-done.6) | copy-start | bytes 1572868
where the time goes:
time: 128 us; the launch traced here: 127 us
  blocking collectives  41.6 us (32%)
  matrix products  37 us (29%)
  local copies, waits for them, and re-layouts  11.4 us (9%)
  waiting for transfers between devices  10.8 us (8%)
  starting transfers between devices  10.2 us (8%)
  between operations  9.27 us (7%)
  other arithmetic  6.93 us (5%)
    psum x1, blocking collectives, body(): total_re, total_im, total_norms = lax.psum((num_re, num_im, norms), 'harm')  41.6 us
    ppermute x4, waiting for transfers between devices, passed_along(): return lax.ppermute(value, axis, pairs)  10.8 us
    ppermute x4, starting transfers between devices, passed_along(): return lax.ppermute(value, axis, pairs)  10.2 us
    dot_general x4, matrix products, body(): jnp.einsum('cri,kio->ckro', other, matrix, preferred_element_type=jnp.flo...  7.56 us
    dot_general x1, matrix products, body(): jnp.einsum('vxf,uxf->vu', qi, wi, precision=hp)  6.01 us
    dot_general x1, matrix products, body(): jnp.einsum('vxf,uxf->vu', qr, wr, precision=hp)  5.52 us
    dot_general x1, matrix products, body(): jnp.einsum('vxf,uxf->vu', qr, wi, precision=hp)  4.85 us
    dot_general x1, matrix products, body(): jnp.einsum('vxf,uxf->vu', qi, wr, precision=hp)  4.58 us
  transfers between devices with their start and end apart: 4, of which 2 were waited for; matrix products, arithmetic and copies ran while one was open for 12% of the time, Pallas kernels for 0%

commit v1 on v0

--- a/solution.py
+++ b/solution.py
@@ -8,6 +8,22 @@
     count = lax.axis_size(axis)
     pairs = [(source, (source + steps) % count) for source in range(count)]
     return lax.ppermute(value, axis, pairs)
+
+
+def summed_over(axes, *parts):
+    flat = jnp.concatenate([part.reshape(-1) for part in parts])
+    count = 1
+    for axis in axes:
+        count = count * lax.axis_size(axis)
+    spread = jnp.broadcast_to(flat[None], (count,) + flat.shape)
+    gathered = lax.all_to_all(spread, axes, 0, 0, tiled=False)
+    total = jnp.sum(gathered, axis=0)
+    out = []
+    start = 0
+    for part in parts:
+        out.append(total[start:start + part.size].reshape(part.shape))
+        start += part.size
+    return out
 
 
 def body(perturbation, coupling, y_operator, x_operator, tile_mask, slot_offsets, detuning):
@@ -54,7 +70,7 @@
         "vxf,uxf->vu", qi, wr, precision=hp
     )
     norms = jnp.sum(qr * qr + qi * qi, axis=(1, 2))
-    total_re, total_im, total_norms = lax.psum((num_re, num_im, norms), "harm")
+    total_re, total_im, total_norms = summed_over(("harm",), num_re, num_im, norms)
     h_re = total_re / (total_norms + 1e-06)[:, None]
     h_im = total_im / (total_norms + 1e-06)[:, None]
     proj_re = (

time: 128 us -> 114 us (0.89)
  blocking collectives: 41.6 us -> 0 us
  starting transfers between devices: 10.2 us -> 25.9 us
  matrix products: 37 us -> 42.7 us
  waiting for transfers between devices: 10.8 us -> 16 us
  local copies, waits for them, and re-layouts: 11.4 us -> 12.7 us
    psum x1 -> x0, blocking collectives: 41.6 us -> none  [body(): total_re, total_im, total_norms = lax.psum((num_re, num_im, norms), 'harm')]
    all_to_all x0 -> x1, starting transfers between devices: none -> 15.7 us  [summed_over(): gathered = lax.all_to_all(spread, axes, 0, 0, tiled=False)]
    all_to_all x0 -> x1, waiting for transfers between devices: none -> 5.22 us  [summed_over(): gathered = lax.all_to_all(spread, axes, 0, 0, tiled=False)]
    dot_general x1, matrix products: 1.79 us -> 3.38 us  [body(): jnp.einsum('vu,vxf->uxf', h_re, qi, precision=hp)]
    dot_general x1, matrix products: 1.79 us -> 3.33 us  [body(): jnp.einsum('vu,vxf->uxf', h_re, qr, precision=hp)]
    unnamed x30 -> x34, local copies, waits for them, and re-layouts: 3.06 us -> 3.05 us
  transfers between devices with their start and end apart: 4 -> 5, of which waited for: 2 -> 3; matrix products, arithmetic and copies ran while one was open for 12% -> 15% of each run, Pallas kernels for 0% -> 0%
where the time goes in v1:
time: 114 us
  matrix products  42.7 us (37%)
  starting transfers between devices  25.9 us (23%)
  waiting for transfers between devices  16 us (14%)
  local copies, waits for them, and re-layouts  12.7 us (11%)
  between operations  9.23 us (8%)
  other arithmetic  7.17 us (6%)
    all_to_all x1, starting transfers between devices, summed_over(): gathered = lax.all_to_all(spread, axes, 0, 0, tiled=False)  15.7 us
    ppermute x4, waiting for transfers between devices, passed_along(): return lax.ppermute(value, axis, pairs)  10.8 us
    ppermute x4, starting transfers between devices, passed_along(): return lax.ppermute(value, axis, pairs)  10.2 us
    dot_general x4, matrix products, body(): jnp.einsum('cri,kio->ckro', other, matrix, preferred_element_type=jnp.flo...  7.56 us
    dot_general x1, matrix products, body(): jnp.einsum('vxf,uxf->vu', qi, wi, precision=hp)  6.01 us
    dot_general x1, matrix products, body(): jnp.einsum('vxf,uxf->vu', qr, wi, precision=hp)  5.78 us
    dot_general x1, matrix products, body(): jnp.einsum('vxf,uxf->vu', qr, wr, precision=hp)  5.5 us
    all_to_all x1, waiting for transfers between devices, summed_over(): gathered = lax.all_to_all(spread, axes, 0, 0, tiled=False)  5.22 us
  transfers between devices with their start and end apart: 5, of which 3 were waited for; matrix products, arithmetic and copies ran while one was open for 15% of the time, Pallas kernels for 0%

profile of v1, /device:TPU:0, one launch (start us, length us, event | category | flops | bytes accessed | tf_op | source)
XLA Modules:
  0.0 113.7 jit_solution(15049378270151384744)
XLA Ops:
  0.6 0.0 copy-start
  0.6 0.5 collective-permute-start.2
  1.1 5.1 %collective-permute-start = (bf16[2,2,256,512]{3,2,1,0:T(8,128)(2,1)}, bf16[2,2,256,512]{3,2,1,0:T(8,128)(2,1)}, u32[]{:S(2)}, u32[]{:S(2)}) collective-permute-start(bf16[2,2,256,512]{3,2,1,0:T(8,128)(2,1)} %bitcast.151), channel_id=1, source_target_pairs={{0,15},{1,0},{2,1},{3,2},{4,3},{5,4},{6,5},{7,6},{8,7},{9,8},{10,9... | collective-permute-start | bytes 3145736 | tf_op jit(solution)/shard_map/ppermute | solution.py:10
  6.2 1.4 %fusion.40 = (s32[]{:T(128)}, s32[]{:T(128)}, s32[]{:T(128)}, s32[]{:T(128)}) fusion(s32[4]{0:T(128)} %param.12), kind=kLoop, calls=%fused_computation.76 | loop fusion | flops 44 | bytes 32 | tf_op jit(solution)/shard_map/reduce_sum | solution.py:53
  12.7 1.7 %reshape_squeeze.3 = bf16[4096,128]{1,0:T(8,128)(2,1)S(1)} reshape(bf16[1,2,2,256,512]{4,3,2,1,0:T(8,128)(2,1)} %param.7) | data formatting | bytes 2097152 | tf_op jit(solution)/shard_map/reshape;squeeze | solution.py:42
  14.4 0.4 fusion.44
  14.8 0.0 copy-start.15
  14.9 0.0 copy-start.1
  14.9 1.5 %reshape.282 = f32[2,2,256,512]{3,2,1,0:T(8,128)} reshape(f32[4096,128]{1,0:T(8,128)S(1)} %fusion.44) | data formatting | bytes 4194304 | tf_op jit(solution)/shard_map/reshape | solution.py:43
  17.0 0.1 fusion.42
  17.1 1.1 %copy.106 = bf16[1,1,2,256,512]{3,2,4,1,0:T(2,128)(2,1)} copy(bf16[1,1,2,256,512]{4,3,2,1,0:T(8,128)(2,1)S(1)} %get-tuple-element.18) | data formatting | bytes 1048576
  18.3 1.1 copy.105
  21.9 0.0 copy-start.3
  21.9 0.3 bitcast_convert_fusion
  22.2 0.0 copy-done.4
  22.2 0.0 copy-done.6
  22.2 0.3 fusion.9
  22.5 0.0 collective-permute-done.2
  22.5 4.6 %collective-permute-start.3 = (bf16[2,2,256,512]{3,2,1,0:T(8,128)(2,1)}, bf16[2,2,256,512]{3,2,1,0:T(8,128)(2,1)S(1)}, u32[]{:S(2)}, u32[]{:S(2)}) collective-permute-start(bf16[2,2,256,512]{3,2,1,0:T(8,128)(2,1)} %collective-permute-done.2), channel_id=1, source_target_pairs={{0,1},{1,2},{2,3},{3,4},{4,5},{5,6},{6,7},{7,8},{8,9},{9,10},{10,1... | collective-permute-start | bytes 3145736 | tf_op jit(solution)/shard_map/ppermute | solution.py:10
  27.1 0.0 collective-permute-done
  27.1 2.5 %convolution_bitcast_fusion.2 = f32[2,2,512,512]{3,2,0,1:T(8,128)S(1)} fusion(bf16[2,512,512,1]{2,1,0,3:T(8,128)(2,1)} %bitcast.18, bf16[4,2,512,512]{3,2,1,0:T(8,128)(2,1)S(1)} %copy-done.3, s32[]{:T(128)S(6)} %select_n.29), kind=kOutput, calls=%fused_computation.2 | convolution fusion | flops 1073741824 | bytes 6291460 | tf_op jit(solution)/shard_map/cri,kio->ckro/dot_general | solution.py:56
  29.6 0.1 collective-permute-start.1
  29.6 2.5 %convolution_bitcast_fusion.1 = f32[2,2,512,512]{3,2,0,1:T(8,128)S(1)} fusion(bf16[2,512,512,1]{2,1,0,3:T(8,128)(2,1)} %bitcast.26, bf16[4,2,512,512]{3,2,1,0:T(8,128)(2,1)S(1)} %copy-done.3, s32[]{:T(128)S(6)} %select_n.31), kind=kOutput, calls=%fused_computation.1 | convolution fusion | flops 1073741824 | bytes 6291460 | tf_op jit(solution)/shard_map/cri,kio->ckro/dot_general | solution.py:56
  32.2 0.5 slice_subtract_fusion.2
  32.7 0.5 slice_subtract_fusion.1
  33.1 6.6 %collective-permute-done.3 = bf16[2,2,256,512]{3,2,1,0:T(8,128)(2,1)S(1)} collective-permute-done((bf16[2,2,256,512]{3,2,1,0:T(8,128)(2,1)}, bf16[2,2,256,512]{3,2,1,0:T(8,128)(2,1)S(1)}, u32[]{:S(2)}, u32[]{:S(2)}) %collective-permute-start.3) | collective-permute-done | bytes 1048608 | tf_op jit(solution)/shard_map/ppermute | solution.py:10
  39.8 1.3 %convolution_bitcast_fusion = f32[2,2,512,512]{3,2,0,1:T(8,128)S(1)} fusion(bf16[2,512,512,1]{2,1,0,3:T(8,128)(2,1)S(1)} %bitcast.161, bf16[4,2,512,512]{3,2,1,0:T(8,128)(2,1)S(1)} %copy-done.3, s32[]{:T(128)S(6)} %select_n.33), kind=kOutput, calls=%fused_computation | convolution fusion | flops 1073741824 | bytes 6291460 | tf_op jit(solution)/shard_map/cri,kio->ckro/dot_general | solution.py:56
  41.0 0.5 slice_subtract_fusion
  41.5 4.2 %collective-permute-done.1 = bf16[2,2,256,512]{3,2,1,0:T(8,128)(2,1)S(1)} collective-permute-done((bf16[2,2,256,512]{3,2,1,0:T(8,128)(2,1)}, bf16[2,2,256,512]{3,2,1,0:T(8,128)(2,1)S(1)}, u32[]{:S(2)}, u32[]{:S(2)}) %collective-permute-start.1) | collective-permute-done | bytes 1048608 | tf_op jit(solution)/shard_map/ppermute | solution.py:10
  45.7 1.3 %convolution_bitcast_fusion.3 = f32[2,2,512,512]{3,2,0,1:T(8,128)S(1)} fusion(bf16[2,512,512,1]{2,1,0,3:T(8,128)(2,1)S(1)} %bitcast.160, bf16[4,2,512,512]{3,2,1,0:T(8,128)(2,1)S(1)} %copy-done.3, s32[]{:T(128)S(6)} %select_n.27), kind=kOutput, calls=%fused_computation.3 | convolution fusion | flops 1073741824 | bytes 6291460 | tf_op jit(solution)/shard_map/cri,kio->ckro/dot_general | solution.py:56
  47.0 0.0 copy-start.14
  47.0 0.5 slice_subtract_fusion.3
  47.5 0.3 broadcast_in_dim.24
  47.9 0.7 copy-done.2
  48.6 0.0 copy-done.14
  48.6 1.0 fusion.2
  49.6 1.2 %slice_bitcast_fusion = (f32[2,256,512]{2,1,0:T(8,128)}, f32[2,256,512]{2,1,0:T(8,128)S(1)}) fusion(f32[2,2,256,512]{3,2,1,0:T(8,128)S(1)} %fusion.2), kind=kLoop, calls=%fused_computation.22 | loop fusion | bytes 4194304 | tf_op jit(solution)/shard_map/squeeze | solution.py:65
  50.8 2.2 %copy.73 = f32[2,256,512]{1,0,2:T(2,128)} copy(f32[2,256,512]{2,1,0:T(8,128)} %get-tuple-element.16) | data formatting | bytes 2097152 | tf_op jit(solution)/shard_map/squeeze | solution.py:65
  53.0 1.3 %copy.71 = f32[2,256,512]{1,0,2:T(2,128)} copy(f32[2,256,512]{2,1,0:T(8,128)S(1)} %get-tuple-element.17) | data formatting | bytes 2097152 | tf_op jit(solution)/shard_map/squeeze | solution.py:64
  54.3 6.0 %convolution_bitcast_fusion.6 = f32[2,2]{1,0:T(2,128)S(1)} fusion(f32[2,256,512]{1,0,2:T(2,128)} %copy.73, bf16[1,1,2,256,512]{3,2,4,1,0:T(2,128)(2,1)} %copy.106), kind=kOutput, calls=%fused_computation.12 | convolution fusion | flops 6291456 | bytes 1572880 | tf_op jit(solution)/shard_map/vxf,uxf->vu/dot_general | solution.py:66
  60.4 0.0 copy-done.13
  60.4 0.0 copy-start.12
  60.4 4.6 %convolution_bitcast_fusion.4 = f32[2,2]{1,0:T(2,128)S(1)} fusion(f32[2,256,512]{1,0,2:T(2,128)S(1)} %copy-done.11, bf16[1,1,2,256,512]{3,2,4,1,0:T(2,128)(2,1)S(1)} %copy-done.13), kind=kOutput, calls=%fused_computation.10 | convolution fusion | flops 6291456 | bytes 1572880 | tf_op jit(solution)/shard_map/vxf,uxf->vu/dot_general | solution.py:69
  65.0 5.5 %fusion.5 = f32[2,2]{0,1:T(2,128)S(1)} fusion(f32[2,2]{1,0:T(2,128)S(1)} %convolution_bitcast_fusion.6, f32[2,256,512]{1,0,2:T(2,128)S(1)} %copy-done.11, bf16[1,1,2,256,512]{3,2,4,1,0:T(2,128)(2,1)S(1)} %copy-done.12), kind=kOutput, calls=%fused_computation.15 | convolution fusion | flops 6291460 | bytes 1572896 | tf_op jit(solution)/shard_map/vxf,uxf->vu/dot_general | solution.py:66
  70.5 0.1 copy.74
  70.6 0.1 reshape.287
  70.7 5.8 %fusion.7 = f32[2,2]{0,1:T(2,128)S(1)} fusion(f32[2,2]{1,0:T(2,128)S(1)} %convolution_bitcast_fusion.4, f32[2,256,512]{1,0,2:T(2,128)S(1)} %copy-done.10, bf16[1,1,2,256,512]{3,2,4,1,0:T(2,128)(2,1)} %copy.105), kind=kOutput, calls=%fused_computation.17 | convolution fusion | flops 6291460 | bytes 1572896 | tf_op jit(solution)/shard_map/vxf,uxf->vu/dot_general | solution.py:69
  76.5 0.1 copy.77
  76.6 0.1 reshape.288
  76.7 0.1 pad_maximum_fusion.1
  76.8 0.6 broadcast_in_dim.26
  77.4 15.7 %all-to-all-start = ((f32[16,1,10]{2,1,0:T(1,128)}), f32[16,1,10]{2,1,0:T(1,128)S(1)}, u32[]{:S(2)}, u32[]{:S(2)}) async-start(f32[16,1,10]{2,1,0:T(1,128)} %broadcast_in_dim.26), calls=%async_computation | async-start | bytes 16384 | tf_op jit(solution)/shard_map/all_to_all | solution.py:19
  93.1 1.1 convert_bitcast_fusion
  94.2 5.2 %all-to-all-done = f32[16,1,10]{2,1,0:T(1,128)S(1)} async-done(((f32[16,1,10]{2,1,0:T(1,128)}), f32[16,1,10]{2,1,0:T(1,128)S(1)}, u32[]{:S(2)}, u32[]{:S(2)}) %all-to-all-start) | async-done | bytes 672 | tf_op jit(solution)/shard_map/all_to_all | solution.py:19
  99.5 0.1 fusion.43
  99.6 0.1 slice_add_fusion.4
  99.6 0.1 slice.118
  99.7 3.4 %fusion.28 = f32[2,256,512]{2,0,1:T(2,128)} fusion(bf16[1,1,2,256,512]{4,3,2,1,0:T(8,128)(2,1)S(1)} %copy-done.5, f32[2,2]{1,0:T(2,128)S(1)} %slice.118, f32[2]{0:T(128)S(1)} %slice_add_fusion.4), kind=kOutput, calls=%fused_computation.58 | convolution fusion | flops 6291460 | bytes 1572888 | tf_op jit(solution)/shard_map/vu,vxf->uxf/dot_general | solution.py:83
  103.1 3.3 %fusion.27 = f32[2,256,512]{2,0,1:T(2,128)} fusion(bf16[1,1,2,256,512]{4,3,2,1,0:T(8,128)(2,1)S(1)} %copy-done.7, f32[2,2]{1,0:T(2,128)S(1)} %slice.118, f32[2]{0:T(128)S(1)} %slice_add_fusion.4), kind=kOutput, calls=%fused_computation.57 | convolution fusion | flops 6291460 | bytes 1572888 | tf_op jit(solution)/shard_map/vu,vxf->uxf/dot_general | solution.py:78
  106.4 0.1 slice.121
  106.5 2.5 %fusion.26 = f32[2,256,512]{2,0,1:T(2,128)S(1)} fusion(bf16[1,1,2,256,512]{4,3,2,1,0:T(8,128)(2,1)S(1)} %copy-done.7, f32[2,2]{1,0:T(2,128)S(1)} %slice.121, f32[2]{0:T(128)S(1)} %slice_add_fusion.4), kind=kOutput, calls=%fused_computation.56 | convolution fusion | flops 6291460 | bytes 1572888 | tf_op jit(solution)/shard_map/vu,vxf->uxf/dot_general | solution.py:84
  109.1 2.6 %fusion.29 = f32[2,256,512]{2,0,1:T(2,128)S(1)} fusion(bf16[1,1,2,256,512]{4,3,2,1,0:T(8,128)(2,1)S(1)} %copy-done.5, f32[2,2]{1,0:T(2,128)S(1)} %slice.121, f32[2]{0:T(128)S(1)} %slice_add_fusion.4), kind=kOutput, calls=%fused_computation.59 | convolution fusion | flops 6291460 | bytes 1572888 | tf_op jit(solution)/shard_map/vu,vxf->uxf/dot_general | solution.py:79
  111.7 0.9 fusion.20
  112.6 1.1 pad_maximum_fusion
  (24 shorter events, 0.1 us)
Async XLA Ops:
  0.6 13.8 %copy-start = (bf16[128,128]{1,0:T(8,128)(2,1)S(1)}, bf16[128,128]{1,0:T(8,128)(2,1)}, u32[]{:S(2)}) copy-start(bf16[128,128]{1,0:T(8,128)(2,1)} %param.9) | copy-start | bytes 98308
  0.6 21.9 %collective-permute-start.2 = (bf16[2,2,256,512]{3,2,1,0:T(8,128)(2,1)}, bf16[2,2,256,512]{3,2,1,0:T(8,128)(2,1)}, u32[]{:S(2)}, u32[]{:S(2)}) collective-permute-start(bf16[2,2,256,512]{3,2,1,0:T(8,128)(2,1)} %bitcast.150), channel_id=1, source_target_pairs={{0,1},{1,2},{2,3},{3,4},{4,5},{5,6},{6,7},{7,8},{8,9},{9,10},{10,1... | collective-permute-start | bytes 3145736 | tf_op jit(solution)/shard_map/ppermute | solution.py:10
  1.1 25.9 %collective-permute-start = (bf16[2,2,256,512]{3,2,1,0:T(8,128)(2,1)}, bf16[2,2,256,512]{3,2,1,0:T(8,128)(2,1)}, u32[]{:S(2)}, u32[]{:S(2)}) collective-permute-start(bf16[2,2,256,512]{3,2,1,0:T(8,128)(2,1)} %bitcast.151), channel_id=1, source_target_pairs={{0,15},{1,0},{2,1},{3,2},{4,3},{5,4},{6,5},{7,6},{8,7},{9,8},{10,9... | collective-permute-start | bytes 3145736 | tf_op jit(solution)/shard_map/ppermute | solution.py:10
  14.8 1.5 %copy-start.15 = (s32[2,2]{1,0:T(2,128)S(1)}, s32[2,2]{1,0:T(2,128)}, u32[]{:S(2)}) copy-start(s32[2,2]{1,0:T(2,128)} %param.11) | copy-start | bytes 52
  14.9 2.2 %copy-start.1 = (bf16[1,2,2,256,512]{4,3,2,1,0:T(8,128)(2,1)S(1)}, bf16[1,2,2,256,512]{4,3,2,1,0:T(8,128)(2,1)}, u32[]{:S(2)}) copy-start(bf16[1,2,2,256,512]{4,3,2,1,0:T(8,128)(2,1)} %param.7) | copy-start | bytes 3145732
  17.1 5.1 %copy-start.4 = (bf16[1,1,2,256,512]{4,3,2,1,0:T(8,128)(2,1)}, bf16[1,1,2,256,512]{4,3,2,1,0:T(8,128)(2,1)S(1)}, u32[]{:S(2)}) copy-start(bf16[1,1,2,256,512]{4,3,2,1,0:T(8,128)(2,1)S(1)} %get-tuple-element.18) | copy-start | bytes 1572868
  17.1 5.1 %copy-start.6 = (bf16[1,1,2,256,512]{4,3,2,1,0:T(8,128)(2,1)}, bf16[1,1,2,256,512]{4,3,2,1,0:T(8,128)(2,1)S(1)}, u32[]{:S(2)}) copy-start(bf16[1,1,2,256,512]{4,3,2,1,0:T(8,128)(2,1)S(1)} %get-tuple-element.19) | copy-start | bytes 1572868
  21.9 5.2 %copy-start.3 = (bf16[4,2,512,512]{3,2,1,0:T(8,128)(2,1)S(1)}, bf16[4,2,512,512]{3,2,1,0:T(8,128)(2,1)}, u32[]{:S(2)}) copy-start(bf16[4,2,512,512]{3,2,1,0:T(8,128)(2,1)} %param.8) | copy-start | bytes 12582916
  22.5 17.2 %collective-permute-start.3 = (bf16[2,2,256,512]{3,2,1,0:T(8,128)(2,1)}, bf16[2,2,256,512]{3,2,1,0:T(8,128)(2,1)S(1)}, u32[]{:S(2)}, u32[]{:S(2)}) collective-permute-start(bf16[2,2,256,512]{3,2,1,0:T(8,128)(2,1)} %collective-permute-done.2), channel_id=1, source_target_pairs={{0,1},{1,2},{2,3},{3,4},{4,5},{5,6},{6,7},{7,8},{8,9},{9,10},{10,1... | collective-permute-start | bytes 3145736 | tf_op jit(solution)/shard_map/ppermute | solution.py:10
  29.6 16.1 %collective-permute-start.1 = (bf16[2,2,256,512]{3,2,1,0:T(8,128)(2,1)}, bf16[2,2,256,512]{3,2,1,0:T(8,128)(2,1)S(1)}, u32[]{:S(2)}, u32[]{:S(2)}) collective-permute-start(bf16[2,2,256,512]{3,2,1,0:T(8,128)(2,1)} %collective-permute-done), channel_id=1, source_target_pairs={{0,15},{1,0},{2,1},{3,2},{4,3},{5,4},{6,5},{7,6},{8,7},{9,8},{10,9... | collective-permute-start | bytes 3145736 | tf_op jit(solution)/shard_map/ppermute | solution.py:10
  47.0 1.6 %copy-start.2 = (f32[2,2,256,512]{3,2,1,0:T(8,128)S(1)}, f32[2,2,256,512]{3,2,1,0:T(8,128)}, u32[]{:S(2)}) copy-start(f32[2,2,256,512]{3,2,1,0:T(8,128)} %reshape.282) | copy-start | bytes 6291460
  47.0 1.6 %copy-start.14 = (bf16[256,256]{1,0:T(8,128)(2,1)S(1)}, bf16[256,256]{1,0:T(8,128)(2,1)}, u32[]{:S(2)}) copy-start(bf16[256,256]{1,0:T(8,128)(2,1)} %param.10) | copy-start | bytes 393220
  54.3 6.0 %copy-start.11 = (f32[2,256,512]{1,0,2:T(2,128)S(1)}, f32[2,256,512]{1,0,2:T(2,128)}, u32[]{:S(2)}) copy-start(f32[2,256,512]{1,0,2:T(2,128)} %copy.71) | copy-start | bytes 3145732
  54.3 6.0 %copy-start.13 = (bf16[1,1,2,256,512]{3,2,4,1,0:T(2,128)(2,1)S(1)}, bf16[1,1,2,256,512]{3,2,4,1,0:T(2,128)(2,1)}, u32[]{:S(2)}) copy-start(bf16[1,1,2,256,512]{3,2,4,1,0:T(2,128)(2,1)} %copy.106) | copy-start | bytes 1572868
  60.4 4.6 %copy-start.12 = (bf16[1,1,2,256,512]{3,2,4,1,0:T(2,128)(2,1)S(1)}, bf16[1,1,2,256,512]{3,2,4,1,0:T(2,128)(2,1)}, u32[]{:S(2)}) copy-start(bf16[1,1,2,256,512]{3,2,4,1,0:T(2,128)(2,1)} %copy.105) | copy-start | bytes 1572868
  65.0 5.7 %copy-start.10 = (f32[2,256,512]{1,0,2:T(2,128)S(1)}, f32[2,256,512]{1,0,2:T(2,128)}, u32[]{:S(2)}) copy-start(f32[2,256,512]{1,0,2:T(2,128)} %copy.73) | copy-start | bytes 3145732
  76.5 23.2 %copy-start.5 = (bf16[1,1,2,256,512]{4,3,2,1,0:T(8,128)(2,1)S(1)}, bf16[1,1,2,256,512]{4,3,2,1,0:T(8,128)(2,1)}, u32[]{:S(2)}) copy-start(bf16[1,1,2,256,512]{4,3,2,1,0:T(8,128)(2,1)} %copy-done.4) | copy-start | bytes 1572868
  77.4 22.1 %all-to-all-start = ((f32[16,1,10]{2,1,0:T(1,128)}), f32[16,1,10]{2,1,0:T(1,128)S(1)}, u32[]{:S(2)}, u32[]{:S(2)}) async-start(f32[16,1,10]{2,1,0:T(1,128)} %broadcast_in_dim.26), calls=%async_computation | async-start | bytes 16384 | tf_op jit(solution)/shard_map/all_to_all | solution.py:19
  93.1 10.0 %copy-start.7 = (bf16[1,1,2,256,512]{4,3,2,1,0:T(8,128)(2,1)S(1)}, bf16[1,1,2,256,512]{4,3,2,1,0:T(8,128)(2,1)}, u32[]{:S(2)}) copy-start(bf16[1,1,2,256,512]{4,3,2,1,0:T(8,128)(2,1)} %copy-done.6) | copy-start | bytes 1572868
  106.5 5.1 %copy-start.8 = (f32[2,256,512]{2,0,1:T(2,128)S(1)}, f32[2,256,512]{2,0,1:T(2,128)}, u32[]{:S(2)}) copy-start(f32[2,256,512]{2,0,1:T(2,128)} %fusion.28) | copy-start | bytes 3145732
  106.5 5.1 %copy-start.9 = (f32[2,256,512]{2,0,1:T(2,128)S(1)}, f32[2,256,512]{2,0,1:T(2,128)}, u32[]{:S(2)}) copy-start(f32[2,256,512]{2,0,1:T(2,128)} %fusion.27) | copy-start | bytes 3145732

commit v2 on v1

--- a/solution.py
+++ b/solution.py
@@ -57,32 +57,19 @@
         real_part = prod[0, 0] - prod[1, 1]
         imag_part = prod[0, 1] + prod[1, 0]
         image = image + jnp.stack([real_part, imag_part]).reshape(block.shape)
-    hp = lax.Precision.HIGHEST
     qfull = block.astype(jnp.float32)
     qr = qfull[0]
     qi = qfull[1]
     wr = image[0]
     wi = image[1]
-    num_re = jnp.einsum("vxf,uxf->vu", qr, wr, precision=hp) + jnp.einsum(
-        "vxf,uxf->vu", qi, wi, precision=hp
-    )
-    num_im = jnp.einsum("vxf,uxf->vu", qr, wi, precision=hp) - jnp.einsum(
-        "vxf,uxf->vu", qi, wr, precision=hp
-    )
+    num_re = jnp.sum(qr[:, None] * wr[None, :] + qi[:, None] * wi[None, :], axis=(2, 3))
+    num_im = jnp.sum(qr[:, None] * wi[None, :] - qi[:, None] * wr[None, :], axis=(2, 3))
     norms = jnp.sum(qr * qr + qi * qi, axis=(1, 2))
     total_re, total_im, total_norms = summed_over(("harm",), num_re, num_im, norms)
-    h_re = total_re / (total_norms + 1e-06)[:, None]
-    h_im = total_im / (total_norms + 1e-06)[:, None]
-    proj_re = (
-        wr
-        - jnp.einsum("vu,vxf->uxf", h_re, qr, precision=hp)
-        + jnp.einsum("vu,vxf->uxf", h_im, qi, precision=hp)
-    )
-    proj_im = (
-        wi
-        - jnp.einsum("vu,vxf->uxf", h_re, qi, precision=hp)
-        - jnp.einsum("vu,vxf->uxf", h_im, qr, precision=hp)
-    )
+    h_re = (total_re / (total_norms + 1e-06)[:, None])[:, :, None, None]
+    h_im = (total_im / (total_norms + 1e-06)[:, None])[:, :, None, None]
+    proj_re = wr - jnp.sum(h_re * qr[:, None] - h_im * qi[:, None], axis=0)
+    proj_im = wi - jnp.sum(h_re * qi[:, None] + h_im * qr[:, None], axis=0)
     projected = jnp.stack([proj_re, proj_im])
     return (image.astype(jnp.bfloat16)[None], projected.astype(jnp.bfloat16)[None])
 

time: 114 us -> 78.7 us (0.69)
  matrix products: 42.7 us -> 8.93 us
  local copies, waits for them, and re-layouts: 12.7 us -> 5.7 us
  other arithmetic: 7.17 us -> 10.2 us
  starting transfers between devices: 25.9 us -> 28.2 us
    dot_general x8 -> x0, matrix products: 33.7 us -> none  [the longest x1 6.01 us: body(): jnp.einsum('vxf,uxf->vu', qi, wi, precision=hp)]
    squeeze x3 -> x0, local copies, waits for them, and re-layouts: 4.77 us -> none  [the longest x2 3.48 us: body(): wi = image[1]]
    reduce_sum x0 -> x2, other arithmetic: none -> 3.39 us  [the longest x1 2.13 us: body(): proj_re = wr - jnp.sum(h_re * qr[:, None] - h_im * qi[:, None], axis=0)]
    unnamed x34 -> x18, local copies, waits for them, and re-layouts: 3.05 us -> 0.77 us
    ppermute x4, starting transfers between devices: 10.2 us -> 12.4 us  [passed_along(): return lax.ppermute(value, axis, pairs)]
  transfers between devices with their start and end apart: 5 -> 5, of which waited for: 3 -> 3; matrix products, arithmetic and copies ran while one was open for 15% -> 19% of each run, Pallas kernels for 0% -> 0%
where the time goes in v2:
time: 78.7 us; the launch traced here: 78.2 us
  starting transfers between devices  28.2 us (36%)
  waiting for transfers between devices  16.1 us (20%)
  other arithmetic  10.2 us (13%)
  between operations  9.08 us (12%)
  matrix products  8.93 us (11%)
  local copies, waits for them, and re-layouts  5.7 us (7%)
    all_to_all x1, starting transfers between devices, summed_over(): gathered = lax.all_to_all(spread, axes, 0, 0, tiled=False)  15.7 us
    ppermute x4, starting transfers between devices, passed_along(): return lax.ppermute(value, axis, pairs)  12.4 us
    ppermute x4, waiting for transfers between devices, passed_along(): return lax.ppermute(value, axis, pairs)  10.8 us
    dot_general x4, matrix products, body(): jnp.einsum('cri,kio->ckro', other, matrix, preferred_element_type=jnp.flo...  7.56 us
    all_to_all x1, waiting for transfers between devices, summed_over(): gathered = lax.all_to_all(spread, axes, 0, 0, tiled=False)  5.3 us
    reduce_sum x1, other arithmetic, body(): proj_re = wr - jnp.sum(h_re * qr[:, None] - h_im * qi[:, None], axis=0)  2.13 us
    sub x4, other arithmetic, body(): real_part = prod[0, 0] - prod[1, 1]  1.92 us
    another operation x1, local copies, waits for them, and re-layouts, body(): rows = block.reshape(-1, ny)  1.7 us
  transfers between devices with their start and end apart: 5, of which 3 were waited for; matrix products, arithmetic and copies ran while one was open for 19% of the time, Pallas kernels for 0%

profile of v2, /device:TPU:0, one launch (start us, length us, event | category | flops | bytes accessed | tf_op | source)
XLA Modules:
  0.0 78.2 jit_solution(14163689775394076427)
XLA Ops:
  0.6 0.0 copy-start
  0.6 0.5 collective-permute-start.2
  1.1 5.1 %collective-permute-start = (bf16[2,2,256,512]{3,2,1,0:T(8,128)(2,1)}, bf16[2,2,256,512]{3,2,1,0:T(8,128)(2,1)}, u32[]{:S(2)}, u32[]{:S(2)}) collective-permute-start(bf16[2,2,256,512]{3,2,1,0:T(8,128)(2,1)} %bitcast.115), channel_id=1, source_target_pairs={{0,15},{1,0},{2,1},{3,2},{4,3},{5,4},{6,5},{7,6},{8,7},{9,8},{10,9... | collective-permute-start | bytes 3145736 | tf_op jit(solution)/shard_map/ppermute | solution.py:10
  6.2 1.4 %fusion.26 = (s32[]{:T(128)}, s32[]{:T(128)}, s32[]{:T(128)}, s32[]{:T(128)}) fusion(s32[4]{0:T(128)} %param.12), kind=kLoop, calls=%fused_computation.57 | loop fusion | flops 44 | bytes 32 | tf_op jit(solution)/shard_map/reduce_sum | solution.py:53
  12.6 1.7 %reshape_squeeze.3 = bf16[4096,128]{1,0:T(8,128)(2,1)S(1)} reshape(bf16[1,2,2,256,512]{4,3,2,1,0:T(8,128)(2,1)} %param.7) | data formatting | bytes 2097152 | tf_op jit(solution)/shard_map/reshape;squeeze | solution.py:42
  14.3 0.0 copy-done
  14.3 0.4 fusion.29
  14.8 0.0 copy-start.8
  14.8 0.0 copy-start.1
  14.8 1.5 %reshape.302 = f32[2,2,256,512]{3,2,1,0:T(8,128)} reshape(f32[4096,128]{1,0:T(8,128)S(1)} %fusion.29) | data formatting | bytes 4194304 | tf_op jit(solution)/shard_map/reshape | solution.py:43
  16.3 0.0 copy-done.8
  19.5 0.0 copy-done.1
  19.5 0.3 bitcast_convert_fusion
  19.8 0.3 add_reduce_fusion.2
  20.1 0.0 copy-start.6
  20.1 0.2 slice_bitcast_fusion.1
  20.2 0.0 copy-start.2
  20.2 0.0 copy-start.4
  20.3 0.0 collective-permute-done.2
  20.3 6.8 %collective-permute-start.3 = (bf16[2,2,256,512]{3,2,1,0:T(8,128)(2,1)}, bf16[2,2,256,512]{3,2,1,0:T(8,128)(2,1)S(1)}, u32[]{:S(2)}, u32[]{:S(2)}) collective-permute-start(bf16[2,2,256,512]{3,2,1,0:T(8,128)(2,1)} %collective-permute-done.2), channel_id=1, source_target_pairs={{0,1},{1,2},{2,3},{3,4},{4,5},{5,6},{6,7},{7,8},{8,9},{9,10},{10,1... | collective-permute-start | bytes 3145736 | tf_op jit(solution)/shard_map/ppermute | solution.py:10
  27.1 0.0 collective-permute-done
  27.1 0.0 copy-done.6
  27.1 2.5 %convolution_bitcast_fusion.2 = f32[2,2,512,512]{3,2,0,1:T(8,128)S(1)} fusion(bf16[2,512,512,1]{2,1,0,3:T(8,128)(2,1)} %bitcast.18, bf16[4,2,512,512]{3,2,1,0:T(8,128)(2,1)S(1)} %copy-done.6, s32[]{:T(128)S(6)} %select_n.29), kind=kOutput, calls=%fused_computation.2 | convolution fusion | flops 1073741824 | bytes 6291460 | tf_op jit(solution)/shard_map/cri,kio->ckro/dot_general | solution.py:56
  29.6 0.1 collective-permute-start.1
  29.7 2.5 %convolution_bitcast_fusion.1 = f32[2,2,512,512]{3,2,0,1:T(8,128)S(1)} fusion(bf16[2,512,512,1]{2,1,0,3:T(8,128)(2,1)} %bitcast.26, bf16[4,2,512,512]{3,2,1,0:T(8,128)(2,1)S(1)} %copy-done.6, s32[]{:T(128)S(6)} %select_n.31), kind=kOutput, calls=%fused_computation.1 | convolution fusion | flops 1073741824 | bytes 6291460 | tf_op jit(solution)/shard_map/cri,kio->ckro/dot_general | solution.py:56
  32.2 0.5 slice_subtract_fusion.2
  32.7 0.5 slice_subtract_fusion.1
  33.1 4.4 %collective-permute-done.3 = bf16[2,2,256,512]{3,2,1,0:T(8,128)(2,1)S(1)} collective-permute-done((bf16[2,2,256,512]{3,2,1,0:T(8,128)(2,1)}, bf16[2,2,256,512]{3,2,1,0:T(8,128)(2,1)S(1)}, u32[]{:S(2)}, u32[]{:S(2)}) %collective-permute-start.3) | collective-permute-done | bytes 1048608 | tf_op jit(solution)/shard_map/ppermute | solution.py:10
  37.6 1.3 %convolution_bitcast_fusion = f32[2,2,512,512]{3,2,0,1:T(8,128)S(1)} fusion(bf16[2,512,512,1]{2,1,0,3:T(8,128)(2,1)S(1)} %bitcast.125, bf16[4,2,512,512]{3,2,1,0:T(8,128)(2,1)S(1)} %copy-done.6, s32[]{:T(128)S(6)} %select_n.33), kind=kOutput, calls=%fused_computation | convolution fusion | flops 1073741824 | bytes 6291460 | tf_op jit(solution)/shard_map/cri,kio->ckro/dot_general | solution.py:56
  38.8 0.5 slice_subtract_fusion
  39.3 6.4 %collective-permute-done.1 = bf16[2,2,256,512]{3,2,1,0:T(8,128)(2,1)S(1)} collective-permute-done((bf16[2,2,256,512]{3,2,1,0:T(8,128)(2,1)}, bf16[2,2,256,512]{3,2,1,0:T(8,128)(2,1)S(1)}, u32[]{:S(2)}, u32[]{:S(2)}) %collective-permute-start.1) | collective-permute-done | bytes 1048608 | tf_op jit(solution)/shard_map/ppermute | solution.py:10
  45.7 1.3 %convolution_bitcast_fusion.3 = f32[2,2,512,512]{3,2,0,1:T(8,128)S(1)} fusion(bf16[2,512,512,1]{2,1,0,3:T(8,128)(2,1)S(1)} %bitcast.124, bf16[4,2,512,512]{3,2,1,0:T(8,128)(2,1)S(1)} %copy-done.6, s32[]{:T(128)S(6)} %select_n.27), kind=kOutput, calls=%fused_computation.3 | convolution fusion | flops 1073741824 | bytes 6291460 | tf_op jit(solution)/shard_map/cri,kio->ckro/dot_general | solution.py:56
  47.0 0.0 copy-start.5
  47.0 0.0 copy-start.7
  47.0 0.5 slice_subtract_fusion.3
  47.5 0.3 broadcast_in_dim.26
  47.9 0.7 copy-done.5
  48.6 0.0 copy-done.7
  48.6 1.0 %fusion.2 = f32[2,2,256,512]{3,2,1,0:T(8,128)S(1)} fusion(f32[1,2,256,512]{3,2,1,0:T(8,128)S(1)} %bitcast.123, f32[1,2,256,512]{3,2,1,0:T(8,128)S(1)} %bitcast.122, f32[1,2,256,512]{3,2,1,0:T(8,128)S(1)} %bitcast.117, f32[1,2,256,512]{3,2,1,0:T(8,128)S(1)} %bitcast.116, f32[1,2,256,512]{3,2,1,0:T(8,128)S(1)} %bitcast.119, ...), kind=kOutput, calls=%fused_computation.7 | convolution fusion | flops 274989056 | bytes 13893636 | tf_op jit(solution)/shard_map/ab,cvbf->cvaf/dot_general | solution.py:46
  49.6 0.2 slice_bitcast_fusion.3
  49.7 0.0 copy-done.2
  49.7 0.0 copy-done.4
  49.8 1.3 %add_reduce_fusion.1 = (f32[2,2]{1,0:T(2,128)S(1)}, f32[2,2]{1,0:T(2,128)S(1)}) fusion(f32[2,256,512]{2,1,0:T(8,128)S(1)} %get-tuple-element.23, f32[2,256,512]{2,1,0:T(8,128)S(1)} %get-tuple-element.21, f32[2,256,512]{2,1,0:T(8,128)S(1)} %get-tuple-element.22, f32[2,256,512]{2,1,0:T(8,128)S(1)} %get-tuple-element.20), kind=kLoop, calls=%fused_computation.13 | loop fusion | flops 4194296 | bytes 4194336 | tf_op jit(solution)/shard_map/reduce_sum | solution.py:65
  51.0 0.0 copy-start.3
  51.0 0.1 reshape.307
  51.1 0.1 reshape.308
  51.2 0.1 pad_maximum_fusion.1
  51.3 0.6 broadcast_in_dim.28
  51.9 15.7 %all-to-all-start = ((f32[16,1,10]{2,1,0:T(1,128)}), f32[16,1,10]{2,1,0:T(1,128)S(1)}, u32[]{:S(2)}, u32[]{:S(2)}) async-start(f32[16,1,10]{2,1,0:T(1,128)} %broadcast_in_dim.28), calls=%async_computation | async-start | bytes 16384 | tf_op jit(solution)/shard_map/all_to_all | solution.py:19
  67.6 1.1 %convert_bitcast_fusion = bf16[1,2,2,256,512]{4,3,2,1,0:T(8,128)(2,1)} fusion(f32[2,2,256,512]{3,2,1,0:T(8,128)S(1)} %fusion.2), kind=kLoop, calls=%fused_computation.34 | loop fusion | flops 524288 | bytes 3145728 | tf_op jit(solution)/shard_map/broadcast_in_dim | solution.py:74
  68.7 5.3 %all-to-all-done = f32[16,1,10]{2,1,0:T(1,128)S(1)} async-done(((f32[16,1,10]{2,1,0:T(1,128)}), f32[16,1,10]{2,1,0:T(1,128)S(1)}, u32[]{:S(2)}, u32[]{:S(2)}) %all-to-all-start) | async-done | bytes 672 | tf_op jit(solution)/shard_map/all_to_all | solution.py:19
  74.1 0.1 fusion.28
  74.1 0.1 slice_add_fusion.4
  74.2 0.1 reshape.309
  74.3 0.1 reshape.310
  74.4 0.1 broadcast_divide_fusion.1
  74.4 0.0 copy-done.3
  74.4 2.1 %subtract_reduce_fusion = (f32[2,256,512]{2,1,0:T(8,128)S(1)}, f32[2,256,512]{2,1,0:T(8,128)S(1)}) fusion(f32[2,2]{1,0:T(2,128)S(1)} %get-tuple-element.25, f32[2,2]{1,0:T(2,128)S(1)} %get-tuple-element.24, f32[2,256,512]{2,1,0:T(8,128)} %copy-done.4, f32[2,256,512]{2,1,0:T(8,128)S(1)} %copy-done.3), kind=kLoop, calls=%fused_computation.11 | loop fusion | flops 3670016 | bytes 4194336 | tf_op jit(solution)/shard_map/reduce_sum | solution.py:71
  76.6 0.6 fusion.14
  77.2 1.1 %pad_maximum_fusion = bf16[1,2,2,256,512]{4,3,2,1,0:T(8,128)(2,1)} fusion(bf16[1,1,2,256,512]{4,3,2,1,0:T(8,128)(2,1)S(1)} %get-tuple-element.19, bf16[1,1,2,256,512]{4,3,2,1,0:T(8,128)(2,1)S(1)} %get-tuple-element.18), kind=kLoop, calls=%fused_computation.24 | loop fusion | flops 524288 | bytes 2097152 | tf_op jit(solution)/shard_map/stack | solution.py:73
  (3 shorter events, 0.0 us)
Async XLA Ops:
  0.6 13.7 %copy-start = (bf16[128,128]{1,0:T(8,128)(2,1)S(1)}, bf16[128,128]{1,0:T(8,128)(2,1)}, u32[]{:S(2)}) copy-start(bf16[128,128]{1,0:T(8,128)(2,1)} %param.9) | copy-start | bytes 98308
  0.6 19.6 %collective-permute-start.2 = (bf16[2,2,256,512]{3,2,1,0:T(8,128)(2,1)}, bf16[2,2,256,512]{3,2,1,0:T(8,128)(2,1)}, u32[]{:S(2)}, u32[]{:S(2)}) collective-permute-start(bf16[2,2,256,512]{3,2,1,0:T(8,128)(2,1)} %bitcast.114), channel_id=1, source_target_pairs={{0,1},{1,2},{2,3},{3,4},{4,5},{5,6},{6,7},{7,8},{8,9},{9,10},{10,1... | collective-permute-start | bytes 3145736 | tf_op jit(solution)/shard_map/ppermute | solution.py:10
  1.1 25.9 %collective-permute-start = (bf16[2,2,256,512]{3,2,1,0:T(8,128)(2,1)}, bf16[2,2,256,512]{3,2,1,0:T(8,128)(2,1)}, u32[]{:S(2)}, u32[]{:S(2)}) collective-permute-start(bf16[2,2,256,512]{3,2,1,0:T(8,128)(2,1)} %bitcast.115), channel_id=1, source_target_pairs={{0,15},{1,0},{2,1},{3,2},{4,3},{5,4},{6,5},{7,6},{8,7},{9,8},{10,9... | collective-permute-start | bytes 3145736 | tf_op jit(solution)/shard_map/ppermute | solution.py:10
  14.8 1.6 %copy-start.8 = (s32[2,2]{1,0:T(2,128)S(1)}, s32[2,2]{1,0:T(2,128)}, u32[]{:S(2)}) copy-start(s32[2,2]{1,0:T(2,128)} %param.11) | copy-start | bytes 52
  14.8 4.7 %copy-start.1 = (bf16[1,2,2,256,512]{4,3,2,1,0:T(8,128)(2,1)S(1)}, bf16[1,2,2,256,512]{4,3,2,1,0:T(8,128)(2,1)}, u32[]{:S(2)}) copy-start(bf16[1,2,2,256,512]{4,3,2,1,0:T(8,128)(2,1)} %param.7) | copy-start | bytes 3145732
  20.1 7.0 %copy-start.6 = (bf16[4,2,512,512]{3,2,1,0:T(8,128)(2,1)S(1)}, bf16[4,2,512,512]{3,2,1,0:T(8,128)(2,1)}, u32[]{:S(2)}) copy-start(bf16[4,2,512,512]{3,2,1,0:T(8,128)(2,1)} %param.8) | copy-start | bytes 12582916
  20.2 29.5 %copy-start.2 = (f32[2,256,512]{2,1,0:T(8,128)}, f32[2,256,512]{2,1,0:T(8,128)S(1)}, u32[]{:S(2)}) copy-start(f32[2,256,512]{2,1,0:T(8,128)S(1)} %get-tuple-element.20) | copy-start | bytes 3145732
  20.2 29.5 %copy-start.4 = (f32[2,256,512]{2,1,0:T(8,128)}, f32[2,256,512]{2,1,0:T(8,128)S(1)}, u32[]{:S(2)}) copy-start(f32[2,256,512]{2,1,0:T(8,128)S(1)} %get-tuple-element.21) | copy-start | bytes 3145732
  20.3 17.3 %collective-permute-start.3 = (bf16[2,2,256,512]{3,2,1,0:T(8,128)(2,1)}, bf16[2,2,256,512]{3,2,1,0:T(8,128)(2,1)S(1)}, u32[]{:S(2)}, u32[]{:S(2)}) collective-permute-start(bf16[2,2,256,512]{3,2,1,0:T(8,128)(2,1)} %collective-permute-done.2), channel_id=1, source_target_pairs={{0,1},{1,2},{2,3},{3,4},{4,5},{5,6},{6,7},{7,8},{8,9},{9,10},{10,1... | collective-permute-start | bytes 3145736 | tf_op jit(solution)/shard_map/ppermute | solution.py:10
  29.6 16.1 %collective-permute-start.1 = (bf16[2,2,256,512]{3,2,1,0:T(8,128)(2,1)}, bf16[2,2,256,512]{3,2,1,0:T(8,128)(2,1)S(1)}, u32[]{:S(2)}, u32[]{:S(2)}) collective-permute-start(bf16[2,2,256,512]{3,2,1,0:T(8,128)(2,1)} %collective-permute-done), channel_id=1, source_target_pairs={{0,15},{1,0},{2,1},{3,2},{4,3},{5,4},{6,5},{7,6},{8,7},{9,8},{10,9... | collective-permute-start | bytes 3145736 | tf_op jit(solution)/shard_map/ppermute | solution.py:10
  47.0 1.6 %copy-start.5 = (f32[2,2,256,512]{3,2,1,0:T(8,128)S(1)}, f32[2,2,256,512]{3,2,1,0:T(8,128)}, u32[]{:S(2)}) copy-start(f32[2,2,256,512]{3,2,1,0:T(8,128)} %reshape.302) | copy-start | bytes 6291460
  47.0 1.6 %copy-start.7 = (bf16[256,256]{1,0:T(8,128)(2,1)S(1)}, bf16[256,256]{1,0:T(8,128)(2,1)}, u32[]{:S(2)}) copy-start(bf16[256,256]{1,0:T(8,128)(2,1)} %param.10) | copy-start | bytes 393220
  51.0 23.4 %copy-start.3 = (f32[2,256,512]{2,1,0:T(8,128)S(1)}, f32[2,256,512]{2,1,0:T(8,128)}, u32[]{:S(2)}) copy-start(f32[2,256,512]{2,1,0:T(8,128)} %copy-done.2) | copy-start | bytes 3145732
  51.9 22.2 %all-to-all-start = ((f32[16,1,10]{2,1,0:T(1,128)}), f32[16,1,10]{2,1,0:T(1,128)S(1)}, u32[]{:S(2)}, u32[]{:S(2)}) async-start(f32[16,1,10]{2,1,0:T(1,128)} %broadcast_in_dim.28), calls=%async_computation | async-start | bytes 16384 | tf_op jit(solution)/shard_map/all_to_all | solution.py:19

commit v3 on v2

--- a/solution.py
+++ b/solution.py
@@ -37,8 +37,8 @@
     tile = width_x // tile_mask.shape[0]
     below_one = passed_along(block, "harm", 1)
     above_one = passed_along(block, "harm", -1)
-    below_two = passed_along(below_one, "harm", 1)
-    above_two = passed_along(above_one, "harm", -1)
+    below_two = passed_along(block, "harm", 2)
+    above_two = passed_along(block, "harm", -2)
     rows = block.reshape(-1, ny)
     along_y = jnp.dot(rows, y_operator, preferred_element_type=jnp.float32).reshape(block.shape)
     full_mask = jnp.repeat(jnp.repeat(tile_mask, tile, axis=0), tile, axis=1).astype(jnp.bfloat16)

time: 78.7 us -> 99.9 us (1.27)
  waiting for transfers between devices: 16.1 us -> 42.8 us
  starting transfers between devices: 28.2 us -> 18.6 us
  matrix products: 8.93 us -> 11.4 us
  local copies, waits for them, and re-layouts: 5.7 us -> 7.27 us
    ppermute x4, waiting for transfers between devices: 10.8 us -> 37.5 us  [passed_along(): return lax.ppermute(value, axis, pairs)]
    all_to_all x1, starting transfers between devices: 15.7 us -> 8.36 us  [summed_over(): gathered = lax.all_to_all(spread, axes, 0, 0, tiled=False)]
    dot_general x4, matrix products: 7.56 us -> 10 us  [body(): jnp.einsum('cri,kio->ckro', other, matrix, preferred_element_type=jnp.flo...]
    ppermute x4, starting transfers between devices: 12.4 us -> 10.3 us  [passed_along(): return lax.ppermute(value, axis, pairs)]
    unnamed x18, local copies, waits for them, and re-layouts: 0.77 us -> 2.35 us
  transfers between devices with their start and end apart: 5 -> 5, of which waited for: 3 -> 5; matrix products, arithmetic and copies ran while one was open for 19% -> 16% of each run, Pallas kernels for 0% -> 0%
where the time goes in v3:
time: 99.9 us; the launch traced here: 99.3 us
  waiting for transfers between devices  42.8 us (43%)
  starting transfers between devices  18.6 us (19%)
  matrix products  11.4 us (11%)
  other arithmetic  10.2 us (10%)
  between operations  9.02 us (9%)
  local copies, waits for them, and re-layouts  7.27 us (7%)
    ppermute x4, waiting for transfers between devices, passed_along(): return lax.ppermute(value, axis, pairs)  37.5 us
    ppermute x4, starting transfers between devices, passed_along(): return lax.ppermute(value, axis, pairs)  10.3 us
    dot_general x4, matrix products, body(): jnp.einsum('cri,kio->ckro', other, matrix, preferred_element_type=jnp.flo...  10 us
    all_to_all x1, starting transfers between devices, summed_over(): gathered = lax.all_to_all(spread, axes, 0, 0, tiled=False)  8.36 us
    all_to_all x1, waiting for transfers between devices, summed_over(): gathered = lax.all_to_all(spread, axes, 0, 0, tiled=False)  5.3 us
    unnamed x18, local copies, waits for them, and re-layouts  2.35 us
    reduce_sum x1, other arithmetic, body(): proj_re = wr - jnp.sum(h_re * qr[:, None] - h_im * qi[:, None], axis=0)  2.13 us
  transfers between devices with their start and end apart: 5, of which 5 were waited for; matrix products, arithmetic and copies ran while one was open for 16% of the time, Pallas kernels for 0%

profile of v3, /device:TPU:0, one launch (start us, length us, event | category | flops | bytes accessed | tf_op | source)
XLA Modules:
  0.0 99.3 jit_solution(8793846860518208136)
XLA Ops:
  0.6 0.0 copy-start
  0.6 5.5 %collective-permute-start.1 = (bf16[2,2,256,512]{3,2,1,0:T(8,128)(2,1)}, bf16[2,2,256,512]{3,2,1,0:T(8,128)(2,1)}, u32[]{:S(2)}, u32[]{:S(2)}) collective-permute-start(bf16[2,2,256,512]{3,2,1,0:T(8,128)(2,1)} %bitcast.114), channel_id=1, source_target_pairs={{0,15},{1,0},{2,1},{3,2},{4,3},{5,4},{6,5},{7,6},{8,7},{9,8},{10,9... | collective-permute-start | bytes 3145736 | tf_op jit(solution)/shard_map/ppermute | solution.py:10
  6.1 0.0 collective-permute-start.2
  6.1 0.0 collective-permute-start.3
  6.1 4.8 %collective-permute-start = (bf16[2,2,256,512]{3,2,1,0:T(8,128)(2,1)}, bf16[2,2,256,512]{3,2,1,0:T(8,128)(2,1)}, u32[]{:S(2)}, u32[]{:S(2)}) collective-permute-start(bf16[2,2,256,512]{3,2,1,0:T(8,128)(2,1)} %bitcast.117), channel_id=1, source_target_pairs={{0,14},{1,15},{2,0},{3,1},{4,2},{5,3},{6,4},{7,5},{8,6},{9,7},{10,... | collective-permute-start | bytes 3145736 | tf_op jit(solution)/shard_map/ppermute | solution.py:10
  10.9 1.4 %fusion.26 = (s32[]{:T(128)}, s32[]{:T(128)}, s32[]{:T(128)}, s32[]{:T(128)}) fusion(s32[4]{0:T(128)} %param.12), kind=kLoop, calls=%fused_computation.57 | loop fusion | flops 44 | bytes 32 | tf_op jit(solution)/shard_map/reduce_sum | solution.py:53
  17.3 1.7 %reshape_squeeze.3 = bf16[4096,128]{1,0:T(8,128)(2,1)S(1)} reshape(bf16[1,2,2,256,512]{4,3,2,1,0:T(8,128)(2,1)} %param.7) | data formatting | bytes 2097152 | tf_op jit(solution)/shard_map/reshape;squeeze | solution.py:42
  19.0 0.0 copy-done
  19.0 0.4 fusion.29
  19.4 0.0 copy-start.8
  19.4 0.0 copy-start.1
  19.4 1.5 %reshape.302 = f32[2,2,256,512]{3,2,1,0:T(8,128)} reshape(f32[4096,128]{1,0:T(8,128)S(1)} %fusion.29) | data formatting | bytes 4194304 | tf_op jit(solution)/shard_map/reshape | solution.py:43
  21.0 0.0 copy-done.8
  24.1 0.0 copy-done.1
  24.1 0.3 bitcast_convert_fusion
  24.4 0.3 add_reduce_fusion.2
  24.7 0.0 copy-start.6
  24.7 0.2 slice_bitcast_fusion.1
  24.9 0.0 copy-start.2
  24.9 0.0 copy-start.4
  24.9 1.2 %collective-permute-done.1 = bf16[2,2,256,512]{3,2,1,0:T(8,128)(2,1)} collective-permute-done((bf16[2,2,256,512]{3,2,1,0:T(8,128)(2,1)}, bf16[2,2,256,512]{3,2,1,0:T(8,128)(2,1)}, u32[]{:S(2)}, u32[]{:S(2)}) %collective-permute-start.1) | collective-permute-done | bytes 1048608 | tf_op jit(solution)/shard_map/ppermute | solution.py:10
  26.1 1.6 %copy-done.6 = bf16[4,2,512,512]{3,2,1,0:T(8,128)(2,1)S(1)} copy-done((bf16[4,2,512,512]{3,2,1,0:T(8,128)(2,1)S(1)}, bf16[4,2,512,512]{3,2,1,0:T(8,128)(2,1)}, u32[]{:S(2)}) %copy-start.6) | copy-done | bytes 4194328
  27.6 2.5 %convolution_bitcast_fusion.2 = f32[2,2,512,512]{3,2,0,1:T(8,128)S(1)} fusion(bf16[2,512,512,1]{2,1,0,3:T(8,128)(2,1)} %bitcast.18, bf16[4,2,512,512]{3,2,1,0:T(8,128)(2,1)S(1)} %copy-done.6, s32[]{:T(128)S(6)} %select_n.29), kind=kOutput, calls=%fused_computation.2 | convolution fusion | flops 1073741824 | bytes 6291460 | tf_op jit(solution)/shard_map/cri,kio->ckro/dot_general | solution.py:56
  30.2 4.0 %collective-permute-done.2 = bf16[2,2,256,512]{3,2,1,0:T(8,128)(2,1)} collective-permute-done((bf16[2,2,256,512]{3,2,1,0:T(8,128)(2,1)}, bf16[2,2,256,512]{3,2,1,0:T(8,128)(2,1)}, u32[]{:S(2)}, u32[]{:S(2)}) %collective-permute-start.2) | collective-permute-done | bytes 1048608 | tf_op jit(solution)/shard_map/ppermute | solution.py:10
  34.2 2.5 %convolution_bitcast_fusion.1 = f32[2,2,512,512]{3,2,0,1:T(8,128)S(1)} fusion(bf16[2,512,512,1]{2,1,0,3:T(8,128)(2,1)} %bitcast.26, bf16[4,2,512,512]{3,2,1,0:T(8,128)(2,1)S(1)} %copy-done.6, s32[]{:T(128)S(6)} %select_n.31), kind=kOutput, calls=%fused_computation.1 | convolution fusion | flops 1073741824 | bytes 6291460 | tf_op jit(solution)/shard_map/cri,kio->ckro/dot_general | solution.py:56
  36.7 0.5 slice_subtract_fusion.2
  37.2 0.5 slice_subtract_fusion.1
  37.6 24.1 %collective-permute-done.3 = bf16[2,2,256,512]{3,2,1,0:T(8,128)(2,1)} collective-permute-done((bf16[2,2,256,512]{3,2,1,0:T(8,128)(2,1)}, bf16[2,2,256,512]{3,2,1,0:T(8,128)(2,1)}, u32[]{:S(2)}, u32[]{:S(2)}) %collective-permute-start.3) | collective-permute-done | bytes 1048608 | tf_op jit(solution)/shard_map/ppermute | solution.py:10
  61.7 2.5 %convolution_bitcast_fusion = f32[2,2,512,512]{3,2,0,1:T(8,128)S(1)} fusion(bf16[2,512,512,1]{2,1,0,3:T(8,128)(2,1)} %bitcast.34, bf16[4,2,512,512]{3,2,1,0:T(8,128)(2,1)S(1)} %copy-done.6, s32[]{:T(128)S(6)} %select_n.33), kind=kOutput, calls=%fused_computation | convolution fusion | flops 1073741824 | bytes 6291460 | tf_op jit(solution)/shard_map/cri,kio->ckro/dot_general | solution.py:56
  64.2 0.5 slice_subtract_fusion
  64.7 8.2 %collective-permute-done = bf16[2,2,256,512]{3,2,1,0:T(8,128)(2,1)} collective-permute-done((bf16[2,2,256,512]{3,2,1,0:T(8,128)(2,1)}, bf16[2,2,256,512]{3,2,1,0:T(8,128)(2,1)}, u32[]{:S(2)}, u32[]{:S(2)}) %collective-permute-start) | collective-permute-done | bytes 1048608 | tf_op jit(solution)/shard_map/ppermute | solution.py:10
  72.9 2.5 %convolution_bitcast_fusion.3 = f32[2,2,512,512]{3,2,0,1:T(8,128)S(1)} fusion(bf16[2,512,512,1]{2,1,0,3:T(8,128)(2,1)} %bitcast.10, bf16[4,2,512,512]{3,2,1,0:T(8,128)(2,1)S(1)} %copy-done.6, s32[]{:T(128)S(6)} %select_n.27), kind=kOutput, calls=%fused_computation.3 | convolution fusion | flops 1073741824 | bytes 6291460 | tf_op jit(solution)/shard_map/cri,kio->ckro/dot_general | solution.py:56
  75.4 0.0 copy-start.5
  75.5 0.0 copy-start.7
  75.5 0.5 slice_subtract_fusion.3
  76.0 0.3 broadcast_in_dim.26
  76.3 0.7 copy-done.5
  77.0 0.0 copy-done.7
  77.0 1.0 fusion.2
  78.0 0.2 slice_bitcast_fusion.3
  78.2 0.0 copy-done.2
  78.2 0.0 copy-done.4
  78.2 1.3 %add_reduce_fusion.1 = (f32[2,2]{1,0:T(2,128)S(1)}, f32[2,2]{1,0:T(2,128)S(1)}) fusion(f32[2,256,512]{2,1,0:T(8,128)S(1)} %get-tuple-element.23, f32[2,256,512]{2,1,0:T(8,128)S(1)} %get-tuple-element.21, f32[2,256,512]{2,1,0:T(8,128)S(1)} %get-tuple-element.22, f32[2,256,512]{2,1,0:T(8,128)S(1)} %get-tuple-element.20), kind=kLoop, calls=%fused_computation.13 | loop fusion | flops 4194296 | bytes 4194336 | tf_op jit(solution)/shard_map/reduce_sum | solution.py:65
  79.5 0.0 copy-start.3
  79.5 0.1 reshape.307
  79.5 0.1 reshape.308
  79.6 0.1 pad_maximum_fusion.1
  79.7 0.6 broadcast_in_dim.28
  80.3 8.4 %all-to-all-start = ((f32[16,1,10]{2,1,0:T(1,128)}), f32[16,1,10]{2,1,0:T(1,128)S(1)}, u32[]{:S(2)}, u32[]{:S(2)}) async-start(f32[16,1,10]{2,1,0:T(1,128)} %broadcast_in_dim.28), calls=%async_computation | async-start | bytes 16384 | tf_op jit(solution)/shard_map/all_to_all | solution.py:19
  88.7 1.1 %convert_bitcast_fusion = bf16[1,2,2,256,512]{4,3,2,1,0:T(8,128)(2,1)} fusion(f32[2,2,256,512]{3,2,1,0:T(8,128)S(1)} %fusion.2), kind=kLoop, calls=%fused_computation.34 | loop fusion | flops 524288 | bytes 3145728 | tf_op jit(solution)/shard_map/broadcast_in_dim | solution.py:74
  89.8 5.3 %all-to-all-done = f32[16,1,10]{2,1,0:T(1,128)S(1)} async-done(((f32[16,1,10]{2,1,0:T(1,128)}), f32[16,1,10]{2,1,0:T(1,128)S(1)}, u32[]{:S(2)}, u32[]{:S(2)}) %all-to-all-start) | async-done | bytes 672 | tf_op jit(solution)/shard_map/all_to_all | solution.py:19
  95.1 0.1 fusion.28
  95.2 0.1 slice_add_fusion.4
  95.3 0.1 reshape.309
  95.4 0.1 reshape.310
  95.4 0.1 broadcast_divide_fusion.1
  95.5 0.0 copy-done.3
  95.5 2.1 %subtract_reduce_fusion = (f32[2,256,512]{2,1,0:T(8,128)S(1)}, f32[2,256,512]{2,1,0:T(8,128)S(1)}) fusion(f32[2,2]{1,0:T(2,128)S(1)} %get-tuple-element.25, f32[2,2]{1,0:T(2,128)S(1)} %get-tuple-element.24, f32[2,256,512]{2,1,0:T(8,128)} %copy-done.4, f32[2,256,512]{2,1,0:T(8,128)S(1)} %copy-done.3), kind=kLoop, calls=%fused_computation.11 | loop fusion | flops 3670016 | bytes 4194336 | tf_op jit(solution)/shard_map/reduce_sum | solution.py:71
  97.6 0.6 fusion.14
  98.2 1.1 %pad_maximum_fusion = bf16[1,2,2,256,512]{4,3,2,1,0:T(8,128)(2,1)} fusion(bf16[1,1,2,256,512]{4,3,2,1,0:T(8,128)(2,1)S(1)} %get-tuple-element.19, bf16[1,1,2,256,512]{4,3,2,1,0:T(8,128)(2,1)S(1)} %get-tuple-element.18), kind=kLoop, calls=%fused_computation.24 | loop fusion | flops 524288 | bytes 2097152 | tf_op jit(solution)/shard_map/stack | solution.py:73
  (3 shorter events, 0.0 us)
Async XLA Ops:
  0.6 18.4 %copy-start = (bf16[128,128]{1,0:T(8,128)(2,1)S(1)}, bf16[128,128]{1,0:T(8,128)(2,1)}, u32[]{:S(2)}) copy-start(bf16[128,128]{1,0:T(8,128)(2,1)} %param.9) | copy-start | bytes 98308
  0.6 25.4 %collective-permute-start.1 = (bf16[2,2,256,512]{3,2,1,0:T(8,128)(2,1)}, bf16[2,2,256,512]{3,2,1,0:T(8,128)(2,1)}, u32[]{:S(2)}, u32[]{:S(2)}) collective-permute-start(bf16[2,2,256,512]{3,2,1,0:T(8,128)(2,1)} %bitcast.114), channel_id=1, source_target_pairs={{0,15},{1,0},{2,1},{3,2},{4,3},{5,4},{6,5},{7,6},{8,7},{9,8},{10,9... | collective-permute-start | bytes 3145736 | tf_op jit(solution)/shard_map/ppermute | solution.py:10
  6.1 28.0 %collective-permute-start.2 = (bf16[2,2,256,512]{3,2,1,0:T(8,128)(2,1)}, bf16[2,2,256,512]{3,2,1,0:T(8,128)(2,1)}, u32[]{:S(2)}, u32[]{:S(2)}) collective-permute-start(bf16[2,2,256,512]{3,2,1,0:T(8,128)(2,1)} %bitcast.115), channel_id=1, source_target_pairs={{0,1},{1,2},{2,3},{3,4},{4,5},{5,6},{6,7},{7,8},{8,9},{9,10},{10,1... | collective-permute-start | bytes 3145736 | tf_op jit(solution)/shard_map/ppermute | solution.py:10
  6.1 55.6 %collective-permute-start.3 = (bf16[2,2,256,512]{3,2,1,0:T(8,128)(2,1)}, bf16[2,2,256,512]{3,2,1,0:T(8,128)(2,1)}, u32[]{:S(2)}, u32[]{:S(2)}) collective-permute-start(bf16[2,2,256,512]{3,2,1,0:T(8,128)(2,1)} %bitcast.116), channel_id=1, source_target_pairs={{0,2},{1,3},{2,4},{3,5},{4,6},{5,7},{6,8},{7,9},{8,10},{9,11},{10,... | collective-permute-start | bytes 3145736 | tf_op jit(solution)/shard_map/ppermute | solution.py:10
  6.1 66.8 %collective-permute-start = (bf16[2,2,256,512]{3,2,1,0:T(8,128)(2,1)}, bf16[2,2,256,512]{3,2,1,0:T(8,128)(2,1)}, u32[]{:S(2)}, u32[]{:S(2)}) collective-permute-start(bf16[2,2,256,512]{3,2,1,0:T(8,128)(2,1)} %bitcast.117), channel_id=1, source_target_pairs={{0,14},{1,15},{2,0},{3,1},{4,2},{5,3},{6,4},{7,5},{8,6},{9,7},{10,... | collective-permute-start | bytes 3145736 | tf_op jit(solution)/shard_map/ppermute | solution.py:10
  19.4 1.6 %copy-start.8 = (s32[2,2]{1,0:T(2,128)S(1)}, s32[2,2]{1,0:T(2,128)}, u32[]{:S(2)}) copy-start(s32[2,2]{1,0:T(2,128)} %param.11) | copy-start | bytes 52
  19.4 4.7 %copy-start.1 = (bf16[1,2,2,256,512]{4,3,2,1,0:T(8,128)(2,1)S(1)}, bf16[1,2,2,256,512]{4,3,2,1,0:T(8,128)(2,1)}, u32[]{:S(2)}) copy-start(bf16[1,2,2,256,512]{4,3,2,1,0:T(8,128)(2,1)} %param.7) | copy-start | bytes 3145732
  24.7 2.9 %copy-start.6 = (bf16[4,2,512,512]{3,2,1,0:T(8,128)(2,1)S(1)}, bf16[4,2,512,512]{3,2,1,0:T(8,128)(2,1)}, u32[]{:S(2)}) copy-start(bf16[4,2,512,512]{3,2,1,0:T(8,128)(2,1)} %param.8) | copy-start | bytes 12582916
  24.9 53.3 %copy-start.2 = (f32[2,256,512]{2,1,0:T(8,128)}, f32[2,256,512]{2,1,0:T(8,128)S(1)}, u32[]{:S(2)}) copy-start(f32[2,256,512]{2,1,0:T(8,128)S(1)} %get-tuple-element.20) | copy-start | bytes 3145732
  24.9 53.3 %copy-start.4 = (f32[2,256,512]{2,1,0:T(8,128)}, f32[2,256,512]{2,1,0:T(8,128)S(1)}, u32[]{:S(2)}) copy-start(f32[2,256,512]{2,1,0:T(8,128)S(1)} %get-tuple-element.21) | copy-start | bytes 3145732
  75.4 1.6 %copy-start.5 = (f32[2,2,256,512]{3,2,1,0:T(8,128)S(1)}, f32[2,2,256,512]{3,2,1,0:T(8,128)}, u32[]{:S(2)}) copy-start(f32[2,2,256,512]{3,2,1,0:T(8,128)} %reshape.302) | copy-start | bytes 6291460
  75.5 1.6 %copy-start.7 = (bf16[256,256]{1,0:T(8,128)(2,1)S(1)}, bf16[256,256]{1,0:T(8,128)(2,1)}, u32[]{:S(2)}) copy-start(bf16[256,256]{1,0:T(8,128)(2,1)} %param.10) | copy-start | bytes 393220
  79.5 16.0 %copy-start.3 = (f32[2,256,512]{2,1,0:T(8,128)S(1)}, f32[2,256,512]{2,1,0:T(8,128)}, u32[]{:S(2)}) copy-start(f32[2,256,512]{2,1,0:T(8,128)} %copy-done.2) | copy-start | bytes 3145732
  80.3 14.8 %all-to-all-start = ((f32[16,1,10]{2,1,0:T(1,128)}), f32[16,1,10]{2,1,0:T(1,128)S(1)}, u32[]{:S(2)}, u32[]{:S(2)}) async-start(f32[16,1,10]{2,1,0:T(1,128)} %broadcast_in_dim.28), calls=%async_computation | async-start | bytes 16384 | tf_op jit(solution)/shard_map/all_to_all | solution.py:19

commit v4 on v3

--- a/solution.py
+++ b/solution.py
@@ -4,10 +4,24 @@
 from jax.sharding import PartitionSpec as P
 
 
-def passed_along(value, axis, steps):
+def passed_along(value, axis, steps, parity=None):
     count = lax.axis_size(axis)
-    pairs = [(source, (source + steps) % count) for source in range(count)]
+    sources = [source for source in range(count) if parity is None or source % 2 == parity]
+    pairs = [(source, (source + steps) % count) for source in sources]
     return lax.ppermute(value, axis, pairs)
+
+
+def two_away(block, below_one, above_one, axis):
+    if lax.axis_size(axis) % 2:
+        return passed_along(below_one, axis, 1), passed_along(above_one, axis, -1)
+    even = lax.axis_index(axis) % 2 == 0
+    far_below = passed_along(block, axis, 2, parity=0)
+    near_below = passed_along(below_one, axis, 1, parity=0)
+    far_above = passed_along(block, axis, -2, parity=1)
+    near_above = passed_along(above_one, axis, -1, parity=1)
+    below_two = jnp.where(even, far_below, near_below)
+    above_two = jnp.where(even, near_above, far_above)
+    return below_two, above_two
 
 
 def summed_over(axes, *parts):
@@ -37,8 +51,7 @@
     tile = width_x // tile_mask.shape[0]
     below_one = passed_along(block, "harm", 1)
     above_one = passed_along(block, "harm", -1)
-    below_two = passed_along(block, "harm", 2)
-    above_two = passed_along(block, "harm", -2)
+    below_two, above_two = two_away(block, below_one, above_one, "harm")
     rows = block.reshape(-1, ny)
     along_y = jnp.dot(rows, y_operator, preferred_element_type=jnp.float32).reshape(block.shape)
     full_mask = jnp.repeat(jnp.repeat(tile_mask, tile, axis=0), tile, axis=1).astype(jnp.bfloat16)

time: 99.9 us -> 83.9 us (0.84)
  waiting for transfers between devices: 42.8 us -> 9.25 us
  starting transfers between devices: 18.6 us -> 38.6 us
  matrix products: 11.4 us -> 8.94 us
  other arithmetic: 10.2 us -> 11.8 us
  local copies, waits for them, and re-layouts: 7.27 us -> 5.7 us
    ppermute x4 -> x6, waiting for transfers between devices: 37.5 us -> 3.94 us  [passed_along(): return lax.ppermute(value, axis, pairs)]
    ppermute x4 -> x6, starting transfers between devices: 10.3 us -> 31.6 us  [passed_along(): return lax.ppermute(value, axis, pairs)]
    dot_general x4, matrix products: 10 us -> 7.57 us  [body(): jnp.einsum('cri,kio->ckro', other, matrix, preferred_element_type=jnp.flo...]
    unnamed x18, local copies, waits for them, and re-layouts: 2.35 us -> 0.77 us
    select_n x0 -> x2, other arithmetic: none -> 1.52 us  [the longest x1 1.37 us: two_away(): below_two = jnp.where(even, far_below, near_below)]
    all_to_all x1, starting transfers between devices: 8.36 us -> 6.97 us  [summed_over(): gathered = lax.all_to_all(spread, axes, 0, 0, tiled=False)]
  transfers between devices with their start and end apart: 5 -> 7, of which waited for: 5 -> 2; matrix products, arithmetic and copies ran while one was open for 16% -> 19% of each run, Pallas kernels for 0% -> 0%
where the time goes in v4:
time: 83.9 us; the launch traced here: 83.4 us
  starting transfers between devices  38.6 us (46%)
  other arithmetic  11.8 us (14%)
  waiting for transfers between devices  9.25 us (11%)
  between operations  9.11 us (11%)
  matrix products  8.94 us (11%)
  local copies, waits for them, and re-layouts  5.7 us (7%)
    ppermute x6, starting transfers between devices, passed_along(): return lax.ppermute(value, axis, pairs)  31.6 us
    dot_general x4, matrix products, body(): jnp.einsum('cri,kio->ckro', other, matrix, preferred_element_type=jnp.flo...  7.57 us
    all_to_all x1, starting transfers between devices, summed_over(): gathered = lax.all_to_all(spread, axes, 0, 0, tiled=False)  6.97 us
    all_to_all x1, waiting for transfers between devices, summed_over(): gathered = lax.all_to_all(spread, axes, 0, 0, tiled=False)  5.3 us
    ppermute x6, waiting for transfers between devices, passed_along(): return lax.ppermute(value, axis, pairs)  3.94 us
    reduce_sum x1, other arithmetic, body(): proj_re = wr - jnp.sum(h_re * qr[:, None] - h_im * qi[:, None], axis=0)  2.13 us
    sub x4, other arithmetic, body(): real_part = prod[0, 0] - prod[1, 1]  1.92 us
    another operation x1, local copies, waits for them, and re-layouts, body(): rows = block.reshape(-1, ny)  1.7 us
  transfers between devices with their start and end apart: 7, of which 2 were waited for; matrix products, arithmetic and copies ran while one was open for 19% of the time, Pallas kernels for 0%

profile of v4, /device:TPU:0, one launch (start us, length us, event | category | flops | bytes accessed | tf_op | source)
XLA Modules:
  0.0 83.4 jit_solution(7359225664272202869)
XLA Ops:
  0.6 0.0 copy-start
  0.6 0.5 collective-permute-start.3
  1.1 4.4 %collective-permute-start.4 = (bf16[2,2,256,512]{3,2,1,0:T(8,128)(2,1)}, bf16[2,2,256,512]{3,2,1,0:T(8,128)(2,1)}, u32[]{:S(2)}, u32[]{:S(2)}) collective-permute-start(bf16[2,2,256,512]{3,2,1,0:T(8,128)(2,1)} %bitcast.115), channel_id=1, source_target_pairs={{0,2},{2,4},{4,6},{6,8},{8,10},{10,12},{12,14},{14,0},{16,18},{18,... | collective-permute-start | bytes 3145736 | tf_op jit(solution)/shard_map/ppermute | solution.py:11
  5.6 2.2 %collective-permute-start = (bf16[2,2,256,512]{3,2,1,0:T(8,128)(2,1)}, bf16[2,2,256,512]{3,2,1,0:T(8,128)(2,1)}, u32[]{:S(2)}, u32[]{:S(2)}) collective-permute-start(bf16[2,2,256,512]{3,2,1,0:T(8,128)(2,1)} %bitcast.116), channel_id=1, source_target_pairs={{0,15},{1,0},{2,1},{3,2},{4,3},{5,4},{6,5},{7,6},{8,7},{9,8},{10,9... | collective-permute-start | bytes 3145736 | tf_op jit(solution)/shard_map/ppermute | solution.py:11
  7.8 1.6 %collective-permute-start.2 = (bf16[2,2,256,512]{3,2,1,0:T(8,128)(2,1)}, bf16[2,2,256,512]{3,2,1,0:T(8,128)(2,1)}, u32[]{:S(2)}, u32[]{:S(2)}) collective-permute-start(bf16[2,2,256,512]{3,2,1,0:T(8,128)(2,1)} %bitcast.117), channel_id=1, source_target_pairs={{1,15},{3,1},{5,3},{7,5},{9,7},{11,9},{13,11},{15,13},{17,31},{19,... | collective-permute-start | bytes 3145736 | tf_op jit(solution)/shard_map/ppermute | solution.py:11
  9.5 1.4 %fusion.26 = (s32[]{:T(128)}, s32[]{:T(128)}, s32[]{:T(128)}, s32[]{:T(128)}) fusion(s32[4]{0:T(128)} %param.12), kind=kLoop, calls=%fused_computation.59 | loop fusion | flops 44 | bytes 32 | tf_op jit(solution)/shard_map/reduce_sum | solution.py:66
  15.9 1.7 %reshape_squeeze.3 = bf16[4096,128]{1,0:T(8,128)(2,1)S(1)} reshape(bf16[1,2,2,256,512]{4,3,2,1,0:T(8,128)(2,1)} %param.7) | data formatting | bytes 2097152 | tf_op jit(solution)/shard_map/reshape;squeeze | solution.py:55
  18.2 0.0 copy-done
  18.2 0.4 fusion.29
  18.7 0.0 copy-start.8
  18.7 0.0 copy-start.1
  18.7 1.5 %reshape.302 = f32[2,2,256,512]{3,2,1,0:T(8,128)} reshape(f32[4096,128]{1,0:T(8,128)S(1)} %fusion.29) | data formatting | bytes 4194304 | tf_op jit(solution)/shard_map/reshape | solution.py:56
  20.2 0.0 copy-done.8
  22.7 0.0 copy-done.1
  22.7 0.3 bitcast_convert_fusion
  23.0 0.3 add_reduce_fusion.2
  23.3 0.2 slice_bitcast_fusion.1
  23.5 0.0 copy-start.2
  23.5 0.0 copy-start.4
  23.5 3.9 %collective-permute-done.3 = bf16[2,2,256,512]{3,2,1,0:T(8,128)(2,1)} collective-permute-done((bf16[2,2,256,512]{3,2,1,0:T(8,128)(2,1)}, bf16[2,2,256,512]{3,2,1,0:T(8,128)(2,1)}, u32[]{:S(2)}, u32[]{:S(2)}) %collective-permute-start.3) | collective-permute-done | bytes 1048608 | tf_op jit(solution)/shard_map/ppermute | solution.py:11
  27.4 21.5 %collective-permute-start.5 = (bf16[2,2,256,512]{3,2,1,0:T(8,128)(2,1)}, bf16[2,2,256,512]{3,2,1,0:T(8,128)(2,1)S(1)}, u32[]{:S(2)}, u32[]{:S(2)}) collective-permute-start(bf16[2,2,256,512]{3,2,1,0:T(8,128)(2,1)} %collective-permute-done.3), channel_id=1, source_target_pairs={{0,1},{2,3},{4,5},{6,7},{8,9},{10,11},{12,13},{14,15},{16,17},{18,... | collective-permute-start | bytes 3145736 | tf_op jit(solution)/shard_map/ppermute | solution.py:11
  49.0 0.0 collective-permute-done
  49.0 0.0 copy-done.6
  49.0 2.5 %convolution_bitcast_fusion.2 = f32[2,2,512,512]{3,2,0,1:T(8,128)S(1)} fusion(bf16[2,512,512,1]{2,1,0,3:T(8,128)(2,1)} %bitcast.18, bf16[4,2,512,512]{3,2,1,0:T(8,128)(2,1)S(1)} %copy-done.6, s32[]{:T(128)S(6)} %select_n.51), kind=kOutput, calls=%fused_computation.2 | convolution fusion | flops 1073741824 | bytes 6291460 | tf_op jit(solution)/shard_map/cri,kio->ckro/dot_general | solution.py:69
  51.5 1.3 %collective-permute-start.1 = (bf16[2,2,256,512]{3,2,1,0:T(8,128)(2,1)}, bf16[2,2,256,512]{3,2,1,0:T(8,128)(2,1)S(1)}, u32[]{:S(2)}, u32[]{:S(2)}) collective-permute-start(bf16[2,2,256,512]{3,2,1,0:T(8,128)(2,1)} %collective-permute-done), channel_id=1, source_target_pairs={{1,0},{3,2},{5,4},{7,6},{9,8},{11,10},{13,12},{15,14},{17,16},{19,... | collective-permute-start | bytes 3145736 | tf_op jit(solution)/shard_map/ppermute | solution.py:11
  52.8 0.5 slice_subtract_fusion.2
  53.3 2.5 %convolution_bitcast_fusion.1 = f32[2,2,512,512]{3,2,0,1:T(8,128)S(1)} fusion(bf16[2,512,512,1]{2,1,0,3:T(8,128)(2,1)} %bitcast.26, bf16[4,2,512,512]{3,2,1,0:T(8,128)(2,1)S(1)} %copy-done.6, s32[]{:T(128)S(6)} %select_n.53), kind=kOutput, calls=%fused_computation.1 | convolution fusion | flops 1073741824 | bytes 6291460 | tf_op jit(solution)/shard_map/cri,kio->ckro/dot_general | solution.py:69
  55.8 0.5 slice_subtract_fusion.1
  56.3 0.0 collective-permute-done.4
  56.3 0.0 collective-permute-done.5
  56.3 1.4 %broadcast_select_fusion = bf16[2,2,256,512]{3,2,1,0:T(8,128)(2,1)S(1)} fusion(bf16[2,2,256,512]{3,2,1,0:T(8,128)(2,1)} %collective-permute-done.4, bf16[2,2,256,512]{3,2,1,0:T(8,128)(2,1)S(1)} %collective-permute-done.5, pred[]{:T(512)S(6)} %eq.18), kind=kLoop, calls=%fused_computation.39 | loop fusion | flops 524288 | bytes 3145729 | tf_op jit(solution)/shard_map/jit(_where)/select_n | solution.py:22
  57.7 1.3 %convolution_bitcast_fusion = f32[2,2,512,512]{3,2,0,1:T(8,128)S(1)} fusion(bf16[2,512,512,1]{2,1,0,3:T(8,128)(2,1)S(1)} %bitcast.119, bf16[4,2,512,512]{3,2,1,0:T(8,128)(2,1)S(1)} %copy-done.6, s32[]{:T(128)S(6)} %select_n.55), kind=kOutput, calls=%fused_computation | convolution fusion | flops 1073741824 | bytes 6291460 | tf_op jit(solution)/shard_map/cri,kio->ckro/dot_general | solution.py:69
  58.9 0.5 slice_subtract_fusion
  59.4 0.0 collective-permute-done.2
  59.4 0.0 collective-permute-done.1
  59.5 0.2 broadcast_select_fusion.1
  59.6 1.3 %convolution_bitcast_fusion.3 = f32[2,2,512,512]{3,2,0,1:T(8,128)S(1)} fusion(bf16[2,512,512,1]{2,1,0,3:T(8,128)(2,1)S(1)} %bitcast.118, bf16[4,2,512,512]{3,2,1,0:T(8,128)(2,1)S(1)} %copy-done.6, s32[]{:T(128)S(6)} %select_n.46), kind=kOutput, calls=%fused_computation.3 | convolution fusion | flops 1073741824 | bytes 6291460 | tf_op jit(solution)/shard_map/cri,kio->ckro/dot_general | solution.py:69
  60.9 0.0 copy-start.5
  60.9 0.0 copy-start.7
  60.9 0.5 slice_subtract_fusion.3
  61.4 0.3 broadcast_in_dim.26
  61.8 0.7 copy-done.5
  62.5 0.0 copy-done.7
  62.5 1.0 %fusion.2 = f32[2,2,256,512]{3,2,1,0:T(8,128)S(1)} fusion(f32[1,2,256,512]{3,2,1,0:T(8,128)S(1)} %bitcast.127, f32[1,2,256,512]{3,2,1,0:T(8,128)S(1)} %bitcast.126, f32[1,2,256,512]{3,2,1,0:T(8,128)S(1)} %bitcast.121, f32[1,2,256,512]{3,2,1,0:T(8,128)S(1)} %bitcast.120, f32[1,2,256,512]{3,2,1,0:T(8,128)S(1)} %bitcast.123, ...), kind=kOutput, calls=%fused_computation.7 | convolution fusion | flops 274989056 | bytes 13893636 | tf_op jit(solution)/shard_map/ab,cvbf->cvaf/dot_general | solution.py:59
  63.4 0.2 slice_bitcast_fusion.3
  63.6 0.0 copy-done.2
  63.6 0.0 copy-done.4
  63.6 1.3 %add_reduce_fusion.1 = (f32[2,2]{1,0:T(2,128)S(1)}, f32[2,2]{1,0:T(2,128)S(1)}) fusion(f32[2,256,512]{2,1,0:T(8,128)S(1)} %get-tuple-element.23, f32[2,256,512]{2,1,0:T(8,128)S(1)} %get-tuple-element.21, f32[2,256,512]{2,1,0:T(8,128)S(1)} %get-tuple-element.22, f32[2,256,512]{2,1,0:T(8,128)S(1)} %get-tuple-element.20), kind=kLoop, calls=%fused_computation.13 | loop fusion | flops 4194296 | bytes 4194336 | tf_op jit(solution)/shard_map/reduce_sum | solution.py:78
  64.9 0.1 reshape.307
  65.0 0.1 reshape.308
  65.1 0.1 pad_maximum_fusion.1
  65.2 0.6 broadcast_in_dim.28
  65.8 7.0 %all-to-all-start = ((f32[16,1,10]{2,1,0:T(1,128)}), f32[16,1,10]{2,1,0:T(1,128)S(1)}, u32[]{:S(2)}, u32[]{:S(2)}) async-start(f32[16,1,10]{2,1,0:T(1,128)} %broadcast_in_dim.28), calls=%async_computation | async-start | bytes 16384 | tf_op jit(solution)/shard_map/all_to_all | solution.py:33
  72.7 1.1 %convert_bitcast_fusion = bf16[1,2,2,256,512]{4,3,2,1,0:T(8,128)(2,1)} fusion(f32[2,2,256,512]{3,2,1,0:T(8,128)S(1)} %fusion.2), kind=kLoop, calls=%fused_computation.34 | loop fusion | flops 524288 | bytes 3145728 | tf_op jit(solution)/shard_map/broadcast_in_dim | solution.py:87
  73.8 5.3 %all-to-all-done = f32[16,1,10]{2,1,0:T(1,128)S(1)} async-done(((f32[16,1,10]{2,1,0:T(1,128)}), f32[16,1,10]{2,1,0:T(1,128)S(1)}, u32[]{:S(2)}, u32[]{:S(2)}) %all-to-all-start) | async-done | bytes 672 | tf_op jit(solution)/shard_map/all_to_all | solution.py:33
  79.2 0.1 fusion.28
  79.3 0.1 slice_add_fusion.4
  79.3 0.1 reshape.309
  79.4 0.1 reshape.310
  79.5 0.1 broadcast_divide_fusion.1
  79.6 0.0 copy-done.3
  79.6 2.1 %subtract_reduce_fusion = (f32[2,256,512]{2,1,0:T(8,128)S(1)}, f32[2,256,512]{2,1,0:T(8,128)S(1)}) fusion(f32[2,2]{1,0:T(2,128)S(1)} %get-tuple-element.25, f32[2,2]{1,0:T(2,128)S(1)} %get-tuple-element.24, f32[2,256,512]{2,1,0:T(8,128)} %copy-done.4, f32[2,256,512]{2,1,0:T(8,128)S(1)} %copy-done.3), kind=kLoop, calls=%fused_computation.11 | loop fusion | flops 3670016 | bytes 4194336 | tf_op jit(solution)/shard_map/reduce_sum | solution.py:84
  81.7 0.6 fusion.14
  82.3 1.1 %pad_maximum_fusion = bf16[1,2,2,256,512]{4,3,2,1,0:T(8,128)(2,1)} fusion(bf16[1,1,2,256,512]{4,3,2,1,0:T(8,128)(2,1)S(1)} %get-tuple-element.19, bf16[1,1,2,256,512]{4,3,2,1,0:T(8,128)(2,1)S(1)} %get-tuple-element.18), kind=kLoop, calls=%fused_computation.24 | loop fusion | flops 524288 | bytes 2097152 | tf_op jit(solution)/shard_map/stack | solution.py:86
  (5 shorter events, 0.1 us)
Async XLA Ops:
  0.6 17.6 %copy-start = (bf16[128,128]{1,0:T(8,128)(2,1)S(1)}, bf16[128,128]{1,0:T(8,128)(2,1)}, u32[]{:S(2)}) copy-start(bf16[128,128]{1,0:T(8,128)(2,1)} %param.9) | copy-start | bytes 98308
  0.6 26.8 %collective-permute-start.3 = (bf16[2,2,256,512]{3,2,1,0:T(8,128)(2,1)}, bf16[2,2,256,512]{3,2,1,0:T(8,128)(2,1)}, u32[]{:S(2)}, u32[]{:S(2)}) collective-permute-start(bf16[2,2,256,512]{3,2,1,0:T(8,128)(2,1)} %bitcast.114), channel_id=1, source_target_pairs={{0,1},{1,2},{2,3},{3,4},{4,5},{5,6},{6,7},{7,8},{8,9},{9,10},{10,1... | collective-permute-start | bytes 3145736 | tf_op jit(solution)/shard_map/ppermute | solution.py:11
  1.1 55.1 %collective-permute-start.4 = (bf16[2,2,256,512]{3,2,1,0:T(8,128)(2,1)}, bf16[2,2,256,512]{3,2,1,0:T(8,128)(2,1)}, u32[]{:S(2)}, u32[]{:S(2)}) collective-permute-start(bf16[2,2,256,512]{3,2,1,0:T(8,128)(2,1)} %bitcast.115), channel_id=1, source_target_pairs={{0,2},{2,4},{4,6},{6,8},{8,10},{10,12},{12,14},{14,0},{16,18},{18,... | collective-permute-start | bytes 3145736 | tf_op jit(solution)/shard_map/ppermute | solution.py:11
  5.6 43.4 %collective-permute-start = (bf16[2,2,256,512]{3,2,1,0:T(8,128)(2,1)}, bf16[2,2,256,512]{3,2,1,0:T(8,128)(2,1)}, u32[]{:S(2)}, u32[]{:S(2)}) collective-permute-start(bf16[2,2,256,512]{3,2,1,0:T(8,128)(2,1)} %bitcast.116), channel_id=1, source_target_pairs={{0,15},{1,0},{2,1},{3,2},{4,3},{5,4},{6,5},{7,6},{8,7},{9,8},{10,9... | collective-permute-start | bytes 3145736 | tf_op jit(solution)/shard_map/ppermute | solution.py:11
  7.8 51.6 %collective-permute-start.2 = (bf16[2,2,256,512]{3,2,1,0:T(8,128)(2,1)}, bf16[2,2,256,512]{3,2,1,0:T(8,128)(2,1)}, u32[]{:S(2)}, u32[]{:S(2)}) collective-permute-start(bf16[2,2,256,512]{3,2,1,0:T(8,128)(2,1)} %bitcast.117), channel_id=1, source_target_pairs={{1,15},{3,1},{5,3},{7,5},{9,7},{11,9},{13,11},{15,13},{17,31},{19,... | collective-permute-start | bytes 3145736 | tf_op jit(solution)/shard_map/ppermute | solution.py:11
  18.7 1.6 %copy-start.8 = (s32[2,2]{1,0:T(2,128)S(1)}, s32[2,2]{1,0:T(2,128)}, u32[]{:S(2)}) copy-start(s32[2,2]{1,0:T(2,128)} %param.11) | copy-start | bytes 52
  18.7 4.1 %copy-start.1 = (bf16[1,2,2,256,512]{4,3,2,1,0:T(8,128)(2,1)S(1)}, bf16[1,2,2,256,512]{4,3,2,1,0:T(8,128)(2,1)}, u32[]{:S(2)}) copy-start(bf16[1,2,2,256,512]{4,3,2,1,0:T(8,128)(2,1)} %param.7) | copy-start | bytes 3145732
  23.3 25.7 %copy-start.6 = (bf16[4,2,512,512]{3,2,1,0:T(8,128)(2,1)S(1)}, bf16[4,2,512,512]{3,2,1,0:T(8,128)(2,1)}, u32[]{:S(2)}) copy-start(bf16[4,2,512,512]{3,2,1,0:T(8,128)(2,1)} %param.8) | copy-start | bytes 12582916
  23.5 40.1 %copy-start.2 = (f32[2,256,512]{2,1,0:T(8,128)}, f32[2,256,512]{2,1,0:T(8,128)S(1)}, u32[]{:S(2)}) copy-start(f32[2,256,512]{2,1,0:T(8,128)S(1)} %get-tuple-element.20) | copy-start | bytes 3145732
  23.5 40.1 %copy-start.4 = (f32[2,256,512]{2,1,0:T(8,128)}, f32[2,256,512]{2,1,0:T(8,128)S(1)}, u32[]{:S(2)}) copy-start(f32[2,256,512]{2,1,0:T(8,128)S(1)} %get-tuple-element.21) | copy-start | bytes 3145732
  27.4 28.8 %collective-permute-start.5 = (bf16[2,2,256,512]{3,2,1,0:T(8,128)(2,1)}, bf16[2,2,256,512]{3,2,1,0:T(8,128)(2,1)S(1)}, u32[]{:S(2)}, u32[]{:S(2)}) collective-permute-start(bf16[2,2,256,512]{3,2,1,0:T(8,128)(2,1)} %collective-permute-done.3), channel_id=1, source_target_pairs={{0,1},{2,3},{4,5},{6,7},{8,9},{10,11},{12,13},{14,15},{16,17},{18,... | collective-permute-start | bytes 3145736 | tf_op jit(solution)/shard_map/ppermute | solution.py:11
  51.5 8.0 %collective-permute-start.1 = (bf16[2,2,256,512]{3,2,1,0:T(8,128)(2,1)}, bf16[2,2,256,512]{3,2,1,0:T(8,128)(2,1)S(1)}, u32[]{:S(2)}, u32[]{:S(2)}) collective-permute-start(bf16[2,2,256,512]{3,2,1,0:T(8,128)(2,1)} %collective-permute-done), channel_id=1, source_target_pairs={{1,0},{3,2},{5,4},{7,6},{9,8},{11,10},{13,12},{15,14},{17,16},{19,... | collective-permute-start | bytes 3145736 | tf_op jit(solution)/shard_map/ppermute | solution.py:11
  60.9 1.6 %copy-start.5 = (f32[2,2,256,512]{3,2,1,0:T(8,128)S(1)}, f32[2,2,256,512]{3,2,1,0:T(8,128)}, u32[]{:S(2)}) copy-start(f32[2,2,256,512]{3,2,1,0:T(8,128)} %reshape.302) | copy-start | bytes 6291460
  60.9 1.6 %copy-start.7 = (bf16[256,256]{1,0:T(8,128)(2,1)S(1)}, bf16[256,256]{1,0:T(8,128)(2,1)}, u32[]{:S(2)}) copy-start(bf16[256,256]{1,0:T(8,128)(2,1)} %param.10) | copy-start | bytes 393220
  64.9 14.7 %copy-start.3 = (f32[2,256,512]{2,1,0:T(8,128)S(1)}, f32[2,256,512]{2,1,0:T(8,128)}, u32[]{:S(2)}) copy-start(f32[2,256,512]{2,1,0:T(8,128)} %copy-done.2) | copy-start | bytes 3145732
  65.8 13.4 %all-to-all-start = ((f32[16,1,10]{2,1,0:T(1,128)}), f32[16,1,10]{2,1,0:T(1,128)S(1)}, u32[]{:S(2)}, u32[]{:S(2)}) async-start(f32[16,1,10]{2,1,0:T(1,128)} %broadcast_in_dim.28), calls=%async_computation | async-start | bytes 16384 | tf_op jit(solution)/shard_map/all_to_all | solution.py:33

commit v5 on v3

--- a/solution.py
+++ b/solution.py
@@ -35,10 +35,12 @@
     harmonics = lax.axis_size("harm")
     position = lax.axis_index("harm")
     tile = width_x // tile_mask.shape[0]
-    below_one = passed_along(block, "harm", 1)
-    above_one = passed_along(block, "harm", -1)
-    below_two = passed_along(block, "harm", 2)
-    above_two = passed_along(block, "harm", -2)
+    pieces = 2 if width_x % 16 == 0 else 1
+    chunks = jnp.split(block, pieces, axis=2)
+    ones_below = [passed_along(chunk, "harm", 1) for chunk in chunks]
+    ones_above = [passed_along(chunk, "harm", -1) for chunk in chunks]
+    twos_below = [passed_along(chunk, "harm", 1) for chunk in ones_below]
+    twos_above = [passed_along(chunk, "harm", -1) for chunk in ones_above]
     rows = block.reshape(-1, ny)
     along_y = jnp.dot(rows, y_operator, preferred_element_type=jnp.float32).reshape(block.shape)
     full_mask = jnp.repeat(jnp.repeat(tile_mask, tile, axis=0), tile, axis=1).astype(jnp.bfloat16)
@@ -47,16 +49,22 @@
     centered = (position - harmonics // 2).astype(jnp.float32) + detuning[0]
     lam = -(centered * centered) / (4.0 * harmonics)
     image = along_y + along_x + lam * block.astype(jnp.float32)
-    sources = (above_two, above_one, below_one, below_two)
+    sources = (twos_above, ones_above, ones_below, twos_below)
     counter = jnp.arange(4, dtype=jnp.int32)
+    coupled = [None] * pieces
     for place in range(4):
         slot = jnp.sum(jnp.where(slot_offsets == place, counter, 0))
         matrix = lax.dynamic_index_in_dim(coupling, slot, 0, keepdims=False)
-        other = sources[place].reshape(2, vecs * width_x, width_fy)
-        prod = jnp.einsum("cri,kio->ckro", other, matrix, preferred_element_type=jnp.float32)
-        real_part = prod[0, 0] - prod[1, 1]
-        imag_part = prod[0, 1] + prod[1, 0]
-        image = image + jnp.stack([real_part, imag_part]).reshape(block.shape)
+        for piece in range(pieces):
+            other = sources[place][piece]
+            rows_shape = other.shape
+            other = other.reshape(2, -1, width_fy)
+            prod = jnp.einsum("cri,kio->ckro", other, matrix, preferred_element_type=jnp.float32)
+            real_part = prod[0, 0] - prod[1, 1]
+            imag_part = prod[0, 1] + prod[1, 0]
+            term = jnp.stack([real_part, imag_part]).reshape(rows_shape)
+            coupled[piece] = term if coupled[piece] is None else coupled[piece] + term
+    image = image + jnp.concatenate(coupled, axis=2)
     qfull = block.astype(jnp.float32)
     qr = qfull[0]
     qi = qfull[1]

time: 99.9 us -> 87.8 us (0.88)
  waiting for transfers between devices: 42.8 us -> 12.2 us
  starting transfers between devices: 18.6 us -> 30.3 us
  local copies, waits for them, and re-layouts: 7.27 us -> 12.1 us
  matrix products: 11.4 us -> 12.6 us
    ppermute x4 -> x8, waiting for transfers between devices: 37.5 us -> 7.01 us  [passed_along(): return lax.ppermute(value, axis, pairs)]
    ppermute x4 -> x8, starting transfers between devices: 10.3 us -> 18.9 us  [passed_along(): return lax.ppermute(value, axis, pairs)]
    all_to_all x1, starting transfers between devices: 8.36 us -> 11.5 us  [summed_over(): gathered = lax.all_to_all(spread, axes, 0, 0, tiled=False)]
    split x0 -> x1, local copies, waits for them, and re-layouts: none -> 2.32 us  [body(): chunks = jnp.split(block, pieces, axis=2)]
    mul x2, local copies, waits for them, and re-layouts: 0.34 us -> 1.65 us  [body(): qr[:, None] * wr[None, :] + qi[:, None] * wi[None, :]]
    dot_general x1, matrix products: 0.42 us -> 1.71 us  [body(): jnp.dot(rows, y_operator, preferred_element_type=jnp.float32)]
    reshape x1, local copies, waits for them, and re-layouts: 1.53 us -> 2.76 us  [body(): jnp.dot(rows, y_operator, preferred_element_type=jnp.float32)]
    add x0 -> x1, other arithmetic: none -> 1.06 us  [body(): coupled[piece] = term if coupled[piece] is None else coupled[piece] + term]
  transfers between devices with their start and end apart: 5 -> 9, of which waited for: 5 -> 3; matrix products, arithmetic and copies ran while one was open for 16% -> 22% of each run, Pallas kernels for 0% -> 0%
where the time goes in v5:
time: 87.8 us; the launch traced here: 87.2 us
  starting transfers between devices  30.3 us (35%)
  matrix products  12.6 us (14%)
  waiting for transfers between devices  12.2 us (14%)
  local copies, waits for them, and re-layouts  12.1 us (14%)
  other arithmetic  10.5 us (12%)
  between operations  9.43 us (11%)
    ppermute x8, starting transfers between devices, passed_along(): return lax.ppermute(value, axis, pairs)  18.9 us
    all_to_all x1, starting transfers between devices, summed_over(): gathered = lax.all_to_all(spread, axes, 0, 0, tiled=False)  11.5 us
    dot_general x8, matrix products, body(): jnp.einsum('cri,kio->ckro', other, matrix, preferred_element_type=jnp.flo...  10.3 us
    ppermute x8, waiting for transfers between devices, passed_along(): return lax.ppermute(value, axis, pairs)  7.01 us
    all_to_all x1, waiting for transfers between devices, summed_over(): gathered = lax.all_to_all(spread, axes, 0, 0, tiled=False)  5.23 us
    reshape x1, local copies, waits for them, and re-layouts, body(): jnp.dot(rows, y_operator, preferred_element_type=jnp.float32)  2.76 us
    unnamed x20, local copies, waits for them, and re-layouts  2.61 us
    split x1, local copies, waits for them, and re-layouts, body(): chunks = jnp.split(block, pieces, axis=2)  2.32 us
  transfers between devices with their start and end apart: 9, of which 3 were waited for; matrix products, arithmetic and copies ran while one was open for 22% of the time, Pallas kernels for 0%

profile of v5, /device:TPU:0, one launch (start us, length us, event | category | flops | bytes accessed | tf_op | source)
XLA Modules:
  0.0 87.2 jit_solution(3536261825073323269)
XLA Ops:
  0.6 0.0 copy-start
  0.7 2.3 %fusion.41 = (bf16[2,2,128,512]{3,2,1,0:T(8,128)(2,1)}, bf16[2,2,128,512]{3,2,1,0:T(8,128)(2,1)}) fusion(bf16[2,2,256,512]{3,2,1,0:T(8,128)(2,1)} %bitcast.154), kind=kLoop, calls=%fused_computation.91 | loop fusion | bytes 2097152 | tf_op jit(solution)/shard_map/split | solution.py:39
  3.0 5.4 %collective-permute-start.4 = (bf16[2,2,128,512]{3,2,1,0:T(8,128)(2,1)}, bf16[2,2,128,512]{3,2,1,0:T(8,128)(2,1)}, u32[]{:S(2)}, u32[]{:S(2)}) collective-permute-start(bf16[2,2,128,512]{3,2,1,0:T(8,128)(2,1)} %get-tuple-element.33), channel_id=1, source_target_pairs={{0,15},{1,0},{2,1},{3,2},{4,3},{5,4},{6,5},{7,6},{8,7},{9,8},{10,9... | collective-permute-start | bytes 1572872 | tf_op jit(solution)/shard_map/ppermute | solution.py:10
  8.4 0.0 collective-permute-start.2
  8.4 4.5 %collective-permute-start = (bf16[2,2,128,512]{3,2,1,0:T(8,128)(2,1)}, bf16[2,2,128,512]{3,2,1,0:T(8,128)(2,1)}, u32[]{:S(2)}, u32[]{:S(2)}) collective-permute-start(bf16[2,2,128,512]{3,2,1,0:T(8,128)(2,1)} %get-tuple-element.32), channel_id=1, source_target_pairs={{0,15},{1,0},{2,1},{3,2},{4,3},{5,4},{6,5},{7,6},{8,7},{9,8},{10,9... | collective-permute-start | bytes 1572872 | tf_op jit(solution)/shard_map/ppermute | solution.py:10
  12.9 1.4 %reshape_squeeze.3 = bf16[4096,128]{1,0:T(8,128)(2,1)} reshape(bf16[1,2,2,256,512]{4,3,2,1,0:T(8,128)(2,1)S(1)} %copy-done.1) | data formatting | bytes 2097152 | tf_op jit(solution)/shard_map/reshape;squeeze | solution.py:44
  14.3 0.3 bitcast_convert_fusion
  14.6 0.9 %copy-done.6 = bf16[4096,128]{1,0:T(8,128)(2,1)S(1)} copy-done((bf16[4096,128]{1,0:T(8,128)(2,1)S(1)}, bf16[4096,128]{1,0:T(8,128)(2,1)}, u32[]{:S(2)}) %copy-start.6) | copy-done | bytes 1048600
  15.6 1.7 %fusion.43 = f32[4096,128]{1,0:T(8,128)} fusion(bf16[4096,128]{1,0:T(8,128)(2,1)S(1)} %copy-done.6, bf16[128,128]{1,0:T(8,128)(2,1)S(1)} %copy-done), kind=kOutput, calls=%fused_computation.93 | convolution fusion | flops 134217728 | bytes 3178496 | tf_op jit(solution)/shard_map/dot_general | solution.py:45
  17.3 1.5 %slice_bitcast_fusion.1 = (f32[2,256,512]{2,1,0:T(8,128)}, f32[2,256,512]{2,1,0:T(8,128)}) fusion(f32[2,2,256,512]{3,2,1,0:T(8,128)S(1)} %bitcast_convert_fusion), kind=kLoop, calls=%fused_computation.16 | loop fusion | bytes 4194304 | tf_op jit(solution)/shard_map/mul | solution.py:73
  18.7 0.7 fusion.39
  24.7 0.0 copy-start.9
  24.7 2.8 %reshape.486 = f32[2,2,256,512]{3,2,1,0:T(8,128)} reshape(f32[4096,128]{1,0:T(8,128)} %fusion.43) | data formatting | bytes 4194304 | tf_op jit(solution)/shard_map/reshape | solution.py:45
  30.8 0.0 copy-start.2
  30.8 0.3 add_reduce_fusion.2
  31.1 2.2 %convolution_bitcast_fusion.6 = f32[2,2,256,512]{3,2,0,1:T(8,128)S(1)} fusion(bf16[2,256,512,1]{2,1,0,3:T(8,128)(2,1)} %bitcast.18, bf16[4,2,512,512]{3,2,1,0:T(8,128)(2,1)} %param.8, s32[]{:T(128)S(6)} %select_n.29), kind=kOutput, calls=%fused_computation.13 | convolution fusion | flops 536870912 | bytes 3670020 | tf_op jit(solution)/shard_map/cri,kio->ckro/dot_general | solution.py:62
  33.3 0.0 collective-permute-done.2
  33.3 0.1 copy-done.2
  33.4 1.7 %convolution_bitcast_fusion.5 = f32[2,2,256,512]{3,2,0,1:T(8,128)S(1)} fusion(bf16[2,256,512,1]{2,1,0,3:T(8,128)(2,1)} %bitcast.26, bf16[4,2,512,512]{3,2,1,0:T(8,128)(2,1)S(1)} %copy-done.2, s32[]{:T(128)S(6)} %select_n.31), kind=kOutput, calls=%fused_computation.12 | convolution fusion | flops 536870912 | bytes 3670020 | tf_op jit(solution)/shard_map/cri,kio->ckro/dot_general | solution.py:62
  35.2 0.2 slice_subtract_fusion.6
  35.4 0.2 slice_subtract_fusion.5
  35.6 0.0 collective-permute-done.4
  35.6 1.8 %convolution_bitcast_fusion.2 = f32[2,2,256,512]{3,2,0,1:T(8,128)S(1)} fusion(bf16[2,256,512,1]{2,1,0,3:T(8,128)(2,1)} %bitcast.46, bf16[4,2,512,512]{3,2,1,0:T(8,128)(2,1)S(1)} %copy-done.2, s32[]{:T(128)S(6)} %select_n.29), kind=kOutput, calls=%fused_computation.9 | convolution fusion | flops 536870912 | bytes 3670020 | tf_op jit(solution)/shard_map/cri,kio->ckro/dot_general | solution.py:62
  37.4 1.8 %convolution_bitcast_fusion.1 = f32[2,2,256,512]{3,2,0,1:T(8,128)S(1)} fusion(bf16[2,256,512,1]{2,1,0,3:T(8,128)(2,1)} %bitcast.52, bf16[4,2,512,512]{3,2,1,0:T(8,128)(2,1)S(1)} %copy-done.2, s32[]{:T(128)S(6)} %select_n.31), kind=kOutput, calls=%fused_computation.8 | convolution fusion | flops 536870912 | bytes 3670020 | tf_op jit(solution)/shard_map/cri,kio->ckro/dot_general | solution.py:62
  39.1 0.1 collective-permute-start.3
  39.2 4.4 %collective-permute-start.5 = (bf16[2,2,128,512]{3,2,1,0:T(8,128)(2,1)}, bf16[2,2,128,512]{3,2,1,0:T(8,128)(2,1)S(1)}, u32[]{:S(2)}, u32[]{:S(2)}) collective-permute-start(bf16[2,2,128,512]{3,2,1,0:T(8,128)(2,1)} %collective-permute-done.4), channel_id=1, source_target_pairs={{0,15},{1,0},{2,1},{3,2},{4,3},{5,4},{6,5},{7,6},{8,7},{9,8},{10,9... | collective-permute-start | bytes 1572872 | tf_op jit(solution)/shard_map/ppermute | solution.py:10
  43.6 4.4 %collective-permute-start.1 = (bf16[2,2,128,512]{3,2,1,0:T(8,128)(2,1)}, bf16[2,2,128,512]{3,2,1,0:T(8,128)(2,1)S(1)}, u32[]{:S(2)}, u32[]{:S(2)}) collective-permute-start(bf16[2,2,128,512]{3,2,1,0:T(8,128)(2,1)} %collective-permute-done), channel_id=1, source_target_pairs={{0,15},{1,0},{2,1},{3,2},{4,3},{5,4},{6,5},{7,6},{8,7},{9,8},{10,9... | collective-permute-start | bytes 1572872 | tf_op jit(solution)/shard_map/ppermute | solution.py:10
  48.1 0.2 slice_subtract_fusion.2
  48.3 0.2 slice_subtract_fusion.1
  48.5 2.3 %collective-permute-done.3 = bf16[2,2,128,512]{3,2,1,0:T(8,128)(2,1)S(1)} collective-permute-done((bf16[2,2,128,512]{3,2,1,0:T(8,128)(2,1)}, bf16[2,2,128,512]{3,2,1,0:T(8,128)(2,1)S(1)}, u32[]{:S(2)}, u32[]{:S(2)}) %collective-permute-start.3) | collective-permute-done | bytes 524320 | tf_op jit(solution)/shard_map/ppermute | solution.py:10
  50.8 0.7 convolution_bitcast_fusion.4
  51.5 0.2 slice_subtract_fusion.4
  51.7 4.7 %collective-permute-done.7 = bf16[2,2,128,512]{3,2,1,0:T(8,128)(2,1)S(1)} collective-permute-done((bf16[2,2,128,512]{3,2,1,0:T(8,128)(2,1)}, bf16[2,2,128,512]{3,2,1,0:T(8,128)(2,1)S(1)}, u32[]{:S(2)}, u32[]{:S(2)}) %collective-permute-start.7) | collective-permute-done | bytes 524320 | tf_op jit(solution)/shard_map/ppermute | solution.py:10
  56.4 0.7 convolution_bitcast_fusion
  57.2 0.7 convolution_bitcast_fusion.3
  57.9 0.2 slice_subtract_fusion.3
  58.1 0.2 slice_subtract_fusion
  58.3 0.7 convolution_bitcast_fusion.7
  59.0 0.2 slice_subtract_fusion.7
  59.3 0.0 copy-start.7
  59.3 1.1 %fusion.2 = (f32[2,2,128,512]{3,2,1,0:T(8,128)S(1)}, f32[2,2,128,512]{3,2,1,0:T(8,128)S(1)}) fusion(f32[1,2,128,512]{3,2,1,0:T(8,128)S(1)} %bitcast.170, f32[1,2,128,512]{3,2,1,0:T(8,128)S(1)} %bitcast.169, f32[1,2,128,512]{3,2,1,0:T(8,128)S(1)} %bitcast.156, f32[1,2,128,512]{3,2,1,0:T(8,128)S(1)} %bitcast.155, f32[1,2,128,512]{3,2,1,0:T(8,128)S(1)} %bitcast.158, ...), kind=kLoop, calls=%fused_computation.19 | loop fusion | flops 3670016 | bytes 10485760 | tf_op jit(solution)/shard_map/add | solution.py:66
  60.4 0.3 broadcast_in_dim.26
  60.7 0.1 copy-done.5
  60.8 0.6 maximum_add_fusion
  61.4 0.0 copy-start.3
  61.5 0.2 slice_bitcast_fusion.3
  61.6 1.0 %copy-done.3 = f32[2,256,512]{2,1,0:T(8,128)S(1)} copy-done((f32[2,256,512]{2,1,0:T(8,128)S(1)}, f32[2,256,512]{2,1,0:T(8,128)}, u32[]{:S(2)}) %copy-start.3) | copy-done | bytes 1048600
  62.7 0.3 copy-done.4
  63.0 1.3 %add_reduce_fusion.1 = (f32[2,2]{1,0:T(2,128)S(1)}, f32[2,2]{1,0:T(2,128)S(1)}) fusion(f32[2,256,512]{2,1,0:T(8,128)S(1)} %get-tuple-element.15, f32[2,256,512]{2,1,0:T(8,128)S(1)} %copy-done.4, f32[2,256,512]{2,1,0:T(8,128)S(1)} %get-tuple-element.14, f32[2,256,512]{2,1,0:T(8,128)S(1)} %copy-done.3), kind=kLoop, calls=%fused_computation.6 | loop fusion | flops 4194296 | bytes 4194336 | tf_op jit(solution)/shard_map/reduce_sum | solution.py:73
  64.3 0.1 reshape.495
  64.4 0.1 reshape.496
  64.4 0.1 pad_maximum_fusion.1
  64.5 0.6 broadcast_in_dim.28
  65.1 11.5 %all-to-all-start = ((f32[16,1,10]{2,1,0:T(1,128)}), f32[16,1,10]{2,1,0:T(1,128)S(1)}, u32[]{:S(2)}, u32[]{:S(2)}) async-start(f32[16,1,10]{2,1,0:T(1,128)} %broadcast_in_dim.28), calls=%async_computation | async-start | bytes 16384 | tf_op jit(solution)/shard_map/all_to_all | solution.py:19
  76.6 1.1 %convert_bitcast_fusion = bf16[1,2,2,256,512]{4,3,2,1,0:T(8,128)(2,1)} fusion(f32[2,2,256,512]{3,2,1,0:T(8,128)S(1)} %maximum_add_fusion), kind=kLoop, calls=%fused_computation.37 | loop fusion | flops 524288 | bytes 3145728 | tf_op jit(solution)/shard_map/broadcast_in_dim | solution.py:82
  77.7 5.2 %all-to-all-done = f32[16,1,10]{2,1,0:T(1,128)S(1)} async-done(((f32[16,1,10]{2,1,0:T(1,128)}), f32[16,1,10]{2,1,0:T(1,128)S(1)}, u32[]{:S(2)}, u32[]{:S(2)}) %all-to-all-start) | async-done | bytes 672 | tf_op jit(solution)/shard_map/all_to_all | solution.py:19
  83.0 0.1 fusion.42
  83.1 0.1 slice_add_fusion.8
  83.1 0.1 reshape.497
  83.2 0.1 reshape.498
  83.3 0.1 broadcast_divide_fusion.1
  83.4 2.1 %subtract_reduce_fusion = (f32[2,256,512]{2,1,0:T(8,128)S(1)}, f32[2,256,512]{2,1,0:T(8,128)S(1)}) fusion(f32[2,2]{1,0:T(2,128)S(1)} %get-tuple-element.35, f32[2,2]{1,0:T(2,128)S(1)} %get-tuple-element.34, f32[2,256,512]{2,1,0:T(8,128)} %get-tuple-element.13, f32[2,256,512]{2,1,0:T(8,128)S(1)} %copy-done.3), kind=kLoop, calls=%fused_computation.4 | loop fusion | flops 3670016 | bytes 4194336 | tf_op jit(solution)/shard_map/reduce_sum | solution.py:79
  85.5 0.6 fusion.23
  86.1 1.1 %pad_maximum_fusion = bf16[1,2,2,256,512]{4,3,2,1,0:T(8,128)(2,1)} fusion(bf16[1,1,2,256,512]{4,3,2,1,0:T(8,128)(2,1)S(1)} %get-tuple-element.11, bf16[1,1,2,256,512]{4,3,2,1,0:T(8,128)(2,1)S(1)} %get-tuple-element.10), kind=kLoop, calls=%fused_computation.23 | loop fusion | flops 524288 | bytes 2097152 | tf_op jit(solution)/shard_map/stack | solution.py:81
  (19 shorter events, 0.1 us)
Async XLA Ops:
  0.6 14.0 %copy-start = (bf16[128,128]{1,0:T(8,128)(2,1)S(1)}, bf16[128,128]{1,0:T(8,128)(2,1)}, u32[]{:S(2)}) copy-start(bf16[128,128]{1,0:T(8,128)(2,1)} %param.9) | copy-start | bytes 98308
  0.6 12.3 %copy-start.1 = (bf16[1,2,2,256,512]{4,3,2,1,0:T(8,128)(2,1)S(1)}, bf16[1,2,2,256,512]{4,3,2,1,0:T(8,128)(2,1)}, u32[]{:S(2)}) copy-start(bf16[1,2,2,256,512]{4,3,2,1,0:T(8,128)(2,1)} %param.7) | copy-start | bytes 3145732
  3.0 32.6 %collective-permute-start.4 = (bf16[2,2,128,512]{3,2,1,0:T(8,128)(2,1)}, bf16[2,2,128,512]{3,2,1,0:T(8,128)(2,1)}, u32[]{:S(2)}, u32[]{:S(2)}) collective-permute-start(bf16[2,2,128,512]{3,2,1,0:T(8,128)(2,1)} %get-tuple-element.33), channel_id=1, source_target_pairs={{0,15},{1,0},{2,1},{3,2},{4,3},{5,4},{6,5},{7,6},{8,7},{9,8},{10,9... | collective-permute-start | bytes 1572872 | tf_op jit(solution)/shard_map/ppermute | solution.py:10
  8.4 29.0 %collective-permute-start.6 = (bf16[2,2,128,512]{3,2,1,0:T(8,128)(2,1)}, bf16[2,2,128,512]{3,2,1,0:T(8,128)(2,1)}, u32[]{:S(2)}, u32[]{:S(2)}) collective-permute-start(bf16[2,2,128,512]{3,2,1,0:T(8,128)(2,1)} %get-tuple-element.33), channel_id=1, source_target_pairs={{0,1},{1,2},{2,3},{3,4},{4,5},{5,6},{6,7},{7,8},{8,9},{9,10},{10,1... | collective-permute-start | bytes 1572872 | tf_op jit(solution)/shard_map/ppermute | solution.py:10
  8.4 24.9 %collective-permute-start.2 = (bf16[2,2,128,512]{3,2,1,0:T(8,128)(2,1)}, bf16[2,2,128,512]{3,2,1,0:T(8,128)(2,1)}, u32[]{:S(2)}, u32[]{:S(2)}) collective-permute-start(bf16[2,2,128,512]{3,2,1,0:T(8,128)(2,1)} %get-tuple-element.32), channel_id=1, source_target_pairs={{0,1},{1,2},{2,3},{3,4},{4,5},{5,6},{6,7},{7,8},{8,9},{9,10},{10,1... | collective-permute-start | bytes 1572872 | tf_op jit(solution)/shard_map/ppermute | solution.py:10
  8.4 22.6 %collective-permute-start = (bf16[2,2,128,512]{3,2,1,0:T(8,128)(2,1)}, bf16[2,2,128,512]{3,2,1,0:T(8,128)(2,1)}, u32[]{:S(2)}, u32[]{:S(2)}) collective-permute-start(bf16[2,2,128,512]{3,2,1,0:T(8,128)(2,1)} %get-tuple-element.32), channel_id=1, source_target_pairs={{0,15},{1,0},{2,1},{3,2},{4,3},{5,4},{6,5},{7,6},{8,7},{9,8},{10,9... | collective-permute-start | bytes 1572872 | tf_op jit(solution)/shard_map/ppermute | solution.py:10
  14.3 1.2 %copy-start.6 = (bf16[4096,128]{1,0:T(8,128)(2,1)S(1)}, bf16[4096,128]{1,0:T(8,128)(2,1)}, u32[]{:S(2)}) copy-start(bf16[4096,128]{1,0:T(8,128)(2,1)} %reshape_squeeze.3) | copy-start | bytes 3145732
  17.3 1.5 %copy-start.8 = (s32[4]{0:T(128)S(1)}, s32[4]{0:T(128)}, u32[]{:S(2)}) copy-start(s32[4]{0:T(128)} %param.12) | copy-start | bytes 52
  24.7 2.8 %copy-start.9 = (s32[2,2]{1,0:T(2,128)S(1)}, s32[2,2]{1,0:T(2,128)}, u32[]{:S(2)}) copy-start(s32[2,2]{1,0:T(2,128)} %param.11) | copy-start | bytes 52
  30.8 2.7 %copy-start.2 = (bf16[4,2,512,512]{3,2,1,0:T(8,128)(2,1)S(1)}, bf16[4,2,512,512]{3,2,1,0:T(8,128)(2,1)}, u32[]{:S(2)}) copy-start(bf16[4,2,512,512]{3,2,1,0:T(8,128)(2,1)} %param.8) | copy-start | bytes 12582916
  39.1 11.7 %collective-permute-start.3 = (bf16[2,2,128,512]{3,2,1,0:T(8,128)(2,1)}, bf16[2,2,128,512]{3,2,1,0:T(8,128)(2,1)S(1)}, u32[]{:S(2)}, u32[]{:S(2)}) collective-permute-start(bf16[2,2,128,512]{3,2,1,0:T(8,128)(2,1)} %collective-permute-done.2), channel_id=1, source_target_pairs={{0,1},{1,2},{2,3},{3,4},{4,5},{5,6},{6,7},{7,8},{8,9},{9,10},{10,1... | collective-permute-start | bytes 1572872 | tf_op jit(solution)/shard_map/ppermute | solution.py:10
  39.2 17.9 %collective-permute-start.5 = (bf16[2,2,128,512]{3,2,1,0:T(8,128)(2,1)}, bf16[2,2,128,512]{3,2,1,0:T(8,128)(2,1)S(1)}, u32[]{:S(2)}, u32[]{:S(2)}) collective-permute-start(bf16[2,2,128,512]{3,2,1,0:T(8,128)(2,1)} %collective-permute-done.4), channel_id=1, source_target_pairs={{0,15},{1,0},{2,1},{3,2},{4,3},{5,4},{6,5},{7,6},{8,7},{9,8},{10,9... | collective-permute-start | bytes 1572872 | tf_op jit(solution)/shard_map/ppermute | solution.py:10
  43.6 12.8 %collective-permute-start.7 = (bf16[2,2,128,512]{3,2,1,0:T(8,128)(2,1)}, bf16[2,2,128,512]{3,2,1,0:T(8,128)(2,1)S(1)}, u32[]{:S(2)}, u32[]{:S(2)}) collective-permute-start(bf16[2,2,128,512]{3,2,1,0:T(8,128)(2,1)} %collective-permute-done.6), channel_id=1, source_target_pairs={{0,1},{1,2},{2,3},{3,4},{4,5},{5,6},{6,7},{7,8},{8,9},{9,10},{10,1... | collective-permute-start | bytes 1572872 | tf_op jit(solution)/shard_map/ppermute | solution.py:10
  43.6 14.7 %collective-permute-start.1 = (bf16[2,2,128,512]{3,2,1,0:T(8,128)(2,1)}, bf16[2,2,128,512]{3,2,1,0:T(8,128)(2,1)S(1)}, u32[]{:S(2)}, u32[]{:S(2)}) collective-permute-start(bf16[2,2,128,512]{3,2,1,0:T(8,128)(2,1)} %collective-permute-done), channel_id=1, source_target_pairs={{0,15},{1,0},{2,1},{3,2},{4,3},{5,4},{6,5},{7,6},{8,7},{9,8},{10,9... | collective-permute-start | bytes 1572872 | tf_op jit(solution)/shard_map/ppermute | solution.py:10
  59.3 1.6 %copy-start.5 = (f32[2,2,256,512]{3,2,1,0:T(8,128)S(1)}, f32[2,2,256,512]{3,2,1,0:T(8,128)}, u32[]{:S(2)}) copy-start(f32[2,2,256,512]{3,2,1,0:T(8,128)} %reshape.486) | copy-start | bytes 6291460
  59.3 1.6 %copy-start.7 = (bf16[256,256]{1,0:T(8,128)(2,1)S(1)}, bf16[256,256]{1,0:T(8,128)(2,1)}, u32[]{:S(2)}) copy-start(bf16[256,256]{1,0:T(8,128)(2,1)} %param.10) | copy-start | bytes 393220
  61.4 1.2 %copy-start.3 = (f32[2,256,512]{2,1,0:T(8,128)S(1)}, f32[2,256,512]{2,1,0:T(8,128)}, u32[]{:S(2)}) copy-start(f32[2,256,512]{2,1,0:T(8,128)} %get-tuple-element.12) | copy-start | bytes 3145732
  61.5 1.5 %copy-start.4 = (f32[2,256,512]{2,1,0:T(8,128)S(1)}, f32[2,256,512]{2,1,0:T(8,128)}, u32[]{:S(2)}) copy-start(f32[2,256,512]{2,1,0:T(8,128)} %get-tuple-element.13) | copy-start | bytes 3145732
  65.1 17.8 %all-to-all-start = ((f32[16,1,10]{2,1,0:T(1,128)}), f32[16,1,10]{2,1,0:T(1,128)S(1)}, u32[]{:S(2)}, u32[]{:S(2)}) async-start(f32[16,1,10]{2,1,0:T(1,128)} %broadcast_in_dim.28), calls=%async_computation | async-start | bytes 16384 | tf_op jit(solution)/shard_map/all_to_all | solution.py:19

commit v6 on v2

--- a/solution.py
+++ b/solution.py
@@ -37,6 +37,7 @@
     tile = width_x // tile_mask.shape[0]
     below_one = passed_along(block, "harm", 1)
     above_one = passed_along(block, "harm", -1)
+    block, below_one, above_one = lax.optimization_barrier((block, below_one, above_one))
     below_two = passed_along(below_one, "harm", 1)
     above_two = passed_along(above_one, "harm", -1)
     rows = block.reshape(-1, ny)

time: 78.7 us -> 140 us (1.78)
  local copies, waits for them, and re-layouts: 5.7 us -> 57.5 us
  waiting for transfers between devices: 16.1 us -> 6.63 us
  matrix products: 8.93 us -> 18.2 us
  other arithmetic: 10.2 us -> 15.1 us
  starting transfers between devices: 28.2 us -> 32.1 us
    ppermute x4, starting transfers between devices: 12.4 us -> 24.7 us  [passed_along(): return lax.ppermute(value, axis, pairs)]
    all_to_all x1, starting transfers between devices: 15.7 us -> 7.4 us  [summed_over(): gathered = lax.all_to_all(spread, axes, 0, 0, tiled=False)]
    mul x2 -> x4, local copies, waits for them, and re-layouts: 0.34 us -> 8.13 us  [body(): qr[:, None] * wr[None, :] + qi[:, None] * wi[None, :]]
    sub x0 -> x4, local copies, waits for them, and re-layouts: none -> 7.78 us  [body(): real_part = prod[0, 0] - prod[1, 1]]
    add x0 -> x4, local copies, waits for them, and re-layouts: none -> 7.73 us  [body(): imag_part = prod[0, 1] + prod[1, 0]]
    ppermute x4, waiting for transfers between devices: 10.8 us -> 3.57 us  [passed_along(): return lax.ppermute(value, axis, pairs)]
    optimization_barrier x0 -> x3, local copies, waits for them, and re-layouts: none -> 5.9 us  [body(): lax.optimization_barrier((block, below_one, above_one))]
    unnamed x18 -> x17, local copies, waits for them, and re-layouts: 0.77 us -> 6.16 us
  transfers between devices with their start and end apart: 5 -> 5, of which waited for: 3 -> 2; matrix products, arithmetic and copies ran while one was open for 19% -> 39% of each run, Pallas kernels for 0% -> 0%
where the time goes in v6:
time: 140 us; the launch traced here: 139 us
  local copies, waits for them, and re-layouts  57.5 us (41%)
  starting transfers between devices  32.1 us (23%)
  matrix products  18.2 us (13%)
  other arithmetic  15.1 us (11%)
  between operations  9.12 us (7%)
  waiting for transfers between devices  6.63 us (5%)
    ppermute x4, starting transfers between devices, passed_along(): return lax.ppermute(value, axis, pairs)  24.7 us
    dot_general x4, matrix products, body(): jnp.einsum('cri,kio->ckro', other, matrix, preferred_element_type=jnp.flo...  10.3 us
    mul x4, local copies, waits for them, and re-layouts, body(): qr[:, None] * wr[None, :] + qi[:, None] * wi[None, :]  8.13 us
    sub x4, local copies, waits for them, and re-layouts, body(): real_part = prod[0, 0] - prod[1, 1]  7.78 us
    add x4, local copies, waits for them, and re-layouts, body(): imag_part = prod[0, 1] + prod[1, 0]  7.73 us
    all_to_all x1, starting transfers between devices, summed_over(): gathered = lax.all_to_all(spread, axes, 0, 0, tiled=False)  7.4 us
    unnamed x17, local copies, waits for them, and re-layouts  6.16 us
    optimization_barrier x3, local copies, waits for them, and re-layouts, body(): lax.optimization_barrier((block, below_one, above_one))  5.9 us
  transfers between devices with their start and end apart: 5, of which 2 were waited for; matrix products, arithmetic and copies ran while one was open for 39% of the time, Pallas kernels for 0%

profile of v6, /device:TPU:0, one launch (start us, length us, event | category | flops | bytes accessed | tf_op | source)
XLA Modules:
  0.0 138.6 jit_solution(14926189716330057432)
XLA Ops:
  0.6 0.0 copy-start
  0.7 1.5 %copy.85 = bf16[1,2,2,256,512]{3,4,2,1,0:T(8,128)(2,1)S(1)} copy(bf16[1,2,2,256,512]{4,3,2,1,0:T(8,128)(2,1)} %param.7) | data formatting | bytes 2097152 | tf_op args[0]
  2.2 0.5 collective-permute-start
  2.7 5.1 %collective-permute-start.1 = (bf16[2,2,256,512]{2,3,1,0:T(8,128)(2,1)S(1)}, bf16[2,2,256,512]{2,3,1,0:T(8,128)(2,1)}, u32[]{:S(2)}, u32[]{:S(2)}) collective-permute-start(bf16[2,2,256,512]{2,3,1,0:T(8,128)(2,1)S(1)} %bitcast.113), channel_id=1, source_target_pairs={{0,15},{1,0},{2,1},{3,2},{4,3},{5,4},{6,5},{7,6},{8,7},{9,8},{10,9... | collective-permute-start | bytes 3145736 | tf_op jit(solution)/shard_map/ppermute | solution.py:10
  7.7 0.7 fusion.26
  16.8 3.6 %collective-permute-done = bf16[2,2,256,512]{2,3,1,0:T(8,128)(2,1)} collective-permute-done((bf16[2,2,256,512]{2,3,1,0:T(8,128)(2,1)S(1)}, bf16[2,2,256,512]{2,3,1,0:T(8,128)(2,1)}, u32[]{:S(2)}, u32[]{:S(2)}) %collective-permute-start) | collective-permute-done | bytes 1048608 | tf_op jit(solution)/shard_map/ppermute | solution.py:10
  20.4 4.5 %collective-permute-start.2 = (bf16[2,2,256,512]{2,3,1,0:T(8,128)(2,1)}, bf16[2,2,256,512]{2,3,1,0:T(8,128)(2,1)}, u32[]{:S(2)}, u32[]{:S(2)}) collective-permute-start(bf16[2,2,256,512]{2,3,1,0:T(8,128)(2,1)} %collective-permute-done.1), channel_id=1, source_target_pairs={{0,15},{1,0},{2,1},{3,2},{4,3},{5,4},{6,5},{7,6},{8,7},{9,8},{10,9... | collective-permute-start | bytes 3145736 | tf_op jit(solution)/shard_map/ppermute | solution.py:10
  24.9 2.3 %copy.91 = bf16[2,2,256,512]{3,2,1,0:T(8,128)(2,1)} copy(bf16[2,2,256,512]{2,3,1,0:T(8,128)(2,1)} %collective-permute-done.1) | data formatting | bytes 2097152 | tf_op jit(solution)/shard_map/optimization_barrier | solution.py:40
  27.2 14.6 %collective-permute-start.3 = (bf16[2,2,256,512]{2,3,1,0:T(8,128)(2,1)}, bf16[2,2,256,512]{2,3,1,0:T(8,128)(2,1)}, u32[]{:S(2)}, u32[]{:S(2)}) collective-permute-start(bf16[2,2,256,512]{2,3,1,0:T(8,128)(2,1)} %collective-permute-done), channel_id=1, source_target_pairs={{0,1},{1,2},{2,3},{3,4},{4,5},{5,6},{6,7},{7,8},{8,9},{9,10},{10,1... | collective-permute-start | bytes 3145736 | tf_op jit(solution)/shard_map/ppermute | solution.py:10
  41.8 2.3 %copy.94 = bf16[2,2,256,512]{3,2,1,0:T(8,128)(2,1)} copy(bf16[2,2,256,512]{2,3,1,0:T(8,128)(2,1)} %collective-permute-done) | data formatting | bytes 2097152 | tf_op jit(solution)/shard_map/optimization_barrier | solution.py:40
  44.1 1.3 copy.86
  45.4 0.2 convert_element_type.33
  45.6 1.0 copy-done.3
  46.6 2.5 %convolution_bitcast_fusion.2 = f32[2,2,512,512]{3,2,0,1:T(8,128)S(1)} fusion(bf16[2,512,512,1]{2,1,0,3:T(8,128)(2,1)S(1)} %bitcast.118, bf16[4,2,512,512]{3,2,1,0:T(8,128)(2,1)} %param.8, s32[]{:T(128)S(6)} %select_n.29), kind=kOutput, calls=%fused_computation.2 | convolution fusion | flops 1073741824 | bytes 6291460 | tf_op jit(solution)/shard_map/cri,kio->ckro/dot_general | solution.py:57
  49.1 1.8 %slice_subtract_fusion.2 = (f32[1,1,512,512]{3,2,0,1:T(8,128)}, f32[1,1,512,512]{3,2,0,1:T(8,128)}) fusion(f32[2,2,512,512]{3,2,0,1:T(8,128)S(1)} %convolution_bitcast_fusion.2), kind=kLoop, calls=%fused_computation.21 | loop fusion | flops 524288 | bytes 6291456 | tf_op jit(solution)/shard_map/sub | solution.py:58
  50.9 2.6 %copy.92 = f32[1,2,256,512]{2,3,1,0:T(8,128)} copy(f32[1,2,256,512]{3,2,1,0:T(8,128)} %bitcast.125) | data formatting | bytes 2097152 | tf_op jit(solution)/shard_map/sub | solution.py:58
  53.5 2.5 %copy.93 = f32[1,2,256,512]{2,3,1,0:T(8,128)} copy(f32[1,2,256,512]{3,2,1,0:T(8,128)} %bitcast.121) | data formatting | bytes 2097152 | tf_op jit(solution)/shard_map/add | solution.py:59
  56.1 2.8 %convolution_bitcast_fusion.1 = f32[2,2,512,512]{3,2,0,1:T(8,128)S(1)} fusion(bf16[2,512,512,1]{2,1,0,3:T(8,128)(2,1)} %bitcast.117, bf16[4,2,512,512]{3,2,1,0:T(8,128)(2,1)} %param.8, s32[]{:T(128)S(6)} %select_n.31), kind=kOutput, calls=%fused_computation.1 | convolution fusion | flops 1073741824 | bytes 6291460 | tf_op jit(solution)/shard_map/cri,kio->ckro/dot_general | solution.py:57
  58.9 1.8 %slice_subtract_fusion.1 = (f32[1,1,512,512]{3,2,0,1:T(8,128)}, f32[1,1,512,512]{3,2,0,1:T(8,128)}) fusion(f32[2,2,512,512]{3,2,0,1:T(8,128)S(1)} %convolution_bitcast_fusion.1), kind=kLoop, calls=%fused_computation.19 | loop fusion | flops 524288 | bytes 6291456 | tf_op jit(solution)/shard_map/sub | solution.py:58
  60.7 2.5 %copy.95 = f32[1,2,256,512]{2,3,1,0:T(8,128)} copy(f32[1,2,256,512]{3,2,1,0:T(8,128)} %bitcast.126) | data formatting | bytes 2097152 | tf_op jit(solution)/shard_map/sub | solution.py:58
  63.2 2.5 %copy.96 = f32[1,2,256,512]{2,3,1,0:T(8,128)} copy(f32[1,2,256,512]{3,2,1,0:T(8,128)} %bitcast.122) | data formatting | bytes 2097152 | tf_op jit(solution)/shard_map/add | solution.py:59
  65.7 2.5 %reshape.305 = bf16[4096,128]{1,0:T(8,128)(2,1)} reshape(bf16[2,2,256,512]{3,2,1,0:T(8,128)(2,1)} %copy.86) | data formatting | bytes 2097152 | tf_op jit(solution)/shard_map/reshape | solution.py:43
  68.2 3.0 %fusion.28 = f32[4096,128]{1,0:T(8,128)} fusion(bf16[4096,128]{1,0:T(8,128)(2,1)} %reshape.305, bf16[128,128]{1,0:T(8,128)(2,1)S(1)} %copy-done), kind=kOutput, calls=%fused_computation.63 | convolution fusion | flops 134217728 | bytes 3178496 | tf_op jit(solution)/shard_map/dot_general | solution.py:44
  71.2 2.7 %reshape.306 = f32[2,2,256,512]{3,2,1,0:T(8,128)} reshape(f32[4096,128]{1,0:T(8,128)} %fusion.28) | data formatting | bytes 4194304 | tf_op jit(solution)/shard_map/reshape | solution.py:44
  73.9 2.9 %copy.87 = f32[2,2,256,512]{2,3,1,0:T(8,128)} copy(f32[2,2,256,512]{3,2,1,0:T(8,128)} %reshape.306) | data formatting | bytes 4194304 | tf_op jit(solution)/shard_map/reshape | solution.py:44
  76.9 1.5 %slice_bitcast_fusion.1 = (f32[2,256,512]{1,2,0:T(8,128)}, f32[2,256,512]{1,2,0:T(8,128)}) fusion(f32[2,2,256,512]{2,3,1,0:T(8,128)S(1)} %convert_element_type.33), kind=kLoop, calls=%fused_computation.15 | loop fusion | bytes 4194304 | tf_op jit(solution)/shard_map/mul | solution.py:66
  78.3 2.5 %copy.100 = f32[2,256,512]{2,1,0:T(8,128)} copy(f32[2,256,512]{1,2,0:T(8,128)} %get-tuple-element.36) | data formatting | bytes 2097152 | tf_op jit(solution)/shard_map/mul | solution.py:66
  80.9 2.5 %copy.102 = f32[2,256,512]{2,1,0:T(8,128)} copy(f32[2,256,512]{1,2,0:T(8,128)} %get-tuple-element.37) | data formatting | bytes 2097152 | tf_op jit(solution)/shard_map/mul | solution.py:66
  83.4 0.3 add_reduce_fusion.2
  83.7 1.5 %copy.97 = bf16[2,2,256,512]{3,2,1,0:T(8,128)(2,1)S(1)} copy(bf16[2,2,256,512]{2,3,1,0:T(8,128)(2,1)} %collective-permute-done.3) | data formatting | bytes 2097152 | tf_op jit(solution)/shard_map/ppermute | solution.py:10
  85.2 2.5 %convolution_bitcast_fusion = f32[2,2,512,512]{3,2,0,1:T(8,128)S(1)} fusion(bf16[2,512,512,1]{2,1,0,3:T(8,128)(2,1)S(1)} %bitcast.119, bf16[4,2,512,512]{3,2,1,0:T(8,128)(2,1)} %param.8, s32[]{:T(128)S(6)} %select_n.33), kind=kOutput, calls=%fused_computation | convolution fusion | flops 1073741824 | bytes 6291460 | tf_op jit(solution)/shard_map/cri,kio->ckro/dot_general | solution.py:57
  87.7 0.5 slice_subtract_fusion
  88.2 1.3 copy.98
  89.5 1.4 copy.99
  90.9 1.7 %copy.88 = bf16[2,2,256,512]{3,2,1,0:T(8,128)(2,1)S(1)} copy(bf16[2,2,256,512]{2,3,1,0:T(8,128)(2,1)} %collective-permute-done.2) | data formatting | bytes 2097152 | tf_op jit(solution)/shard_map/ppermute | solution.py:10
  92.5 2.5 %convolution_bitcast_fusion.3 = f32[2,2,512,512]{3,2,0,1:T(8,128)S(1)} fusion(bf16[2,512,512,1]{2,1,0,3:T(8,128)(2,1)S(1)} %bitcast.120, bf16[4,2,512,512]{3,2,1,0:T(8,128)(2,1)} %param.8, s32[]{:T(128)S(6)} %select_n.27), kind=kOutput, calls=%fused_computation.3 | convolution fusion | flops 1073741824 | bytes 6291460 | tf_op jit(solution)/shard_map/cri,kio->ckro/dot_general | solution.py:57
  95.1 0.5 slice_subtract_fusion.3
  95.6 1.3 copy.89
  96.9 1.3 copy.90
  98.2 0.3 broadcast_in_dim.26
  98.5 4.9 %fusion.2 = f32[2,2,256,512]{2,3,1,0:T(8,128)S(1)} fusion(f32[1,2,256,512]{2,3,1,0:T(8,128)} %copy.90, f32[1,2,256,512]{2,3,1,0:T(8,128)} %copy.89, f32[1,2,256,512]{2,3,1,0:T(8,128)} %copy.93, f32[1,2,256,512]{2,3,1,0:T(8,128)} %copy.92, f32[1,2,256,512]{2,3,1,0:T(8,128)} %copy.96, f32[1,2,256,512]{2,3,1,0:T(8,128)} %copy.95, f32[1,2,256,512]{2,3,1,0:T(8,128)} %copy.99, ...), kind=kOutput, calls=%fused_computation.7 | convolution fusion | flops 274792448 | bytes 13893636 | tf_op jit(solution)/shard_map/ab,cvbf->cvaf/dot_general | solution.py:47
  103.4 1.5 %slice_bitcast_fusion.3 = (f32[2,256,512]{1,2,0:T(8,128)}, f32[2,256,512]{1,2,0:T(8,128)}) fusion(f32[2,2,256,512]{2,3,1,0:T(8,128)S(1)} %fusion.2), kind=kLoop, calls=%fused_computation.40 | loop fusion | bytes 4194304 | tf_op jit(solution)/shard_map/mul | solution.py:66
  104.9 2.6 %copy.101 = f32[2,256,512]{2,1,0:T(8,128)} copy(f32[2,256,512]{1,2,0:T(8,128)} %get-tuple-element.38) | data formatting | bytes 2097152 | tf_op jit(solution)/shard_map/mul | solution.py:66
  107.5 2.5 %copy.103 = f32[2,256,512]{2,1,0:T(8,128)} copy(f32[2,256,512]{1,2,0:T(8,128)} %get-tuple-element.39) | data formatting | bytes 2097152 | tf_op jit(solution)/shard_map/mul | solution.py:66
  110.1 3.0 %add_reduce_fusion.1 = (f32[2,2]{1,0:T(2,128)S(1)}, f32[2,2]{1,0:T(2,128)S(1)}) fusion(f32[2,256,512]{2,1,0:T(8,128)} %copy.103, f32[2,256,512]{2,1,0:T(8,128)} %copy.102, f32[2,256,512]{2,1,0:T(8,128)} %copy.101, f32[2,256,512]{2,1,0:T(8,128)S(1)} %copy-done.2), kind=kLoop, calls=%fused_computation.13 | loop fusion | flops 4194296 | bytes 4194336 | tf_op jit(solution)/shard_map/reduce_sum | solution.py:66
  113.0 0.1 reshape.311
  113.1 0.1 reshape.312
  113.2 0.1 pad_maximum_fusion.1
  113.3 0.6 broadcast_in_dim.28
  113.9 7.4 %all-to-all-start = ((f32[16,1,10]{2,1,0:T(1,128)}), f32[16,1,10]{2,1,0:T(1,128)S(1)}, u32[]{:S(2)}, u32[]{:S(2)}) async-start(f32[16,1,10]{2,1,0:T(1,128)} %broadcast_in_dim.28), calls=%async_computation | async-start | bytes 16384 | tf_op jit(solution)/shard_map/all_to_all | solution.py:19
  121.3 1.1 convert_bitcast_fusion
  122.4 2.3 %copy.107 = bf16[1,2,2,256,512]{4,3,2,1,0:T(8,128)(2,1)} copy(bf16[1,2,2,256,512]{3,4,2,1,0:T(8,128)(2,1)} %convert_bitcast_fusion) | data formatting | bytes 2097152
  124.6 3.1 %all-to-all-done = f32[16,1,10]{2,1,0:T(1,128)S(1)} async-done(((f32[16,1,10]{2,1,0:T(1,128)}), f32[16,1,10]{2,1,0:T(1,128)S(1)}, u32[]{:S(2)}, u32[]{:S(2)}) %all-to-all-start) | async-done | bytes 672 | tf_op jit(solution)/shard_map/all_to_all | solution.py:19
  127.7 0.1 fusion.27
  127.8 0.1 slice_add_fusion.4
  127.9 0.1 reshape.313
  128.0 0.1 reshape.314
  128.0 0.1 broadcast_divide_fusion.1
  128.1 3.4 %subtract_reduce_fusion = (f32[2,256,512]{2,1,0:T(8,128)}, f32[2,256,512]{2,1,0:T(8,128)}) fusion(f32[2,2]{1,0:T(2,128)S(1)} %get-tuple-element.41, f32[2,2]{1,0:T(2,128)S(1)} %get-tuple-element.40, f32[2,256,512]{2,1,0:T(8,128)} %copy.102, f32[2,256,512]{2,1,0:T(8,128)S(1)} %copy-done.2), kind=kLoop, calls=%fused_computation.11 | loop fusion | flops 3670016 | bytes 4194336 | tf_op jit(solution)/shard_map/reduce_sum | solution.py:72
  131.5 1.6 %copy.105 = f32[2,256,512]{1,2,0:T(8,128)S(1)} copy(f32[2,256,512]{2,1,0:T(8,128)} %get-tuple-element.20) | data formatting | bytes 2097152 | tf_op jit(solution)/shard_map/reduce_sum | solution.py:72
  133.1 2.5 %copy.106 = f32[2,256,512]{1,2,0:T(8,128)} copy(f32[2,256,512]{2,1,0:T(8,128)} %get-tuple-element.21) | data formatting | bytes 2097152 | tf_op jit(solution)/shard_map/reduce_sum | solution.py:73
  135.6 1.5 %fusion.14 = (bf16[1,1,2,256,512]{3,4,2,1,0:T(8,128)(2,1)S(1)}, bf16[1,1,2,256,512]{3,4,2,1,0:T(8,128)(2,1)S(1)}) fusion(f32[2,256,512]{1,2,0:T(8,128)S(1)} %copy.105, f32[2,2,256,512]{2,3,1,0:T(8,128)S(1)} %fusion.2, f32[2,256,512]{1,2,0:T(8,128)} %copy.106), kind=kLoop, calls=%fused_computation.41 | loop fusion | flops 1048576 | bytes 5242880 | tf_op jit(solution)/shard_map/stack | solution.py:74
  137.2 0.1 pad_maximum_fusion
  137.3 1.3 copy.108
  (18 shorter events, 0.1 us)
Async XLA Ops:
  0.6 67.6 %copy-start = (bf16[128,128]{1,0:T(8,128)(2,1)S(1)}, bf16[128,128]{1,0:T(8,128)(2,1)}, u32[]{:S(2)}) copy-start(bf16[128,128]{1,0:T(8,128)(2,1)} %param.9) | copy-start | bytes 98308
  0.6 7.1 %copy-start.5 = (s32[4]{0:T(128)S(1)}, s32[4]{0:T(128)}, u32[]{:S(2)}) copy-start(s32[4]{0:T(128)} %param.12) | copy-start | bytes 52
  0.7 12.9 %copy-start.6 = (s32[2,2]{1,0:T(2,128)S(1)}, s32[2,2]{1,0:T(2,128)}, u32[]{:S(2)}) copy-start(s32[2,2]{1,0:T(2,128)} %param.11) | copy-start | bytes 52
  2.2 18.2 %collective-permute-start = (bf16[2,2,256,512]{2,3,1,0:T(8,128)(2,1)S(1)}, bf16[2,2,256,512]{2,3,1,0:T(8,128)(2,1)}, u32[]{:S(2)}, u32[]{:S(2)}) collective-permute-start(bf16[2,2,256,512]{2,3,1,0:T(8,128)(2,1)S(1)} %bitcast.112), channel_id=1, source_target_pairs={{0,1},{1,2},{2,3},{3,4},{4,5},{5,6},{6,7},{7,8},{8,9},{9,10},{10,1... | collective-permute-start | bytes 3145736 | tf_op jit(solution)/shard_map/ppermute | solution.py:10
  2.7 17.7 %collective-permute-start.1 = (bf16[2,2,256,512]{2,3,1,0:T(8,128)(2,1)S(1)}, bf16[2,2,256,512]{2,3,1,0:T(8,128)(2,1)}, u32[]{:S(2)}, u32[]{:S(2)}) collective-permute-start(bf16[2,2,256,512]{2,3,1,0:T(8,128)(2,1)S(1)} %bitcast.113), channel_id=1, source_target_pairs={{0,15},{1,0},{2,1},{3,2},{4,3},{5,4},{6,5},{7,6},{8,7},{9,8},{10,9... | collective-permute-start | bytes 3145736 | tf_op jit(solution)/shard_map/ppermute | solution.py:10
  20.4 70.5 %collective-permute-start.2 = (bf16[2,2,256,512]{2,3,1,0:T(8,128)(2,1)}, bf16[2,2,256,512]{2,3,1,0:T(8,128)(2,1)}, u32[]{:S(2)}, u32[]{:S(2)}) collective-permute-start(bf16[2,2,256,512]{2,3,1,0:T(8,128)(2,1)} %collective-permute-done.1), channel_id=1, source_target_pairs={{0,15},{1,0},{2,1},{3,2},{4,3},{5,4},{6,5},{7,6},{8,7},{9,8},{10,9... | collective-permute-start | bytes 3145736 | tf_op jit(solution)/shard_map/ppermute | solution.py:10
  27.2 56.5 %collective-permute-start.3 = (bf16[2,2,256,512]{2,3,1,0:T(8,128)(2,1)}, bf16[2,2,256,512]{2,3,1,0:T(8,128)(2,1)}, u32[]{:S(2)}, u32[]{:S(2)}) collective-permute-start(bf16[2,2,256,512]{2,3,1,0:T(8,128)(2,1)} %collective-permute-done), channel_id=1, source_target_pairs={{0,1},{1,2},{2,3},{3,4},{4,5},{5,6},{6,7},{7,8},{8,9},{9,10},{10,1... | collective-permute-start | bytes 3145736 | tf_op jit(solution)/shard_map/ppermute | solution.py:10
  45.4 1.2 copy-start.3
  95.5 3.0 %copy-start.4 = (bf16[256,256]{1,0:T(8,128)(2,1)S(1)}, bf16[256,256]{1,0:T(8,128)(2,1)}, u32[]{:S(2)}) copy-start(bf16[256,256]{1,0:T(8,128)(2,1)} %param.10) | copy-start | bytes 393220
  104.9 5.2 %copy-start.2 = (f32[2,256,512]{2,1,0:T(8,128)S(1)}, f32[2,256,512]{2,1,0:T(8,128)}, u32[]{:S(2)}) copy-start(f32[2,256,512]{2,1,0:T(8,128)} %copy.100) | copy-start | bytes 3145732
  113.9 13.8 %all-to-all-start = ((f32[16,1,10]{2,1,0:T(1,128)}), f32[16,1,10]{2,1,0:T(1,128)S(1)}, u32[]{:S(2)}, u32[]{:S(2)}) async-start(f32[16,1,10]{2,1,0:T(1,128)} %broadcast_in_dim.28), calls=%async_computation | async-start | bytes 16384 | tf_op jit(solution)/shard_map/all_to_all | solution.py:19
  137.2 1.4 %copy-start.1 = (bf16[128,128]{1,0:T(8,128)(2,1)S(1)}, bf16[128,128]{1,0:T(8,128)(2,1)}, u32[]{:S(2)}) copy-start(bf16[128,128]{1,0:T(8,128)(2,1)} %param.9) | copy-start | bytes 98308

commit v7 on v2

--- a/solution.py
+++ b/solution.py
@@ -46,7 +46,19 @@
     along_x = jnp.einsum("ab,cvbf->cvaf", masked, block, preferred_element_type=jnp.float32)
     centered = (position - harmonics // 2).astype(jnp.float32) + detuning[0]
     lam = -(centered * centered) / (4.0 * harmonics)
-    image = along_y + along_x + lam * block.astype(jnp.float32)
+    qfull = block.astype(jnp.float32)
+    qr = qfull[0]
+    qi = qfull[1]
+
+    def products(term):
+        tr = term[0]
+        ti = term[1]
+        part_re = jnp.sum(qr[:, None] * tr[None, :] + qi[:, None] * ti[None, :], axis=(2, 3))
+        part_im = jnp.sum(qr[:, None] * ti[None, :] - qi[:, None] * tr[None, :], axis=(2, 3))
+        return part_re, part_im
+
+    image = along_y + along_x + lam * qfull
+    num_re, num_im = products(image)
     sources = (above_two, above_one, below_one, below_two)
     counter = jnp.arange(4, dtype=jnp.int32)
     for place in range(4):
@@ -56,14 +68,13 @@
         prod = jnp.einsum("cri,kio->ckro", other, matrix, preferred_element_type=jnp.float32)
         real_part = prod[0, 0] - prod[1, 1]
         imag_part = prod[0, 1] + prod[1, 0]
-        image = image + jnp.stack([real_part, imag_part]).reshape(block.shape)
-    qfull = block.astype(jnp.float32)
-    qr = qfull[0]
-    qi = qfull[1]
+        term = jnp.stack([real_part, imag_part]).reshape(block.shape)
+        part_re, part_im = products(term)
+        num_re = num_re + part_re
+        num_im = num_im + part_im
+        image = image + term
     wr = image[0]
     wi = image[1]
-    num_re = jnp.sum(qr[:, None] * wr[None, :] + qi[:, None] * wi[None, :], axis=(2, 3))
-    num_im = jnp.sum(qr[:, None] * wi[None, :] - qi[:, None] * wr[None, :], axis=(2, 3))
     norms = jnp.sum(qr * qr + qi * qi, axis=(1, 2))
     total_re, total_im, total_norms = summed_over(("harm",), num_re, num_im, norms)
     h_re = (total_re / (total_norms + 1e-06)[:, None])[:, :, None, None]

time: 78.7 us -> 83.6 us (1.062)
  other arithmetic: 10.2 us -> 21.1 us
  starting transfers between devices: 28.2 us -> 20.1 us
  waiting for transfers between devices: 16.1 us -> 12 us
  local copies, waits for them, and re-layouts: 5.7 us -> 9.49 us
  matrix products: 8.93 us -> 11.3 us
    all_to_all x1, starting transfers between devices: 15.7 us -> 9.85 us  [summed_over(): gathered = lax.all_to_all(spread, axes, 0, 0, tiled=False)]
    all_to_all x1, waiting for transfers between devices: 5.3 us -> 0.04 us  [summed_over(): gathered = lax.all_to_all(spread, axes, 0, 0, tiled=False)]
    broadcast_in_dim x1, other arithmetic: 1.1 us -> 6.37 us  [body(): image.astype(jnp.bfloat16)[None]]
    reduce_sum x1, other arithmetic: 1.26 us -> 6.04 us  [products(): jnp.sum(qr[:, None] * tr[None, :] + qi[:, None] * ti[None, :], axis=(2, 3))]
    ppermute x4, starting transfers between devices: 12.4 us -> 10.2 us  [passed_along(): return lax.ppermute(value, axis, pairs)]
    unnamed x18 -> x36, local copies, waits for them, and re-layouts: 0.77 us -> 2.24 us
    mul x2, local copies, waits for them, and re-layouts: 0.34 us -> 1.66 us  [the longest x1 1.49 us: products(): qr[:, None] * tr[None, :] + qi[:, None] * ti[None, :]]
    dot_general x1, matrix products: 0.41 us -> 1.7 us  [body(): jnp.dot(rows, y_operator, preferred_element_type=jnp.float32)]
  transfers between devices with their start and end apart: 5 -> 5, of which waited for: 3 -> 2; matrix products, arithmetic and copies ran while one was open for 19% -> 32% of each run, Pallas kernels for 0% -> 0%
where the time goes in v7:
time: 83.6 us; the launch traced here: 83.1 us
  other arithmetic  21.1 us (25%)
  starting transfers between devices  20.1 us (24%)
  waiting for transfers between devices  12 us (14%)
  matrix products  11.3 us (14%)
  local copies, waits for them, and re-layouts  9.49 us (11%)
  between operations  9.2 us (11%)
    ppermute x4, waiting for transfers between devices, passed_along(): return lax.ppermute(value, axis, pairs)  11.9 us
    ppermute x4, starting transfers between devices, passed_along(): return lax.ppermute(value, axis, pairs)  10.2 us
    all_to_all x1, starting transfers between devices, summed_over(): gathered = lax.all_to_all(spread, axes, 0, 0, tiled=False)  9.85 us
    dot_general x4, matrix products, body(): jnp.einsum('cri,kio->ckro', other, matrix, preferred_element_type=jnp.flo...  7.55 us
    broadcast_in_dim x1, other arithmetic, body(): image.astype(jnp.bfloat16)[None]  6.37 us
    reduce_sum x1, other arithmetic, products(): jnp.sum(qr[:, None] * tr[None, :] + qi[:, None] * ti[None, :], axis=(2, 3))  6.04 us
    reshape x1, local copies, waits for them, and re-layouts, body(): jnp.dot(rows, y_operator, preferred_element_type=jnp.float32)  2.8 us
    reduce_sum x1, other arithmetic, body(): proj_re = wr - jnp.sum(h_re * qr[:, None] - h_im * qi[:, None], axis=0)  2.26 us
  transfers between devices with their start and end apart: 5, of which 2 were waited for; matrix products, arithmetic and copies ran while one was open for 32% of the time, Pallas kernels for 0%

profile of v7, /device:TPU:0, one launch (start us, length us, event | category | flops | bytes accessed | tf_op | source)
XLA Modules:
  0.0 83.1 jit_solution(7223023822241078312)
XLA Ops:
  0.6 0.0 copy-start
  0.6 0.0 copy-start.1
  0.7 5.5 %collective-permute-start = (bf16[2,2,256,512]{3,2,1,0:T(8,128)(2,1)}, bf16[2,2,256,512]{3,2,1,0:T(8,128)(2,1)}, u32[]{:S(2)}, u32[]{:S(2)}) collective-permute-start(bf16[2,2,256,512]{3,2,1,0:T(8,128)(2,1)} %bitcast.116), channel_id=1, source_target_pairs={{0,15},{1,0},{2,1},{3,2},{4,3},{5,4},{6,5},{7,6},{8,7},{9,8},{10,9... | collective-permute-start | bytes 3145736 | tf_op jit(solution)/shard_map/ppermute | solution.py:10
  6.2 0.0 collective-permute-start.2
  6.2 1.5 %bitcast_convert_fusion = f32[2,2,256,512]{3,2,1,0:T(8,128)S(1)} fusion(bf16[1,2,2,256,512]{4,3,2,1,0:T(8,128)(2,1)} %param.7), kind=kLoop, calls=%fused_computation.72 | loop fusion | flops 524288 | bytes 3145728 | tf_op jit(solution)/shard_map/convert_element_type | solution.py:49
  7.7 0.0 copy-done.1
  7.7 1.4 %reshape_squeeze.3 = bf16[4096,128]{1,0:T(8,128)(2,1)} reshape(bf16[1,2,2,256,512]{4,3,2,1,0:T(8,128)(2,1)S(1)} %copy-done.1) | data formatting | bytes 2097152 | tf_op jit(solution)/shard_map/reshape;squeeze | solution.py:42
  9.2 0.3 add_reduce_fusion.6
  9.4 0.0 copy-done
  9.4 0.9 %copy-done.14 = bf16[4096,128]{1,0:T(8,128)(2,1)S(1)} copy-done((bf16[4096,128]{1,0:T(8,128)(2,1)S(1)}, bf16[4096,128]{1,0:T(8,128)(2,1)}, u32[]{:S(2)}) %copy-start.14) | copy-done | bytes 1048600
  10.4 1.7 %fusion.30 = f32[4096,128]{1,0:T(8,128)} fusion(bf16[4096,128]{1,0:T(8,128)(2,1)S(1)} %copy-done.14, bf16[128,128]{1,0:T(8,128)(2,1)S(1)} %copy-done), kind=kOutput, calls=%fused_computation.75 | convolution fusion | flops 134217728 | bytes 3178496 | tf_op jit(solution)/shard_map/dot_general | solution.py:43
  12.1 1.5 %slice_bitcast_fusion.3 = (f32[2,256,512]{2,1,0:T(8,128)}, f32[2,256,512]{2,1,0:T(8,128)}) fusion(f32[2,2,256,512]{3,2,1,0:T(8,128)S(1)} %bitcast_convert_fusion), kind=kLoop, calls=%fused_computation.27 | loop fusion | bytes 4194304 | tf_op jit(solution)/shard_map/mul | solution.py:56
  13.6 0.0 copy-done.16
  13.6 0.7 fusion.26
  19.3 0.0 copy-start.17
  19.4 0.0 copy-start.15
  19.4 2.8 %reshape.396 = f32[2,2,256,512]{3,2,1,0:T(8,128)} reshape(f32[4096,128]{1,0:T(8,128)} %fusion.30) | data formatting | bytes 4194304 | tf_op jit(solution)/shard_map/reshape | solution.py:43
  22.2 0.0 copy-done.17
  25.4 0.3 broadcast_in_dim.26
  25.7 0.0 copy-done.15
  25.7 2.0 %fusion.3 = f32[2,2,256,512]{3,2,1,0:T(8,128)S(1)} fusion(f32[2,2,256,512]{3,2,1,0:T(8,128)} %reshape.396, f32[]{:T(128)S(6)} %div.25, bf16[256,256]{1,0:T(8,128)(2,1)S(1)} %copy-done.15, bf16[32,8,2,128]{3,2,1,0:T(2,128)(2,1)S(1)} %bitcast.136, bf16[1,2,2,256,512]{4,3,2,1,0:T(8,128)(2,1)S(1)} %copy-done.1), kind=kOutput, calls=%fused_computation.9 | convolution fusion | flops 270794752 | bytes 5505028 | tf_op jit(solution)/shard_map/ab,cvbf->cvaf/dot_general | solution.py:46
  27.8 0.0 copy-start.13
  27.8 0.2 slice_bitcast_fusion
  28.0 0.0 collective-permute-done
  28.0 4.5 %collective-permute-start.1 = (bf16[2,2,256,512]{3,2,1,0:T(8,128)(2,1)}, bf16[2,2,256,512]{3,2,1,0:T(8,128)(2,1)S(1)}, u32[]{:S(2)}, u32[]{:S(2)}) collective-permute-start(bf16[2,2,256,512]{3,2,1,0:T(8,128)(2,1)} %collective-permute-done), channel_id=1, source_target_pairs={{0,15},{1,0},{2,1},{3,2},{4,3},{5,4},{6,5},{7,6},{8,7},{9,8},{10,9... | collective-permute-start | bytes 3145736 | tf_op jit(solution)/shard_map/ppermute | solution.py:10
  32.5 0.0 copy-done.13
  32.5 2.5 %convolution_bitcast_fusion.2 = f32[2,2,512,512]{3,2,0,1:T(8,128)S(1)} fusion(bf16[2,512,512,1]{2,1,0,3:T(8,128)(2,1)} %bitcast.18, bf16[4,2,512,512]{3,2,1,0:T(8,128)(2,1)S(1)} %copy-done.13, s32[]{:T(128)S(6)} %select_n.29), kind=kOutput, calls=%fused_computation.2 | convolution fusion | flops 1073741824 | bytes 6291460 | tf_op jit(solution)/shard_map/cri,kio->ckro/dot_general | solution.py:68
  35.0 0.0 collective-permute-done.2
  35.0 0.2 collective-permute-start.3
  35.2 2.5 %convolution_bitcast_fusion.1 = f32[2,2,512,512]{3,2,0,1:T(8,128)S(1)} fusion(bf16[2,512,512,1]{2,1,0,3:T(8,128)(2,1)} %bitcast.26, bf16[4,2,512,512]{3,2,1,0:T(8,128)(2,1)S(1)} %copy-done.13, s32[]{:T(128)S(6)} %select_n.31), kind=kOutput, calls=%fused_computation.1 | convolution fusion | flops 1073741824 | bytes 6291460 | tf_op jit(solution)/shard_map/cri,kio->ckro/dot_general | solution.py:68
  37.8 0.5 slice_subtract_fusion.4
  38.3 0.0 copy-start.4
  38.3 0.0 copy-start.5
  38.3 0.5 slice_subtract_fusion.3
  38.8 0.0 copy-start.6
  38.8 0.0 copy-start.7
  38.8 6.3 %collective-permute-done.1 = bf16[2,2,256,512]{3,2,1,0:T(8,128)(2,1)S(1)} collective-permute-done((bf16[2,2,256,512]{3,2,1,0:T(8,128)(2,1)}, bf16[2,2,256,512]{3,2,1,0:T(8,128)(2,1)S(1)}, u32[]{:S(2)}, u32[]{:S(2)}) %collective-permute-start.1) | collective-permute-done | bytes 1048608 | tf_op jit(solution)/shard_map/ppermute | solution.py:10
  45.1 1.3 %convolution_bitcast_fusion.3 = f32[2,2,512,512]{3,2,0,1:T(8,128)S(1)} fusion(bf16[2,512,512,1]{2,1,0,3:T(8,128)(2,1)S(1)} %bitcast.135, bf16[4,2,512,512]{3,2,1,0:T(8,128)(2,1)S(1)} %copy-done.13, s32[]{:T(128)S(6)} %select_n.27), kind=kOutput, calls=%fused_computation.3 | convolution fusion | flops 1073741824 | bytes 6291460 | tf_op jit(solution)/shard_map/cri,kio->ckro/dot_general | solution.py:68
  46.4 0.5 slice_subtract_fusion.5
  46.9 5.6 %collective-permute-done.3 = bf16[2,2,256,512]{3,2,1,0:T(8,128)(2,1)S(1)} collective-permute-done((bf16[2,2,256,512]{3,2,1,0:T(8,128)(2,1)}, bf16[2,2,256,512]{3,2,1,0:T(8,128)(2,1)S(1)}, u32[]{:S(2)}, u32[]{:S(2)}) %collective-permute-start.3) | collective-permute-done | bytes 1048608 | tf_op jit(solution)/shard_map/ppermute | solution.py:10
  52.5 1.3 %convolution_bitcast_fusion = f32[2,2,512,512]{3,2,0,1:T(8,128)S(1)} fusion(bf16[2,512,512,1]{2,1,0,3:T(8,128)(2,1)S(1)} %bitcast.134, bf16[4,2,512,512]{3,2,1,0:T(8,128)(2,1)S(1)} %copy-done.13, s32[]{:T(128)S(6)} %select_n.33), kind=kOutput, calls=%fused_computation | convolution fusion | flops 1073741824 | bytes 6291460 | tf_op jit(solution)/shard_map/cri,kio->ckro/dot_general | solution.py:68
  53.7 0.0 copy-start.2
  53.8 0.5 slice_subtract_fusion.2
  54.3 0.0 copy-start.11
  54.3 0.6 copy-done.2
  55.0 0.6 copy-done.3
  55.5 6.0 %add_reduce_fusion.4 = (f32[2,2]{1,0:T(2,128)S(1)}, f32[2,2]{1,0:T(2,128)S(1)}, f32[2,2]{1,0:T(2,128)S(1)}, f32[2,2]{1,0:T(2,128)S(1)}, f32[2,2]{1,0:T(2,128)S(1...) fusion(f32[2,256,512]{2,1,0:T(8,128)S(1)} %bitcast.128, ...), kind=kLoop, calls=%fused_computation.20 | loop fusion | flops 20971480 | bytes 12583072 | tf_op jit(solution)/shard_map/reduce_sum | solution.py:56
  61.6 0.0 copy-done.11
  61.6 0.1 add.216
  61.7 0.1 add.221
  61.8 0.1 pad_maximum_fusion.1
  61.9 0.6 broadcast_in_dim.28
  62.5 9.8 %all-to-all-start = ((f32[16,1,10]{2,1,0:T(1,128)}), f32[16,1,10]{2,1,0:T(1,128)S(1)}, u32[]{:S(2)}, u32[]{:S(2)}) async-start(f32[16,1,10]{2,1,0:T(1,128)} %broadcast_in_dim.28), calls=%async_computation | async-start | bytes 16384 | tf_op jit(solution)/shard_map/all_to_all | solution.py:19
  72.3 6.4 %convert_bitcast_fusion = (bf16[1,2,2,256,512]{4,3,2,1,0:T(8,128)(2,1)}, f32[2,2,256,512]{3,2,1,0:T(8,128)}) fusion(f32[1,2,256,512]{3,2,1,0:T(8,128)} %bitcast.133, f32[1,2,256,512]{3,2,1,0:T(8,128)} %bitcast.131, f32[1,2,256,512]{3,2,1,0:T(8,128)} %bitcast.125, f32[1,2,256,512]{3,2,1,0:T(8,128)} %bitcast.123, f32[1,2,256,512]{3,2,1,0:T(8,128)} %bitcast.121, ...), kind=kLoop, calls=%fused_computation.44 | loop fusion | flops 4718592 | bytes 13631488 | tf_op jit(solution)/shard_map/broadcast_in_dim | solution.py:85
  78.7 0.0 all-to-all-done
  78.7 0.1 fusion.29
  78.8 0.1 slice_add_fusion.4
  78.9 0.1 reshape.401
  79.0 0.1 reshape.402
  79.1 0.1 broadcast_divide_fusion.1
  79.1 2.3 %subtract_reduce_fusion = (f32[2,256,512]{2,1,0:T(8,128)S(1)}, f32[2,256,512]{2,1,0:T(8,128)S(1)}) fusion(f32[2,2]{1,0:T(2,128)S(1)} %get-tuple-element.43, f32[2,2]{1,0:T(2,128)S(1)} %get-tuple-element.42, f32[2,256,512]{2,1,0:T(8,128)} %get-tuple-element.41, f32[2,256,512]{2,1,0:T(8,128)S(1)} %copy-done.2), kind=kLoop, calls=%fused_computation.11 | loop fusion | flops 3670016 | bytes 4194336 | tf_op jit(solution)/shard_map/reduce_sum | solution.py:82
  81.4 0.0 copy-done.12
  81.4 0.6 fusion.14
  82.0 1.1 %pad_maximum_fusion = bf16[1,2,2,256,512]{4,3,2,1,0:T(8,128)(2,1)} fusion(bf16[1,1,2,256,512]{4,3,2,1,0:T(8,128)(2,1)S(1)} %get-tuple-element.37, bf16[1,1,2,256,512]{4,3,2,1,0:T(8,128)(2,1)S(1)} %get-tuple-element.36), kind=kLoop, calls=%fused_computation.38 | loop fusion | flops 524288 | bytes 2097152 | tf_op jit(solution)/shard_map/stack | solution.py:84
  (18 shorter events, 0.1 us)
Async XLA Ops:
  0.6 8.8 %copy-start = (bf16[128,128]{1,0:T(8,128)(2,1)S(1)}, bf16[128,128]{1,0:T(8,128)(2,1)}, u32[]{:S(2)}) copy-start(bf16[128,128]{1,0:T(8,128)(2,1)} %param.9) | copy-start | bytes 98308
  0.6 7.1 %copy-start.1 = (bf16[1,2,2,256,512]{4,3,2,1,0:T(8,128)(2,1)S(1)}, bf16[1,2,2,256,512]{4,3,2,1,0:T(8,128)(2,1)}, u32[]{:S(2)}) copy-start(bf16[1,2,2,256,512]{4,3,2,1,0:T(8,128)(2,1)} %param.7) | copy-start | bytes 3145732
  0.7 27.3 %collective-permute-start = (bf16[2,2,256,512]{3,2,1,0:T(8,128)(2,1)}, bf16[2,2,256,512]{3,2,1,0:T(8,128)(2,1)}, u32[]{:S(2)}, u32[]{:S(2)}) collective-permute-start(bf16[2,2,256,512]{3,2,1,0:T(8,128)(2,1)} %bitcast.116), channel_id=1, source_target_pairs={{0,15},{1,0},{2,1},{3,2},{4,3},{5,4},{6,5},{7,6},{8,7},{9,8},{10,9... | collective-permute-start | bytes 3145736 | tf_op jit(solution)/shard_map/ppermute | solution.py:10
  6.2 28.8 %collective-permute-start.2 = (bf16[2,2,256,512]{3,2,1,0:T(8,128)(2,1)}, bf16[2,2,256,512]{3,2,1,0:T(8,128)(2,1)}, u32[]{:S(2)}, u32[]{:S(2)}) collective-permute-start(bf16[2,2,256,512]{3,2,1,0:T(8,128)(2,1)} %bitcast.117), channel_id=1, source_target_pairs={{0,1},{1,2},{2,3},{3,4},{4,5},{5,6},{6,7},{7,8},{8,9},{9,10},{10,1... | collective-permute-start | bytes 3145736 | tf_op jit(solution)/shard_map/ppermute | solution.py:10
  9.2 1.2 %copy-start.14 = (bf16[4096,128]{1,0:T(8,128)(2,1)S(1)}, bf16[4096,128]{1,0:T(8,128)(2,1)}, u32[]{:S(2)}) copy-start(bf16[4096,128]{1,0:T(8,128)(2,1)} %reshape_squeeze.3) | copy-start | bytes 3145732
  12.1 1.5 %copy-start.16 = (s32[4]{0:T(128)S(1)}, s32[4]{0:T(128)}, u32[]{:S(2)}) copy-start(s32[4]{0:T(128)} %param.12) | copy-start | bytes 52
  19.3 2.8 %copy-start.17 = (s32[2,2]{1,0:T(2,128)S(1)}, s32[2,2]{1,0:T(2,128)}, u32[]{:S(2)}) copy-start(s32[2,2]{1,0:T(2,128)} %param.11) | copy-start | bytes 52
  19.4 6.3 %copy-start.15 = (bf16[256,256]{1,0:T(8,128)(2,1)S(1)}, bf16[256,256]{1,0:T(8,128)(2,1)}, u32[]{:S(2)}) copy-start(bf16[256,256]{1,0:T(8,128)(2,1)} %param.10) | copy-start | bytes 393220
  27.8 4.7 %copy-start.13 = (bf16[4,2,512,512]{3,2,1,0:T(8,128)(2,1)S(1)}, bf16[4,2,512,512]{3,2,1,0:T(8,128)(2,1)}, u32[]{:S(2)}) copy-start(bf16[4,2,512,512]{3,2,1,0:T(8,128)(2,1)} %param.8) | copy-start | bytes 12582916
  28.0 17.1 %collective-permute-start.1 = (bf16[2,2,256,512]{3,2,1,0:T(8,128)(2,1)}, bf16[2,2,256,512]{3,2,1,0:T(8,128)(2,1)S(1)}, u32[]{:S(2)}, u32[]{:S(2)}) collective-permute-start(bf16[2,2,256,512]{3,2,1,0:T(8,128)(2,1)} %collective-permute-done), channel_id=1, source_target_pairs={{0,15},{1,0},{2,1},{3,2},{4,3},{5,4},{6,5},{7,6},{8,7},{9,8},{10,9... | collective-permute-start | bytes 3145736 | tf_op jit(solution)/shard_map/ppermute | solution.py:10
  35.0 17.5 %collective-permute-start.3 = (bf16[2,2,256,512]{3,2,1,0:T(8,128)(2,1)}, bf16[2,2,256,512]{3,2,1,0:T(8,128)(2,1)S(1)}, u32[]{:S(2)}, u32[]{:S(2)}) collective-permute-start(bf16[2,2,256,512]{3,2,1,0:T(8,128)(2,1)} %collective-permute-done.2), channel_id=1, source_target_pairs={{0,1},{1,2},{2,3},{3,4},{4,5},{5,6},{6,7},{7,8},{8,9},{9,10},{10,1... | collective-permute-start | bytes 3145736 | tf_op jit(solution)/shard_map/ppermute | solution.py:10
  38.3 16.0 %copy-start.4 = (f32[1,1,512,512]{3,2,0,1:T(8,128)}, f32[1,1,512,512]{3,2,0,1:T(8,128)S(1)}, u32[]{:S(2)}) copy-start(f32[1,1,512,512]{3,2,0,1:T(8,128)S(1)} %get-tuple-element.30) | copy-start | bytes 3145732
  38.3 16.0 %copy-start.5 = (f32[1,1,512,512]{3,2,0,1:T(8,128)}, f32[1,1,512,512]{3,2,0,1:T(8,128)S(1)}, u32[]{:S(2)}) copy-start(f32[1,1,512,512]{3,2,0,1:T(8,128)S(1)} %get-tuple-element.31) | copy-start | bytes 3145732
  38.8 15.5 %copy-start.6 = (f32[1,1,512,512]{3,2,0,1:T(8,128)}, f32[1,1,512,512]{3,2,0,1:T(8,128)S(1)}, u32[]{:S(2)}) copy-start(f32[1,1,512,512]{3,2,0,1:T(8,128)S(1)} %get-tuple-element.32) | copy-start | bytes 3145732
  38.8 15.5 %copy-start.7 = (f32[1,1,512,512]{3,2,0,1:T(8,128)}, f32[1,1,512,512]{3,2,0,1:T(8,128)S(1)}, u32[]{:S(2)}) copy-start(f32[1,1,512,512]{3,2,0,1:T(8,128)S(1)} %get-tuple-element.33) | copy-start | bytes 3145732
  46.9 7.5 %copy-start.8 = (f32[1,1,512,512]{3,2,0,1:T(8,128)}, f32[1,1,512,512]{3,2,0,1:T(8,128)S(1)}, u32[]{:S(2)}) copy-start(f32[1,1,512,512]{3,2,0,1:T(8,128)S(1)} %get-tuple-element.28) | copy-start | bytes 3145732
  46.9 7.5 %copy-start.9 = (f32[1,1,512,512]{3,2,0,1:T(8,128)}, f32[1,1,512,512]{3,2,0,1:T(8,128)S(1)}, u32[]{:S(2)}) copy-start(f32[1,1,512,512]{3,2,0,1:T(8,128)S(1)} %get-tuple-element.29) | copy-start | bytes 3145732
  53.7 1.2 %copy-start.2 = (f32[2,256,512]{2,1,0:T(8,128)S(1)}, f32[2,256,512]{2,1,0:T(8,128)}, u32[]{:S(2)}) copy-start(f32[2,256,512]{2,1,0:T(8,128)} %get-tuple-element.40) | copy-start | bytes 3145732
  53.8 1.8 %copy-start.3 = (f32[2,256,512]{2,1,0:T(8,128)S(1)}, f32[2,256,512]{2,1,0:T(8,128)}, u32[]{:S(2)}) copy-start(f32[2,256,512]{2,1,0:T(8,128)} %get-tuple-element.41) | copy-start | bytes 3145732
  54.2 7.3 %copy-start.10 = (f32[1,1,512,512]{3,2,0,1:T(8,128)}, f32[1,1,512,512]{3,2,0,1:T(8,128)S(1)}, u32[]{:S(2)}) copy-start(f32[1,1,512,512]{3,2,0,1:T(8,128)S(1)} %get-tuple-element.34) | copy-start | bytes 3145732
  54.3 7.3 %copy-start.11 = (f32[1,1,512,512]{3,2,0,1:T(8,128)}, f32[1,1,512,512]{3,2,0,1:T(8,128)S(1)}, u32[]{:S(2)}) copy-start(f32[1,1,512,512]{3,2,0,1:T(8,128)S(1)} %get-tuple-element.35) | copy-start | bytes 3145732
  62.5 16.3 %all-to-all-start = ((f32[16,1,10]{2,1,0:T(1,128)}), f32[16,1,10]{2,1,0:T(1,128)S(1)}, u32[]{:S(2)}, u32[]{:S(2)}) async-start(f32[16,1,10]{2,1,0:T(1,128)} %broadcast_in_dim.28), calls=%async_computation | async-start | bytes 16384 | tf_op jit(solution)/shard_map/all_to_all | solution.py:19
  79.1 2.3 %copy-start.12 = (f32[2,2,256,512]{3,2,1,0:T(8,128)S(1)}, f32[2,2,256,512]{3,2,1,0:T(8,128)}, u32[]{:S(2)}) copy-start(f32[2,2,256,512]{3,2,1,0:T(8,128)} %get-tuple-element.27) | copy-start | bytes 6291460

commit v8 on v2

--- a/solution.py
+++ b/solution.py
@@ -28,9 +28,7 @@
 
 def body(perturbation, coupling, y_operator, x_operator, tile_mask, slot_offsets, detuning):
     block = perturbation[0]
-    vecs = block.shape[1]
-    width_x = block.shape[2]
-    width_fy = block.shape[3]
+    parts, vecs, width_x, width_fy = block.shape
     ny = y_operator.shape[0]
     harmonics = lax.axis_size("harm")
     position = lax.axis_index("harm")
@@ -43,34 +41,30 @@
     along_y = jnp.dot(rows, y_operator, preferred_element_type=jnp.float32).reshape(block.shape)
     full_mask = jnp.repeat(jnp.repeat(tile_mask, tile, axis=0), tile, axis=1).astype(jnp.bfloat16)
     masked = x_operator * full_mask
-    along_x = jnp.einsum("ab,cvbf->cvaf", masked, block, preferred_element_type=jnp.float32)
+    planes = block.reshape(parts * vecs, width_x, width_fy)
+    spread = jnp.broadcast_to(masked, (parts * vecs,) + masked.shape)
+    along_x = jnp.einsum("nab,nbf->naf", spread, planes, preferred_element_type=jnp.float32)
     centered = (position - harmonics // 2).astype(jnp.float32) + detuning[0]
     lam = -(centered * centered) / (4.0 * harmonics)
-    image = along_y + along_x + lam * block.astype(jnp.float32)
+    qfull = block.astype(jnp.float32)
+    image = along_y + along_x.reshape(block.shape) + lam * qfull
     sources = (above_two, above_one, below_one, below_two)
     counter = jnp.arange(4, dtype=jnp.int32)
     for place in range(4):
         slot = jnp.sum(jnp.where(slot_offsets == place, counter, 0))
         matrix = lax.dynamic_index_in_dim(coupling, slot, 0, keepdims=False)
-        other = sources[place].reshape(2, vecs * width_x, width_fy)
-        prod = jnp.einsum("cri,kio->ckro", other, matrix, preferred_element_type=jnp.float32)
-        real_part = prod[0, 0] - prod[1, 1]
-        imag_part = prod[0, 1] + prod[1, 0]
-        image = image + jnp.stack([real_part, imag_part]).reshape(block.shape)
-    qfull = block.astype(jnp.float32)
-    qr = qfull[0]
-    qi = qfull[1]
-    wr = image[0]
-    wi = image[1]
-    num_re = jnp.sum(qr[:, None] * wr[None, :] + qi[:, None] * wi[None, :], axis=(2, 3))
-    num_im = jnp.sum(qr[:, None] * wi[None, :] - qi[:, None] * wr[None, :], axis=(2, 3))
-    norms = jnp.sum(qr * qr + qi * qi, axis=(1, 2))
+        real_form = jnp.stack([jnp.stack([matrix[0], matrix[1]]), jnp.stack([-matrix[1], matrix[0]])])
+        other = sources[place].reshape(parts, vecs * width_x, width_fy)
+        term = jnp.einsum("cri,cdio->dro", other, real_form, preferred_element_type=jnp.float32)
+        image = image + term.reshape(block.shape)
+    turned = jnp.stack([-qfull[1], qfull[0]])
+    num_re = jnp.sum(qfull[:, :, None] * image[:, None], axis=(0, 3, 4))
+    num_im = jnp.sum(turned[:, :, None] * image[:, None], axis=(0, 3, 4))
+    norms = jnp.sum(qfull * qfull, axis=(0, 2, 3))
     total_re, total_im, total_norms = summed_over(("harm",), num_re, num_im, norms)
-    h_re = (total_re / (total_norms + 1e-06)[:, None])[:, :, None, None]
-    h_im = (total_im / (total_norms + 1e-06)[:, None])[:, :, None, None]
-    proj_re = wr - jnp.sum(h_re * qr[:, None] - h_im * qi[:, None], axis=0)
-    proj_im = wi - jnp.sum(h_re * qi[:, None] + h_im * qr[:, None], axis=0)
-    projected = jnp.stack([proj_re, proj_im])
+    h_re = (total_re / (total_norms + 1e-06)[:, None])[None, :, :, None, None]
+    h_im = (total_im / (total_norms + 1e-06)[:, None])[None, :, :, None, None]
+    projected = image - jnp.sum(h_re * qfull[:, :, None] + h_im * turned[:, :, None], axis=1)
     return (image.astype(jnp.bfloat16)[None], projected.astype(jnp.bfloat16)[None])
 
 

time: 78.7 us -> 91.8 us (1.17)
  other arithmetic: 10.2 us -> 23.2 us
  local copies, waits for them, and re-layouts: 5.7 us -> 15 us
  waiting for transfers between devices: 16.1 us -> 9.92 us
  starting transfers between devices: 28.2 us -> 22.1 us
  matrix products: 8.93 us -> 11.6 us
    convert_element_type x1 -> x2, other arithmetic: 0.27 us -> 6.46 us  [the longest x1 6.18 us: body(): projected.astype(jnp.bfloat16)[None]]
    neg x0 -> x2, other arithmetic: none -> 5.4 us  [the longest x1 3.75 us: body(): -matrix[1]]
    ppermute x4, waiting for transfers between devices: 10.8 us -> 6.37 us  [passed_along(): return lax.ppermute(value, axis, pairs)]
    reshape x1 -> x2, local copies, waits for them, and re-layouts: 1.53 us -> 5.55 us  [body(): jnp.dot(rows, y_operator, preferred_element_type=jnp.float32)]
    all_to_all x1, starting transfers between devices: 15.7 us -> 12 us  [summed_over(): gathered = lax.all_to_all(spread, axes, 0, 0, tiled=False)]
    unnamed x18 -> x52, local copies, waits for them, and re-layouts: 0.77 us -> 4.23 us
    dot_general x1, matrix products: 0.41 us -> 2.98 us  [body(): jnp.dot(rows, y_operator, preferred_element_type=jnp.float32)]
    ppermute x4, starting transfers between devices: 12.4 us -> 10.1 us  [passed_along(): return lax.ppermute(value, axis, pairs)]
  transfers between devices with their start and end apart: 5 -> 5, of which waited for: 3 -> 2; matrix products, arithmetic and copies ran while one was open for 19% -> 34% of each run, Pallas kernels for 0% -> 0%
where the time goes in v8:
time: 91.8 us; the launch traced here: 91.2 us
  other arithmetic  23.2 us (25%)
  starting transfers between devices  22.1 us (24%)
  local copies, waits for them, and re-layouts  15 us (16%)
  matrix products  11.6 us (13%)
  waiting for transfers between devices  9.92 us (11%)
  between operations  9.36 us (10%)
    all_to_all x1, starting transfers between devices, summed_over(): gathered = lax.all_to_all(spread, axes, 0, 0, tiled=False)  12 us
    ppermute x4, starting transfers between devices, passed_along(): return lax.ppermute(value, axis, pairs)  10.1 us
    dot_general x4, matrix products, body(): jnp.einsum('cri,cdio->dro', other, real_form, preferred_element_type=jnp....  8.19 us
    ppermute x4, waiting for transfers between devices, passed_along(): return lax.ppermute(value, axis, pairs)  6.37 us
    convert_element_type x1, other arithmetic, body(): projected.astype(jnp.bfloat16)[None]  6.18 us
    reshape x2, local copies, waits for them, and re-layouts, body(): jnp.dot(rows, y_operator, preferred_element_type=jnp.float32)  5.55 us
    unnamed x52, local copies, waits for them, and re-layouts  4.23 us
    neg x1, other arithmetic, body(): -matrix[1]  3.75 us
  transfers between devices with their start and end apart: 5, of which 2 were waited for; matrix products, arithmetic and copies ran while one was open for 34% of the time, Pallas kernels for 0%

profile of v8, /device:TPU:0, one launch (start us, length us, event | category | flops | bytes accessed | tf_op | source)
XLA Modules:
  0.0 91.2 jit_solution(1305708835734605272)
XLA Ops:
  0.6 0.0 copy-start
  0.6 0.0 copy-start.1
  0.7 0.5 collective-permute-start.2
  1.2 5.1 %collective-permute-start = (bf16[2,2,256,512]{3,2,1,0:T(8,128)(2,1)}, bf16[2,2,256,512]{3,2,1,0:T(8,128)(2,1)}, u32[]{:S(2)}, u32[]{:S(2)}) collective-permute-start(bf16[2,2,256,512]{3,2,1,0:T(8,128)(2,1)} %bitcast.116), channel_id=1, source_target_pairs={{0,15},{1,0},{2,1},{3,2},{4,3},{5,4},{6,5},{7,6},{8,7},{9,8},{10,9... | collective-permute-start | bytes 3145736 | tf_op jit(solution)/shard_map/ppermute | solution.py:10
  6.2 1.4 %fusion.19 = (s32[]{:T(128)}, s32[]{:T(128)}, s32[]{:T(128)}, s32[]{:T(128)}) fusion(s32[4]{0:T(128)} %param.12), kind=kLoop, calls=%fused_computation.49 | loop fusion | flops 44 | bytes 32 | tf_op jit(solution)/shard_map/reduce_sum | solution.py:54
  12.7 2.5 %reshape_squeeze.6 = bf16[4096,128]{1,0:T(8,128)(2,1)} reshape(bf16[1,2,2,256,512]{4,3,2,1,0:T(8,128)(2,1)} %param.7) | data formatting | bytes 2097152 | tf_op jit(solution)/shard_map/reshape;squeeze | solution.py:40
  15.2 0.0 copy-done.1
  15.2 0.3 bitcast_convert_fusion
  15.5 1.6 %slice_negate_fusion = (f32[1,2,256,512]{3,2,1,0:T(8,128)}, f32[1,2,256,512]{3,2,1,0:T(8,128)}) fusion(f32[2,2,256,512]{3,2,1,0:T(8,128)S(1)} %bitcast_convert_fusion), kind=kLoop, calls=%fused_computation.25 | loop fusion | flops 262144 | bytes 4194304 | tf_op jit(solution)/shard_map/neg | solution.py:60
  19.7 3.0 %fusion.32 = f32[4096,128]{1,0:T(8,128)} fusion(bf16[4096,128]{1,0:T(8,128)(2,1)} %reshape_squeeze.6, bf16[128,128]{1,0:T(8,128)(2,1)S(1)} %copy-done), kind=kOutput, calls=%fused_computation.67 | convolution fusion | flops 134217728 | bytes 3178496 | tf_op jit(solution)/shard_map/dot_general | solution.py:41
  22.7 3.7 %fusion.27 = (bf16[1,512,512]{2,1,0:T(8,128)(2,1)}, bf16[1,512,512]{2,1,0:T(8,128)(2,1)}, bf16[1,512,512]{2,1,0:T(8,128)(2,1)}, bf16[1,512,512]{2,1,0:T(8,128)(2...) fusion(bf16[4,2,512,512]{3,2,1,0:T(8,128)(2,1)} %param.8, ...), kind=kLoop, calls=%fused_computation.62 | loop fusion | flops 1048576 | bytes 6291476 | tf_op jit(solution)/shard_map/neg | solution.py:56
  26.5 1.4 %dynamic-slice_bitcast_fusion.7 = (bf16[1,512,512]{2,1,0:T(8,128)(2,1)}, bf16[1,512,512]{2,1,0:T(8,128)(2,1)}, bf16[1,512,512]{2,1,0:T(8,128)(2,1)}, bf16[1,512,512]{2,1,0:T(8,128)(2,1)}) fusion(bf16[4,2,512,512]{3,2,1,0:T(8,128)(2,1)S(1)} %copy-done.12, s32[]{:T(128)S(6)} %select_n.27, s32[]{:T(128)S(6)} %select_n.33, s32[]{:T(128)S(6)} %select_n.31, ...), kind=kLoop, calls=%fused_computation.41 | loop fusion | bytes 4194320 | tf_op jit(solution)/shard_map/slice | solution.py:56
  27.8 0.5 copy-done.13
  28.3 0.5 copy-done.14
  28.8 1.5 %pad_maximum_fusion = f32[2,2,256,512]{3,2,1,0:T(8,128)} fusion(f32[1,2,256,512]{3,2,1,0:T(8,128)S(1)} %copy-done.14, f32[1,2,256,512]{3,2,1,0:T(8,128)S(1)} %copy-done.13), kind=kLoop, calls=%fused_computation.19 | loop fusion | flops 524288 | bytes 4194304 | tf_op jit(solution)/shard_map/stack | solution.py:60
  30.2 2.8 %reshape.250 = f32[2,2,256,512]{3,2,1,0:T(8,128)} reshape(f32[4096,128]{1,0:T(8,128)} %fusion.32) | data formatting | bytes 4194304 | tf_op jit(solution)/shard_map/reshape | solution.py:41
  33.7 0.0 copy-done.25
  33.7 1.8 %maximum_bitcast_fusion.6 = (bf16[1,2,512,512]{3,2,0,1:T(8,128)(2,1)S(1)}, bf16[1,2,512,512]{3,2,0,1:T(8,128)(2,1)S(1)}) fusion(bf16[1,512,512]{2,1,0:T(8,128)(2,1)} %get-tuple-element.21, bf16[1,512,512]{2,1,0:T(8,128)(2,1)} %get-tuple-element.25, bf16[1,512,512]{2,1,0:T(8,128)(2,1)} %get-tuple-element.20), kind=kLoop, calls=%fused_computation.32 | loop fusion | flops 1048576 | bytes 3670016 | tf_op jit(solution)/shard_map/stack | solution.py:56
  35.6 0.1 copy-done.23
  35.7 0.2 maximum_bitcast_fusion.4
  35.9 0.0 copy-start.24
  35.9 0.7 copy-done.17
  36.6 0.2 copy-done.18
  36.8 0.2 copy-done.22
  36.9 0.2 maximum_bitcast_fusion.2
  37.1 0.0 copy-start.15
  37.2 0.3 broadcast_in_dim.14
  37.5 0.0 collective-permute-done.2
  37.6 0.1 collective-permute-start.3
  37.6 0.4 fusion.17
  38.1 0.0 collective-permute-done
  38.1 4.5 %collective-permute-start.1 = (bf16[2,2,256,512]{3,2,1,0:T(8,128)(2,1)}, bf16[2,2,256,512]{3,2,1,0:T(8,128)(2,1)S(1)}, u32[]{:S(2)}, u32[]{:S(2)}) collective-permute-start(bf16[2,2,256,512]{3,2,1,0:T(8,128)(2,1)} %collective-permute-done), channel_id=1, source_target_pairs={{0,15},{1,0},{2,1},{3,2},{4,3},{5,4},{6,5},{7,6},{8,7},{9,8},{10,9... | collective-permute-start | bytes 3145736 | tf_op jit(solution)/shard_map/ppermute | solution.py:10
  42.6 0.0 copy-done.16
  42.6 0.2 maximum_bitcast_fusion
  42.8 2.5 %fusion.8 = f32[2,512,512,1]{1,2,3,0:T(8,128)S(1)} fusion(bf16[2,512,512,1]{2,1,0,3:T(8,128)(2,1)} %bitcast.33, bf16[1,2,512,512]{3,2,0,1:T(8,128)(2,1)S(1)} %get-tuple-element.37, bf16[1,2,512,512]{3,2,0,1:T(8,128)(2,1)S(1)} %get-tuple-element.36), kind=kOutput, calls=%fused_computation.11 | convolution fusion | flops 1077936128 | bytes 5242880 | tf_op jit(solution)/shard_map/cri,cdio->dro/dot_general | solution.py:58
  45.2 3.2 %fusion.4 = f32[2,512,512,1]{1,2,3,0:T(8,128)S(1)} fusion(bf16[2,512,512,1]{2,1,0,3:T(8,128)(2,1)} %bitcast.22, bf16[1,2,512,512]{3,2,0,1:T(8,128)(2,1)S(1)} %get-tuple-element.35, bf16[1,2,512,512]{3,2,0,1:T(8,128)(2,1)S(1)} %get-tuple-element.34), kind=kOutput, calls=%fused_computation.7 | convolution fusion | flops 1077936128 | bytes 5242880 | tf_op jit(solution)/shard_map/cri,cdio->dro/dot_general | solution.py:58
  48.5 6.4 %collective-permute-done.3 = bf16[2,2,256,512]{3,2,1,0:T(8,128)(2,1)S(1)} collective-permute-done((bf16[2,2,256,512]{3,2,1,0:T(8,128)(2,1)}, bf16[2,2,256,512]{3,2,1,0:T(8,128)(2,1)S(1)}, u32[]{:S(2)}, u32[]{:S(2)}) %collective-permute-start.3) | collective-permute-done | bytes 1048608 | tf_op jit(solution)/shard_map/ppermute | solution.py:10
  54.8 1.2 %fusion.12 = f32[2,512,512,1]{1,2,3,0:T(8,128)S(1)} fusion(bf16[2,512,512,1]{2,1,0,3:T(8,128)(2,1)S(1)} %bitcast.129, bf16[1,2,512,512]{3,2,0,1:T(8,128)(2,1)S(1)} %get-tuple-element.39, bf16[1,2,512,512]{3,2,0,1:T(8,128)(2,1)S(1)} %get-tuple-element.38), kind=kOutput, calls=%fused_computation.15 | convolution fusion | flops 1077936128 | bytes 5242880 | tf_op jit(solution)/shard_map/cri,cdio->dro/dot_general | solution.py:58
  56.1 0.0 collective-permute-done.1
  56.1 1.2 %fusion = f32[2,512,512,1]{1,2,3,0:T(8,128)S(1)} fusion(bf16[2,512,512,1]{2,1,0,3:T(8,128)(2,1)S(1)} %bitcast.130, bf16[1,2,512,512]{3,2,0,1:T(8,128)(2,1)S(1)} %get-tuple-element.33, bf16[1,2,512,512]{3,2,0,1:T(8,128)(2,1)S(1)} %get-tuple-element.32), kind=kOutput, calls=%fused_computation.3 | convolution fusion | flops 1077936128 | bytes 5242880 | tf_op jit(solution)/shard_map/cri,cdio->dro/dot_general | solution.py:58
  57.4 0.0 copy-start.10
  57.4 0.0 copy-done.2
  57.4 0.0 copy-done.5
  57.4 0.0 copy-done.7
  57.4 0.0 copy-done.9
  57.4 1.3 %copy-done.11 = f32[2,2,256,512]{3,2,1,0:T(8,128)S(1)} copy-done((f32[2,2,256,512]{3,2,1,0:T(8,128)S(1)}, f32[2,2,256,512]{3,2,1,0:T(8,128)}, u32[]{:S(2)}) %copy-start.11) | copy-done | bytes 2097176
  58.8 2.0 %add_add_fusion = (f32[2,2,256,512]{3,2,1,0:T(8,128)S(1)}, f32[2]{0:T(128)S(1)}) fusion(f32[2,2,256,512]{3,2,1,0:T(8,128)S(1)} %bitcast.123, f32[2,2,256,512]{3,2,1,0:T(8,128)S(1)} %bitcast.119, f32[2,2,256,512]{3,2,1,0:T(8,128)S(1)} %bitcast.121, f32[2,2,256,512]{3,2,1,0:T(8,128)S(1)} %bitcast.125, f32[2,2,256,512]{3,2,1,0:T(8,128)S(1)} %copy-done.11, ...), kind=kLoop, calls=%fused_computation.23 | loop fusion | flops 5242878 | bytes 15728652 | tf_op jit(solution)/shard_map/add | solution.py:59
  60.7 1.1 %multiply_reduce_fusion.1 = (f32[2,2]{1,0:T(2,128)S(1)}, f32[2,2]{1,0:T(2,128)S(1)}) fusion(f32[2,2,256,512]{3,2,1,0:T(8,128)S(1)} %get-tuple-element.30, f32[2,2,256,512]{3,2,1,0:T(8,128)S(1)} %bitcast_convert_fusion, f32[2,2,256,512]{3,2,1,0:T(8,128)S(1)} %copy-done.4), kind=kLoop, calls=%fused_computation.2 | loop fusion | flops 4194296 | bytes 6291488 | tf_op jit(solution)/shard_map/reduce_sum | solution.py:61
  61.9 0.1 reshape.257
  61.9 0.1 reshape.256
  62.0 0.1 pad_maximum_fusion.1
  62.1 0.6 broadcast_in_dim.16
  62.7 12.0 %all-to-all-start = ((f32[16,1,10]{2,1,0:T(1,128)}), f32[16,1,10]{2,1,0:T(1,128)S(1)}, u32[]{:S(2)}, u32[]{:S(2)}) async-start(f32[16,1,10]{2,1,0:T(1,128)} %broadcast_in_dim.16), calls=%async_computation | async-start | bytes 16384 | tf_op jit(solution)/shard_map/all_to_all | solution.py:19
  74.8 2.8 %reshape.240 = f32[1,2,2,256,512]{4,3,2,1,0:T(8,128)} reshape(f32[4096,128]{1,0:T(8,128)} %fusion.32) | data formatting | bytes 4194304 | tf_op jit(solution)/shard_map/reshape | solution.py:41
  77.5 3.5 %all-to-all-done = f32[16,1,10]{2,1,0:T(1,128)S(1)} async-done(((f32[16,1,10]{2,1,0:T(1,128)}), f32[16,1,10]{2,1,0:T(1,128)S(1)}, u32[]{:S(2)}, u32[]{:S(2)}) %all-to-all-start) | async-done | bytes 672 | tf_op jit(solution)/shard_map/all_to_all | solution.py:19
  81.1 0.1 fusion.31
  81.2 0.1 slice_add_fusion
  81.3 0.1 reshape.258
  81.4 0.1 reshape.259
  81.4 0.1 broadcast_divide_fusion.1
  81.5 2.7 %add_reduce_fusion = f32[2,2,256,512]{3,2,1,0:T(8,128)S(1)} fusion(f32[2,2]{1,0:T(2,128)S(1)} %get-tuple-element.41, f32[2,2]{1,0:T(2,128)S(1)} %get-tuple-element.40, f32[2,2,256,512]{3,2,1,0:T(8,128)} %pad_maximum_fusion, f32[2,2,256,512]{3,2,1,0:T(8,128)S(1)} %bitcast_convert_fusion), kind=kLoop, calls=%fused_computation | loop fusion | flops 3670016 | bytes 6291488 | tf_op jit(solution)/shard_map/reduce_sum | solution.py:67
  84.3 0.1 copy-done.6
  84.4 0.6 copy-done.8
  85.0 6.2 %fusion.16 = (bf16[1,2,2,256,512]{4,3,2,1,0:T(8,128)(2,1)}, bf16[1,2,2,256,512]{4,3,2,1,0:T(8,128)(2,1)}) fusion(f32[2,2,256,512]{3,2,1,0:T(8,128)S(1)} %add_reduce_fusion, f32[1,2,2,256,512]{4,3,2,1,0:T(8,128)} %bitcast.124, f32[1,2,2,256,512]{4,3,2,1,0:T(8,128)S(1)} %bitcast.120, f32[1,2,2,256,512]{4,3,2,1,0:T(8,128)S(1)} %bitcast.122, ...), kind=kLoop, calls=%fused_computation.21 | loop fusion | flops 5767168 | bytes 17825796 | tf_op jit(solution)/shard_map/convert_element_type | solution.py:68
  (35 shorter events, 0.1 us)
Async XLA Ops:
  0.6 19.1 %copy-start = (bf16[128,128]{1,0:T(8,128)(2,1)S(1)}, bf16[128,128]{1,0:T(8,128)(2,1)}, u32[]{:S(2)}) copy-start(bf16[128,128]{1,0:T(8,128)(2,1)} %param.9) | copy-start | bytes 98308
  0.6 14.6 %copy-start.1 = (bf16[1,2,2,256,512]{4,3,2,1,0:T(8,128)(2,1)S(1)}, bf16[1,2,2,256,512]{4,3,2,1,0:T(8,128)(2,1)}, u32[]{:S(2)}) copy-start(bf16[1,2,2,256,512]{4,3,2,1,0:T(8,128)(2,1)} %param.7) | copy-start | bytes 3145732
  0.7 36.9 %collective-permute-start.2 = (bf16[2,2,256,512]{3,2,1,0:T(8,128)(2,1)}, bf16[2,2,256,512]{3,2,1,0:T(8,128)(2,1)}, u32[]{:S(2)}, u32[]{:S(2)}) collective-permute-start(bf16[2,2,256,512]{3,2,1,0:T(8,128)(2,1)} %bitcast.115), channel_id=1, source_target_pairs={{0,1},{1,2},{2,3},{3,4},{4,5},{5,6},{6,7},{7,8},{8,9},{9,10},{10,1... | collective-permute-start | bytes 3145736 | tf_op jit(solution)/shard_map/ppermute | solution.py:10
  1.2 36.9 %collective-permute-start = (bf16[2,2,256,512]{3,2,1,0:T(8,128)(2,1)}, bf16[2,2,256,512]{3,2,1,0:T(8,128)(2,1)}, u32[]{:S(2)}, u32[]{:S(2)}) collective-permute-start(bf16[2,2,256,512]{3,2,1,0:T(8,128)(2,1)} %bitcast.116), channel_id=1, source_target_pairs={{0,15},{1,0},{2,1},{3,2},{4,3},{5,4},{6,5},{7,6},{8,7},{9,8},{10,9... | collective-permute-start | bytes 3145736 | tf_op jit(solution)/shard_map/ppermute | solution.py:10
  22.7 3.8 %copy-start.12 = (bf16[4,2,512,512]{3,2,1,0:T(8,128)(2,1)S(1)}, bf16[4,2,512,512]{3,2,1,0:T(8,128)(2,1)}, u32[]{:S(2)}) copy-start(bf16[4,2,512,512]{3,2,1,0:T(8,128)(2,1)} %param.8) | copy-start | bytes 12582916
  26.5 1.8 %copy-start.13 = (f32[1,2,256,512]{3,2,1,0:T(8,128)S(1)}, f32[1,2,256,512]{3,2,1,0:T(8,128)}, u32[]{:S(2)}) copy-start(f32[1,2,256,512]{3,2,1,0:T(8,128)} %get-tuple-element.28) | copy-start | bytes 3145732
  26.5 2.3 %copy-start.14 = (f32[1,2,256,512]{3,2,1,0:T(8,128)S(1)}, f32[1,2,256,512]{3,2,1,0:T(8,128)}, u32[]{:S(2)}) copy-start(f32[1,2,256,512]{3,2,1,0:T(8,128)} %get-tuple-element.29) | copy-start | bytes 3145732
  30.2 3.4 %copy-start.25 = (s32[2,2]{1,0:T(2,128)S(1)}, s32[2,2]{1,0:T(2,128)}, u32[]{:S(2)}) copy-start(s32[2,2]{1,0:T(2,128)} %param.11) | copy-start | bytes 52
  33.7 1.9 %copy-start.19 = (bf16[1,512,512]{2,1,0:T(8,128)(2,1)S(1)}, bf16[1,512,512]{2,1,0:T(8,128)(2,1)}, u32[]{:S(2)}) copy-start(bf16[1,512,512]{2,1,0:T(8,128)(2,1)} %get-tuple-element.22) | copy-start | bytes 1572868
  33.7 1.9 %copy-start.20 = (bf16[1,512,512]{2,1,0:T(8,128)(2,1)S(1)}, bf16[1,512,512]{2,1,0:T(8,128)(2,1)}, u32[]{:S(2)}) copy-start(bf16[1,512,512]{2,1,0:T(8,128)(2,1)} %get-tuple-element.23) | copy-start | bytes 1572868
  33.7 2.0 %copy-start.23 = (bf16[1,512,512]{2,1,0:T(8,128)(2,1)S(1)}, bf16[1,512,512]{2,1,0:T(8,128)(2,1)}, u32[]{:S(2)}) copy-start(bf16[1,512,512]{2,1,0:T(8,128)(2,1)} %get-tuple-element.26) | copy-start | bytes 1572868
  35.5 1.1 %copy-start.17 = (bf16[1,512,512]{2,1,0:T(8,128)(2,1)S(1)}, bf16[1,512,512]{2,1,0:T(8,128)(2,1)}, u32[]{:S(2)}) copy-start(bf16[1,512,512]{2,1,0:T(8,128)(2,1)} %get-tuple-element.18) | copy-start | bytes 1572868
  35.6 1.2 %copy-start.18 = (bf16[1,512,512]{2,1,0:T(8,128)(2,1)S(1)}, bf16[1,512,512]{2,1,0:T(8,128)(2,1)}, u32[]{:S(2)}) copy-start(bf16[1,512,512]{2,1,0:T(8,128)(2,1)} %get-tuple-element.19) | copy-start | bytes 1572868
  35.6 1.4 %copy-start.22 = (bf16[1,512,512]{2,1,0:T(8,128)(2,1)S(1)}, bf16[1,512,512]{2,1,0:T(8,128)(2,1)}, u32[]{:S(2)}) copy-start(bf16[1,512,512]{2,1,0:T(8,128)(2,1)} %get-tuple-element.27) | copy-start | bytes 1572868
  35.9 1.6 %copy-start.24 = (bf16[256,256]{1,0:T(8,128)(2,1)S(1)}, bf16[256,256]{1,0:T(8,128)(2,1)}, u32[]{:S(2)}) copy-start(bf16[256,256]{1,0:T(8,128)(2,1)} %param.10) | copy-start | bytes 393220
  37.1 5.4 %copy-start.15 = (bf16[1,512,512]{2,1,0:T(8,128)(2,1)S(1)}, bf16[1,512,512]{2,1,0:T(8,128)(2,1)}, u32[]{:S(2)}) copy-start(bf16[1,512,512]{2,1,0:T(8,128)(2,1)} %get-tuple-element.10) | copy-start | bytes 1572868
  37.1 5.4 %copy-start.16 = (bf16[1,512,512]{2,1,0:T(8,128)(2,1)S(1)}, bf16[1,512,512]{2,1,0:T(8,128)(2,1)}, u32[]{:S(2)}) copy-start(bf16[1,512,512]{2,1,0:T(8,128)(2,1)} %get-tuple-element.11) | copy-start | bytes 1572868
  37.1 5.4 %copy-start.21 = (bf16[1,512,512]{2,1,0:T(8,128)(2,1)S(1)}, bf16[1,512,512]{2,1,0:T(8,128)(2,1)}, u32[]{:S(2)}) copy-start(bf16[1,512,512]{2,1,0:T(8,128)(2,1)} %get-tuple-element.24) | copy-start | bytes 1572868
  37.6 17.3 %collective-permute-start.3 = (bf16[2,2,256,512]{3,2,1,0:T(8,128)(2,1)}, bf16[2,2,256,512]{3,2,1,0:T(8,128)(2,1)S(1)}, u32[]{:S(2)}, u32[]{:S(2)}) collective-permute-start(bf16[2,2,256,512]{3,2,1,0:T(8,128)(2,1)} %collective-permute-done.2), channel_id=1, source_target_pairs={{0,1},{1,2},{2,3},{3,4},{4,5},{5,6},{6,7},{7,8},{8,9},{9,10},{10,1... | collective-permute-start | bytes 3145736 | tf_op jit(solution)/shard_map/ppermute | solution.py:10
  38.1 19.3 %copy-start.2 = (f32[4,256,512]{2,1,0:T(8,128)}, f32[4,256,512]{2,1,0:T(8,128)S(1)}, u32[]{:S(2)}) copy-start(f32[4,256,512]{2,1,0:T(8,128)S(1)} %fusion.17) | copy-start | bytes 6291460
  38.1 18.0 %collective-permute-start.1 = (bf16[2,2,256,512]{3,2,1,0:T(8,128)(2,1)}, bf16[2,2,256,512]{3,2,1,0:T(8,128)(2,1)S(1)}, u32[]{:S(2)}, u32[]{:S(2)}) collective-permute-start(bf16[2,2,256,512]{3,2,1,0:T(8,128)(2,1)} %collective-permute-done), channel_id=1, source_target_pairs={{0,15},{1,0},{2,1},{3,2},{4,3},{5,4},{6,5},{7,6},{8,7},{9,8},{10,9... | collective-permute-start | bytes 3145736 | tf_op jit(solution)/shard_map/ppermute | solution.py:10
  45.2 12.2 %copy-start.5 = (f32[2,512,512,1]{1,2,3,0:T(8,128)}, f32[2,512,512,1]{1,2,3,0:T(8,128)S(1)}, u32[]{:S(2)}) copy-start(f32[2,512,512,1]{1,2,3,0:T(8,128)S(1)} %fusion.8) | copy-start | bytes 6291460
  48.5 8.9 %copy-start.7 = (f32[2,512,512,1]{1,2,3,0:T(8,128)}, f32[2,512,512,1]{1,2,3,0:T(8,128)S(1)}, u32[]{:S(2)}) copy-start(f32[2,512,512,1]{1,2,3,0:T(8,128)S(1)} %fusion.4) | copy-start | bytes 6291460
  56.1 1.3 %copy-start.9 = (f32[2,512,512,1]{1,2,3,0:T(8,128)}, f32[2,512,512,1]{1,2,3,0:T(8,128)S(1)}, u32[]{:S(2)}) copy-start(f32[2,512,512,1]{1,2,3,0:T(8,128)S(1)} %fusion.12) | copy-start | bytes 6291460
  56.1 2.6 %copy-start.11 = (f32[2,2,256,512]{3,2,1,0:T(8,128)S(1)}, f32[2,2,256,512]{3,2,1,0:T(8,128)}, u32[]{:S(2)}) copy-start(f32[2,2,256,512]{3,2,1,0:T(8,128)} %reshape.250) | copy-start | bytes 6291460
  57.4 3.3 %copy-start.10 = (f32[2,512,512,1]{1,2,3,0:T(8,128)}, f32[2,512,512,1]{1,2,3,0:T(8,128)S(1)}, u32[]{:S(2)}) copy-start(f32[2,512,512,1]{1,2,3,0:T(8,128)S(1)} %fusion) | copy-start | bytes 6291460
  58.8 2.0 %copy-start.4 = (f32[2,2,256,512]{3,2,1,0:T(8,128)S(1)}, f32[2,2,256,512]{3,2,1,0:T(8,128)}, u32[]{:S(2)}) copy-start(f32[2,2,256,512]{3,2,1,0:T(8,128)} %pad_maximum_fusion) | copy-start | bytes 6291460
  62.7 18.4 %all-to-all-start = ((f32[16,1,10]{2,1,0:T(1,128)}), f32[16,1,10]{2,1,0:T(1,128)S(1)}, u32[]{:S(2)}, u32[]{:S(2)}) async-start(f32[16,1,10]{2,1,0:T(1,128)} %broadcast_in_dim.16), calls=%async_computation | async-start | bytes 16384 | tf_op jit(solution)/shard_map/all_to_all | solution.py:19
  81.5 2.8 %copy-start.3 = (f32[4,256,512]{2,1,0:T(8,128)S(1)}, f32[4,256,512]{2,1,0:T(8,128)}, u32[]{:S(2)}) copy-start(f32[4,256,512]{2,1,0:T(8,128)} %copy-done.2) | copy-start | bytes 6291460
  81.5 2.9 %copy-start.6 = (f32[2,512,512,1]{1,2,3,0:T(8,128)S(1)}, f32[2,512,512,1]{1,2,3,0:T(8,128)}, u32[]{:S(2)}) copy-start(f32[2,512,512,1]{1,2,3,0:T(8,128)} %copy-done.5) | copy-start | bytes 6291460
  81.5 3.5 %copy-start.8 = (f32[2,512,512,1]{1,2,3,0:T(8,128)S(1)}, f32[2,512,512,1]{1,2,3,0:T(8,128)}, u32[]{:S(2)}) copy-start(f32[2,512,512,1]{1,2,3,0:T(8,128)} %copy-done.7) | copy-start | bytes 6291460

commit v9 on v2

--- a/solution.py
+++ b/solution.py
@@ -66,11 +66,13 @@
     num_im = jnp.sum(qr[:, None] * wi[None, :] - qi[:, None] * wr[None, :], axis=(2, 3))
     norms = jnp.sum(qr * qr + qi * qi, axis=(1, 2))
     total_re, total_im, total_norms = summed_over(("harm",), num_re, num_im, norms)
-    h_re = (total_re / (total_norms + 1e-06)[:, None])[:, :, None, None]
-    h_im = (total_im / (total_norms + 1e-06)[:, None])[:, :, None, None]
-    proj_re = wr - jnp.sum(h_re * qr[:, None] - h_im * qi[:, None], axis=0)
-    proj_im = wi - jnp.sum(h_re * qi[:, None] + h_im * qr[:, None], axis=0)
-    projected = jnp.stack([proj_re, proj_im])
+    h_re = total_re / (total_norms + 1e-06)[:, None]
+    h_im = total_im / (total_norms + 1e-06)[:, None]
+    turned = jnp.stack([-qi, qr])
+    projected = image
+    for vec in range(vecs):
+        projected = projected - (h_re[vec, :, None, None] * qfull[:, vec][:, None]
+                                 + h_im[vec, :, None, None] * turned[:, vec][:, None])
     return (image.astype(jnp.bfloat16)[None], projected.astype(jnp.bfloat16)[None])
 
 

time: 78.7 us -> 79.1 us (level)
  other arithmetic: 10.2 us -> 14.3 us
  waiting for transfers between devices: 16.1 us -> 13.5 us
  starting transfers between devices: 28.2 us -> 25.8 us
  local copies, waits for them, and re-layouts: 5.7 us -> 6.99 us
    mul x0 -> x2, other arithmetic: none -> 4.75 us  [the longest x1 3.11 us: body(): h_im[vec, :, None, None] * turned[:, vec][:, None]]
    broadcast_in_dim x1, other arithmetic: 1.1 us -> 4.06 us  [body(): projected.astype(jnp.bfloat16)[None]]
    ppermute x4, starting transfers between devices: 12.4 us -> 10.1 us  [passed_along(): return lax.ppermute(value, axis, pairs)]
    reduce_sum x1 -> x0, other arithmetic: 2.13 us -> none  [body(): proj_re = wr - jnp.sum(h_re * qr[:, None] - h_im * qi[:, None], axis=0)]
    all_to_all x1, waiting for transfers between devices: 5.3 us -> 3.28 us  [summed_over(): gathered = lax.all_to_all(spread, axes, 0, 0, tiled=False)]
    another operation x2 -> x0, other arithmetic: 1.66 us -> none  [body(): projected = jnp.stack([proj_re, proj_im])]
    mul x0 -> x2, local copies, waits for them, and re-layouts: none -> 1.49 us  [the longest x1 1.48 us: body(): h_re[vec, :, None, None] * qfull[:, vec][:, None]]
  transfers between devices with their start and end apart: 5 -> 5, of which waited for: 3 -> 3; matrix products, arithmetic and copies ran while one was open for 19% -> 25% of each run, Pallas kernels for 0% -> 0%
where the time goes in v9:
time: 79.1 us; the launch traced here: 78.7 us
  starting transfers between devices  25.8 us (33%)
  other arithmetic  14.3 us (18%)
  waiting for transfers between devices  13.5 us (17%)
  between operations  9.07 us (11%)
  matrix products  9.02 us (11%)
  local copies, waits for them, and re-layouts  6.99 us (9%)
    all_to_all x1, starting transfers between devices, summed_over(): gathered = lax.all_to_all(spread, axes, 0, 0, tiled=False)  15.7 us
    ppermute x4, waiting for transfers between devices, passed_along(): return lax.ppermute(value, axis, pairs)  10.3 us
    ppermute x4, starting transfers between devices, passed_along(): return lax.ppermute(value, axis, pairs)  10.1 us
    dot_general x4, matrix products, body(): jnp.einsum('cri,kio->ckro', other, matrix, preferred_element_type=jnp.flo...  7.5 us
    broadcast_in_dim x1, other arithmetic, body(): projected.astype(jnp.bfloat16)[None]  4.06 us
    all_to_all x1, waiting for transfers between devices, summed_over(): gathered = lax.all_to_all(spread, axes, 0, 0, tiled=False)  3.28 us
    mul x1, other arithmetic, body(): h_im[vec, :, None, None] * turned[:, vec][:, None]  3.11 us
    sub x4, other arithmetic, body(): real_part = prod[0, 0] - prod[1, 1]  1.92 us
  transfers between devices with their start and end apart: 5, of which 3 were waited for; matrix products, arithmetic and copies ran while one was open for 25% of the time, Pallas kernels for 0%

profile of v9, /device:TPU:0, one launch (start us, length us, event | category | flops | bytes accessed | tf_op | source)
XLA Modules:
  0.0 78.7 jit_solution(2856606376107645950)
XLA Ops:
  0.6 0.0 copy-start
  0.6 0.5 collective-permute-start.2
  1.1 5.1 %collective-permute-start = (bf16[2,2,256,512]{3,2,1,0:T(8,128)(2,1)}, bf16[2,2,256,512]{3,2,1,0:T(8,128)(2,1)}, u32[]{:S(2)}, u32[]{:S(2)}) collective-permute-start(bf16[2,2,256,512]{3,2,1,0:T(8,128)(2,1)} %bitcast.116), channel_id=1, source_target_pairs={{0,15},{1,0},{2,1},{3,2},{4,3},{5,4},{6,5},{7,6},{8,7},{9,8},{10,9... | collective-permute-start | bytes 3145736 | tf_op jit(solution)/shard_map/ppermute | solution.py:10
  6.2 1.4 %fusion.26 = (s32[]{:T(128)}, s32[]{:T(128)}, s32[]{:T(128)}, s32[]{:T(128)}) fusion(s32[4]{0:T(128)} %param.12), kind=kLoop, calls=%fused_computation.58 | loop fusion | flops 44 | bytes 32 | tf_op jit(solution)/shard_map/reduce_sum | solution.py:53
  12.7 1.7 %reshape_squeeze.3 = bf16[4096,128]{1,0:T(8,128)(2,1)S(1)} reshape(bf16[1,2,2,256,512]{4,3,2,1,0:T(8,128)(2,1)} %param.7) | data formatting | bytes 2097152 | tf_op jit(solution)/shard_map/reshape;squeeze | solution.py:42
  14.4 0.0 copy-done
  14.4 0.4 fusion.29
  14.8 0.0 copy-start.6
  14.8 0.0 copy-start.1
  14.8 1.5 %reshape.236 = f32[2,2,256,512]{3,2,1,0:T(8,128)} reshape(f32[4096,128]{1,0:T(8,128)S(1)} %fusion.29) | data formatting | bytes 4194304 | tf_op jit(solution)/shard_map/reshape | solution.py:43
  16.3 0.0 copy-done.6
  19.5 0.0 copy-done.1
  19.6 0.3 bitcast_convert_fusion
  19.8 0.3 add_reduce_fusion.1
  20.1 1.6 %slice_bitcast_fusion.9 = (f32[2,256,512]{2,1,0:T(8,128)S(1)}, f32[2,256,512]{2,1,0:T(8,128)S(1)}, f32[1,2,256,512]{3,2,1,0:T(8,128)}, f32[1,2,256,512]{3,2,1,0:T(8,128)}) fusion(f32[2,2,256,512]{3,2,1,0:T(8,128)S(1)} %bitcast_convert_fusion), kind=kLoop, calls=%fused_computation.69 | loop fusion | flops 262144 | bytes 6291456 | tf_op jit(solution)/shard_map/mul | solution.py:65
  21.8 0.0 copy-start.3
  21.8 1.5 %slice_bitcast_fusion.1 = (f32[2,256,512]{2,1,0:T(8,128)}, f32[2,256,512]{2,1,0:T(8,128)}) fusion(f32[2,2,256,512]{3,2,1,0:T(8,128)S(1)} %bitcast_convert_fusion), kind=kLoop, calls=%fused_computation.21 | loop fusion | bytes 4194304 | tf_op jit(solution)/shard_map/mul | solution.py:74
  23.2 0.0 collective-permute-done.2
  23.2 3.8 %collective-permute-start.3 = (bf16[2,2,256,512]{3,2,1,0:T(8,128)(2,1)}, bf16[2,2,256,512]{3,2,1,0:T(8,128)(2,1)S(1)}, u32[]{:S(2)}, u32[]{:S(2)}) collective-permute-start(bf16[2,2,256,512]{3,2,1,0:T(8,128)(2,1)} %collective-permute-done.2), channel_id=1, source_target_pairs={{0,1},{1,2},{2,3},{3,4},{4,5},{5,6},{6,7},{7,8},{8,9},{9,10},{10,1... | collective-permute-start | bytes 3145736 | tf_op jit(solution)/shard_map/ppermute | solution.py:10
  27.1 0.0 collective-permute-done
  27.1 0.0 copy-done.3
  27.1 2.5 %convolution_bitcast_fusion.2 = f32[2,2,512,512]{3,2,0,1:T(8,128)S(1)} fusion(bf16[2,512,512,1]{2,1,0,3:T(8,128)(2,1)} %bitcast.18, bf16[4,2,512,512]{3,2,1,0:T(8,128)(2,1)S(1)} %copy-done.3, s32[]{:T(128)S(6)} %select_n.29), kind=kOutput, calls=%fused_computation.2 | convolution fusion | flops 1073741824 | bytes 6291460 | tf_op jit(solution)/shard_map/cri,kio->ckro/dot_general | solution.py:56
  29.6 0.7 collective-permute-start.1
  30.2 2.5 %convolution_bitcast_fusion.1 = f32[2,2,512,512]{3,2,0,1:T(8,128)S(1)} fusion(bf16[2,512,512,1]{2,1,0,3:T(8,128)(2,1)} %bitcast.26, bf16[4,2,512,512]{3,2,1,0:T(8,128)(2,1)S(1)} %copy-done.3, s32[]{:T(128)S(6)} %select_n.31), kind=kOutput, calls=%fused_computation.1 | convolution fusion | flops 1073741824 | bytes 6291460 | tf_op jit(solution)/shard_map/cri,kio->ckro/dot_general | solution.py:56
  32.7 0.5 slice_subtract_fusion.2
  33.2 0.5 slice_subtract_fusion.1
  33.7 6.8 %collective-permute-done.3 = bf16[2,2,256,512]{3,2,1,0:T(8,128)(2,1)S(1)} collective-permute-done((bf16[2,2,256,512]{3,2,1,0:T(8,128)(2,1)}, bf16[2,2,256,512]{3,2,1,0:T(8,128)(2,1)S(1)}, u32[]{:S(2)}, u32[]{:S(2)}) %collective-permute-start.3) | collective-permute-done | bytes 1048608 | tf_op jit(solution)/shard_map/ppermute | solution.py:10
  40.5 1.3 %convolution_bitcast_fusion = f32[2,2,512,512]{3,2,0,1:T(8,128)S(1)} fusion(bf16[2,512,512,1]{2,1,0,3:T(8,128)(2,1)S(1)} %bitcast.126, bf16[4,2,512,512]{3,2,1,0:T(8,128)(2,1)S(1)} %copy-done.3, s32[]{:T(128)S(6)} %select_n.33), kind=kOutput, calls=%fused_computation | convolution fusion | flops 1073741824 | bytes 6291460 | tf_op jit(solution)/shard_map/cri,kio->ckro/dot_general | solution.py:56
  41.8 0.5 slice_subtract_fusion
  42.2 3.5 %collective-permute-done.1 = bf16[2,2,256,512]{3,2,1,0:T(8,128)(2,1)S(1)} collective-permute-done((bf16[2,2,256,512]{3,2,1,0:T(8,128)(2,1)}, bf16[2,2,256,512]{3,2,1,0:T(8,128)(2,1)S(1)}, u32[]{:S(2)}, u32[]{:S(2)}) %collective-permute-start.1) | collective-permute-done | bytes 1048608 | tf_op jit(solution)/shard_map/ppermute | solution.py:10
  45.7 1.3 %convolution_bitcast_fusion.3 = f32[2,2,512,512]{3,2,0,1:T(8,128)S(1)} fusion(bf16[2,512,512,1]{2,1,0,3:T(8,128)(2,1)S(1)} %bitcast.125, bf16[4,2,512,512]{3,2,1,0:T(8,128)(2,1)S(1)} %copy-done.3, s32[]{:T(128)S(6)} %select_n.27), kind=kOutput, calls=%fused_computation.3 | convolution fusion | flops 1073741824 | bytes 6291460 | tf_op jit(solution)/shard_map/cri,kio->ckro/dot_general | solution.py:56
  47.0 0.0 copy-start.2
  47.0 0.0 copy-start.5
  47.0 0.5 slice_subtract_fusion.3
  47.5 0.3 broadcast_in_dim.26
  47.8 0.7 copy-done.2
  48.6 0.0 copy-done.5
  48.6 1.1 %fusion.2 = f32[2,2,256,512]{3,2,1,0:T(8,128)S(1)} fusion(f32[1,2,256,512]{3,2,1,0:T(8,128)S(1)} %bitcast.124, f32[1,2,256,512]{3,2,1,0:T(8,128)S(1)} %bitcast.123, f32[1,2,256,512]{3,2,1,0:T(8,128)S(1)} %bitcast.118, f32[1,2,256,512]{3,2,1,0:T(8,128)S(1)} %bitcast.117, f32[1,2,256,512]{3,2,1,0:T(8,128)S(1)} %bitcast.120, ...), kind=kOutput, calls=%fused_computation.7 | convolution fusion | flops 274989056 | bytes 13893636 | tf_op jit(solution)/shard_map/ab,cvbf->cvaf/dot_general | solution.py:46
  49.7 0.2 slice_bitcast_fusion.3
  49.9 1.3 %add_reduce_fusion = (f32[2,2]{1,0:T(2,128)S(1)}, f32[2,2]{1,0:T(2,128)S(1)}) fusion(f32[2,256,512]{2,1,0:T(8,128)S(1)} %get-tuple-element.27, f32[2,256,512]{2,1,0:T(8,128)S(1)} %get-tuple-element.23, f32[2,256,512]{2,1,0:T(8,128)S(1)} %get-tuple-element.26, f32[2,256,512]{2,1,0:T(8,128)S(1)} %get-tuple-element.22), kind=kLoop, calls=%fused_computation.14 | loop fusion | flops 4194296 | bytes 4194336 | tf_op jit(solution)/shard_map/reduce_sum | solution.py:65
  51.2 0.1 reshape.241
  51.3 0.1 reshape.242
  51.4 0.1 pad_maximum_fusion.1
  51.4 0.6 broadcast_in_dim.28
  52.0 15.7 %all-to-all-start = ((f32[16,1,10]{2,1,0:T(1,128)}), f32[16,1,10]{2,1,0:T(1,128)S(1)}, u32[]{:S(2)}, u32[]{:S(2)}) async-start(f32[16,1,10]{2,1,0:T(1,128)} %broadcast_in_dim.28), calls=%async_computation | async-start | bytes 16384 | tf_op jit(solution)/shard_map/all_to_all | solution.py:19
  67.8 0.0 copy-start.4
  67.8 3.1 %fusion.6 = (f32[2,256,512]{2,1,0:T(8,128)}, f32[2,256,512]{2,1,0:T(8,128)}) fusion(f32[1,2,256,512]{3,2,1,0:T(8,128)} %get-tuple-element.25, f32[1,2,256,512]{3,2,1,0:T(8,128)} %get-tuple-element.24), kind=kLoop, calls=%fused_computation.17 | loop fusion | flops 524288 | bytes 4194304 | tf_op jit(solution)/shard_map/mul | solution.py:75
  70.9 3.3 %all-to-all-done = f32[16,1,10]{2,1,0:T(1,128)S(1)} async-done(((f32[16,1,10]{2,1,0:T(1,128)}), f32[16,1,10]{2,1,0:T(1,128)S(1)}, u32[]{:S(2)}, u32[]{:S(2)}) %all-to-all-start) | async-done | bytes 672 | tf_op jit(solution)/shard_map/all_to_all | solution.py:19
  74.2 0.1 fusion.28
  74.3 0.1 slice_add_fusion.4
  74.4 0.1 reshape.243
  74.5 0.1 reshape.244
  74.5 0.1 broadcast_divide_fusion.1
  74.6 0.0 copy-done.4
  74.6 4.1 %fusion.4 = (bf16[1,2,2,256,512]{4,3,2,1,0:T(8,128)(2,1)}, bf16[1,2,2,256,512]{4,3,2,1,0:T(8,128)(2,1)}) fusion(f32[2,2,256,512]{3,2,1,0:T(8,128)S(1)} %fusion.2, f32[2,256,512]{2,1,0:T(8,128)} %get-tuple-element.21, f32[2]{0:T(128)S(1)} %get-tuple-element.31, f32[2,256,512]{2,1,0:T(8,128)} %get-tuple-element.19, f32[2]{0:T(128)S(1)} %get-tuple-element.36, ...), kind=kLoop, calls=%fused_computation.15 | loop fusion | flops 5242880 | bytes 8388640 | tf_op jit(solution)/shard_map/broadcast_in_dim | solution.py:76
  (4 shorter events, 0.1 us)
Async XLA Ops:
  0.6 13.8 %copy-start = (bf16[128,128]{1,0:T(8,128)(2,1)S(1)}, bf16[128,128]{1,0:T(8,128)(2,1)}, u32[]{:S(2)}) copy-start(bf16[128,128]{1,0:T(8,128)(2,1)} %param.9) | copy-start | bytes 98308
  0.6 22.6 %collective-permute-start.2 = (bf16[2,2,256,512]{3,2,1,0:T(8,128)(2,1)}, bf16[2,2,256,512]{3,2,1,0:T(8,128)(2,1)}, u32[]{:S(2)}, u32[]{:S(2)}) collective-permute-start(bf16[2,2,256,512]{3,2,1,0:T(8,128)(2,1)} %bitcast.115), channel_id=1, source_target_pairs={{0,1},{1,2},{2,3},{3,4},{4,5},{5,6},{6,7},{7,8},{8,9},{9,10},{10,1... | collective-permute-start | bytes 3145736 | tf_op jit(solution)/shard_map/ppermute | solution.py:10
  1.1 25.9 %collective-permute-start = (bf16[2,2,256,512]{3,2,1,0:T(8,128)(2,1)}, bf16[2,2,256,512]{3,2,1,0:T(8,128)(2,1)}, u32[]{:S(2)}, u32[]{:S(2)}) collective-permute-start(bf16[2,2,256,512]{3,2,1,0:T(8,128)(2,1)} %bitcast.116), channel_id=1, source_target_pairs={{0,15},{1,0},{2,1},{3,2},{4,3},{5,4},{6,5},{7,6},{8,7},{9,8},{10,9... | collective-permute-start | bytes 3145736 | tf_op jit(solution)/shard_map/ppermute | solution.py:10
  14.8 1.5 %copy-start.6 = (s32[2,2]{1,0:T(2,128)S(1)}, s32[2,2]{1,0:T(2,128)}, u32[]{:S(2)}) copy-start(s32[2,2]{1,0:T(2,128)} %param.11) | copy-start | bytes 52
  14.8 4.7 %copy-start.1 = (bf16[1,2,2,256,512]{4,3,2,1,0:T(8,128)(2,1)S(1)}, bf16[1,2,2,256,512]{4,3,2,1,0:T(8,128)(2,1)}, u32[]{:S(2)}) copy-start(bf16[1,2,2,256,512]{4,3,2,1,0:T(8,128)(2,1)} %param.7) | copy-start | bytes 3145732
  21.8 5.3 %copy-start.3 = (bf16[4,2,512,512]{3,2,1,0:T(8,128)(2,1)S(1)}, bf16[4,2,512,512]{3,2,1,0:T(8,128)(2,1)}, u32[]{:S(2)}) copy-start(bf16[4,2,512,512]{3,2,1,0:T(8,128)(2,1)} %param.8) | copy-start | bytes 12582916
  23.2 17.2 %collective-permute-start.3 = (bf16[2,2,256,512]{3,2,1,0:T(8,128)(2,1)}, bf16[2,2,256,512]{3,2,1,0:T(8,128)(2,1)S(1)}, u32[]{:S(2)}, u32[]{:S(2)}) collective-permute-start(bf16[2,2,256,512]{3,2,1,0:T(8,128)(2,1)} %collective-permute-done.2), channel_id=1, source_target_pairs={{0,1},{1,2},{2,3},{3,4},{4,5},{5,6},{6,7},{7,8},{8,9},{9,10},{10,1... | collective-permute-start | bytes 3145736 | tf_op jit(solution)/shard_map/ppermute | solution.py:10
  29.6 16.1 %collective-permute-start.1 = (bf16[2,2,256,512]{3,2,1,0:T(8,128)(2,1)}, bf16[2,2,256,512]{3,2,1,0:T(8,128)(2,1)S(1)}, u32[]{:S(2)}, u32[]{:S(2)}) collective-permute-start(bf16[2,2,256,512]{3,2,1,0:T(8,128)(2,1)} %collective-permute-done), channel_id=1, source_target_pairs={{0,15},{1,0},{2,1},{3,2},{4,3},{5,4},{6,5},{7,6},{8,7},{9,8},{10,9... | collective-permute-start | bytes 3145736 | tf_op jit(solution)/shard_map/ppermute | solution.py:10
  47.0 1.6 %copy-start.2 = (f32[2,2,256,512]{3,2,1,0:T(8,128)S(1)}, f32[2,2,256,512]{3,2,1,0:T(8,128)}, u32[]{:S(2)}) copy-start(f32[2,2,256,512]{3,2,1,0:T(8,128)} %reshape.236) | copy-start | bytes 6291460
  47.0 1.6 %copy-start.5 = (bf16[256,256]{1,0:T(8,128)(2,1)S(1)}, bf16[256,256]{1,0:T(8,128)(2,1)}, u32[]{:S(2)}) copy-start(bf16[256,256]{1,0:T(8,128)(2,1)} %param.10) | copy-start | bytes 393220
  52.0 22.2 %all-to-all-start = ((f32[16,1,10]{2,1,0:T(1,128)}), f32[16,1,10]{2,1,0:T(1,128)S(1)}, u32[]{:S(2)}, u32[]{:S(2)}) async-start(f32[16,1,10]{2,1,0:T(1,128)} %broadcast_in_dim.28), calls=%async_computation | async-start | bytes 16384 | tf_op jit(solution)/shard_map/all_to_all | solution.py:19
  67.8 6.8 %copy-start.4 = (f32[2,256,512]{2,1,0:T(8,128)S(1)}, f32[2,256,512]{2,1,0:T(8,128)}, u32[]{:S(2)}) copy-start(f32[2,256,512]{2,1,0:T(8,128)} %get-tuple-element.18) | copy-start | bytes 3145732

commit v10 on v9

--- a/solution.py
+++ b/solution.py
@@ -43,7 +43,10 @@
     along_y = jnp.dot(rows, y_operator, preferred_element_type=jnp.float32).reshape(block.shape)
     full_mask = jnp.repeat(jnp.repeat(tile_mask, tile, axis=0), tile, axis=1).astype(jnp.bfloat16)
     masked = x_operator * full_mask
-    along_x = jnp.einsum("ab,cvbf->cvaf", masked, block, preferred_element_type=jnp.float32)
+    planes = block.reshape(-1, width_x, width_fy)
+    spread = jnp.broadcast_to(masked, (planes.shape[0],) + masked.shape)
+    along_x = jnp.einsum("nab,nbf->naf", spread, planes, preferred_element_type=jnp.float32)
+    along_x = along_x.reshape(block.shape)
     centered = (position - harmonics // 2).astype(jnp.float32) + detuning[0]
     lam = -(centered * centered) / (4.0 * harmonics)
     image = along_y + along_x + lam * block.astype(jnp.float32)

time: 79.1 us -> 85.8 us (1.085)
  starting transfers between devices: 25.8 us -> 19.2 us
  local copies, waits for them, and re-layouts: 6.99 us -> 13.2 us
  other arithmetic: 14.3 us -> 20.4 us
  matrix products: 9.02 us -> 10.9 us
  waiting for transfers between devices: 13.5 us -> 12.5 us
    convert_element_type x0 -> x1, other arithmetic: none -> 7.43 us  [body(): projected.astype(jnp.bfloat16)[None]]
    all_to_all x1, starting transfers between devices: 15.7 us -> 8.99 us  [summed_over(): gathered = lax.all_to_all(spread, axes, 0, 0, tiled=False)]
    broadcast_in_dim x1 -> x0, other arithmetic: 4.06 us -> none  [body(): projected.astype(jnp.bfloat16)[None]]
    reshape x1 -> x2, local copies, waits for them, and re-layouts: 1.51 us -> 5.47 us  [body(): jnp.dot(rows, y_operator, preferred_element_type=jnp.float32)]
    all_to_all x1, waiting for transfers between devices: 3.28 us -> 0.58 us  [summed_over(): gathered = lax.all_to_all(spread, axes, 0, 0, tiled=False)]
    dot_general x1, matrix products: 0.41 us -> 2.98 us  [body(): jnp.dot(rows, y_operator, preferred_element_type=jnp.float32)]
    unnamed x14 -> x34, local copies, waits for them, and re-layouts: 0.76 us -> 3.27 us
    ppermute x4, waiting for transfers between devices: 10.3 us -> 11.9 us  [passed_along(): return lax.ppermute(value, axis, pairs)]
  transfers between devices with their start and end apart: 5 -> 5, of which waited for: 3 -> 3; matrix products, arithmetic and copies ran while one was open for 25% -> 33% of each run, Pallas kernels for 0% -> 0%
where the time goes in v10:
time: 85.8 us; the launch traced here: 85.2 us
  other arithmetic  20.4 us (24%)
  starting transfers between devices  19.2 us (22%)
  local copies, waits for them, and re-layouts  13.2 us (15%)
  waiting for transfers between devices  12.5 us (15%)
  matrix products  10.9 us (13%)
  between operations  8.88 us (10%)
    ppermute x4, waiting for transfers between devices, passed_along(): return lax.ppermute(value, axis, pairs)  11.9 us
    ppermute x4, starting transfers between devices, passed_along(): return lax.ppermute(value, axis, pairs)  10.2 us
    all_to_all x1, starting transfers between devices, summed_over(): gathered = lax.all_to_all(spread, axes, 0, 0, tiled=False)  8.99 us
    dot_general x4, matrix products, body(): jnp.einsum('cri,kio->ckro', other, matrix, preferred_element_type=jnp.flo...  7.52 us
    convert_element_type x1, other arithmetic, body(): projected.astype(jnp.bfloat16)[None]  7.43 us
    reshape x2, local copies, waits for them, and re-layouts, body(): jnp.dot(rows, y_operator, preferred_element_type=jnp.float32)  5.47 us
    unnamed x34, local copies, waits for them, and re-layouts  3.27 us
    mul x1, other arithmetic, body(): h_im[vec, :, None, None] * turned[:, vec][:, None]  3.03 us
  transfers between devices with their start and end apart: 5, of which 3 were waited for; matrix products, arithmetic and copies ran while one was open for 33% of the time, Pallas kernels for 0%

profile of v10, /device:TPU:0, one launch (start us, length us, event | category | flops | bytes accessed | tf_op | source)
XLA Modules:
  0.0 85.2 jit_solution(12745174877025708765)
XLA Ops:
  0.6 0.0 copy-start
  0.6 0.0 copy-start.16
  0.7 5.5 %collective-permute-start = (bf16[2,2,256,512]{3,2,1,0:T(8,128)(2,1)}, bf16[2,2,256,512]{3,2,1,0:T(8,128)(2,1)}, u32[]{:S(2)}, u32[]{:S(2)}) collective-permute-start(bf16[2,2,256,512]{3,2,1,0:T(8,128)(2,1)} %bitcast.108), channel_id=1, source_target_pairs={{0,15},{1,0},{2,1},{3,2},{4,3},{5,4},{6,5},{7,6},{8,7},{9,8},{10,9... | collective-permute-start | bytes 3145736 | tf_op jit(solution)/shard_map/ppermute | solution.py:10
  6.2 0.0 collective-permute-start.2
  6.2 1.5 %bitcast_convert_fusion = f32[2,2,256,512]{3,2,1,0:T(8,128)S(1)} fusion(bf16[1,2,2,256,512]{4,3,2,1,0:T(8,128)(2,1)} %param.7), kind=kLoop, calls=%fused_computation.67 | loop fusion | flops 524288 | bytes 3145728 | tf_op jit(solution)/shard_map/convert_element_type | solution.py:52
  7.7 0.0 copy-done.16
  7.7 0.0 copy-start.14
  7.7 2.3 %slice_bitcast_fusion.9 = (f32[2,256,512]{2,1,0:T(8,128)}, f32[2,256,512]{2,1,0:T(8,128)}, f32[1,2,256,512]{3,2,1,0:T(8,128)}, f32[1,2,256,512]{3,2,1,0:T(8,128)}) fusion(f32[2,2,256,512]{3,2,1,0:T(8,128)S(1)} %bitcast_convert_fusion), kind=kLoop, calls=%fused_computation.68 | loop fusion | flops 262144 | bytes 6291456 | tf_op jit(solution)/shard_map/mul | solution.py:68
  10.0 0.3 broadcast_in_dim.25
  10.4 0.0 copy-done.14
  10.4 0.3 add_reduce_fusion.1
  10.7 0.6 copy-done.1
  11.2 1.4 %reshape_squeeze.6 = bf16[4096,128]{1,0:T(8,128)(2,1)} reshape(bf16[1,2,2,256,512]{4,3,2,1,0:T(8,128)(2,1)S(1)} %copy-done.1) | data formatting | bytes 2097152 | tf_op jit(solution)/shard_map/reshape;squeeze | solution.py:42
  12.7 3.0 %fusion.29 = f32[4096,128]{1,0:T(8,128)} fusion(bf16[4096,128]{1,0:T(8,128)(2,1)} %reshape_squeeze.6, bf16[128,128]{1,0:T(8,128)(2,1)S(1)} %copy-done), kind=kOutput, calls=%fused_computation.70 | convolution fusion | flops 134217728 | bytes 3178496 | tf_op jit(solution)/shard_map/dot_general | solution.py:43
  15.6 0.0 copy-done.15
  15.6 0.7 fusion.26
  21.1 2.8 %reshape.406 = f32[2,2,256,512]{3,2,1,0:T(8,128)} reshape(f32[4096,128]{1,0:T(8,128)} %fusion.29) | data formatting | bytes 4194304 | tf_op jit(solution)/shard_map/reshape | solution.py:43
  26.8 0.0 copy-start.11
  26.9 1.5 %slice_bitcast_fusion.1 = (f32[2,256,512]{2,1,0:T(8,128)}, f32[2,256,512]{2,1,0:T(8,128)}) fusion(f32[2,2,256,512]{3,2,1,0:T(8,128)S(1)} %bitcast_convert_fusion), kind=kLoop, calls=%fused_computation.22 | loop fusion | bytes 4194304 | tf_op jit(solution)/shard_map/mul | solution.py:77
  28.4 0.4 fusion.17
  28.8 0.0 collective-permute-done
  28.8 4.5 %collective-permute-start.1 = (bf16[2,2,256,512]{3,2,1,0:T(8,128)(2,1)}, bf16[2,2,256,512]{3,2,1,0:T(8,128)(2,1)S(1)}, u32[]{:S(2)}, u32[]{:S(2)}) collective-permute-start(bf16[2,2,256,512]{3,2,1,0:T(8,128)(2,1)} %collective-permute-done), channel_id=1, source_target_pairs={{0,15},{1,0},{2,1},{3,2},{4,3},{5,4},{6,5},{7,6},{8,7},{9,8},{10,9... | collective-permute-start | bytes 3145736 | tf_op jit(solution)/shard_map/ppermute | solution.py:10
  33.3 2.5 %convolution_bitcast_fusion.2 = f32[2,2,512,512]{3,2,0,1:T(8,128)S(1)} fusion(bf16[2,512,512,1]{2,1,0,3:T(8,128)(2,1)} %bitcast.17, bf16[4,2,512,512]{3,2,1,0:T(8,128)(2,1)S(1)} %copy-done.11, s32[]{:T(128)S(6)} %select_n.29), kind=kOutput, calls=%fused_computation.2 | convolution fusion | flops 1073741824 | bytes 6291460 | tf_op jit(solution)/shard_map/cri,kio->ckro/dot_general | solution.py:59
  35.8 0.0 collective-permute-done.2
  35.9 0.2 collective-permute-start.3
  36.1 2.5 %convolution_bitcast_fusion.1 = f32[2,2,512,512]{3,2,0,1:T(8,128)S(1)} fusion(bf16[2,512,512,1]{2,1,0,3:T(8,128)(2,1)} %bitcast.25, bf16[4,2,512,512]{3,2,1,0:T(8,128)(2,1)S(1)} %copy-done.11, s32[]{:T(128)S(6)} %select_n.31), kind=kOutput, calls=%fused_computation.1 | convolution fusion | flops 1073741824 | bytes 6291460 | tf_op jit(solution)/shard_map/cri,kio->ckro/dot_general | solution.py:59
  38.6 0.5 slice_subtract_fusion.2
  39.1 0.5 slice_subtract_fusion.1
  39.6 6.3 %collective-permute-done.1 = bf16[2,2,256,512]{3,2,1,0:T(8,128)(2,1)S(1)} collective-permute-done((bf16[2,2,256,512]{3,2,1,0:T(8,128)(2,1)}, bf16[2,2,256,512]{3,2,1,0:T(8,128)(2,1)S(1)}, u32[]{:S(2)}, u32[]{:S(2)}) %collective-permute-start.1) | collective-permute-done | bytes 1048608 | tf_op jit(solution)/shard_map/ppermute | solution.py:10
  46.0 1.3 %convolution_bitcast_fusion.3 = f32[2,2,512,512]{3,2,0,1:T(8,128)S(1)} fusion(bf16[2,512,512,1]{2,1,0,3:T(8,128)(2,1)S(1)} %bitcast.130, bf16[4,2,512,512]{3,2,1,0:T(8,128)(2,1)S(1)} %copy-done.11, s32[]{:T(128)S(6)} %select_n.27), kind=kOutput, calls=%fused_computation.3 | convolution fusion | flops 1073741824 | bytes 6291460 | tf_op jit(solution)/shard_map/cri,kio->ckro/dot_general | solution.py:59
  47.2 0.5 slice_subtract_fusion.3
  47.7 5.6 %collective-permute-done.3 = bf16[2,2,256,512]{3,2,1,0:T(8,128)(2,1)S(1)} collective-permute-done((bf16[2,2,256,512]{3,2,1,0:T(8,128)(2,1)}, bf16[2,2,256,512]{3,2,1,0:T(8,128)(2,1)S(1)}, u32[]{:S(2)}, u32[]{:S(2)}) %collective-permute-start.3) | collective-permute-done | bytes 1048608 | tf_op jit(solution)/shard_map/ppermute | solution.py:10
  53.3 1.3 %convolution_bitcast_fusion = f32[2,2,512,512]{3,2,0,1:T(8,128)S(1)} fusion(bf16[2,512,512,1]{2,1,0,3:T(8,128)(2,1)S(1)} %bitcast.129, bf16[4,2,512,512]{3,2,1,0:T(8,128)(2,1)S(1)} %copy-done.11, s32[]{:T(128)S(6)} %select_n.33), kind=kOutput, calls=%fused_computation | convolution fusion | flops 1073741824 | bytes 6291460 | tf_op jit(solution)/shard_map/cri,kio->ckro/dot_general | solution.py:59
  54.6 0.5 slice_subtract_fusion
  55.1 0.0 copy-start.8
  55.1 0.0 copy-start.9
  55.1 0.0 copy-done.2
  55.1 0.0 copy-done.3
  55.1 0.0 copy-done.4
  55.1 0.0 copy-done.5
  55.1 0.0 copy-done.6
  55.2 0.0 copy-done.7
  55.2 1.3 %copy-done.10 = f32[2,2,256,512]{3,2,1,0:T(8,128)S(1)} copy-done((f32[2,2,256,512]{3,2,1,0:T(8,128)S(1)}, f32[2,2,256,512]{3,2,1,0:T(8,128)}, u32[]{:S(2)}) %copy-start.10) | copy-done | bytes 2097176
  56.5 1.6 %fusion.5 = f32[2,2,256,512]{3,2,1,0:T(8,128)S(1)} fusion(f32[1,2,256,512]{3,2,1,0:T(8,128)S(1)} %bitcast.123, f32[1,2,256,512]{3,2,1,0:T(8,128)S(1)} %bitcast.121, f32[1,2,256,512]{3,2,1,0:T(8,128)S(1)} %bitcast.115, f32[1,2,256,512]{3,2,1,0:T(8,128)S(1)} %bitcast.113, f32[1,2,256,512]{3,2,1,0:T(8,128)S(1)} %bitcast.119, ...), kind=kLoop, calls=%fused_computation.11 | loop fusion | flops 6291456 | bytes 15728644 | tf_op jit(solution)/shard_map/add | solution.py:62
  58.1 0.0 copy-start.12
  58.1 0.0 copy-start.13
  58.2 0.2 slice_bitcast_fusion.3
  58.3 1.0 %copy-done.12 = f32[2,256,512]{2,1,0:T(8,128)S(1)} copy-done((f32[2,256,512]{2,1,0:T(8,128)S(1)}, f32[2,256,512]{2,1,0:T(8,128)}, u32[]{:S(2)}) %copy-start.12) | copy-done | bytes 1048600
  59.4 0.3 copy-done.13
  59.7 1.3 %add_reduce_fusion = (f32[2,2]{1,0:T(2,128)S(1)}, f32[2,2]{1,0:T(2,128)S(1)}) fusion(f32[2,256,512]{2,1,0:T(8,128)S(1)} %get-tuple-element.27, f32[2,256,512]{2,1,0:T(8,128)S(1)} %copy-done.13, f32[2,256,512]{2,1,0:T(8,128)S(1)} %get-tuple-element.26, f32[2,256,512]{2,1,0:T(8,128)S(1)} %copy-done.12), kind=kLoop, calls=%fused_computation.16 | loop fusion | flops 4194296 | bytes 4194336 | tf_op jit(solution)/shard_map/reduce_sum | solution.py:68
  61.0 0.1 reshape.408
  61.0 0.1 reshape.409
  61.1 0.1 pad_maximum_fusion.1
  61.2 0.6 broadcast_in_dim.27
  61.8 9.0 %all-to-all-start = ((f32[16,1,10]{2,1,0:T(1,128)}), f32[16,1,10]{2,1,0:T(1,128)S(1)}, u32[]{:S(2)}, u32[]{:S(2)}) async-start(f32[16,1,10]{2,1,0:T(1,128)} %broadcast_in_dim.27), calls=%async_computation | async-start | bytes 16384 | tf_op jit(solution)/shard_map/all_to_all | solution.py:19
  70.8 3.0 %fusion.7 = (f32[2,256,512]{2,1,0:T(8,128)}, f32[2,256,512]{2,1,0:T(8,128)}) fusion(f32[1,2,256,512]{3,2,1,0:T(8,128)} %get-tuple-element.24, f32[1,2,256,512]{3,2,1,0:T(8,128)} %get-tuple-element.25), kind=kLoop, calls=%fused_computation.18 | loop fusion | flops 524288 | bytes 4194304 | tf_op jit(solution)/shard_map/mul | solution.py:78
  73.8 2.7 %reshape.400 = f32[1,2,2,256,512]{4,3,2,1,0:T(8,128)} reshape(f32[4096,128]{1,0:T(8,128)} %fusion.29) | data formatting | bytes 4194304 | tf_op jit(solution)/shard_map/reshape | solution.py:43
  76.6 0.6 all-to-all-done
  77.2 0.1 fusion.28
  77.3 0.1 slice_add_fusion.4
  77.3 0.1 reshape.410
  77.4 0.1 reshape.411
  77.5 0.1 broadcast_divide_fusion.1
  77.6 7.4 %subtract_convert_fusion = (bf16[1,2,2,256,512]{4,3,2,1,0:T(8,128)(2,1)}, bf16[1,2,2,256,512]{4,3,2,1,0:T(8,128)(2,1)}) fusion(f32[2,256,512]{2,1,0:T(8,128)} %get-tuple-element.21, f32[2]{0:T(128)S(1)} %get-tuple-element.31, f32[2,256,512]{2,1,0:T(8,128)} %get-tuple-element.19, f32[2]{0:T(128)S(1)} %get-tuple-element.36, ...), kind=kLoop, calls=%fused_computation.14 | loop fusion | flops 11534336 | bytes 19922980 | tf_op jit(solution)/shard_map/convert_element_type | solution.py:79
  (18 shorter events, 0.1 us)
Async XLA Ops:
  0.6 12.0 %copy-start = (bf16[128,128]{1,0:T(8,128)(2,1)S(1)}, bf16[128,128]{1,0:T(8,128)(2,1)}, u32[]{:S(2)}) copy-start(bf16[128,128]{1,0:T(8,128)(2,1)} %param.9) | copy-start | bytes 98308
  0.6 7.1 %copy-start.16 = (s32[2,2]{1,0:T(2,128)S(1)}, s32[2,2]{1,0:T(2,128)}, u32[]{:S(2)}) copy-start(s32[2,2]{1,0:T(2,128)} %param.11) | copy-start | bytes 52
  0.7 28.2 %collective-permute-start = (bf16[2,2,256,512]{3,2,1,0:T(8,128)(2,1)}, bf16[2,2,256,512]{3,2,1,0:T(8,128)(2,1)}, u32[]{:S(2)}, u32[]{:S(2)}) collective-permute-start(bf16[2,2,256,512]{3,2,1,0:T(8,128)(2,1)} %bitcast.108), channel_id=1, source_target_pairs={{0,15},{1,0},{2,1},{3,2},{4,3},{5,4},{6,5},{7,6},{8,7},{9,8},{10,9... | collective-permute-start | bytes 3145736 | tf_op jit(solution)/shard_map/ppermute | solution.py:10
  6.2 29.7 %collective-permute-start.2 = (bf16[2,2,256,512]{3,2,1,0:T(8,128)(2,1)}, bf16[2,2,256,512]{3,2,1,0:T(8,128)(2,1)}, u32[]{:S(2)}, u32[]{:S(2)}) collective-permute-start(bf16[2,2,256,512]{3,2,1,0:T(8,128)(2,1)} %bitcast.109), channel_id=1, source_target_pairs={{0,1},{1,2},{2,3},{3,4},{4,5},{5,6},{6,7},{7,8},{8,9},{9,10},{10,1... | collective-permute-start | bytes 3145736 | tf_op jit(solution)/shard_map/ppermute | solution.py:10
  7.7 2.6 %copy-start.14 = (bf16[256,256]{1,0:T(8,128)(2,1)S(1)}, bf16[256,256]{1,0:T(8,128)(2,1)}, u32[]{:S(2)}) copy-start(bf16[256,256]{1,0:T(8,128)(2,1)} %param.10) | copy-start | bytes 393220
  10.0 1.2 %copy-start.1 = (bf16[1,2,2,256,512]{4,3,2,1,0:T(8,128)(2,1)S(1)}, bf16[1,2,2,256,512]{4,3,2,1,0:T(8,128)(2,1)}, u32[]{:S(2)}) copy-start(bf16[1,2,2,256,512]{4,3,2,1,0:T(8,128)(2,1)} %param.7) | copy-start | bytes 3145732
  12.6 3.0 %copy-start.15 = (s32[4]{0:T(128)S(1)}, s32[4]{0:T(128)}, u32[]{:S(2)}) copy-start(s32[4]{0:T(128)} %param.12) | copy-start | bytes 52
  26.8 6.5 %copy-start.11 = (bf16[4,2,512,512]{3,2,1,0:T(8,128)(2,1)S(1)}, bf16[4,2,512,512]{3,2,1,0:T(8,128)(2,1)}, u32[]{:S(2)}) copy-start(bf16[4,2,512,512]{3,2,1,0:T(8,128)(2,1)} %param.8) | copy-start | bytes 12582916
  28.8 17.1 %collective-permute-start.1 = (bf16[2,2,256,512]{3,2,1,0:T(8,128)(2,1)}, bf16[2,2,256,512]{3,2,1,0:T(8,128)(2,1)S(1)}, u32[]{:S(2)}, u32[]{:S(2)}) collective-permute-start(bf16[2,2,256,512]{3,2,1,0:T(8,128)(2,1)} %collective-permute-done), channel_id=1, source_target_pairs={{0,15},{1,0},{2,1},{3,2},{4,3},{5,4},{6,5},{7,6},{8,7},{9,8},{10,9... | collective-permute-start | bytes 3145736 | tf_op jit(solution)/shard_map/ppermute | solution.py:10
  35.9 17.5 %collective-permute-start.3 = (bf16[2,2,256,512]{3,2,1,0:T(8,128)(2,1)}, bf16[2,2,256,512]{3,2,1,0:T(8,128)(2,1)S(1)}, u32[]{:S(2)}, u32[]{:S(2)}) collective-permute-start(bf16[2,2,256,512]{3,2,1,0:T(8,128)(2,1)} %collective-permute-done.2), channel_id=1, source_target_pairs={{0,1},{1,2},{2,3},{3,4},{4,5},{5,6},{6,7},{7,8},{8,9},{9,10},{10,1... | collective-permute-start | bytes 3145736 | tf_op jit(solution)/shard_map/ppermute | solution.py:10
  39.1 16.0 %copy-start.2 = (f32[1,1,512,512]{3,2,0,1:T(8,128)}, f32[1,1,512,512]{3,2,0,1:T(8,128)S(1)}, u32[]{:S(2)}) copy-start(f32[1,1,512,512]{3,2,0,1:T(8,128)S(1)} %get-tuple-element.14) | copy-start | bytes 3145732
  39.1 16.0 %copy-start.3 = (f32[1,1,512,512]{3,2,0,1:T(8,128)}, f32[1,1,512,512]{3,2,0,1:T(8,128)S(1)}, u32[]{:S(2)}) copy-start(f32[1,1,512,512]{3,2,0,1:T(8,128)S(1)} %get-tuple-element.15) | copy-start | bytes 3145732
  39.6 15.5 %copy-start.4 = (f32[1,1,512,512]{3,2,0,1:T(8,128)}, f32[1,1,512,512]{3,2,0,1:T(8,128)S(1)}, u32[]{:S(2)}) copy-start(f32[1,1,512,512]{3,2,0,1:T(8,128)S(1)} %get-tuple-element.12) | copy-start | bytes 3145732
  39.6 15.5 %copy-start.5 = (f32[1,1,512,512]{3,2,0,1:T(8,128)}, f32[1,1,512,512]{3,2,0,1:T(8,128)S(1)}, u32[]{:S(2)}) copy-start(f32[1,1,512,512]{3,2,0,1:T(8,128)S(1)} %get-tuple-element.13) | copy-start | bytes 3145732
  47.7 7.4 %copy-start.6 = (f32[1,1,512,512]{3,2,0,1:T(8,128)}, f32[1,1,512,512]{3,2,0,1:T(8,128)S(1)}, u32[]{:S(2)}) copy-start(f32[1,1,512,512]{3,2,0,1:T(8,128)S(1)} %get-tuple-element.16) | copy-start | bytes 3145732
  47.7 7.4 %copy-start.7 = (f32[1,1,512,512]{3,2,0,1:T(8,128)}, f32[1,1,512,512]{3,2,0,1:T(8,128)S(1)}, u32[]{:S(2)}) copy-start(f32[1,1,512,512]{3,2,0,1:T(8,128)S(1)} %get-tuple-element.17) | copy-start | bytes 3145732
  54.6 1.9 %copy-start.10 = (f32[2,2,256,512]{3,2,1,0:T(8,128)S(1)}, f32[2,2,256,512]{3,2,1,0:T(8,128)}, u32[]{:S(2)}) copy-start(f32[2,2,256,512]{3,2,1,0:T(8,128)} %reshape.406) | copy-start | bytes 6291460
  55.1 3.0 %copy-start.8 = (f32[1,1,512,512]{3,2,0,1:T(8,128)}, f32[1,1,512,512]{3,2,0,1:T(8,128)S(1)}, u32[]{:S(2)}) copy-start(f32[1,1,512,512]{3,2,0,1:T(8,128)S(1)} %get-tuple-element.10) | copy-start | bytes 3145732
  55.1 3.0 %copy-start.9 = (f32[1,1,512,512]{3,2,0,1:T(8,128)}, f32[1,1,512,512]{3,2,0,1:T(8,128)S(1)}, u32[]{:S(2)}) copy-start(f32[1,1,512,512]{3,2,0,1:T(8,128)S(1)} %get-tuple-element.11) | copy-start | bytes 3145732
  58.1 1.2 %copy-start.12 = (f32[2,256,512]{2,1,0:T(8,128)S(1)}, f32[2,256,512]{2,1,0:T(8,128)}, u32[]{:S(2)}) copy-start(f32[2,256,512]{2,1,0:T(8,128)} %get-tuple-element.22) | copy-start | bytes 3145732
  58.1 1.5 %copy-start.13 = (f32[2,256,512]{2,1,0:T(8,128)S(1)}, f32[2,256,512]{2,1,0:T(8,128)}, u32[]{:S(2)}) copy-start(f32[2,256,512]{2,1,0:T(8,128)} %get-tuple-element.23) | copy-start | bytes 3145732
  61.8 15.3 %all-to-all-start = ((f32[16,1,10]{2,1,0:T(1,128)}), f32[16,1,10]{2,1,0:T(1,128)S(1)}, u32[]{:S(2)}, u32[]{:S(2)}) async-start(f32[16,1,10]{2,1,0:T(1,128)} %broadcast_in_dim.27), calls=%async_computation | async-start | bytes 16384 | tf_op jit(solution)/shard_map/all_to_all | solution.py:19

commit v11 on v9

--- a/solution.py
+++ b/solution.py
@@ -1,6 +1,8 @@
 import jax
 import jax.numpy as jnp
 from jax import lax
+from jax.experimental import pallas as pl
+from jax.experimental.pallas import tpu as pltpu
 from jax.sharding import PartitionSpec as P
 
 
@@ -68,12 +70,42 @@
     total_re, total_im, total_norms = summed_over(("harm",), num_re, num_im, norms)
     h_re = total_re / (total_norms + 1e-06)[:, None]
     h_im = total_im / (total_norms + 1e-06)[:, None]
-    turned = jnp.stack([-qi, qr])
-    projected = image
-    for vec in range(vecs):
-        projected = projected - (h_re[vec, :, None, None] * qfull[:, vec][:, None]
-                                 + h_im[vec, :, None, None] * turned[:, vec][:, None])
-    return (image.astype(jnp.bfloat16)[None], projected.astype(jnp.bfloat16)[None])
+    weights = jnp.concatenate([h_re.reshape(-1), h_im.reshape(-1)])
+    projected = removed_projections(weights, image, perturbation)
+    return (image.astype(jnp.bfloat16)[None], projected)
+
+
+def project_kernel(weights_ref, image_ref, block_ref, out_ref):
+    vecs = image_ref.shape[1]
+    block = block_ref[0].astype(jnp.float32)
+    for u in range(vecs):
+        out_re = image_ref[0, u]
+        out_im = image_ref[1, u]
+        for v in range(vecs):
+            a = weights_ref[v * vecs + u]
+            b = weights_ref[vecs * vecs + v * vecs + u]
+            q_re = block[0, v]
+            q_im = block[1, v]
+            out_re = out_re - (a * q_re - b * q_im)
+            out_im = out_im - (a * q_im + b * q_re)
+        out_ref[0, 0, u] = out_re.astype(out_ref.dtype)
+        out_ref[0, 1, u] = out_im.astype(out_ref.dtype)
+
+
+def removed_projections(weights, image, perturbation):
+    parts, vecs, width_x, width_fy = image.shape
+    rows = 64 if width_x % 64 == 0 else width_x
+    return pl.pallas_call(
+        project_kernel,
+        grid=(width_x // rows,),
+        in_specs=[
+            pl.BlockSpec(memory_space=pltpu.SMEM),
+            pl.BlockSpec((parts, vecs, rows, width_fy), lambda i: (0, 0, i, 0)),
+            pl.BlockSpec((1, parts, vecs, rows, width_fy), lambda i: (0, 0, 0, i, 0)),
+        ],
+        out_specs=pl.BlockSpec((1, parts, vecs, rows, width_fy), lambda i: (0, 0, 0, i, 0)),
+        out_shape=jax.ShapeDtypeStruct(perturbation.shape, jnp.bfloat16),
+    )(weights, image, perturbation)
 
 
 def solution(mesh):

time: 79.1 us -> 79.4 us (level)
  other arithmetic: 14.3 us -> 7.11 us
  Pallas kernels: 0 us -> 4.03 us
  waiting for transfers between devices: 13.5 us -> 16.1 us
  starting transfers between devices: 25.8 us -> 28.2 us
  local copies, waits for them, and re-layouts: 6.99 us -> 5.61 us
    mul x2 -> x0, other arithmetic: 4.75 us -> none  [the longest x1 3.11 us: body(): h_im[vec, :, None, None] * turned[:, vec][:, None]]
    pallas_call x0 -> x1, Pallas kernels: none -> 4.03 us  [removed_projections(): pl.pallas_call(project_kernel, grid=(width_x // rows,), in_specs=[pl.Bloc...]
    broadcast_in_dim x1, other arithmetic: 4.06 us -> 1.1 us  [body(): return (image.astype(jnp.bfloat16)[None], projected)]
    ppermute x4, starting transfers between devices: 10.1 us -> 12.4 us  [passed_along(): return lax.ppermute(value, axis, pairs)]
    all_to_all x1, waiting for transfers between devices: 3.28 us -> 5.22 us  [summed_over(): gathered = lax.all_to_all(spread, axes, 0, 0, tiled=False)]
    mul x2 -> x0, local copies, waits for them, and re-layouts: 1.49 us -> none  [the longest x1 1.48 us: body(): h_re[vec, :, None, None] * qfull[:, vec][:, None]]
  transfers between devices with their start and end apart: 5 -> 5, of which waited for: 3 -> 3; matrix products, arithmetic and copies ran while one was open for 25% -> 18% of each run, Pallas kernels for 0% -> 0%
where the time goes in v11:
time: 79.4 us; the launch traced here: 78.9 us
  starting transfers between devices  28.2 us (36%)
  waiting for transfers between devices  16.1 us (20%)
  between operations  9.06 us (11%)
  matrix products  8.81 us (11%)
  other arithmetic  7.11 us (9%)
  local copies, waits for them, and re-layouts  5.61 us (7%)
  Pallas kernels  4.03 us (5%)
    all_to_all x1, starting transfers between devices, summed_over(): gathered = lax.all_to_all(spread, axes, 0, 0, tiled=False)  15.7 us
    ppermute x4, starting transfers between devices, passed_along(): return lax.ppermute(value, axis, pairs)  12.4 us
    ppermute x4, waiting for transfers between devices, passed_along(): return lax.ppermute(value, axis, pairs)  10.9 us
    dot_general x4, matrix products, body(): jnp.einsum('cri,kio->ckro', other, matrix, preferred_element_type=jnp.flo...  7.49 us
    all_to_all x1, waiting for transfers between devices, summed_over(): gathered = lax.all_to_all(spread, axes, 0, 0, tiled=False)  5.22 us
    pallas_call x1, Pallas kernels, removed_projections(): pl.pallas_call(project_kernel, grid=(width_x // rows,), in_specs=[pl.Bloc...  4.03 us
    sub x4, other arithmetic, body(): real_part = prod[0, 0] - prod[1, 1]  1.92 us
    another operation x1, local copies, waits for them, and re-layouts, body(): rows = block.reshape(-1, ny)  1.7 us
  transfers between devices with their start and end apart: 5, of which 3 were waited for; matrix products, arithmetic and copies ran while one was open for 18% of the time, Pallas kernels for 0%

profile of v11, /device:TPU:0, one launch (start us, length us, event | category | flops | bytes accessed | tf_op | source)
XLA Modules:
  0.0 78.9 jit_solution(9353320196549427684)
XLA Ops:
  0.6 0.0 copy-start
  0.6 0.5 collective-permute-start.2
  1.1 5.1 %collective-permute-start = (bf16[2,2,256,512]{3,2,1,0:T(8,128)(2,1)}, bf16[2,2,256,512]{3,2,1,0:T(8,128)(2,1)}, u32[]{:S(2)}, u32[]{:S(2)}) collective-permute-start(bf16[2,2,256,512]{3,2,1,0:T(8,128)(2,1)} %bitcast.99), channel_id=1, source_target_pairs={{0,15},{1,0},{2,1},{3,2},{4,3},{5,4},{6,5},{7,6},{8,7},{9,8},{10,9... | collective-permute-start | bytes 3145736 | tf_op jit(solution)/shard_map/ppermute | solution.py:12
  6.2 1.4 %fusion.22 = (s32[]{:T(128)}, s32[]{:T(128)}, s32[]{:T(128)}, s32[]{:T(128)}) fusion(s32[4]{0:T(128)} %param.12), kind=kLoop, calls=%fused_computation.48 | loop fusion | flops 44 | bytes 32 | tf_op jit(solution)/shard_map/reduce_sum | solution.py:55
  12.6 1.7 %reshape_squeeze.3 = bf16[4096,128]{1,0:T(8,128)(2,1)S(1)} reshape(bf16[1,2,2,256,512]{4,3,2,1,0:T(8,128)(2,1)} %block_ref.1) | data formatting | bytes 2097152 | tf_op jit(solution)/shard_map/reshape;squeeze | solution.py:44
  14.3 0.0 copy-done
  14.3 0.4 fusion.24
  14.8 0.0 copy-start.6
  14.8 0.0 copy-start.2
  14.8 1.5 %reshape.218 = f32[2,2,256,512]{3,2,1,0:T(8,128)} reshape(f32[4096,128]{1,0:T(8,128)S(1)} %fusion.24) | data formatting | bytes 4194304 | tf_op jit(solution)/shard_map/reshape | solution.py:45
  16.3 0.0 copy-done.6
  19.5 0.0 copy-done.2
  19.5 0.3 bitcast_convert_fusion
  19.8 0.3 add_reduce_fusion.1
  20.1 0.0 copy-start.4
  20.1 0.2 slice_bitcast_fusion.3
  20.2 0.0 collective-permute-done.2
  20.2 6.8 %collective-permute-start.3 = (bf16[2,2,256,512]{3,2,1,0:T(8,128)(2,1)}, bf16[2,2,256,512]{3,2,1,0:T(8,128)(2,1)S(1)}, u32[]{:S(2)}, u32[]{:S(2)}) collective-permute-start(bf16[2,2,256,512]{3,2,1,0:T(8,128)(2,1)} %collective-permute-done.2), channel_id=1, source_target_pairs={{0,1},{1,2},{2,3},{3,4},{4,5},{5,6},{6,7},{7,8},{8,9},{9,10},{10,1... | collective-permute-start | bytes 3145736 | tf_op jit(solution)/shard_map/ppermute | solution.py:12
  27.1 0.0 collective-permute-done
  27.1 0.0 copy-done.4
  27.1 2.5 %convolution_bitcast_fusion.2 = f32[2,2,512,512]{3,2,0,1:T(8,128)S(1)} fusion(bf16[2,512,512,1]{2,1,0,3:T(8,128)(2,1)} %bitcast.18, bf16[4,2,512,512]{3,2,1,0:T(8,128)(2,1)S(1)} %copy-done.4, s32[]{:T(128)S(6)} %select_n.29), kind=kOutput, calls=%fused_computation.2 | convolution fusion | flops 1073741824 | bytes 6291460 | tf_op jit(solution)/shard_map/cri,kio->ckro/dot_general | solution.py:58
  29.6 0.1 collective-permute-start.1
  29.6 2.5 %convolution_bitcast_fusion.1 = f32[2,2,512,512]{3,2,0,1:T(8,128)S(1)} fusion(bf16[2,512,512,1]{2,1,0,3:T(8,128)(2,1)} %bitcast.26, bf16[4,2,512,512]{3,2,1,0:T(8,128)(2,1)S(1)} %copy-done.4, s32[]{:T(128)S(6)} %select_n.31), kind=kOutput, calls=%fused_computation.1 | convolution fusion | flops 1073741824 | bytes 6291460 | tf_op jit(solution)/shard_map/cri,kio->ckro/dot_general | solution.py:58
  32.1 0.5 slice_subtract_fusion.2
  32.6 0.5 slice_subtract_fusion.1
  33.1 4.4 %collective-permute-done.3 = bf16[2,2,256,512]{3,2,1,0:T(8,128)(2,1)S(1)} collective-permute-done((bf16[2,2,256,512]{3,2,1,0:T(8,128)(2,1)}, bf16[2,2,256,512]{3,2,1,0:T(8,128)(2,1)S(1)}, u32[]{:S(2)}, u32[]{:S(2)}) %collective-permute-start.3) | collective-permute-done | bytes 1048608 | tf_op jit(solution)/shard_map/ppermute | solution.py:12
  37.5 1.3 %convolution_bitcast_fusion = f32[2,2,512,512]{3,2,0,1:T(8,128)S(1)} fusion(bf16[2,512,512,1]{2,1,0,3:T(8,128)(2,1)S(1)} %bitcast.109, bf16[4,2,512,512]{3,2,1,0:T(8,128)(2,1)S(1)} %copy-done.4, s32[]{:T(128)S(6)} %select_n.33), kind=kOutput, calls=%fused_computation | convolution fusion | flops 1073741824 | bytes 6291460 | tf_op jit(solution)/shard_map/cri,kio->ckro/dot_general | solution.py:58
  38.8 0.5 slice_subtract_fusion
  39.3 6.4 %collective-permute-done.1 = bf16[2,2,256,512]{3,2,1,0:T(8,128)(2,1)S(1)} collective-permute-done((bf16[2,2,256,512]{3,2,1,0:T(8,128)(2,1)}, bf16[2,2,256,512]{3,2,1,0:T(8,128)(2,1)S(1)}, u32[]{:S(2)}, u32[]{:S(2)}) %collective-permute-start.1) | collective-permute-done | bytes 1048608 | tf_op jit(solution)/shard_map/ppermute | solution.py:12
  45.7 1.3 %convolution_bitcast_fusion.3 = f32[2,2,512,512]{3,2,0,1:T(8,128)S(1)} fusion(bf16[2,512,512,1]{2,1,0,3:T(8,128)(2,1)S(1)} %bitcast.108, bf16[4,2,512,512]{3,2,1,0:T(8,128)(2,1)S(1)} %copy-done.4, s32[]{:T(128)S(6)} %select_n.27), kind=kOutput, calls=%fused_computation.3 | convolution fusion | flops 1073741824 | bytes 6291460 | tf_op jit(solution)/shard_map/cri,kio->ckro/dot_general | solution.py:58
  47.0 0.0 copy-start.3
  47.0 0.0 copy-start.5
  47.0 0.5 slice_subtract_fusion.3
  47.5 0.3 broadcast_in_dim.23
  47.8 0.7 copy-done.3
  48.6 0.0 copy-done.5
  48.6 0.9 %fusion.2.image_ref = f32[2,2,256,512]{3,2,1,0:T(8,128)S(1)} fusion(f32[1,2,256,512]{3,2,1,0:T(8,128)S(1)} %bitcast.107, f32[1,2,256,512]{3,2,1,0:T(8,128)S(1)} %bitcast.106, f32[1,2,256,512]{3,2,1,0:T(8,128)S(1)} %bitcast.101, f32[1,2,256,512]{3,2,1,0:T(8,128)S(1)} %bitcast.100, f32[1,2,256,512]{3,2,1,0:T(8,128)S(1)} %bitcast.103, ...), kind=kOutput, calls=%fused_computation.7 | convolution fusion | flops 274989056 | bytes 13893636 | tf_op jit(solution)/shard_map/ab,cvbf->cvaf/dot_general | solution.py:48
  49.5 0.0 copy-start.1
  49.5 0.2 slice_bitcast_fusion.2
  49.7 1.3 %add_reduce_fusion = (f32[2,2]{1,0:T(2,128)S(1)}, f32[2,2]{1,0:T(2,128)S(1)}) fusion(f32[2,256,512]{2,1,0:T(8,128)S(1)} %get-tuple-element.19, f32[2,256,512]{2,1,0:T(8,128)S(1)} %get-tuple-element.17, f32[2,256,512]{2,1,0:T(8,128)S(1)} %get-tuple-element.18, f32[2,256,512]{2,1,0:T(8,128)S(1)} %get-tuple-element.16), kind=kLoop, calls=%fused_computation.11 | loop fusion | flops 4194296 | bytes 4194336 | tf_op jit(solution)/shard_map/reduce_sum | solution.py:67
  51.0 0.1 reshape.223
  51.1 0.1 reshape.224
  51.1 0.1 pad_maximum_fusion
  51.2 0.6 broadcast_in_dim.25
  51.8 15.7 %all-to-all-start = ((f32[16,1,10]{2,1,0:T(1,128)}), f32[16,1,10]{2,1,0:T(1,128)S(1)}, u32[]{:S(2)}, u32[]{:S(2)}) async-start(f32[16,1,10]{2,1,0:T(1,128)} %broadcast_in_dim.25), calls=%async_computation | async-start | bytes 16384 | tf_op jit(solution)/shard_map/all_to_all | solution.py:21
  67.6 0.0 copy-done.1
  67.6 1.1 %convert_bitcast_fusion = bf16[1,2,2,256,512]{4,3,2,1,0:T(8,128)(2,1)} fusion(f32[2,2,256,512]{3,2,1,0:T(8,128)S(1)} %fusion.2.image_ref), kind=kLoop, calls=%fused_computation.29 | loop fusion | flops 524288 | bytes 3145728 | tf_op jit(solution)/shard_map/broadcast_in_dim | solution.py:75
  68.7 5.2 %all-to-all-done = f32[16,1,10]{2,1,0:T(1,128)S(1)} async-done(((f32[16,1,10]{2,1,0:T(1,128)}), f32[16,1,10]{2,1,0:T(1,128)S(1)}, u32[]{:S(2)}, u32[]{:S(2)}) %all-to-all-start) | async-done | bytes 672 | tf_op jit(solution)/shard_map/all_to_all | solution.py:21
  73.9 0.1 slice_add_fusion.4
  74.0 0.1 div.22
  74.1 0.1 div.23
  74.2 0.1 slice_divide_fusion.1
  74.3 0.6 pad_maximum_fusion.1.weights_ref
  74.9 4.0 %shard_map.86 = bf16[1,2,2,256,512]{4,3,2,1,0:T(8,128)(2,1)} custom-call(f32[8]{0:T(128)} %pad_maximum_fusion.1.weights_ref, f32[2,2,256,512]{3,2,1,0:T(8,128)} %copy-done.1, bf16[1,2,2,256,512]{4,3,2,1,0:T(8,128)(2,1)} %block_ref.1), custom_call_target="tpu_custom_call" | custom-call | tf_op jit(solution)/shard_map/pallas_call | solution.py:98
  (3 shorter events, 0.0 us)
Async XLA Ops:
  0.6 13.7 %copy-start = (bf16[128,128]{1,0:T(8,128)(2,1)S(1)}, bf16[128,128]{1,0:T(8,128)(2,1)}, u32[]{:S(2)}) copy-start(bf16[128,128]{1,0:T(8,128)(2,1)} %param.9) | copy-start | bytes 98308
  0.6 19.6 %collective-permute-start.2 = (bf16[2,2,256,512]{3,2,1,0:T(8,128)(2,1)}, bf16[2,2,256,512]{3,2,1,0:T(8,128)(2,1)}, u32[]{:S(2)}, u32[]{:S(2)}) collective-permute-start(bf16[2,2,256,512]{3,2,1,0:T(8,128)(2,1)} %bitcast.98), channel_id=1, source_target_pairs={{0,1},{1,2},{2,3},{3,4},{4,5},{5,6},{6,7},{7,8},{8,9},{9,10},{10,1... | collective-permute-start | bytes 3145736 | tf_op jit(solution)/shard_map/ppermute | solution.py:12
  1.1 25.9 %collective-permute-start = (bf16[2,2,256,512]{3,2,1,0:T(8,128)(2,1)}, bf16[2,2,256,512]{3,2,1,0:T(8,128)(2,1)}, u32[]{:S(2)}, u32[]{:S(2)}) collective-permute-start(bf16[2,2,256,512]{3,2,1,0:T(8,128)(2,1)} %bitcast.99), channel_id=1, source_target_pairs={{0,15},{1,0},{2,1},{3,2},{4,3},{5,4},{6,5},{7,6},{8,7},{9,8},{10,9... | collective-permute-start | bytes 3145736 | tf_op jit(solution)/shard_map/ppermute | solution.py:12
  14.8 1.6 %copy-start.6 = (s32[2,2]{1,0:T(2,128)S(1)}, s32[2,2]{1,0:T(2,128)}, u32[]{:S(2)}) copy-start(s32[2,2]{1,0:T(2,128)} %param.11) | copy-start | bytes 52
  14.8 4.7 %copy-start.2 = (bf16[1,2,2,256,512]{4,3,2,1,0:T(8,128)(2,1)S(1)}, bf16[1,2,2,256,512]{4,3,2,1,0:T(8,128)(2,1)}, u32[]{:S(2)}) copy-start(bf16[1,2,2,256,512]{4,3,2,1,0:T(8,128)(2,1)} %block_ref.1) | copy-start | bytes 3145732
  20.1 7.0 %copy-start.4 = (bf16[4,2,512,512]{3,2,1,0:T(8,128)(2,1)S(1)}, bf16[4,2,512,512]{3,2,1,0:T(8,128)(2,1)}, u32[]{:S(2)}) copy-start(bf16[4,2,512,512]{3,2,1,0:T(8,128)(2,1)} %param.8) | copy-start | bytes 12582916
  20.2 17.3 %collective-permute-start.3 = (bf16[2,2,256,512]{3,2,1,0:T(8,128)(2,1)}, bf16[2,2,256,512]{3,2,1,0:T(8,128)(2,1)S(1)}, u32[]{:S(2)}, u32[]{:S(2)}) collective-permute-start(bf16[2,2,256,512]{3,2,1,0:T(8,128)(2,1)} %collective-permute-done.2), channel_id=1, source_target_pairs={{0,1},{1,2},{2,3},{3,4},{4,5},{5,6},{6,7},{7,8},{8,9},{9,10},{10,1... | collective-permute-start | bytes 3145736 | tf_op jit(solution)/shard_map/ppermute | solution.py:12
  29.6 16.1 %collective-permute-start.1 = (bf16[2,2,256,512]{3,2,1,0:T(8,128)(2,1)}, bf16[2,2,256,512]{3,2,1,0:T(8,128)(2,1)S(1)}, u32[]{:S(2)}, u32[]{:S(2)}) collective-permute-start(bf16[2,2,256,512]{3,2,1,0:T(8,128)(2,1)} %collective-permute-done), channel_id=1, source_target_pairs={{0,15},{1,0},{2,1},{3,2},{4,3},{5,4},{6,5},{7,6},{8,7},{9,8},{10,9... | collective-permute-start | bytes 3145736 | tf_op jit(solution)/shard_map/ppermute | solution.py:12
  47.0 1.6 %copy-start.3 = (f32[2,2,256,512]{3,2,1,0:T(8,128)S(1)}, f32[2,2,256,512]{3,2,1,0:T(8,128)}, u32[]{:S(2)}) copy-start(f32[2,2,256,512]{3,2,1,0:T(8,128)} %reshape.218) | copy-start | bytes 6291460
  47.0 1.6 %copy-start.5 = (bf16[256,256]{1,0:T(8,128)(2,1)S(1)}, bf16[256,256]{1,0:T(8,128)(2,1)}, u32[]{:S(2)}) copy-start(bf16[256,256]{1,0:T(8,128)(2,1)} %param.10) | copy-start | bytes 393220
  49.5 18.1 %copy-start.1 = (f32[2,2,256,512]{3,2,1,0:T(8,128)}, f32[2,2,256,512]{3,2,1,0:T(8,128)S(1)}, u32[]{:S(2)}) copy-start(f32[2,2,256,512]{3,2,1,0:T(8,128)S(1)} %fusion.2.image_ref) | copy-start | bytes 6291460
  51.8 22.1 %all-to-all-start = ((f32[16,1,10]{2,1,0:T(1,128)}), f32[16,1,10]{2,1,0:T(1,128)S(1)}, u32[]{:S(2)}, u32[]{:S(2)}) async-start(f32[16,1,10]{2,1,0:T(1,128)} %broadcast_in_dim.25), calls=%async_computation | async-start | bytes 16384 | tf_op jit(solution)/shard_map/all_to_all | solution.py:21

commit v12 on v11

--- a/solution.py
+++ b/solution.py
@@ -70,20 +70,19 @@
     total_re, total_im, total_norms = summed_over(("harm",), num_re, num_im, norms)
     h_re = total_re / (total_norms + 1e-06)[:, None]
     h_im = total_im / (total_norms + 1e-06)[:, None]
-    weights = jnp.concatenate([h_re.reshape(-1), h_im.reshape(-1)])
-    projected = removed_projections(weights, image, perturbation)
+    projected = removed_projections(h_re.reshape(-1), h_im.reshape(-1), image, perturbation)
     return (image.astype(jnp.bfloat16)[None], projected)
 
 
-def project_kernel(weights_ref, image_ref, block_ref, out_ref):
+def project_kernel(real_ref, imag_ref, image_ref, block_ref, out_ref):
     vecs = image_ref.shape[1]
     block = block_ref[0].astype(jnp.float32)
     for u in range(vecs):
         out_re = image_ref[0, u]
         out_im = image_ref[1, u]
         for v in range(vecs):
-            a = weights_ref[v * vecs + u]
-            b = weights_ref[vecs * vecs + v * vecs + u]
+            a = real_ref[v * vecs + u]
+            b = imag_ref[v * vecs + u]
             q_re = block[0, v]
             q_im = block[1, v]
             out_re = out_re - (a * q_re - b * q_im)
@@ -92,20 +91,21 @@
         out_ref[0, 1, u] = out_im.astype(out_ref.dtype)
 
 
-def removed_projections(weights, image, perturbation):
+def removed_projections(real, imag, image, perturbation):
     parts, vecs, width_x, width_fy = image.shape
-    rows = 64 if width_x % 64 == 0 else width_x
+    rows = 128 if width_x % 128 == 0 else width_x
     return pl.pallas_call(
         project_kernel,
         grid=(width_x // rows,),
         in_specs=[
+            pl.BlockSpec(memory_space=pltpu.SMEM),
             pl.BlockSpec(memory_space=pltpu.SMEM),
             pl.BlockSpec((parts, vecs, rows, width_fy), lambda i: (0, 0, i, 0)),
             pl.BlockSpec((1, parts, vecs, rows, width_fy), lambda i: (0, 0, 0, i, 0)),
         ],
         out_specs=pl.BlockSpec((1, parts, vecs, rows, width_fy), lambda i: (0, 0, 0, i, 0)),
         out_shape=jax.ShapeDtypeStruct(perturbation.shape, jnp.bfloat16),
-    )(weights, image, perturbation)
+    )(real, imag, image, perturbation)
 
 
 def solution(mesh):

time: 79.4 us -> 78.2 us (0.985)
  Pallas kernels: 4.03 us -> 2.97 us
    pallas_call x1, Pallas kernels: 4.03 us -> 2.97 us  [removed_projections(): pl.pallas_call(project_kernel, grid=(width_x // rows,), in_specs=[pl.Bloc...]
  transfers between devices with their start and end apart: 5 -> 5, of which waited for: 3 -> 3; matrix products, arithmetic and copies ran while one was open for 18% -> 19% of each run, Pallas kernels for 0% -> 0%
where the time goes in v12:
time: 78.2 us; the launch traced here: 77.7 us
  starting transfers between devices  28.2 us (36%)
  waiting for transfers between devices  16.1 us (21%)
  between operations  9.06 us (12%)
  matrix products  8.81 us (11%)
  other arithmetic  7.04 us (9%)
  local copies, waits for them, and re-layouts  5.61 us (7%)
  Pallas kernels  2.97 us (4%)
    all_to_all x1, starting transfers between devices, summed_over(): gathered = lax.all_to_all(spread, axes, 0, 0, tiled=False)  15.7 us
    ppermute x4, starting transfers between devices, passed_along(): return lax.ppermute(value, axis, pairs)  12.4 us
    ppermute x4, waiting for transfers between devices, passed_along(): return lax.ppermute(value, axis, pairs)  10.9 us
    dot_general x4, matrix products, body(): jnp.einsum('cri,kio->ckro', other, matrix, preferred_element_type=jnp.flo...  7.49 us
    all_to_all x1, waiting for transfers between devices, summed_over(): gathered = lax.all_to_all(spread, axes, 0, 0, tiled=False)  5.22 us
    pallas_call x1, Pallas kernels, removed_projections(): pl.pallas_call(project_kernel, grid=(width_x // rows,), in_specs=[pl.Bloc...  2.97 us
    sub x4, other arithmetic, body(): real_part = prod[0, 0] - prod[1, 1]  1.92 us
    another operation x1, local copies, waits for them, and re-layouts, body(): rows = block.reshape(-1, ny)  1.7 us
  transfers between devices with their start and end apart: 5, of which 3 were waited for; matrix products, arithmetic and copies ran while one was open for 19% of the time, Pallas kernels for 0%

profile of v12, /device:TPU:0, one launch (start us, length us, event | category | flops | bytes accessed | tf_op | source)
XLA Modules:
  0.0 77.7 jit_solution(18084051549019713796)
XLA Ops:
  0.6 0.0 copy-start
  0.6 0.5 collective-permute-start.2
  1.1 5.1 %collective-permute-start = (bf16[2,2,256,512]{3,2,1,0:T(8,128)(2,1)}, bf16[2,2,256,512]{3,2,1,0:T(8,128)(2,1)}, u32[]{:S(2)}, u32[]{:S(2)}) collective-permute-start(bf16[2,2,256,512]{3,2,1,0:T(8,128)(2,1)} %bitcast.99), channel_id=1, source_target_pairs={{0,15},{1,0},{2,1},{3,2},{4,3},{5,4},{6,5},{7,6},{8,7},{9,8},{10,9... | collective-permute-start | bytes 3145736 | tf_op jit(solution)/shard_map/ppermute | solution.py:12
  6.2 1.4 %fusion.22 = (s32[]{:T(128)}, s32[]{:T(128)}, s32[]{:T(128)}, s32[]{:T(128)}) fusion(s32[4]{0:T(128)} %param.12), kind=kLoop, calls=%fused_computation.48 | loop fusion | flops 44 | bytes 32 | tf_op jit(solution)/shard_map/reduce_sum | solution.py:55
  12.6 1.7 %reshape_squeeze.3 = bf16[4096,128]{1,0:T(8,128)(2,1)S(1)} reshape(bf16[1,2,2,256,512]{4,3,2,1,0:T(8,128)(2,1)} %block_ref.1) | data formatting | bytes 2097152 | tf_op jit(solution)/shard_map/reshape;squeeze | solution.py:44
  14.3 0.0 copy-done
  14.3 0.4 fusion.24
  14.8 0.0 copy-start.6
  14.8 0.0 copy-start.2
  14.8 1.5 %reshape.218 = f32[2,2,256,512]{3,2,1,0:T(8,128)} reshape(f32[4096,128]{1,0:T(8,128)S(1)} %fusion.24) | data formatting | bytes 4194304 | tf_op jit(solution)/shard_map/reshape | solution.py:45
  16.3 0.0 copy-done.6
  19.5 0.0 copy-done.2
  19.5 0.3 bitcast_convert_fusion
  19.8 0.3 add_reduce_fusion.1
  20.1 0.0 copy-start.4
  20.1 0.2 slice_bitcast_fusion.3
  20.2 0.0 collective-permute-done.2
  20.2 6.8 %collective-permute-start.3 = (bf16[2,2,256,512]{3,2,1,0:T(8,128)(2,1)}, bf16[2,2,256,512]{3,2,1,0:T(8,128)(2,1)S(1)}, u32[]{:S(2)}, u32[]{:S(2)}) collective-permute-start(bf16[2,2,256,512]{3,2,1,0:T(8,128)(2,1)} %collective-permute-done.2), channel_id=1, source_target_pairs={{0,1},{1,2},{2,3},{3,4},{4,5},{5,6},{6,7},{7,8},{8,9},{9,10},{10,1... | collective-permute-start | bytes 3145736 | tf_op jit(solution)/shard_map/ppermute | solution.py:12
  27.1 0.0 collective-permute-done
  27.1 0.0 copy-done.4
  27.1 2.5 %convolution_bitcast_fusion.2 = f32[2,2,512,512]{3,2,0,1:T(8,128)S(1)} fusion(bf16[2,512,512,1]{2,1,0,3:T(8,128)(2,1)} %bitcast.18, bf16[4,2,512,512]{3,2,1,0:T(8,128)(2,1)S(1)} %copy-done.4, s32[]{:T(128)S(6)} %select_n.29), kind=kOutput, calls=%fused_computation.2 | convolution fusion | flops 1073741824 | bytes 6291460 | tf_op jit(solution)/shard_map/cri,kio->ckro/dot_general | solution.py:58
  29.6 0.1 collective-permute-start.1
  29.6 2.5 %convolution_bitcast_fusion.1 = f32[2,2,512,512]{3,2,0,1:T(8,128)S(1)} fusion(bf16[2,512,512,1]{2,1,0,3:T(8,128)(2,1)} %bitcast.26, bf16[4,2,512,512]{3,2,1,0:T(8,128)(2,1)S(1)} %copy-done.4, s32[]{:T(128)S(6)} %select_n.31), kind=kOutput, calls=%fused_computation.1 | convolution fusion | flops 1073741824 | bytes 6291460 | tf_op jit(solution)/shard_map/cri,kio->ckro/dot_general | solution.py:58
  32.1 0.5 slice_subtract_fusion.2
  32.6 0.5 slice_subtract_fusion.1
  33.1 4.4 %collective-permute-done.3 = bf16[2,2,256,512]{3,2,1,0:T(8,128)(2,1)S(1)} collective-permute-done((bf16[2,2,256,512]{3,2,1,0:T(8,128)(2,1)}, bf16[2,2,256,512]{3,2,1,0:T(8,128)(2,1)S(1)}, u32[]{:S(2)}, u32[]{:S(2)}) %collective-permute-start.3) | collective-permute-done | bytes 1048608 | tf_op jit(solution)/shard_map/ppermute | solution.py:12
  37.5 1.3 %convolution_bitcast_fusion = f32[2,2,512,512]{3,2,0,1:T(8,128)S(1)} fusion(bf16[2,512,512,1]{2,1,0,3:T(8,128)(2,1)S(1)} %bitcast.109, bf16[4,2,512,512]{3,2,1,0:T(8,128)(2,1)S(1)} %copy-done.4, s32[]{:T(128)S(6)} %select_n.33), kind=kOutput, calls=%fused_computation | convolution fusion | flops 1073741824 | bytes 6291460 | tf_op jit(solution)/shard_map/cri,kio->ckro/dot_general | solution.py:58
  38.8 0.5 slice_subtract_fusion
  39.3 6.4 %collective-permute-done.1 = bf16[2,2,256,512]{3,2,1,0:T(8,128)(2,1)S(1)} collective-permute-done((bf16[2,2,256,512]{3,2,1,0:T(8,128)(2,1)}, bf16[2,2,256,512]{3,2,1,0:T(8,128)(2,1)S(1)}, u32[]{:S(2)}, u32[]{:S(2)}) %collective-permute-start.1) | collective-permute-done | bytes 1048608 | tf_op jit(solution)/shard_map/ppermute | solution.py:12
  45.7 1.3 %convolution_bitcast_fusion.3 = f32[2,2,512,512]{3,2,0,1:T(8,128)S(1)} fusion(bf16[2,512,512,1]{2,1,0,3:T(8,128)(2,1)S(1)} %bitcast.108, bf16[4,2,512,512]{3,2,1,0:T(8,128)(2,1)S(1)} %copy-done.4, s32[]{:T(128)S(6)} %select_n.27), kind=kOutput, calls=%fused_computation.3 | convolution fusion | flops 1073741824 | bytes 6291460 | tf_op jit(solution)/shard_map/cri,kio->ckro/dot_general | solution.py:58
  47.0 0.0 copy-start.3
  47.0 0.0 copy-start.5
  47.0 0.5 slice_subtract_fusion.3
  47.5 0.3 broadcast_in_dim.23
  47.8 0.7 copy-done.3
  48.6 0.0 copy-done.5
  48.6 0.9 %fusion.2.image_ref = f32[2,2,256,512]{3,2,1,0:T(8,128)S(1)} fusion(f32[1,2,256,512]{3,2,1,0:T(8,128)S(1)} %bitcast.107, f32[1,2,256,512]{3,2,1,0:T(8,128)S(1)} %bitcast.106, f32[1,2,256,512]{3,2,1,0:T(8,128)S(1)} %bitcast.101, f32[1,2,256,512]{3,2,1,0:T(8,128)S(1)} %bitcast.100, f32[1,2,256,512]{3,2,1,0:T(8,128)S(1)} %bitcast.103, ...), kind=kOutput, calls=%fused_computation.7 | convolution fusion | flops 274989056 | bytes 13893636 | tf_op jit(solution)/shard_map/ab,cvbf->cvaf/dot_general | solution.py:48
  49.5 0.0 copy-start.1
  49.5 0.2 slice_bitcast_fusion.2
  49.7 1.3 %add_reduce_fusion = (f32[2,2]{1,0:T(2,128)S(1)}, f32[2,2]{1,0:T(2,128)S(1)}) fusion(f32[2,256,512]{2,1,0:T(8,128)S(1)} %get-tuple-element.19, f32[2,256,512]{2,1,0:T(8,128)S(1)} %get-tuple-element.17, f32[2,256,512]{2,1,0:T(8,128)S(1)} %get-tuple-element.18, f32[2,256,512]{2,1,0:T(8,128)S(1)} %get-tuple-element.16), kind=kLoop, calls=%fused_computation.11 | loop fusion | flops 4194296 | bytes 4194336 | tf_op jit(solution)/shard_map/reduce_sum | solution.py:67
  51.0 0.1 reshape.223
  51.1 0.1 reshape.224
  51.1 0.1 pad_maximum_fusion
  51.2 0.6 broadcast_in_dim.25
  51.8 15.7 %all-to-all-start = ((f32[16,1,10]{2,1,0:T(1,128)}), f32[16,1,10]{2,1,0:T(1,128)S(1)}, u32[]{:S(2)}, u32[]{:S(2)}) async-start(f32[16,1,10]{2,1,0:T(1,128)} %broadcast_in_dim.25), calls=%async_computation | async-start | bytes 16384 | tf_op jit(solution)/shard_map/all_to_all | solution.py:21
  67.6 0.0 copy-done.1
  67.6 1.1 %convert_bitcast_fusion = bf16[1,2,2,256,512]{4,3,2,1,0:T(8,128)(2,1)} fusion(f32[2,2,256,512]{3,2,1,0:T(8,128)S(1)} %fusion.2.image_ref), kind=kLoop, calls=%fused_computation.29 | loop fusion | flops 524288 | bytes 3145728 | tf_op jit(solution)/shard_map/broadcast_in_dim | solution.py:74
  68.7 5.2 %all-to-all-done = f32[16,1,10]{2,1,0:T(1,128)S(1)} async-done(((f32[16,1,10]{2,1,0:T(1,128)}), f32[16,1,10]{2,1,0:T(1,128)S(1)}, u32[]{:S(2)}, u32[]{:S(2)}) %all-to-all-start) | async-done | bytes 672 | tf_op jit(solution)/shard_map/all_to_all | solution.py:21
  73.9 0.1 slice_add_fusion.4
  74.0 0.1 div.22
  74.1 0.1 div.23
  74.2 0.6 slice_divide_fusion
  74.8 3.0 %shard_map.86 = bf16[1,2,2,256,512]{4,3,2,1,0:T(8,128)(2,1)} custom-call(f32[4]{0:T(128)} %get-tuple-element.21.real_ref, f32[4]{0:T(128)} %get-tuple-element.20.imag_ref, f32[2,2,256,512]{3,2,1,0:T(8,128)} %copy-done.1, bf16[1,2,2,256,512]{4,3,2,1,0:T(8,128)(2,1)} %block_ref.1), custom_call_target="tpu_custom_call" | custom-call | tf_op jit(solution)/shard_map/pallas_call | solution.py:97
  (3 shorter events, 0.0 us)
Async XLA Ops:
  0.6 13.7 %copy-start = (bf16[128,128]{1,0:T(8,128)(2,1)S(1)}, bf16[128,128]{1,0:T(8,128)(2,1)}, u32[]{:S(2)}) copy-start(bf16[128,128]{1,0:T(8,128)(2,1)} %param.9) | copy-start | bytes 98308
  0.6 19.6 %collective-permute-start.2 = (bf16[2,2,256,512]{3,2,1,0:T(8,128)(2,1)}, bf16[2,2,256,512]{3,2,1,0:T(8,128)(2,1)}, u32[]{:S(2)}, u32[]{:S(2)}) collective-permute-start(bf16[2,2,256,512]{3,2,1,0:T(8,128)(2,1)} %bitcast.98), channel_id=1, source_target_pairs={{0,1},{1,2},{2,3},{3,4},{4,5},{5,6},{6,7},{7,8},{8,9},{9,10},{10,1... | collective-permute-start | bytes 3145736 | tf_op jit(solution)/shard_map/ppermute | solution.py:12
  1.1 25.9 %collective-permute-start = (bf16[2,2,256,512]{3,2,1,0:T(8,128)(2,1)}, bf16[2,2,256,512]{3,2,1,0:T(8,128)(2,1)}, u32[]{:S(2)}, u32[]{:S(2)}) collective-permute-start(bf16[2,2,256,512]{3,2,1,0:T(8,128)(2,1)} %bitcast.99), channel_id=1, source_target_pairs={{0,15},{1,0},{2,1},{3,2},{4,3},{5,4},{6,5},{7,6},{8,7},{9,8},{10,9... | collective-permute-start | bytes 3145736 | tf_op jit(solution)/shard_map/ppermute | solution.py:12
  14.8 1.6 %copy-start.6 = (s32[2,2]{1,0:T(2,128)S(1)}, s32[2,2]{1,0:T(2,128)}, u32[]{:S(2)}) copy-start(s32[2,2]{1,0:T(2,128)} %param.11) | copy-start | bytes 52
  14.8 4.7 %copy-start.2 = (bf16[1,2,2,256,512]{4,3,2,1,0:T(8,128)(2,1)S(1)}, bf16[1,2,2,256,512]{4,3,2,1,0:T(8,128)(2,1)}, u32[]{:S(2)}) copy-start(bf16[1,2,2,256,512]{4,3,2,1,0:T(8,128)(2,1)} %block_ref.1) | copy-start | bytes 3145732
  20.1 7.0 %copy-start.4 = (bf16[4,2,512,512]{3,2,1,0:T(8,128)(2,1)S(1)}, bf16[4,2,512,512]{3,2,1,0:T(8,128)(2,1)}, u32[]{:S(2)}) copy-start(bf16[4,2,512,512]{3,2,1,0:T(8,128)(2,1)} %param.8) | copy-start | bytes 12582916
  20.2 17.3 %collective-permute-start.3 = (bf16[2,2,256,512]{3,2,1,0:T(8,128)(2,1)}, bf16[2,2,256,512]{3,2,1,0:T(8,128)(2,1)S(1)}, u32[]{:S(2)}, u32[]{:S(2)}) collective-permute-start(bf16[2,2,256,512]{3,2,1,0:T(8,128)(2,1)} %collective-permute-done.2), channel_id=1, source_target_pairs={{0,1},{1,2},{2,3},{3,4},{4,5},{5,6},{6,7},{7,8},{8,9},{9,10},{10,1... | collective-permute-start | bytes 3145736 | tf_op jit(solution)/shard_map/ppermute | solution.py:12
  29.6 16.1 %collective-permute-start.1 = (bf16[2,2,256,512]{3,2,1,0:T(8,128)(2,1)}, bf16[2,2,256,512]{3,2,1,0:T(8,128)(2,1)S(1)}, u32[]{:S(2)}, u32[]{:S(2)}) collective-permute-start(bf16[2,2,256,512]{3,2,1,0:T(8,128)(2,1)} %collective-permute-done), channel_id=1, source_target_pairs={{0,15},{1,0},{2,1},{3,2},{4,3},{5,4},{6,5},{7,6},{8,7},{9,8},{10,9... | collective-permute-start | bytes 3145736 | tf_op jit(solution)/shard_map/ppermute | solution.py:12
  47.0 1.6 %copy-start.3 = (f32[2,2,256,512]{3,2,1,0:T(8,128)S(1)}, f32[2,2,256,512]{3,2,1,0:T(8,128)}, u32[]{:S(2)}) copy-start(f32[2,2,256,512]{3,2,1,0:T(8,128)} %reshape.218) | copy-start | bytes 6291460
  47.0 1.6 %copy-start.5 = (bf16[256,256]{1,0:T(8,128)(2,1)S(1)}, bf16[256,256]{1,0:T(8,128)(2,1)}, u32[]{:S(2)}) copy-start(bf16[256,256]{1,0:T(8,128)(2,1)} %param.10) | copy-start | bytes 393220
  49.5 18.1 %copy-start.1 = (f32[2,2,256,512]{3,2,1,0:T(8,128)}, f32[2,2,256,512]{3,2,1,0:T(8,128)S(1)}, u32[]{:S(2)}) copy-start(f32[2,2,256,512]{3,2,1,0:T(8,128)S(1)} %fusion.2.image_ref) | copy-start | bytes 6291460
  51.8 22.1 %all-to-all-start = ((f32[16,1,10]{2,1,0:T(1,128)}), f32[16,1,10]{2,1,0:T(1,128)S(1)}, u32[]{:S(2)}, u32[]{:S(2)}) async-start(f32[16,1,10]{2,1,0:T(1,128)} %broadcast_in_dim.25), calls=%async_computation | async-start | bytes 16384 | tf_op jit(solution)/shard_map/all_to_all | solution.py:21

commit v13 on v12

--- a/solution.py
+++ b/solution.py
@@ -12,20 +12,12 @@
     return lax.ppermute(value, axis, pairs)
 
 
-def summed_over(axes, *parts):
-    flat = jnp.concatenate([part.reshape(-1) for part in parts])
+def exchanged(axes, *parts):
     count = 1
     for axis in axes:
         count = count * lax.axis_size(axis)
-    spread = jnp.broadcast_to(flat[None], (count,) + flat.shape)
-    gathered = lax.all_to_all(spread, axes, 0, 0, tiled=False)
-    total = jnp.sum(gathered, axis=0)
-    out = []
-    start = 0
-    for part in parts:
-        out.append(total[start:start + part.size].reshape(part.shape))
-        start += part.size
-    return out
+    spread = jnp.concatenate([jnp.broadcast_to(part.reshape(1, -1), (count, part.size)) for part in parts], axis=1)
+    return lax.all_to_all(spread, axes, 0, 0, tiled=True)
 
 
 def body(perturbation, coupling, y_operator, x_operator, tile_mask, slot_offsets, detuning):
@@ -67,22 +59,28 @@
     num_re = jnp.sum(qr[:, None] * wr[None, :] + qi[:, None] * wi[None, :], axis=(2, 3))
     num_im = jnp.sum(qr[:, None] * wi[None, :] - qi[:, None] * wr[None, :], axis=(2, 3))
     norms = jnp.sum(qr * qr + qi * qi, axis=(1, 2))
-    total_re, total_im, total_norms = summed_over(("harm",), num_re, num_im, norms)
-    h_re = total_re / (total_norms + 1e-06)[:, None]
-    h_im = total_im / (total_norms + 1e-06)[:, None]
-    projected = removed_projections(h_re.reshape(-1), h_im.reshape(-1), image, perturbation)
+    gathered = exchanged(("harm",), num_re, num_im, norms)
+    projected = removed_projections(gathered, image, perturbation)
     return (image.astype(jnp.bfloat16)[None], projected)
 
 
-def project_kernel(real_ref, imag_ref, image_ref, block_ref, out_ref):
+def project_kernel(gathered_ref, image_ref, block_ref, out_ref):
     vecs = image_ref.shape[1]
+    count, values = gathered_ref.shape
+    totals = []
+    for j in range(values):
+        total = gathered_ref[0, j]
+        for i in range(1, count):
+            total = total + gathered_ref[i, j]
+        totals.append(total)
     block = block_ref[0].astype(jnp.float32)
     for u in range(vecs):
         out_re = image_ref[0, u]
         out_im = image_ref[1, u]
         for v in range(vecs):
-            a = real_ref[v * vecs + u]
-            b = imag_ref[v * vecs + u]
+            scale = jnp.full((1, 1), totals[2 * vecs * vecs + v] + 1e-06, jnp.float32)
+            a = jnp.full((1, 1), totals[v * vecs + u], jnp.float32) / scale
+            b = jnp.full((1, 1), totals[vecs * vecs + v * vecs + u], jnp.float32) / scale
             q_re = block[0, v]
             q_im = block[1, v]
             out_re = out_re - (a * q_re - b * q_im)
@@ -91,7 +89,7 @@
         out_ref[0, 1, u] = out_im.astype(out_ref.dtype)
 
 
-def removed_projections(real, imag, image, perturbation):
+def removed_projections(gathered, image, perturbation):
     parts, vecs, width_x, width_fy = image.shape
     rows = 128 if width_x % 128 == 0 else width_x
     return pl.pallas_call(
@@ -99,13 +97,12 @@
         grid=(width_x // rows,),
         in_specs=[
             pl.BlockSpec(memory_space=pltpu.SMEM),
-            pl.BlockSpec(memory_space=pltpu.SMEM),
             pl.BlockSpec((parts, vecs, rows, width_fy), lambda i: (0, 0, i, 0)),
             pl.BlockSpec((1, parts, vecs, rows, width_fy), lambda i: (0, 0, 0, i, 0)),
         ],
         out_specs=pl.BlockSpec((1, parts, vecs, rows, width_fy), lambda i: (0, 0, 0, i, 0)),
         out_shape=jax.ShapeDtypeStruct(perturbation.shape, jnp.bfloat16),
-    )(real, imag, image, perturbation)
+    )(gathered, image, perturbation)
 
 
 def solution(mesh):

time: 78.2 us -> 77.9 us (level)
  no operation moved by 1% of the time
where the time goes in v13:
time: 77.9 us; the launch traced here: 77.5 us
  starting transfers between devices  28.1 us (36%)
  waiting for transfers between devices  16.1 us (21%)
  between operations  9.16 us (12%)
  matrix products  8.81 us (11%)
  other arithmetic  6.38 us (8%)
  local copies, waits for them, and re-layouts  6.03 us (8%)
  Pallas kernels  3.02 us (4%)
    all_to_all x1, starting transfers between devices, exchanged(): return lax.all_to_all(spread, axes, 0, 0, tiled=True)  15.7 us
    ppermute x4, starting transfers between devices, passed_along(): return lax.ppermute(value, axis, pairs)  12.3 us
    ppermute x4, waiting for transfers between devices, passed_along(): return lax.ppermute(value, axis, pairs)  10.9 us
    dot_general x4, matrix products, body(): jnp.einsum('cri,kio->ckro', other, matrix, preferred_element_type=jnp.flo...  7.49 us
    all_to_all x1, waiting for transfers between devices, exchanged(): return lax.all_to_all(spread, axes, 0, 0, tiled=True)  5.22 us
    pallas_call x1, Pallas kernels, removed_projections(): pl.pallas_call(project_kernel, grid=(width_x // rows,), in_specs=[pl.Bloc...  3.02 us
    sub x4, other arithmetic, body(): real_part = prod[0, 0] - prod[1, 1]  1.92 us
    another operation x1, local copies, waits for them, and re-layouts, body(): rows = block.reshape(-1, ny)  1.7 us
  transfers between devices with their start and end apart: 5, of which 3 were waited for; matrix products, arithmetic and copies ran while one was open for 19% of the time, Pallas kernels for 0%

profile of v13, /device:TPU:0, one launch (start us, length us, event | category | flops | bytes accessed | tf_op | source)
XLA Modules:
  0.0 77.5 jit_solution(1235004104452659352)
XLA Ops:
  0.6 0.0 copy-start
  0.6 0.5 collective-permute-start.2
  1.1 5.1 %collective-permute-start = (bf16[2,2,256,512]{3,2,1,0:T(8,128)(2,1)}, bf16[2,2,256,512]{3,2,1,0:T(8,128)(2,1)}, u32[]{:S(2)}, u32[]{:S(2)}) collective-permute-start(bf16[2,2,256,512]{3,2,1,0:T(8,128)(2,1)} %bitcast.101), channel_id=1, source_target_pairs={{0,15},{1,0},{2,1},{3,2},{4,3},{5,4},{6,5},{7,6},{8,7},{9,8},{10,9... | collective-permute-start | bytes 3145736 | tf_op jit(solution)/shard_map/ppermute | solution.py:12
  6.2 1.4 %fusion.22 = (s32[]{:T(128)}, s32[]{:T(128)}, s32[]{:T(128)}, s32[]{:T(128)}) fusion(s32[4]{0:T(128)} %param.12), kind=kLoop, calls=%fused_computation.48 | loop fusion | flops 44 | bytes 32 | tf_op jit(solution)/shard_map/reduce_sum | solution.py:47
  12.7 1.7 %reshape_squeeze.3 = bf16[4096,128]{1,0:T(8,128)(2,1)S(1)} reshape(bf16[1,2,2,256,512]{4,3,2,1,0:T(8,128)(2,1)} %block_ref.1) | data formatting | bytes 2097152 | tf_op jit(solution)/shard_map/reshape;squeeze | solution.py:36
  14.4 0.0 copy-done
  14.4 0.4 fusion.24
  14.9 0.0 copy-start.7
  14.9 0.0 copy-start.2
  14.9 1.5 %reshape.205 = f32[2,2,256,512]{3,2,1,0:T(8,128)} reshape(f32[4096,128]{1,0:T(8,128)S(1)} %fusion.24) | data formatting | bytes 4194304 | tf_op jit(solution)/shard_map/reshape | solution.py:37
  16.4 0.0 copy-done.7
  19.6 0.0 copy-done.2
  19.6 0.3 bitcast_convert_fusion
  19.9 0.3 add_reduce_fusion.1
  20.2 0.0 copy-start.4
  20.2 0.2 slice_bitcast_fusion.3
  20.4 0.0 collective-permute-done.2
  20.4 6.7 %collective-permute-start.3 = (bf16[2,2,256,512]{3,2,1,0:T(8,128)(2,1)}, bf16[2,2,256,512]{3,2,1,0:T(8,128)(2,1)S(1)}, u32[]{:S(2)}, u32[]{:S(2)}) collective-permute-start(bf16[2,2,256,512]{3,2,1,0:T(8,128)(2,1)} %collective-permute-done.2), channel_id=1, source_target_pairs={{0,1},{1,2},{2,3},{3,4},{4,5},{5,6},{6,7},{7,8},{8,9},{9,10},{10,1... | collective-permute-start | bytes 3145736 | tf_op jit(solution)/shard_map/ppermute | solution.py:12
  27.1 0.0 collective-permute-done
  27.1 0.0 copy-done.4
  27.1 2.5 %convolution_bitcast_fusion.2 = f32[2,2,512,512]{3,2,0,1:T(8,128)S(1)} fusion(bf16[2,512,512,1]{2,1,0,3:T(8,128)(2,1)} %bitcast.18, bf16[4,2,512,512]{3,2,1,0:T(8,128)(2,1)S(1)} %copy-done.4, s32[]{:T(128)S(6)} %select_n.29), kind=kOutput, calls=%fused_computation.2 | convolution fusion | flops 1073741824 | bytes 6291460 | tf_op jit(solution)/shard_map/cri,kio->ckro/dot_general | solution.py:50
  29.6 0.1 collective-permute-start.1
  29.6 2.5 %convolution_bitcast_fusion.1 = f32[2,2,512,512]{3,2,0,1:T(8,128)S(1)} fusion(bf16[2,512,512,1]{2,1,0,3:T(8,128)(2,1)} %bitcast.26, bf16[4,2,512,512]{3,2,1,0:T(8,128)(2,1)S(1)} %copy-done.4, s32[]{:T(128)S(6)} %select_n.31), kind=kOutput, calls=%fused_computation.1 | convolution fusion | flops 1073741824 | bytes 6291460 | tf_op jit(solution)/shard_map/cri,kio->ckro/dot_general | solution.py:50
  32.1 0.5 slice_subtract_fusion.2
  32.6 0.5 slice_subtract_fusion.1
  33.1 4.6 %collective-permute-done.3 = bf16[2,2,256,512]{3,2,1,0:T(8,128)(2,1)S(1)} collective-permute-done((bf16[2,2,256,512]{3,2,1,0:T(8,128)(2,1)}, bf16[2,2,256,512]{3,2,1,0:T(8,128)(2,1)S(1)}, u32[]{:S(2)}, u32[]{:S(2)}) %collective-permute-start.3) | collective-permute-done | bytes 1048608 | tf_op jit(solution)/shard_map/ppermute | solution.py:12
  37.7 1.3 %convolution_bitcast_fusion = f32[2,2,512,512]{3,2,0,1:T(8,128)S(1)} fusion(bf16[2,512,512,1]{2,1,0,3:T(8,128)(2,1)S(1)} %bitcast.111, bf16[4,2,512,512]{3,2,1,0:T(8,128)(2,1)S(1)} %copy-done.4, s32[]{:T(128)S(6)} %select_n.33), kind=kOutput, calls=%fused_computation | convolution fusion | flops 1073741824 | bytes 6291460 | tf_op jit(solution)/shard_map/cri,kio->ckro/dot_general | solution.py:50
  38.9 0.5 slice_subtract_fusion
  39.4 6.3 %collective-permute-done.1 = bf16[2,2,256,512]{3,2,1,0:T(8,128)(2,1)S(1)} collective-permute-done((bf16[2,2,256,512]{3,2,1,0:T(8,128)(2,1)}, bf16[2,2,256,512]{3,2,1,0:T(8,128)(2,1)S(1)}, u32[]{:S(2)}, u32[]{:S(2)}) %collective-permute-start.1) | collective-permute-done | bytes 1048608 | tf_op jit(solution)/shard_map/ppermute | solution.py:12
  45.7 1.3 %convolution_bitcast_fusion.3 = f32[2,2,512,512]{3,2,0,1:T(8,128)S(1)} fusion(bf16[2,512,512,1]{2,1,0,3:T(8,128)(2,1)S(1)} %bitcast.110, bf16[4,2,512,512]{3,2,1,0:T(8,128)(2,1)S(1)} %copy-done.4, s32[]{:T(128)S(6)} %select_n.27), kind=kOutput, calls=%fused_computation.3 | convolution fusion | flops 1073741824 | bytes 6291460 | tf_op jit(solution)/shard_map/cri,kio->ckro/dot_general | solution.py:50
  47.0 0.0 copy-start.3
  47.0 0.0 copy-start.5
  47.0 0.5 slice_subtract_fusion.3
  47.5 0.3 broadcast_in_dim.34
  47.8 0.7 copy-done.3
  48.6 0.0 copy-done.5
  48.6 0.9 %fusion.2.image_ref = f32[2,2,256,512]{3,2,1,0:T(8,128)S(1)} fusion(f32[1,2,256,512]{3,2,1,0:T(8,128)S(1)} %bitcast.109, f32[1,2,256,512]{3,2,1,0:T(8,128)S(1)} %bitcast.108, f32[1,2,256,512]{3,2,1,0:T(8,128)S(1)} %bitcast.103, f32[1,2,256,512]{3,2,1,0:T(8,128)S(1)} %bitcast.102, f32[1,2,256,512]{3,2,1,0:T(8,128)S(1)} %bitcast.105, ...), kind=kOutput, calls=%fused_computation.7 | convolution fusion | flops 274989056 | bytes 13893636 | tf_op jit(solution)/shard_map/ab,cvbf->cvaf/dot_general | solution.py:40
  49.5 0.0 copy-start.1
  49.5 0.2 slice_bitcast_fusion.2
  49.7 1.3 %add_reduce_fusion = (f32[2,2]{1,0:T(2,128)S(1)}, f32[2,2]{1,0:T(2,128)S(1)}) fusion(f32[2,256,512]{2,1,0:T(8,128)S(1)} %get-tuple-element.19, f32[2,256,512]{2,1,0:T(8,128)S(1)} %get-tuple-element.17, f32[2,256,512]{2,1,0:T(8,128)S(1)} %get-tuple-element.18, f32[2,256,512]{2,1,0:T(8,128)S(1)} %get-tuple-element.16), kind=kLoop, calls=%fused_computation.11 | loop fusion | flops 4194296 | bytes 4194336 | tf_op jit(solution)/shard_map/reduce_sum | solution.py:59
  51.0 0.1 reshape.219
  51.1 0.1 reshape.220
  51.1 0.1 maximum_maximum_fusion
  51.2 0.6 broadcast.23
  51.8 15.7 %all-to-all-start = ((f32[16,1,10]{2,1,0:T(1,128)}), f32[16,1,10]{2,1,0:T(1,128)S(1)}, u32[]{:S(2)}, u32[]{:S(2)}) async-start(f32[16,1,10]{2,1,0:T(1,128)} %bitcast.43), calls=%async_computation | async-start | bytes 16384 | tf_op jit(solution)/shard_map/all_to_all | solution.py:20
  67.6 0.0 copy-done.1
  67.6 1.1 %convert_bitcast_fusion = bf16[1,2,2,256,512]{4,3,2,1,0:T(8,128)(2,1)} fusion(f32[2,2,256,512]{3,2,1,0:T(8,128)S(1)} %fusion.2.image_ref), kind=kLoop, calls=%fused_computation.29 | loop fusion | flops 524288 | bytes 3145728 | tf_op jit(solution)/shard_map/broadcast_in_dim | solution.py:64
  68.7 5.2 %all-to-all-done = f32[16,1,10]{2,1,0:T(1,128)S(1)} async-done(((f32[16,1,10]{2,1,0:T(1,128)}), f32[16,1,10]{2,1,0:T(1,128)S(1)}, u32[]{:S(2)}, u32[]{:S(2)}) %all-to-all-start) | async-done | bytes 672 | tf_op jit(solution)/shard_map/all_to_all | solution.py:20
  73.9 0.0 copy-start.6
  73.9 0.6 copy-done.6
  74.5 3.0 %shard_map.86 = bf16[1,2,2,256,512]{4,3,2,1,0:T(8,128)(2,1)} custom-call(f32[16,10]{1,0:T(8,128)} %bitcast.114, f32[2,2,256,512]{3,2,1,0:T(8,128)} %copy-done.1, bf16[1,2,2,256,512]{4,3,2,1,0:T(8,128)(2,1)} %block_ref.1), custom_call_target="tpu_custom_call" | custom-call | tf_op jit(solution)/shard_map/pallas_call | solution.py:95
  (2 shorter events, 0.0 us)
Async XLA Ops:
  0.6 13.8 %copy-start = (bf16[128,128]{1,0:T(8,128)(2,1)S(1)}, bf16[128,128]{1,0:T(8,128)(2,1)}, u32[]{:S(2)}) copy-start(bf16[128,128]{1,0:T(8,128)(2,1)} %param.9) | copy-start | bytes 98308
  0.6 19.7 %collective-permute-start.2 = (bf16[2,2,256,512]{3,2,1,0:T(8,128)(2,1)}, bf16[2,2,256,512]{3,2,1,0:T(8,128)(2,1)}, u32[]{:S(2)}, u32[]{:S(2)}) collective-permute-start(bf16[2,2,256,512]{3,2,1,0:T(8,128)(2,1)} %bitcast.100), channel_id=1, source_target_pairs={{0,1},{1,2},{2,3},{3,4},{4,5},{5,6},{6,7},{7,8},{8,9},{9,10},{10,1... | collective-permute-start | bytes 3145736 | tf_op jit(solution)/shard_map/ppermute | solution.py:12
  1.1 25.9 %collective-permute-start = (bf16[2,2,256,512]{3,2,1,0:T(8,128)(2,1)}, bf16[2,2,256,512]{3,2,1,0:T(8,128)(2,1)}, u32[]{:S(2)}, u32[]{:S(2)}) collective-permute-start(bf16[2,2,256,512]{3,2,1,0:T(8,128)(2,1)} %bitcast.101), channel_id=1, source_target_pairs={{0,15},{1,0},{2,1},{3,2},{4,3},{5,4},{6,5},{7,6},{8,7},{9,8},{10,9... | collective-permute-start | bytes 3145736 | tf_op jit(solution)/shard_map/ppermute | solution.py:12
  14.9 1.5 %copy-start.7 = (s32[2,2]{1,0:T(2,128)S(1)}, s32[2,2]{1,0:T(2,128)}, u32[]{:S(2)}) copy-start(s32[2,2]{1,0:T(2,128)} %param.11) | copy-start | bytes 52
  14.9 4.7 %copy-start.2 = (bf16[1,2,2,256,512]{4,3,2,1,0:T(8,128)(2,1)S(1)}, bf16[1,2,2,256,512]{4,3,2,1,0:T(8,128)(2,1)}, u32[]{:S(2)}) copy-start(bf16[1,2,2,256,512]{4,3,2,1,0:T(8,128)(2,1)} %block_ref.1) | copy-start | bytes 3145732
  20.2 6.9 %copy-start.4 = (bf16[4,2,512,512]{3,2,1,0:T(8,128)(2,1)S(1)}, bf16[4,2,512,512]{3,2,1,0:T(8,128)(2,1)}, u32[]{:S(2)}) copy-start(bf16[4,2,512,512]{3,2,1,0:T(8,128)(2,1)} %param.8) | copy-start | bytes 12582916
  20.4 17.3 %collective-permute-start.3 = (bf16[2,2,256,512]{3,2,1,0:T(8,128)(2,1)}, bf16[2,2,256,512]{3,2,1,0:T(8,128)(2,1)S(1)}, u32[]{:S(2)}, u32[]{:S(2)}) collective-permute-start(bf16[2,2,256,512]{3,2,1,0:T(8,128)(2,1)} %collective-permute-done.2), channel_id=1, source_target_pairs={{0,1},{1,2},{2,3},{3,4},{4,5},{5,6},{6,7},{7,8},{8,9},{9,10},{10,1... | collective-permute-start | bytes 3145736 | tf_op jit(solution)/shard_map/ppermute | solution.py:12
  29.6 16.1 %collective-permute-start.1 = (bf16[2,2,256,512]{3,2,1,0:T(8,128)(2,1)}, bf16[2,2,256,512]{3,2,1,0:T(8,128)(2,1)S(1)}, u32[]{:S(2)}, u32[]{:S(2)}) collective-permute-start(bf16[2,2,256,512]{3,2,1,0:T(8,128)(2,1)} %collective-permute-done), channel_id=1, source_target_pairs={{0,15},{1,0},{2,1},{3,2},{4,3},{5,4},{6,5},{7,6},{8,7},{9,8},{10,9... | collective-permute-start | bytes 3145736 | tf_op jit(solution)/shard_map/ppermute | solution.py:12
  47.0 1.6 %copy-start.3 = (f32[2,2,256,512]{3,2,1,0:T(8,128)S(1)}, f32[2,2,256,512]{3,2,1,0:T(8,128)}, u32[]{:S(2)}) copy-start(f32[2,2,256,512]{3,2,1,0:T(8,128)} %reshape.205) | copy-start | bytes 6291460
  47.0 1.6 %copy-start.5 = (bf16[256,256]{1,0:T(8,128)(2,1)S(1)}, bf16[256,256]{1,0:T(8,128)(2,1)}, u32[]{:S(2)}) copy-start(bf16[256,256]{1,0:T(8,128)(2,1)} %param.10) | copy-start | bytes 393220
  49.5 18.1 %copy-start.1 = (f32[2,2,256,512]{3,2,1,0:T(8,128)}, f32[2,2,256,512]{3,2,1,0:T(8,128)S(1)}, u32[]{:S(2)}) copy-start(f32[2,2,256,512]{3,2,1,0:T(8,128)S(1)} %fusion.2.image_ref) | copy-start | bytes 6291460
  51.8 22.1 %all-to-all-start = ((f32[16,1,10]{2,1,0:T(1,128)}), f32[16,1,10]{2,1,0:T(1,128)S(1)}, u32[]{:S(2)}, u32[]{:S(2)}) async-start(f32[16,1,10]{2,1,0:T(1,128)} %bitcast.43), calls=%async_computation | async-start | bytes 16384 | tf_op jit(solution)/shard_map/all_to_all | solution.py:20
  73.9 0.6 copy-start.6

commit v14 on v13

--- a/solution.py
+++ b/solution.py
@@ -12,12 +12,18 @@
     return lax.ppermute(value, axis, pairs)
 
 
-def exchanged(axes, *parts):
-    count = 1
-    for axis in axes:
-        count = count * lax.axis_size(axis)
-    spread = jnp.concatenate([jnp.broadcast_to(part.reshape(1, -1), (count, part.size)) for part in parts], axis=1)
-    return lax.all_to_all(spread, axes, 0, 0, tiled=True)
+def summed_over(axis, *parts):
+    flat = jnp.concatenate([part.reshape(1, -1) for part in parts], axis=1)
+    count = lax.axis_size(axis)
+    if count & (count - 1) == 0:
+        step = 1
+        while step < count:
+            flat = flat + lax.ppermute(flat, axis, [(i, i ^ step) for i in range(count)])
+            step *= 2
+        return flat
+    spread = jnp.broadcast_to(flat, (count, flat.shape[1]))
+    gathered = lax.all_to_all(spread, axis, 0, 0, tiled=True)
+    return jnp.sum(gathered, axis=0, keepdims=True)
 
 
 def body(perturbation, coupling, y_operator, x_operator, tile_mask, slot_offsets, detuning):
@@ -59,7 +65,7 @@
     num_re = jnp.sum(qr[:, None] * wr[None, :] + qi[:, None] * wi[None, :], axis=(2, 3))
     num_im = jnp.sum(qr[:, None] * wi[None, :] - qi[:, None] * wr[None, :], axis=(2, 3))
     norms = jnp.sum(qr * qr + qi * qi, axis=(1, 2))
-    gathered = exchanged(("harm",), num_re, num_im, norms)
+    gathered = summed_over("harm", num_re, num_im, norms)
     projected = removed_projections(gathered, image, perturbation)
     return (image.astype(jnp.bfloat16)[None], projected)
 

time: 77.9 us -> 81.8 us (1.050)
  waiting for transfers between devices: 16.1 us -> 20.7 us
    all_to_all x1 -> x0, starting transfers between devices: 15.7 us -> none  [exchanged(): return lax.all_to_all(spread, axes, 0, 0, tiled=True)]
    ppermute x0 -> x4, starting transfers between devices: none -> 14.5 us  [summed_over(): lax.ppermute(flat, axis, [(i, i ^ step) for i in range(count)])]
    ppermute x0 -> x4, waiting for transfers between devices: none -> 9.87 us  [summed_over(): lax.ppermute(flat, axis, [(i, i ^ step) for i in range(count)])]
    all_to_all x1 -> x0, waiting for transfers between devices: 5.22 us -> none  [exchanged(): return lax.all_to_all(spread, axes, 0, 0, tiled=True)]
    unnamed x16 -> x14, local copies, waits for them, and re-layouts: 1.36 us -> 1.91 us
  transfers between devices with their start and end apart: 5 -> 8, of which waited for: 3 -> 6; matrix products, arithmetic and copies ran while one was open for 19% -> 16% of each run, Pallas kernels for 0% -> 0%
where the time goes in v14:
time: 81.8 us; the launch traced here: 81.4 us
  starting transfers between devices  27.3 us (33%)
  waiting for transfers between devices  20.7 us (25%)
  matrix products  8.8 us (11%)
  between operations  8.75 us (11%)
  other arithmetic  6.86 us (8%)
  local copies, waits for them, and re-layouts  5.97 us (7%)
  Pallas kernels  2.97 us (4%)
    ppermute x4, starting transfers between devices, summed_over(): lax.ppermute(flat, axis, [(i, i ^ step) for i in range(count)])  14.5 us
    ppermute x4, starting transfers between devices, passed_along(): return lax.ppermute(value, axis, pairs)  12.8 us
    ppermute x4, waiting for transfers between devices, passed_along(): return lax.ppermute(value, axis, pairs)  10.9 us
    ppermute x4, waiting for transfers between devices, summed_over(): lax.ppermute(flat, axis, [(i, i ^ step) for i in range(count)])  9.87 us
    dot_general x4, matrix products, body(): jnp.einsum('cri,kio->ckro', other, matrix, preferred_element_type=jnp.flo...  7.49 us
    pallas_call x1, Pallas kernels, removed_projections(): pl.pallas_call(project_kernel, grid=(width_x // rows,), in_specs=[pl.Bloc...  2.97 us
    sub x4, other arithmetic, body(): real_part = prod[0, 0] - prod[1, 1]  1.92 us
    unnamed x14, local copies, waits for them, and re-layouts  1.91 us
  transfers between devices with their start and end apart: 8, of which 6 were waited for; matrix products, arithmetic and copies ran while one was open for 16% of the time, Pallas kernels for 0%

profile of v14, /device:TPU:0, one launch (start us, length us, event | category | flops | bytes accessed | tf_op | source)
XLA Modules:
  0.0 81.4 jit_solution(15106765806990458338)
XLA Ops:
  0.6 0.0 copy-start
  0.6 0.5 collective-permute-start.2
  1.1 5.1 %collective-permute-start = (bf16[2,2,256,512]{3,2,1,0:T(8,128)(2,1)}, bf16[2,2,256,512]{3,2,1,0:T(8,128)(2,1)}, u32[]{:S(2)}, u32[]{:S(2)}) collective-permute-start(bf16[2,2,256,512]{3,2,1,0:T(8,128)(2,1)} %bitcast.100), channel_id=1, source_target_pairs={{0,15},{1,0},{2,1},{3,2},{4,3},{5,4},{6,5},{7,6},{8,7},{9,8},{10,9... | collective-permute-start | bytes 3145736 | tf_op jit(solution)/shard_map/ppermute | solution.py:12
  6.2 1.3 %fusion.22 = (s32[]{:T(128)}, s32[]{:T(128)}, s32[]{:T(128)}, s32[]{:T(128)}) fusion(s32[4]{0:T(128)} %param.12), kind=kLoop, calls=%fused_computation.48 | loop fusion | flops 44 | bytes 32 | tf_op jit(solution)/shard_map/reduce_sum | solution.py:53
  12.4 1.7 %reshape_squeeze.3 = bf16[4096,128]{1,0:T(8,128)(2,1)S(1)} reshape(bf16[1,2,2,256,512]{4,3,2,1,0:T(8,128)(2,1)} %block_ref.1) | data formatting | bytes 2097152 | tf_op jit(solution)/shard_map/reshape;squeeze | solution.py:42
  14.1 0.0 copy-done
  14.1 0.4 fusion.24
  14.5 0.0 copy-start.6
  14.5 0.0 copy-start.2
  14.5 1.5 %reshape.206 = f32[2,2,256,512]{3,2,1,0:T(8,128)} reshape(f32[4096,128]{1,0:T(8,128)S(1)} %fusion.24) | data formatting | bytes 4194304 | tf_op jit(solution)/shard_map/reshape | solution.py:43
  16.1 0.0 copy-done.6
  19.1 0.0 copy-done.2
  19.1 0.3 bitcast_convert_fusion
  19.4 0.3 add_reduce_fusion.1
  19.7 0.0 copy-start.4
  19.7 0.2 slice_bitcast_fusion.3
  19.9 0.0 collective-permute-done.2
  19.9 7.2 %collective-permute-start.3 = (bf16[2,2,256,512]{3,2,1,0:T(8,128)(2,1)}, bf16[2,2,256,512]{3,2,1,0:T(8,128)(2,1)S(1)}, u32[]{:S(2)}, u32[]{:S(2)}) collective-permute-start(bf16[2,2,256,512]{3,2,1,0:T(8,128)(2,1)} %collective-permute-done.2), channel_id=1, source_target_pairs={{0,1},{1,2},{2,3},{3,4},{4,5},{5,6},{6,7},{7,8},{8,9},{9,10},{10,1... | collective-permute-start | bytes 3145736 | tf_op jit(solution)/shard_map/ppermute | solution.py:12
  27.1 0.0 collective-permute-done
  27.1 0.0 copy-done.4
  27.1 2.5 %convolution_bitcast_fusion.2 = f32[2,2,512,512]{3,2,0,1:T(8,128)S(1)} fusion(bf16[2,512,512,1]{2,1,0,3:T(8,128)(2,1)} %bitcast.18, bf16[4,2,512,512]{3,2,1,0:T(8,128)(2,1)S(1)} %copy-done.4, s32[]{:T(128)S(6)} %select_n.29), kind=kOutput, calls=%fused_computation.2 | convolution fusion | flops 1073741824 | bytes 6291460 | tf_op jit(solution)/shard_map/cri,kio->ckro/dot_general | solution.py:56
  29.6 0.1 collective-permute-start.1
  29.6 2.5 %convolution_bitcast_fusion.1 = f32[2,2,512,512]{3,2,0,1:T(8,128)S(1)} fusion(bf16[2,512,512,1]{2,1,0,3:T(8,128)(2,1)} %bitcast.26, bf16[4,2,512,512]{3,2,1,0:T(8,128)(2,1)S(1)} %copy-done.4, s32[]{:T(128)S(6)} %select_n.31), kind=kOutput, calls=%fused_computation.1 | convolution fusion | flops 1073741824 | bytes 6291460 | tf_op jit(solution)/shard_map/cri,kio->ckro/dot_general | solution.py:56
  32.1 0.5 slice_subtract_fusion.2
  32.6 0.5 slice_subtract_fusion.1
  33.1 4.1 %collective-permute-done.3 = bf16[2,2,256,512]{3,2,1,0:T(8,128)(2,1)S(1)} collective-permute-done((bf16[2,2,256,512]{3,2,1,0:T(8,128)(2,1)}, bf16[2,2,256,512]{3,2,1,0:T(8,128)(2,1)S(1)}, u32[]{:S(2)}, u32[]{:S(2)}) %collective-permute-start.3) | collective-permute-done | bytes 1048608 | tf_op jit(solution)/shard_map/ppermute | solution.py:12
  37.2 1.3 %convolution_bitcast_fusion = f32[2,2,512,512]{3,2,0,1:T(8,128)S(1)} fusion(bf16[2,512,512,1]{2,1,0,3:T(8,128)(2,1)S(1)} %bitcast.110, bf16[4,2,512,512]{3,2,1,0:T(8,128)(2,1)S(1)} %copy-done.4, s32[]{:T(128)S(6)} %select_n.33), kind=kOutput, calls=%fused_computation | convolution fusion | flops 1073741824 | bytes 6291460 | tf_op jit(solution)/shard_map/cri,kio->ckro/dot_general | solution.py:56
  38.4 0.5 slice_subtract_fusion
  38.9 6.8 %collective-permute-done.1 = bf16[2,2,256,512]{3,2,1,0:T(8,128)(2,1)S(1)} collective-permute-done((bf16[2,2,256,512]{3,2,1,0:T(8,128)(2,1)}, bf16[2,2,256,512]{3,2,1,0:T(8,128)(2,1)S(1)}, u32[]{:S(2)}, u32[]{:S(2)}) %collective-permute-start.1) | collective-permute-done | bytes 1048608 | tf_op jit(solution)/shard_map/ppermute | solution.py:12
  45.7 1.3 %convolution_bitcast_fusion.3 = f32[2,2,512,512]{3,2,0,1:T(8,128)S(1)} fusion(bf16[2,512,512,1]{2,1,0,3:T(8,128)(2,1)S(1)} %bitcast.109, bf16[4,2,512,512]{3,2,1,0:T(8,128)(2,1)S(1)} %copy-done.4, s32[]{:T(128)S(6)} %select_n.27), kind=kOutput, calls=%fused_computation.3 | convolution fusion | flops 1073741824 | bytes 6291460 | tf_op jit(solution)/shard_map/cri,kio->ckro/dot_general | solution.py:56
  47.0 0.0 copy-start.3
  47.0 0.0 copy-start.5
  47.0 0.5 slice_subtract_fusion.3
  47.5 0.3 broadcast_in_dim.15
  47.8 0.7 copy-done.3
  48.6 0.0 copy-done.5
  48.6 0.9 %fusion.2.image_ref = f32[2,2,256,512]{3,2,1,0:T(8,128)S(1)} fusion(f32[1,2,256,512]{3,2,1,0:T(8,128)S(1)} %bitcast.108, f32[1,2,256,512]{3,2,1,0:T(8,128)S(1)} %bitcast.107, f32[1,2,256,512]{3,2,1,0:T(8,128)S(1)} %bitcast.102, f32[1,2,256,512]{3,2,1,0:T(8,128)S(1)} %bitcast.101, f32[1,2,256,512]{3,2,1,0:T(8,128)S(1)} %bitcast.104, ...), kind=kOutput, calls=%fused_computation.7 | convolution fusion | flops 274989056 | bytes 13893636 | tf_op jit(solution)/shard_map/ab,cvbf->cvaf/dot_general | solution.py:46
  49.5 0.0 copy-start.1
  49.5 0.2 slice_bitcast_fusion.2
  49.7 1.1 %copy-done.1 = f32[2,2,256,512]{3,2,1,0:T(8,128)} copy-done((f32[2,2,256,512]{3,2,1,0:T(8,128)}, f32[2,2,256,512]{3,2,1,0:T(8,128)S(1)}, u32[]{:S(2)}) %copy-start.1) | copy-done | bytes 2097176
  50.8 1.1 %convert_bitcast_fusion = bf16[1,2,2,256,512]{4,3,2,1,0:T(8,128)(2,1)} fusion(f32[2,2,256,512]{3,2,1,0:T(8,128)S(1)} %fusion.2.image_ref), kind=kLoop, calls=%fused_computation.29 | loop fusion | flops 524288 | bytes 3145728 | tf_op jit(solution)/shard_map/broadcast_in_dim | solution.py:70
  51.9 1.3 %add_reduce_fusion = (f32[2,2]{1,0:T(2,128)S(1)}, f32[2,2]{1,0:T(2,128)S(1)}) fusion(f32[2,256,512]{2,1,0:T(8,128)S(1)} %get-tuple-element.19, f32[2,256,512]{2,1,0:T(8,128)S(1)} %get-tuple-element.17, f32[2,256,512]{2,1,0:T(8,128)S(1)} %get-tuple-element.18, f32[2,256,512]{2,1,0:T(8,128)S(1)} %get-tuple-element.16), kind=kLoop, calls=%fused_computation.11 | loop fusion | flops 4194296 | bytes 4194336 | tf_op jit(solution)/shard_map/reduce_sum | solution.py:65
  53.2 0.1 reshape.211
  53.3 0.1 reshape.212
  53.4 0.1 pad_maximum_fusion
  53.5 12.1 %collective-permute-start.4 = (f32[1,10]{1,0:T(1,128)S(1)}, f32[1,10]{1,0:T(1,128)S(1)}, u32[]{:S(2)}, u32[]{:S(2)}) collective-permute-start(f32[1,10]{1,0:T(1,128)S(1)} %pad_maximum_fusion), channel_id=1, source_target_pairs={{0,1},{1,0},{2,3},{3,2},{4,5},{5,4},{6,7},{7,6},{8,9},{9,8},{10,11... | collective-permute-start | bytes 128 | tf_op jit(solution)/shard_map/ppermute | solution.py:21
  65.5 0.8 %collective-permute-done.4 = f32[1,10]{1,0:T(1,128)S(1)} collective-permute-done((f32[1,10]{1,0:T(1,128)S(1)}, f32[1,10]{1,0:T(1,128)S(1)}, u32[]{:S(2)}, u32[]{:S(2)}) %collective-permute-start.4) | collective-permute-done | bytes 72 | tf_op jit(solution)/shard_map/ppermute | solution.py:21
  66.4 0.1 fusion.31
  66.4 0.1 collective-permute-start.5
  66.6 3.4 %collective-permute-done.5 = f32[1,10]{1,0:T(1,128)S(1)} collective-permute-done((f32[1,10]{1,0:T(1,128)S(1)}, f32[1,10]{1,0:T(1,128)S(1)}, u32[]{:S(2)}, u32[]{:S(2)}) %collective-permute-start.5) | collective-permute-done | bytes 72 | tf_op jit(solution)/shard_map/ppermute | solution.py:21
  70.0 0.7 collective-permute-start.6
  70.6 2.9 %collective-permute-done.6 = f32[1,10]{1,0:T(1,128)S(1)} collective-permute-done((f32[1,10]{1,0:T(1,128)S(1)}, f32[1,10]{1,0:T(1,128)S(1)}, u32[]{:S(2)}, u32[]{:S(2)}) %collective-permute-start.6) | collective-permute-done | bytes 72 | tf_op jit(solution)/shard_map/ppermute | solution.py:21
  73.5 1.7 %collective-permute-start.7 = (f32[1,10]{1,0:T(1,128)S(1)}, f32[1,10]{1,0:T(1,128)S(1)}, u32[]{:S(2)}, u32[]{:S(2)}) collective-permute-start(f32[1,10]{1,0:T(1,128)S(1)} %add.132), channel_id=1, source_target_pairs={{0,8},{1,9},{2,10},{3,11},{4,12},{5,13},{6,14},{7,15},{8,0},{9,1},... | collective-permute-start | bytes 128 | tf_op jit(solution)/shard_map/ppermute | solution.py:21
  75.2 2.8 %collective-permute-done.7 = f32[1,10]{1,0:T(1,128)S(1)} collective-permute-done((f32[1,10]{1,0:T(1,128)S(1)}, f32[1,10]{1,0:T(1,128)S(1)}, u32[]{:S(2)}, u32[]{:S(2)}) %collective-permute-start.7) | collective-permute-done | bytes 72 | tf_op jit(solution)/shard_map/ppermute | solution.py:21
  78.0 0.5 add.133.gathered_ref
  78.5 3.0 %shard_map.86 = bf16[1,2,2,256,512]{4,3,2,1,0:T(8,128)(2,1)} custom-call(f32[1,10]{1,0:T(1,128)} %add.133.gathered_ref, f32[2,2,256,512]{3,2,1,0:T(8,128)} %copy-done.1, bf16[1,2,2,256,512]{4,3,2,1,0:T(8,128)(2,1)} %block_ref.1), custom_call_target="tpu_custom_call" | custom-call | tf_op jit(solution)/shard_map/pallas_call | solution.py:101
  (4 shorter events, 0.0 us)
Async XLA Ops:
  0.6 13.5 %copy-start = (bf16[128,128]{1,0:T(8,128)(2,1)S(1)}, bf16[128,128]{1,0:T(8,128)(2,1)}, u32[]{:S(2)}) copy-start(bf16[128,128]{1,0:T(8,128)(2,1)} %param.9) | copy-start | bytes 98308
  0.6 19.2 %collective-permute-start.2 = (bf16[2,2,256,512]{3,2,1,0:T(8,128)(2,1)}, bf16[2,2,256,512]{3,2,1,0:T(8,128)(2,1)}, u32[]{:S(2)}, u32[]{:S(2)}) collective-permute-start(bf16[2,2,256,512]{3,2,1,0:T(8,128)(2,1)} %bitcast.99), channel_id=1, source_target_pairs={{0,1},{1,2},{2,3},{3,4},{4,5},{5,6},{6,7},{7,8},{8,9},{9,10},{10,1... | collective-permute-start | bytes 3145736 | tf_op jit(solution)/shard_map/ppermute | solution.py:12
  1.1 25.9 %collective-permute-start = (bf16[2,2,256,512]{3,2,1,0:T(8,128)(2,1)}, bf16[2,2,256,512]{3,2,1,0:T(8,128)(2,1)}, u32[]{:S(2)}, u32[]{:S(2)}) collective-permute-start(bf16[2,2,256,512]{3,2,1,0:T(8,128)(2,1)} %bitcast.100), channel_id=1, source_target_pairs={{0,15},{1,0},{2,1},{3,2},{4,3},{5,4},{6,5},{7,6},{8,7},{9,8},{10,9... | collective-permute-start | bytes 3145736 | tf_op jit(solution)/shard_map/ppermute | solution.py:12
  14.5 1.5 %copy-start.6 = (s32[2,2]{1,0:T(2,128)S(1)}, s32[2,2]{1,0:T(2,128)}, u32[]{:S(2)}) copy-start(s32[2,2]{1,0:T(2,128)} %param.11) | copy-start | bytes 52
  14.5 4.6 %copy-start.2 = (bf16[1,2,2,256,512]{4,3,2,1,0:T(8,128)(2,1)S(1)}, bf16[1,2,2,256,512]{4,3,2,1,0:T(8,128)(2,1)}, u32[]{:S(2)}) copy-start(bf16[1,2,2,256,512]{4,3,2,1,0:T(8,128)(2,1)} %block_ref.1) | copy-start | bytes 3145732
  19.7 7.4 %copy-start.4 = (bf16[4,2,512,512]{3,2,1,0:T(8,128)(2,1)S(1)}, bf16[4,2,512,512]{3,2,1,0:T(8,128)(2,1)}, u32[]{:S(2)}) copy-start(bf16[4,2,512,512]{3,2,1,0:T(8,128)(2,1)} %param.8) | copy-start | bytes 12582916
  19.9 17.3 %collective-permute-start.3 = (bf16[2,2,256,512]{3,2,1,0:T(8,128)(2,1)}, bf16[2,2,256,512]{3,2,1,0:T(8,128)(2,1)S(1)}, u32[]{:S(2)}, u32[]{:S(2)}) collective-permute-start(bf16[2,2,256,512]{3,2,1,0:T(8,128)(2,1)} %collective-permute-done.2), channel_id=1, source_target_pairs={{0,1},{1,2},{2,3},{3,4},{4,5},{5,6},{6,7},{7,8},{8,9},{9,10},{10,1... | collective-permute-start | bytes 3145736 | tf_op jit(solution)/shard_map/ppermute | solution.py:12
  29.6 16.1 %collective-permute-start.1 = (bf16[2,2,256,512]{3,2,1,0:T(8,128)(2,1)}, bf16[2,2,256,512]{3,2,1,0:T(8,128)(2,1)S(1)}, u32[]{:S(2)}, u32[]{:S(2)}) collective-permute-start(bf16[2,2,256,512]{3,2,1,0:T(8,128)(2,1)} %collective-permute-done), channel_id=1, source_target_pairs={{0,15},{1,0},{2,1},{3,2},{4,3},{5,4},{6,5},{7,6},{8,7},{9,8},{10,9... | collective-permute-start | bytes 3145736 | tf_op jit(solution)/shard_map/ppermute | solution.py:12
  47.0 1.6 %copy-start.3 = (f32[2,2,256,512]{3,2,1,0:T(8,128)S(1)}, f32[2,2,256,512]{3,2,1,0:T(8,128)}, u32[]{:S(2)}) copy-start(f32[2,2,256,512]{3,2,1,0:T(8,128)} %reshape.206) | copy-start | bytes 6291460
  47.0 1.6 %copy-start.5 = (bf16[256,256]{1,0:T(8,128)(2,1)S(1)}, bf16[256,256]{1,0:T(8,128)(2,1)}, u32[]{:S(2)}) copy-start(bf16[256,256]{1,0:T(8,128)(2,1)} %param.10) | copy-start | bytes 393220
  49.5 1.3 %copy-start.1 = (f32[2,2,256,512]{3,2,1,0:T(8,128)}, f32[2,2,256,512]{3,2,1,0:T(8,128)S(1)}, u32[]{:S(2)}) copy-start(f32[2,2,256,512]{3,2,1,0:T(8,128)S(1)} %fusion.2.image_ref) | copy-start | bytes 6291460
  53.5 12.9 %collective-permute-start.4 = (f32[1,10]{1,0:T(1,128)S(1)}, f32[1,10]{1,0:T(1,128)S(1)}, u32[]{:S(2)}, u32[]{:S(2)}) collective-permute-start(f32[1,10]{1,0:T(1,128)S(1)} %pad_maximum_fusion), channel_id=1, source_target_pairs={{0,1},{1,0},{2,3},{3,2},{4,5},{5,4},{6,7},{7,6},{8,9},{9,8},{10,11... | collective-permute-start | bytes 128 | tf_op jit(solution)/shard_map/ppermute | solution.py:21
  66.4 3.5 %collective-permute-start.5 = (f32[1,10]{1,0:T(1,128)S(1)}, f32[1,10]{1,0:T(1,128)S(1)}, u32[]{:S(2)}, u32[]{:S(2)}) collective-permute-start(f32[1,10]{1,0:T(1,128)S(1)} %fusion.31), channel_id=1, source_target_pairs={{0,2},{1,3},{2,0},{3,1},{4,6},{5,7},{6,4},{7,5},{8,10},{9,11},{10,... | collective-permute-start | bytes 128 | tf_op jit(solution)/shard_map/ppermute | solution.py:21
  70.0 3.5 %collective-permute-start.6 = (f32[1,10]{1,0:T(1,128)S(1)}, f32[1,10]{1,0:T(1,128)S(1)}, u32[]{:S(2)}, u32[]{:S(2)}) collective-permute-start(f32[1,10]{1,0:T(1,128)S(1)} %add.131), channel_id=1, source_target_pairs={{0,4},{1,5},{2,6},{3,7},{4,0},{5,1},{6,2},{7,3},{8,12},{9,13},{10,... | collective-permute-start | bytes 128 | tf_op jit(solution)/shard_map/ppermute | solution.py:21
  73.5 4.4 %collective-permute-start.7 = (f32[1,10]{1,0:T(1,128)S(1)}, f32[1,10]{1,0:T(1,128)S(1)}, u32[]{:S(2)}, u32[]{:S(2)}) collective-permute-start(f32[1,10]{1,0:T(1,128)S(1)} %add.132), channel_id=1, source_target_pairs={{0,8},{1,9},{2,10},{3,11},{4,12},{5,13},{6,14},{7,15},{8,0},{9,1},... | collective-permute-start | bytes 128 | tf_op jit(solution)/shard_map/ppermute | solution.py:21

commit v15 on v13

--- a/solution.py
+++ b/solution.py
@@ -6,10 +6,32 @@
 from jax.sharding import PartitionSpec as P
 
 
-def passed_along(value, axis, steps):
+def passed_along(value, axis, steps, parity=None):
     count = lax.axis_size(axis)
-    pairs = [(source, (source + steps) % count) for source in range(count)]
+    sources = [source for source in range(count) if parity is None or source % 2 == parity]
+    pairs = [(source, (source + steps) % count) for source in sources]
     return lax.ppermute(value, axis, pairs)
+
+
+def neighbours(block, axis):
+    if lax.axis_size(axis) % 2:
+        below_one = passed_along(block, axis, 1)
+        above_one = passed_along(block, axis, -1)
+        return below_one, above_one, passed_along(below_one, axis, 1), passed_along(above_one, axis, -1)
+    even = lax.axis_index(axis) % 2 == 0
+    near_up = passed_along(block, axis, 1, parity=0)
+    far_up = passed_along(block, axis, 1, parity=1)
+    near_down = passed_along(block, axis, -1, parity=1)
+    far_down = passed_along(block, axis, -1, parity=0)
+    far_up_two = passed_along(near_up, axis, 1, parity=1)
+    far_down_two = passed_along(near_down, axis, -1, parity=0)
+    near_up_two = passed_along(far_up, axis, 1, parity=0)
+    near_down_two = passed_along(far_down, axis, -1, parity=1)
+    below_one = jnp.where(even, far_up, near_up)
+    above_one = jnp.where(even, near_down, far_down)
+    below_two = jnp.where(even, far_up_two, near_up_two)
+    above_two = jnp.where(even, near_down_two, far_down_two)
+    return below_one, above_one, below_two, above_two
 
 
 def exchanged(axes, *parts):
@@ -29,10 +51,7 @@
     harmonics = lax.axis_size("harm")
     position = lax.axis_index("harm")
     tile = width_x // tile_mask.shape[0]
-    below_one = passed_along(block, "harm", 1)
-    above_one = passed_along(block, "harm", -1)
-    below_two = passed_along(below_one, "harm", 1)
-    above_two = passed_along(above_one, "harm", -1)
+    below_one, above_one, below_two, above_two = neighbours(block, "harm")
     rows = block.reshape(-1, ny)
     along_y = jnp.dot(rows, y_operator, preferred_element_type=jnp.float32).reshape(block.shape)
     full_mask = jnp.repeat(jnp.repeat(tile_mask, tile, axis=0), tile, axis=1).astype(jnp.bfloat16)

time: 77.9 us -> 85.3 us (1.095)
  starting transfers between devices: 28.1 us -> 36.6 us
  waiting for transfers between devices: 16.1 us -> 9.99 us
  other arithmetic: 6.38 us -> 9.93 us
  local copies, waits for them, and re-layouts: 6.03 us -> 7.98 us
  matrix products: 8.81 us -> 7.69 us
    ppermute x4 -> x8, starting transfers between devices: 12.3 us -> 26.5 us  [passed_along(): return lax.ppermute(value, axis, pairs)]
    ppermute x4 -> x8, waiting for transfers between devices: 10.9 us -> 4.78 us  [passed_along(): return lax.ppermute(value, axis, pairs)]
    all_to_all x1, starting transfers between devices: 15.7 us -> 10.1 us  [exchanged(): return lax.all_to_all(spread, axes, 0, 0, tiled=True)]
    select_n x0 -> x3, other arithmetic: none -> 2.9 us  [the longest x1 1.35 us: neighbours(): above_one = jnp.where(even, near_down, far_down)]
    dot_general x4, matrix products: 7.49 us -> 5.07 us  [body(): jnp.einsum('cri,kio->ckro', other, matrix, preferred_element_type=jnp.flo...]
    dot_general x1, matrix products: 0.41 us -> 1.71 us  [body(): jnp.dot(rows, y_operator, preferred_element_type=jnp.float32)]
    reshape x1, local copies, waits for them, and re-layouts: 1.52 us -> 2.76 us  [body(): jnp.dot(rows, y_operator, preferred_element_type=jnp.float32)]
    convert_element_type x1, other arithmetic: 0.27 us -> 1.5 us  [body(): image = along_y + along_x + lam * block.astype(jnp.float32)]
  transfers between devices with their start and end apart: 5 -> 9, of which waited for: 3 -> 3; matrix products, arithmetic and copies ran while one was open for 19% -> 19% of each run, Pallas kernels for 0% -> 0%
where the time goes in v15:
time: 85.3 us; the launch traced here: 84.7 us
  starting transfers between devices  36.6 us (43%)
  waiting for transfers between devices  9.99 us (12%)
  other arithmetic  9.93 us (12%)
  between operations  9.42 us (11%)
  local copies, waits for them, and re-layouts  7.98 us (9%)
  matrix products  7.69 us (9%)
  Pallas kernels  3.02 us (4%)
    ppermute x8, starting transfers between devices, passed_along(): return lax.ppermute(value, axis, pairs)  26.5 us
    all_to_all x1, starting transfers between devices, exchanged(): return lax.all_to_all(spread, axes, 0, 0, tiled=True)  10.1 us
    all_to_all x1, waiting for transfers between devices, exchanged(): return lax.all_to_all(spread, axes, 0, 0, tiled=True)  5.22 us
    dot_general x4, matrix products, body(): jnp.einsum('cri,kio->ckro', other, matrix, preferred_element_type=jnp.flo...  5.07 us
    ppermute x8, waiting for transfers between devices, passed_along(): return lax.ppermute(value, axis, pairs)  4.78 us
    pallas_call x1, Pallas kernels, removed_projections(): pl.pallas_call(project_kernel, grid=(width_x // rows,), in_specs=[pl.Bloc...  3.02 us
    reshape x1, local copies, waits for them, and re-layouts, body(): jnp.dot(rows, y_operator, preferred_element_type=jnp.float32)  2.76 us
    unnamed x20, local copies, waits for them, and re-layouts  2.31 us
  transfers between devices with their start and end apart: 9, of which 3 were waited for; matrix products, arithmetic and copies ran while one was open for 19% of the time, Pallas kernels for 0%

profile of v15, /device:TPU:0, one launch (start us, length us, event | category | flops | bytes accessed | tf_op | source)
XLA Modules:
  0.0 84.7 jit_solution(15264176782854981839)
XLA Ops:
  0.6 0.0 copy-start
  0.6 0.0 copy-start.2
  0.7 3.5 %collective-permute-start.5 = (bf16[2,2,256,512]{3,2,1,0:T(8,128)(2,1)}, bf16[2,2,256,512]{3,2,1,0:T(8,128)(2,1)}, u32[]{:S(2)}, u32[]{:S(2)}) collective-permute-start(bf16[2,2,256,512]{3,2,1,0:T(8,128)(2,1)} %bitcast.100), channel_id=1, source_target_pairs={{0,1},{2,3},{4,5},{6,7},{8,9},{10,11},{12,13},{14,15},{16,17},{18,... | collective-permute-start | bytes 3145736 | tf_op jit(solution)/shard_map/ppermute | solution.py:13
  4.1 1.3 %collective-permute-start.4 = (bf16[2,2,256,512]{3,2,1,0:T(8,128)(2,1)}, bf16[2,2,256,512]{3,2,1,0:T(8,128)(2,1)}, u32[]{:S(2)}, u32[]{:S(2)}) collective-permute-start(bf16[2,2,256,512]{3,2,1,0:T(8,128)(2,1)} %bitcast.101), channel_id=1, source_target_pairs={{1,2},{3,4},{5,6},{7,8},{9,10},{11,12},{13,14},{15,0},{17,18},{19,... | collective-permute-start | bytes 3145736 | tf_op jit(solution)/shard_map/ppermute | solution.py:13
  5.4 9.0 %collective-permute-start = (bf16[2,2,256,512]{3,2,1,0:T(8,128)(2,1)}, bf16[2,2,256,512]{3,2,1,0:T(8,128)(2,1)}, u32[]{:S(2)}, u32[]{:S(2)}) collective-permute-start(bf16[2,2,256,512]{3,2,1,0:T(8,128)(2,1)} %bitcast.102), channel_id=1, source_target_pairs={{0,15},{2,1},{4,3},{6,5},{8,7},{10,9},{12,11},{14,13},{16,31},{18,... | collective-permute-start | bytes 3145736 | tf_op jit(solution)/shard_map/ppermute | solution.py:13
  14.4 1.3 %collective-permute-start.2 = (bf16[2,2,256,512]{3,2,1,0:T(8,128)(2,1)}, bf16[2,2,256,512]{3,2,1,0:T(8,128)(2,1)}, u32[]{:S(2)}, u32[]{:S(2)}) collective-permute-start(bf16[2,2,256,512]{3,2,1,0:T(8,128)(2,1)} %bitcast.103), channel_id=1, source_target_pairs={{1,0},{3,2},{5,4},{7,6},{9,8},{11,10},{13,12},{15,14},{17,16},{19,... | collective-permute-start | bytes 3145736 | tf_op jit(solution)/shard_map/ppermute | solution.py:13
  15.7 1.5 %bitcast_convert_fusion = f32[2,2,256,512]{3,2,1,0:T(8,128)S(1)} fusion(bf16[1,2,2,256,512]{4,3,2,1,0:T(8,128)(2,1)} %block_ref.1), kind=kLoop, calls=%fused_computation.54 | loop fusion | flops 524288 | bytes 3145728 | tf_op jit(solution)/shard_map/convert_element_type | solution.py:62
  17.2 0.0 copy-done.2
  17.2 1.4 %reshape_squeeze.3 = bf16[4096,128]{1,0:T(8,128)(2,1)} reshape(bf16[1,2,2,256,512]{4,3,2,1,0:T(8,128)(2,1)S(1)} %copy-done.2) | data formatting | bytes 2097152 | tf_op jit(solution)/shard_map/reshape;squeeze | solution.py:55
  18.6 0.3 add_reduce_fusion.1
  18.9 0.0 copy-done
  18.9 0.9 %copy-done.5 = bf16[4096,128]{1,0:T(8,128)(2,1)S(1)} copy-done((bf16[4096,128]{1,0:T(8,128)(2,1)S(1)}, bf16[4096,128]{1,0:T(8,128)(2,1)}, u32[]{:S(2)}) %copy-start.5) | copy-done | bytes 1048600
  19.9 0.0 copy-start.8
  19.9 1.7 %fusion.24 = f32[4096,128]{1,0:T(8,128)} fusion(bf16[4096,128]{1,0:T(8,128)(2,1)S(1)} %copy-done.5, bf16[128,128]{1,0:T(8,128)(2,1)S(1)} %copy-done), kind=kOutput, calls=%fused_computation.56 | convolution fusion | flops 134217728 | bytes 3178496 | tf_op jit(solution)/shard_map/dot_general | solution.py:56
  21.6 0.0 copy-done.8
  21.6 0.7 fusion.22
  27.6 0.0 copy-start.9
  27.6 2.8 %reshape.205 = f32[2,2,256,512]{3,2,1,0:T(8,128)} reshape(f32[4096,128]{1,0:T(8,128)} %fusion.24) | data formatting | bytes 4194304 | tf_op jit(solution)/shard_map/reshape | solution.py:56
  31.0 0.0 copy-done.9
  33.6 0.0 copy-start.4
  33.6 0.2 slice_bitcast_fusion.3
  33.8 0.0 collective-permute-done.5
  33.8 1.6 %collective-permute-start.6 = (bf16[2,2,256,512]{3,2,1,0:T(8,128)(2,1)}, bf16[2,2,256,512]{3,2,1,0:T(8,128)(2,1)S(1)}, u32[]{:S(2)}, u32[]{:S(2)}) collective-permute-start(bf16[2,2,256,512]{3,2,1,0:T(8,128)(2,1)} %collective-permute-done.5), channel_id=1, source_target_pairs={{1,2},{3,4},{5,6},{7,8},{9,10},{11,12},{13,14},{15,0},{17,18},{19,... | collective-permute-start | bytes 3145736 | tf_op jit(solution)/shard_map/ppermute | solution.py:13
  35.4 0.0 collective-permute-done
  35.4 1.3 %collective-permute-start.1 = (bf16[2,2,256,512]{3,2,1,0:T(8,128)(2,1)}, bf16[2,2,256,512]{3,2,1,0:T(8,128)(2,1)S(1)}, u32[]{:S(2)}, u32[]{:S(2)}) collective-permute-start(bf16[2,2,256,512]{3,2,1,0:T(8,128)(2,1)} %collective-permute-done), channel_id=1, source_target_pairs={{1,0},{3,2},{5,4},{7,6},{9,8},{11,10},{13,12},{15,14},{17,16},{19,... | collective-permute-start | bytes 3145736 | tf_op jit(solution)/shard_map/ppermute | solution.py:13
  36.7 0.0 collective-permute-done.2
  36.7 7.2 %collective-permute-start.3 = (bf16[2,2,256,512]{3,2,1,0:T(8,128)(2,1)}, bf16[2,2,256,512]{3,2,1,0:T(8,128)(2,1)S(1)}, u32[]{:S(2)}, u32[]{:S(2)}) collective-permute-start(bf16[2,2,256,512]{3,2,1,0:T(8,128)(2,1)} %collective-permute-done.2), channel_id=1, source_target_pairs={{0,15},{2,1},{4,3},{6,5},{8,7},{10,9},{12,11},{14,13},{16,31},{18,... | collective-permute-start | bytes 3145736 | tf_op jit(solution)/shard_map/ppermute | solution.py:13
  43.9 1.3 %broadcast_select_fusion.2 = bf16[2,2,256,512]{3,2,1,0:T(8,128)(2,1)S(1)} fusion(bf16[2,2,256,512]{3,2,1,0:T(8,128)(2,1)} %collective-permute-done.2, bf16[2,2,256,512]{3,2,1,0:T(8,128)(2,1)} %collective-permute-done, pred[]{:T(512)S(6)} %eq.18), kind=kLoop, calls=%fused_computation.36 | loop fusion | flops 524288 | bytes 3145729 | tf_op jit(solution)/shard_map/jit(_where)/select_n | solution.py:31
  45.2 0.0 copy-done.4
  45.2 1.3 %convolution_bitcast_fusion.2 = f32[2,2,512,512]{3,2,0,1:T(8,128)S(1)} fusion(bf16[2,512,512,1]{2,1,0,3:T(8,128)(2,1)S(1)} %bitcast.106, bf16[4,2,512,512]{3,2,1,0:T(8,128)(2,1)S(1)} %copy-done.4, s32[]{:T(128)S(6)} %select_n.59), kind=kOutput, calls=%fused_computation.2 | convolution fusion | flops 1073741824 | bytes 6291460 | tf_op jit(solution)/shard_map/cri,kio->ckro/dot_general | solution.py:69
  46.5 0.0 collective-permute-done.4
  46.5 1.5 %collective-permute-start.7 = (bf16[2,2,256,512]{3,2,1,0:T(8,128)(2,1)}, bf16[2,2,256,512]{3,2,1,0:T(8,128)(2,1)S(1)}, u32[]{:S(2)}, u32[]{:S(2)}) collective-permute-start(bf16[2,2,256,512]{3,2,1,0:T(8,128)(2,1)} %collective-permute-done.4), channel_id=1, source_target_pairs={{0,1},{2,3},{4,5},{6,7},{8,9},{10,11},{12,13},{14,15},{16,17},{18,... | collective-permute-start | bytes 3145736 | tf_op jit(solution)/shard_map/ppermute | solution.py:13
  48.0 0.5 slice_subtract_fusion.2
  48.5 1.3 %broadcast_select_fusion.1 = bf16[2,2,256,512]{3,2,1,0:T(8,128)(2,1)S(1)} fusion(bf16[2,2,256,512]{3,2,1,0:T(8,128)(2,1)} %collective-permute-done.4, bf16[2,2,256,512]{3,2,1,0:T(8,128)(2,1)} %collective-permute-done.5, pred[]{:T(512)S(6)} %eq.18), kind=kLoop, calls=%fused_computation.35 | loop fusion | flops 524288 | bytes 3145729 | tf_op jit(solution)/shard_map/jit(_where)/select_n | solution.py:30
  49.9 1.3 %convolution_bitcast_fusion.1 = f32[2,2,512,512]{3,2,0,1:T(8,128)S(1)} fusion(bf16[2,512,512,1]{2,1,0,3:T(8,128)(2,1)S(1)} %bitcast.107, bf16[4,2,512,512]{3,2,1,0:T(8,128)(2,1)S(1)} %copy-done.4, s32[]{:T(128)S(6)} %select_n.62), kind=kOutput, calls=%fused_computation.1 | convolution fusion | flops 1073741824 | bytes 6291460 | tf_op jit(solution)/shard_map/cri,kio->ckro/dot_general | solution.py:69
  51.1 0.5 slice_subtract_fusion.1
  51.6 1.6 %collective-permute-done.6 = bf16[2,2,256,512]{3,2,1,0:T(8,128)(2,1)S(1)} collective-permute-done((bf16[2,2,256,512]{3,2,1,0:T(8,128)(2,1)}, bf16[2,2,256,512]{3,2,1,0:T(8,128)(2,1)S(1)}, u32[]{:S(2)}, u32[]{:S(2)}) %collective-permute-start.6) | collective-permute-done | bytes 1048608 | tf_op jit(solution)/shard_map/ppermute | solution.py:13
  53.2 0.0 collective-permute-done.7
  53.2 0.0 collective-permute-done.1
  53.2 3.2 %collective-permute-done.3 = bf16[2,2,256,512]{3,2,1,0:T(8,128)(2,1)S(1)} collective-permute-done((bf16[2,2,256,512]{3,2,1,0:T(8,128)(2,1)}, bf16[2,2,256,512]{3,2,1,0:T(8,128)(2,1)S(1)}, u32[]{:S(2)}, u32[]{:S(2)}) %collective-permute-start.3) | collective-permute-done | bytes 1048608 | tf_op jit(solution)/shard_map/ppermute | solution.py:13
  56.4 0.2 broadcast_select_fusion
  56.6 1.3 %convolution_bitcast_fusion.3 = f32[2,2,512,512]{3,2,0,1:T(8,128)S(1)} fusion(bf16[2,512,512,1]{2,1,0,3:T(8,128)(2,1)S(1)} %bitcast.105, bf16[4,2,512,512]{3,2,1,0:T(8,128)(2,1)S(1)} %copy-done.4, s32[]{:T(128)S(6)} %select_n.54), kind=kOutput, calls=%fused_computation.3 | convolution fusion | flops 1073741824 | bytes 6291460 | tf_op jit(solution)/shard_map/cri,kio->ckro/dot_general | solution.py:69
  57.9 0.5 slice_subtract_fusion.3
  58.4 1.3 %convolution_bitcast_fusion = f32[2,2,512,512]{3,2,0,1:T(8,128)S(1)} fusion(bf16[2,512,512,1]{2,1,0,3:T(8,128)(2,1)S(1)} %bitcast.104, bf16[4,2,512,512]{3,2,1,0:T(8,128)(2,1)S(1)} %copy-done.4, s32[]{:T(128)S(6)} %select_n.65), kind=kOutput, calls=%fused_computation | convolution fusion | flops 1073741824 | bytes 6291460 | tf_op jit(solution)/shard_map/cri,kio->ckro/dot_general | solution.py:69
  59.6 0.0 copy-start.3
  59.6 0.0 copy-start.6
  59.7 0.5 slice_subtract_fusion
  60.2 0.3 broadcast_in_dim.34
  60.5 0.7 copy-done.3
  61.2 0.0 copy-done.6
  61.2 0.9 %fusion.2.image_ref = f32[2,2,256,512]{3,2,1,0:T(8,128)S(1)} fusion(f32[1,2,256,512]{3,2,1,0:T(8,128)S(1)} %bitcast.113, f32[1,2,256,512]{3,2,1,0:T(8,128)S(1)} %bitcast.112, f32[1,2,256,512]{3,2,1,0:T(8,128)S(1)} %bitcast.109, f32[1,2,256,512]{3,2,1,0:T(8,128)S(1)} %bitcast.108, f32[1,2,256,512]{3,2,1,0:T(8,128)S(1)} %bitcast.111, ...), kind=kOutput, calls=%fused_computation.7 | convolution fusion | flops 274989056 | bytes 13893636 | tf_op jit(solution)/shard_map/ab,cvbf->cvaf/dot_general | solution.py:59
  62.1 0.0 copy-start.1
  62.2 0.2 slice_bitcast_fusion.2
  62.3 1.4 %add_reduce_fusion = (f32[2,2]{1,0:T(2,128)S(1)}, f32[2,2]{1,0:T(2,128)S(1)}) fusion(f32[2,256,512]{2,1,0:T(8,128)S(1)} %get-tuple-element.19, f32[2,256,512]{2,1,0:T(8,128)S(1)} %get-tuple-element.17, f32[2,256,512]{2,1,0:T(8,128)S(1)} %get-tuple-element.18, f32[2,256,512]{2,1,0:T(8,128)S(1)} %get-tuple-element.16), kind=kLoop, calls=%fused_computation.11 | loop fusion | flops 4194296 | bytes 4194336 | tf_op jit(solution)/shard_map/reduce_sum | solution.py:78
  63.7 0.1 reshape.220
  63.8 0.1 reshape.219
  63.9 0.1 maximum_maximum_fusion
  64.0 0.6 broadcast.24
  64.6 10.1 %all-to-all-start = ((f32[16,1,10]{2,1,0:T(1,128)}), f32[16,1,10]{2,1,0:T(1,128)S(1)}, u32[]{:S(2)}, u32[]{:S(2)}) async-start(f32[16,1,10]{2,1,0:T(1,128)} %bitcast.43), calls=%async_computation | async-start | bytes 16384 | tf_op jit(solution)/shard_map/all_to_all | solution.py:42
  74.7 0.0 copy-done.1
  74.7 1.1 %convert_bitcast_fusion = bf16[1,2,2,256,512]{4,3,2,1,0:T(8,128)(2,1)} fusion(f32[2,2,256,512]{3,2,1,0:T(8,128)S(1)} %fusion.2.image_ref), kind=kLoop, calls=%fused_computation.29 | loop fusion | flops 524288 | bytes 3145728 | tf_op jit(solution)/shard_map/broadcast_in_dim | solution.py:83
  75.8 5.2 %all-to-all-done = f32[16,1,10]{2,1,0:T(1,128)S(1)} async-done(((f32[16,1,10]{2,1,0:T(1,128)}), f32[16,1,10]{2,1,0:T(1,128)S(1)}, u32[]{:S(2)}, u32[]{:S(2)}) %all-to-all-start) | async-done | bytes 672 | tf_op jit(solution)/shard_map/all_to_all | solution.py:42
  81.1 0.6 copy-done.7
  81.7 3.0 %shard_map.86 = bf16[1,2,2,256,512]{4,3,2,1,0:T(8,128)(2,1)} custom-call(f32[16,10]{1,0:T(8,128)} %bitcast.118, f32[2,2,256,512]{3,2,1,0:T(8,128)} %copy-done.1, bf16[1,2,2,256,512]{4,3,2,1,0:T(8,128)(2,1)} %block_ref.1), custom_call_target="tpu_custom_call" | custom-call | tf_op jit(solution)/shard_map/pallas_call | solution.py:114
  (4 shorter events, 0.0 us)
Async XLA Ops:
  0.6 18.3 %copy-start = (bf16[128,128]{1,0:T(8,128)(2,1)S(1)}, bf16[128,128]{1,0:T(8,128)(2,1)}, u32[]{:S(2)}) copy-start(bf16[128,128]{1,0:T(8,128)(2,1)} %param.9) | copy-start | bytes 98308
  0.6 16.5 %copy-start.2 = (bf16[1,2,2,256,512]{4,3,2,1,0:T(8,128)(2,1)S(1)}, bf16[1,2,2,256,512]{4,3,2,1,0:T(8,128)(2,1)}, u32[]{:S(2)}) copy-start(bf16[1,2,2,256,512]{4,3,2,1,0:T(8,128)(2,1)} %block_ref.1) | copy-start | bytes 3145732
  0.7 33.1 %collective-permute-start.5 = (bf16[2,2,256,512]{3,2,1,0:T(8,128)(2,1)}, bf16[2,2,256,512]{3,2,1,0:T(8,128)(2,1)}, u32[]{:S(2)}, u32[]{:S(2)}) collective-permute-start(bf16[2,2,256,512]{3,2,1,0:T(8,128)(2,1)} %bitcast.100), channel_id=1, source_target_pairs={{0,1},{2,3},{4,5},{6,7},{8,9},{10,11},{12,13},{14,15},{16,17},{18,... | collective-permute-start | bytes 3145736 | tf_op jit(solution)/shard_map/ppermute | solution.py:13
  4.1 42.4 %collective-permute-start.4 = (bf16[2,2,256,512]{3,2,1,0:T(8,128)(2,1)}, bf16[2,2,256,512]{3,2,1,0:T(8,128)(2,1)}, u32[]{:S(2)}, u32[]{:S(2)}) collective-permute-start(bf16[2,2,256,512]{3,2,1,0:T(8,128)(2,1)} %bitcast.101), channel_id=1, source_target_pairs={{1,2},{3,4},{5,6},{7,8},{9,10},{11,12},{13,14},{15,0},{17,18},{19,... | collective-permute-start | bytes 3145736 | tf_op jit(solution)/shard_map/ppermute | solution.py:13
  5.4 30.0 %collective-permute-start = (bf16[2,2,256,512]{3,2,1,0:T(8,128)(2,1)}, bf16[2,2,256,512]{3,2,1,0:T(8,128)(2,1)}, u32[]{:S(2)}, u32[]{:S(2)}) collective-permute-start(bf16[2,2,256,512]{3,2,1,0:T(8,128)(2,1)} %bitcast.102), channel_id=1, source_target_pairs={{0,15},{2,1},{4,3},{6,5},{8,7},{10,9},{12,11},{14,13},{16,31},{18,... | collective-permute-start | bytes 3145736 | tf_op jit(solution)/shard_map/ppermute | solution.py:13
  14.4 22.3 %collective-permute-start.2 = (bf16[2,2,256,512]{3,2,1,0:T(8,128)(2,1)}, bf16[2,2,256,512]{3,2,1,0:T(8,128)(2,1)}, u32[]{:S(2)}, u32[]{:S(2)}) collective-permute-start(bf16[2,2,256,512]{3,2,1,0:T(8,128)(2,1)} %bitcast.103), channel_id=1, source_target_pairs={{1,0},{3,2},{5,4},{7,6},{9,8},{11,10},{13,12},{15,14},{17,16},{19,... | collective-permute-start | bytes 3145736 | tf_op jit(solution)/shard_map/ppermute | solution.py:13
  18.6 1.2 %copy-start.5 = (bf16[4096,128]{1,0:T(8,128)(2,1)S(1)}, bf16[4096,128]{1,0:T(8,128)(2,1)}, u32[]{:S(2)}) copy-start(bf16[4096,128]{1,0:T(8,128)(2,1)} %reshape_squeeze.3) | copy-start | bytes 3145732
  19.9 1.7 %copy-start.8 = (s32[4]{0:T(128)S(1)}, s32[4]{0:T(128)}, u32[]{:S(2)}) copy-start(s32[4]{0:T(128)} %param.12) | copy-start | bytes 52
  27.6 3.4 %copy-start.9 = (s32[2,2]{1,0:T(2,128)S(1)}, s32[2,2]{1,0:T(2,128)}, u32[]{:S(2)}) copy-start(s32[2,2]{1,0:T(2,128)} %param.11) | copy-start | bytes 52
  33.6 11.6 %copy-start.4 = (bf16[4,2,512,512]{3,2,1,0:T(8,128)(2,1)S(1)}, bf16[4,2,512,512]{3,2,1,0:T(8,128)(2,1)}, u32[]{:S(2)}) copy-start(bf16[4,2,512,512]{3,2,1,0:T(8,128)(2,1)} %param.8) | copy-start | bytes 12582916
  33.8 19.4 %collective-permute-start.6 = (bf16[2,2,256,512]{3,2,1,0:T(8,128)(2,1)}, bf16[2,2,256,512]{3,2,1,0:T(8,128)(2,1)S(1)}, u32[]{:S(2)}, u32[]{:S(2)}) collective-permute-start(bf16[2,2,256,512]{3,2,1,0:T(8,128)(2,1)} %collective-permute-done.5), channel_id=1, source_target_pairs={{1,2},{3,4},{5,6},{7,8},{9,10},{11,12},{13,14},{15,0},{17,18},{19,... | collective-permute-start | bytes 3145736 | tf_op jit(solution)/shard_map/ppermute | solution.py:13
  35.4 17.8 %collective-permute-start.1 = (bf16[2,2,256,512]{3,2,1,0:T(8,128)(2,1)}, bf16[2,2,256,512]{3,2,1,0:T(8,128)(2,1)S(1)}, u32[]{:S(2)}, u32[]{:S(2)}) collective-permute-start(bf16[2,2,256,512]{3,2,1,0:T(8,128)(2,1)} %collective-permute-done), channel_id=1, source_target_pairs={{1,0},{3,2},{5,4},{7,6},{9,8},{11,10},{13,12},{15,14},{17,16},{19,... | collective-permute-start | bytes 3145736 | tf_op jit(solution)/shard_map/ppermute | solution.py:13
  36.7 19.7 %collective-permute-start.3 = (bf16[2,2,256,512]{3,2,1,0:T(8,128)(2,1)}, bf16[2,2,256,512]{3,2,1,0:T(8,128)(2,1)S(1)}, u32[]{:S(2)}, u32[]{:S(2)}) collective-permute-start(bf16[2,2,256,512]{3,2,1,0:T(8,128)(2,1)} %collective-permute-done.2), channel_id=1, source_target_pairs={{0,15},{2,1},{4,3},{6,5},{8,7},{10,9},{12,11},{14,13},{16,31},{18,... | collective-permute-start | bytes 3145736 | tf_op jit(solution)/shard_map/ppermute | solution.py:13
  46.5 6.7 %collective-permute-start.7 = (bf16[2,2,256,512]{3,2,1,0:T(8,128)(2,1)}, bf16[2,2,256,512]{3,2,1,0:T(8,128)(2,1)S(1)}, u32[]{:S(2)}, u32[]{:S(2)}) collective-permute-start(bf16[2,2,256,512]{3,2,1,0:T(8,128)(2,1)} %collective-permute-done.4), channel_id=1, source_target_pairs={{0,1},{2,3},{4,5},{6,7},{8,9},{10,11},{12,13},{14,15},{16,17},{18,... | collective-permute-start | bytes 3145736 | tf_op jit(solution)/shard_map/ppermute | solution.py:13
  59.6 1.6 %copy-start.3 = (f32[2,2,256,512]{3,2,1,0:T(8,128)S(1)}, f32[2,2,256,512]{3,2,1,0:T(8,128)}, u32[]{:S(2)}) copy-start(f32[2,2,256,512]{3,2,1,0:T(8,128)} %reshape.205) | copy-start | bytes 6291460
  59.6 1.6 %copy-start.6 = (bf16[256,256]{1,0:T(8,128)(2,1)S(1)}, bf16[256,256]{1,0:T(8,128)(2,1)}, u32[]{:S(2)}) copy-start(bf16[256,256]{1,0:T(8,128)(2,1)} %param.10) | copy-start | bytes 393220
  62.1 12.6 %copy-start.1 = (f32[2,2,256,512]{3,2,1,0:T(8,128)}, f32[2,2,256,512]{3,2,1,0:T(8,128)S(1)}, u32[]{:S(2)}) copy-start(f32[2,2,256,512]{3,2,1,0:T(8,128)S(1)} %fusion.2.image_ref) | copy-start | bytes 6291460
  64.6 16.5 %all-to-all-start = ((f32[16,1,10]{2,1,0:T(1,128)}), f32[16,1,10]{2,1,0:T(1,128)S(1)}, u32[]{:S(2)}, u32[]{:S(2)}) async-start(f32[16,1,10]{2,1,0:T(1,128)} %bitcast.43), calls=%async_computation | async-start | bytes 16384 | tf_op jit(solution)/shard_map/all_to_all | solution.py:42
  81.1 0.6 copy-start.7

commit v16 on v13

--- a/solution.py
+++ b/solution.py
@@ -31,6 +31,7 @@
     tile = width_x // tile_mask.shape[0]
     below_one = passed_along(block, "harm", 1)
     above_one = passed_along(block, "harm", -1)
+    below_one, above_one = lax.optimization_barrier((below_one, above_one))
     below_two = passed_along(below_one, "harm", 1)
     above_two = passed_along(above_one, "harm", -1)
     rows = block.reshape(-1, ny)

time: 77.9 us -> 88.1 us (1.13)
  starting transfers between devices: 28.1 us -> 44.2 us
  waiting for transfers between devices: 16.1 us -> 10.1 us
    ppermute x4, starting transfers between devices: 12.3 us -> 26 us  [passed_along(): return lax.ppermute(value, axis, pairs)]
    ppermute x4, waiting for transfers between devices: 10.9 us -> 4.89 us  [passed_along(): return lax.ppermute(value, axis, pairs)]
    all_to_all x1, starting transfers between devices: 15.7 us -> 18.2 us  [exchanged(): return lax.all_to_all(spread, axes, 0, 0, tiled=True)]
  transfers between devices with their start and end apart: 5 -> 5, of which waited for: 3 -> 2; matrix products, arithmetic and copies ran while one was open for 19% -> 17% of each run, Pallas kernels for 0% -> 0%
where the time goes in v16:
time: 88.1 us; the launch traced here: 87.7 us
  starting transfers between devices  44.2 us (50%)
  waiting for transfers between devices  10.1 us (11%)
  between operations  9.17 us (10%)
  matrix products  8.84 us (10%)
  other arithmetic  6.38 us (7%)
  local copies, waits for them, and re-layouts  6.03 us (7%)
  Pallas kernels  3.02 us (3%)
    ppermute x4, starting transfers between devices, passed_along(): return lax.ppermute(value, axis, pairs)  26 us
    all_to_all x1, starting transfers between devices, exchanged(): return lax.all_to_all(spread, axes, 0, 0, tiled=True)  18.2 us
    dot_general x4, matrix products, body(): jnp.einsum('cri,kio->ckro', other, matrix, preferred_element_type=jnp.flo...  7.53 us
    all_to_all x1, waiting for transfers between devices, exchanged(): return lax.all_to_all(spread, axes, 0, 0, tiled=True)  5.22 us
    ppermute x4, waiting for transfers between devices, passed_along(): return lax.ppermute(value, axis, pairs)  4.89 us
    pallas_call x1, Pallas kernels, removed_projections(): pl.pallas_call(project_kernel, grid=(width_x // rows,), in_specs=[pl.Bloc...  3.02 us
    sub x4, other arithmetic, body(): real_part = prod[0, 0] - prod[1, 1]  1.92 us
  transfers between devices with their start and end apart: 5, of which 2 were waited for; matrix products, arithmetic and copies ran while one was open for 17% of the time, Pallas kernels for 0%

profile of v16, /device:TPU:0, one launch (start us, length us, event | category | flops | bytes accessed | tf_op | source)
XLA Modules:
  0.0 87.7 jit_solution(15078408303855149696)
XLA Ops:
  0.6 0.0 copy-start
  0.6 0.5 collective-permute-start
  1.1 5.1 %collective-permute-start.1 = (bf16[2,2,256,512]{3,2,1,0:T(8,128)(2,1)}, bf16[2,2,256,512]{3,2,1,0:T(8,128)(2,1)}, u32[]{:S(2)}, u32[]{:S(2)}) collective-permute-start(bf16[2,2,256,512]{3,2,1,0:T(8,128)(2,1)} %bitcast.101), channel_id=1, source_target_pairs={{0,15},{1,0},{2,1},{3,2},{4,3},{5,4},{6,5},{7,6},{8,7},{9,8},{10,9... | collective-permute-start | bytes 3145736 | tf_op jit(solution)/shard_map/ppermute | solution.py:12
  6.2 1.4 %fusion.22 = (s32[]{:T(128)}, s32[]{:T(128)}, s32[]{:T(128)}, s32[]{:T(128)}) fusion(s32[4]{0:T(128)} %param.12), kind=kLoop, calls=%fused_computation.48 | loop fusion | flops 44 | bytes 32 | tf_op jit(solution)/shard_map/reduce_sum | solution.py:48
  12.7 1.7 %reshape_squeeze.3 = bf16[4096,128]{1,0:T(8,128)(2,1)S(1)} reshape(bf16[1,2,2,256,512]{4,3,2,1,0:T(8,128)(2,1)} %block_ref.1) | data formatting | bytes 2097152 | tf_op jit(solution)/shard_map/reshape;squeeze | solution.py:37
  14.4 0.0 copy-done
  14.4 0.4 fusion.24
  14.9 0.0 copy-start.7
  14.9 0.0 copy-start.2
  14.9 1.5 %reshape.205 = f32[2,2,256,512]{3,2,1,0:T(8,128)} reshape(f32[4096,128]{1,0:T(8,128)S(1)} %fusion.24) | data formatting | bytes 4194304 | tf_op jit(solution)/shard_map/reshape | solution.py:38
  16.4 0.0 copy-done.7
  19.6 0.0 copy-done.2
  19.6 0.3 bitcast_convert_fusion
  19.9 0.3 add_reduce_fusion.1
  20.2 0.0 copy-start.4
  20.2 0.2 slice_bitcast_fusion.3
  20.4 0.0 collective-permute-done
  20.4 0.0 collective-permute-done.1
  20.4 20.4 %collective-permute-start.3 = (bf16[2,2,256,512]{3,2,1,0:T(8,128)(2,1)}, bf16[2,2,256,512]{3,2,1,0:T(8,128)(2,1)S(1)}, u32[]{:S(2)}, u32[]{:S(2)}) collective-permute-start(bf16[2,2,256,512]{3,2,1,0:T(8,128)(2,1)} %collective-permute-done), channel_id=1, source_target_pairs={{0,1},{1,2},{2,3},{3,4},{4,5},{5,6},{6,7},{7,8},{8,9},{9,10},{10,1... | collective-permute-start | bytes 3145736 | tf_op jit(solution)/shard_map/ppermute | solution.py:12
  40.8 0.0 collective-permute-start.2
  40.8 0.0 copy-done.4
  40.8 2.5 %convolution_bitcast_fusion.2 = f32[2,2,512,512]{3,2,0,1:T(8,128)S(1)} fusion(bf16[2,512,512,1]{2,1,0,3:T(8,128)(2,1)} %bitcast.18, bf16[4,2,512,512]{3,2,1,0:T(8,128)(2,1)S(1)} %copy-done.4, s32[]{:T(128)S(6)} %select_n.29), kind=kOutput, calls=%fused_computation.2 | convolution fusion | flops 1073741824 | bytes 6291460 | tf_op jit(solution)/shard_map/cri,kio->ckro/dot_general | solution.py:51
  43.3 2.5 %convolution_bitcast_fusion.1 = f32[2,2,512,512]{3,2,0,1:T(8,128)S(1)} fusion(bf16[2,512,512,1]{2,1,0,3:T(8,128)(2,1)} %bitcast.26, bf16[4,2,512,512]{3,2,1,0:T(8,128)(2,1)S(1)} %copy-done.4, s32[]{:T(128)S(6)} %select_n.31), kind=kOutput, calls=%fused_computation.1 | convolution fusion | flops 1073741824 | bytes 6291460 | tf_op jit(solution)/shard_map/cri,kio->ckro/dot_general | solution.py:51
  45.8 0.5 slice_subtract_fusion.2
  46.3 0.5 slice_subtract_fusion.1
  46.8 0.0 collective-permute-done.3
  46.8 1.3 %convolution_bitcast_fusion = f32[2,2,512,512]{3,2,0,1:T(8,128)S(1)} fusion(bf16[2,512,512,1]{2,1,0,3:T(8,128)(2,1)S(1)} %bitcast.111, bf16[4,2,512,512]{3,2,1,0:T(8,128)(2,1)S(1)} %copy-done.4, s32[]{:T(128)S(6)} %select_n.33), kind=kOutput, calls=%fused_computation | convolution fusion | flops 1073741824 | bytes 6291460 | tf_op jit(solution)/shard_map/cri,kio->ckro/dot_general | solution.py:51
  48.1 0.5 slice_subtract_fusion
  48.5 4.9 %collective-permute-done.2 = bf16[2,2,256,512]{3,2,1,0:T(8,128)(2,1)S(1)} collective-permute-done((bf16[2,2,256,512]{3,2,1,0:T(8,128)(2,1)}, bf16[2,2,256,512]{3,2,1,0:T(8,128)(2,1)S(1)}, u32[]{:S(2)}, u32[]{:S(2)}) %collective-permute-start.2) | collective-permute-done | bytes 1048608 | tf_op jit(solution)/shard_map/ppermute | solution.py:12
  53.4 1.3 %convolution_bitcast_fusion.3 = f32[2,2,512,512]{3,2,0,1:T(8,128)S(1)} fusion(bf16[2,512,512,1]{2,1,0,3:T(8,128)(2,1)S(1)} %bitcast.110, bf16[4,2,512,512]{3,2,1,0:T(8,128)(2,1)S(1)} %copy-done.4, s32[]{:T(128)S(6)} %select_n.27), kind=kOutput, calls=%fused_computation.3 | convolution fusion | flops 1073741824 | bytes 6291460 | tf_op jit(solution)/shard_map/cri,kio->ckro/dot_general | solution.py:51
  54.7 0.0 copy-start.3
  54.7 0.0 copy-start.5
  54.7 0.5 slice_subtract_fusion.3
  55.2 0.3 broadcast_in_dim.34
  55.6 0.7 copy-done.3
  56.3 0.0 copy-done.5
  56.3 0.9 %fusion.2.image_ref = f32[2,2,256,512]{3,2,1,0:T(8,128)S(1)} fusion(f32[1,2,256,512]{3,2,1,0:T(8,128)S(1)} %bitcast.109, f32[1,2,256,512]{3,2,1,0:T(8,128)S(1)} %bitcast.108, f32[1,2,256,512]{3,2,1,0:T(8,128)S(1)} %bitcast.103, f32[1,2,256,512]{3,2,1,0:T(8,128)S(1)} %bitcast.102, f32[1,2,256,512]{3,2,1,0:T(8,128)S(1)} %bitcast.105, ...), kind=kOutput, calls=%fused_computation.7 | convolution fusion | flops 274989056 | bytes 13893636 | tf_op jit(solution)/shard_map/ab,cvbf->cvaf/dot_general | solution.py:41
  57.2 0.0 copy-start.1
  57.2 0.2 slice_bitcast_fusion.2
  57.4 1.3 %add_reduce_fusion = (f32[2,2]{1,0:T(2,128)S(1)}, f32[2,2]{1,0:T(2,128)S(1)}) fusion(f32[2,256,512]{2,1,0:T(8,128)S(1)} %get-tuple-element.23, f32[2,256,512]{2,1,0:T(8,128)S(1)} %get-tuple-element.21, f32[2,256,512]{2,1,0:T(8,128)S(1)} %get-tuple-element.22, f32[2,256,512]{2,1,0:T(8,128)S(1)} %get-tuple-element.20), kind=kLoop, calls=%fused_computation.11 | loop fusion | flops 4194296 | bytes 4194336 | tf_op jit(solution)/shard_map/reduce_sum | solution.py:60
  58.7 0.1 reshape.219
  58.8 0.1 reshape.220
  58.9 0.1 maximum_maximum_fusion
  58.9 0.6 broadcast.23
  59.6 18.2 %all-to-all-start = ((f32[16,1,10]{2,1,0:T(1,128)}), f32[16,1,10]{2,1,0:T(1,128)S(1)}, u32[]{:S(2)}, u32[]{:S(2)}) async-start(f32[16,1,10]{2,1,0:T(1,128)} %bitcast.43), calls=%async_computation | async-start | bytes 16384 | tf_op jit(solution)/shard_map/all_to_all | solution.py:20
  77.8 0.0 copy-done.1
  77.8 1.1 %convert_bitcast_fusion = bf16[1,2,2,256,512]{4,3,2,1,0:T(8,128)(2,1)} fusion(f32[2,2,256,512]{3,2,1,0:T(8,128)S(1)} %fusion.2.image_ref), kind=kLoop, calls=%fused_computation.29 | loop fusion | flops 524288 | bytes 3145728 | tf_op jit(solution)/shard_map/broadcast_in_dim | solution.py:65
  78.9 5.2 %all-to-all-done = f32[16,1,10]{2,1,0:T(1,128)S(1)} async-done(((f32[16,1,10]{2,1,0:T(1,128)}), f32[16,1,10]{2,1,0:T(1,128)S(1)}, u32[]{:S(2)}, u32[]{:S(2)}) %all-to-all-start) | async-done | bytes 672 | tf_op jit(solution)/shard_map/all_to_all | solution.py:20
  84.1 0.0 copy-start.6
  84.1 0.6 copy-done.6
  84.7 3.0 %shard_map.86 = bf16[1,2,2,256,512]{4,3,2,1,0:T(8,128)(2,1)} custom-call(f32[16,10]{1,0:T(8,128)} %bitcast.114, f32[2,2,256,512]{3,2,1,0:T(8,128)} %copy-done.1, bf16[1,2,2,256,512]{4,3,2,1,0:T(8,128)(2,1)} %block_ref.1), custom_call_target="tpu_custom_call" | custom-call | tf_op jit(solution)/shard_map/pallas_call | solution.py:96
  (2 shorter events, 0.0 us)
Async XLA Ops:
  0.6 13.8 %copy-start = (bf16[128,128]{1,0:T(8,128)(2,1)S(1)}, bf16[128,128]{1,0:T(8,128)(2,1)}, u32[]{:S(2)}) copy-start(bf16[128,128]{1,0:T(8,128)(2,1)} %param.9) | copy-start | bytes 98308
  0.6 19.7 %collective-permute-start = (bf16[2,2,256,512]{3,2,1,0:T(8,128)(2,1)}, bf16[2,2,256,512]{3,2,1,0:T(8,128)(2,1)}, u32[]{:S(2)}, u32[]{:S(2)}) collective-permute-start(bf16[2,2,256,512]{3,2,1,0:T(8,128)(2,1)} %bitcast.100), channel_id=1, source_target_pairs={{0,1},{1,2},{2,3},{3,4},{4,5},{5,6},{6,7},{7,8},{8,9},{9,10},{10,1... | collective-permute-start | bytes 3145736 | tf_op jit(solution)/shard_map/ppermute | solution.py:12
  1.1 19.2 %collective-permute-start.1 = (bf16[2,2,256,512]{3,2,1,0:T(8,128)(2,1)}, bf16[2,2,256,512]{3,2,1,0:T(8,128)(2,1)}, u32[]{:S(2)}, u32[]{:S(2)}) collective-permute-start(bf16[2,2,256,512]{3,2,1,0:T(8,128)(2,1)} %bitcast.101), channel_id=1, source_target_pairs={{0,15},{1,0},{2,1},{3,2},{4,3},{5,4},{6,5},{7,6},{8,7},{9,8},{10,9... | collective-permute-start | bytes 3145736 | tf_op jit(solution)/shard_map/ppermute | solution.py:12
  14.9 1.5 %copy-start.7 = (s32[2,2]{1,0:T(2,128)S(1)}, s32[2,2]{1,0:T(2,128)}, u32[]{:S(2)}) copy-start(s32[2,2]{1,0:T(2,128)} %param.11) | copy-start | bytes 52
  14.9 4.7 %copy-start.2 = (bf16[1,2,2,256,512]{4,3,2,1,0:T(8,128)(2,1)S(1)}, bf16[1,2,2,256,512]{4,3,2,1,0:T(8,128)(2,1)}, u32[]{:S(2)}) copy-start(bf16[1,2,2,256,512]{4,3,2,1,0:T(8,128)(2,1)} %block_ref.1) | copy-start | bytes 3145732
  20.2 20.6 %copy-start.4 = (bf16[4,2,512,512]{3,2,1,0:T(8,128)(2,1)S(1)}, bf16[4,2,512,512]{3,2,1,0:T(8,128)(2,1)}, u32[]{:S(2)}) copy-start(bf16[4,2,512,512]{3,2,1,0:T(8,128)(2,1)} %param.8) | copy-start | bytes 12582916
  20.4 26.4 %collective-permute-start.3 = (bf16[2,2,256,512]{3,2,1,0:T(8,128)(2,1)}, bf16[2,2,256,512]{3,2,1,0:T(8,128)(2,1)S(1)}, u32[]{:S(2)}, u32[]{:S(2)}) collective-permute-start(bf16[2,2,256,512]{3,2,1,0:T(8,128)(2,1)} %collective-permute-done), channel_id=1, source_target_pairs={{0,1},{1,2},{2,3},{3,4},{4,5},{5,6},{6,7},{7,8},{8,9},{9,10},{10,1... | collective-permute-start | bytes 3145736 | tf_op jit(solution)/shard_map/ppermute | solution.py:12
  40.8 12.6 %collective-permute-start.2 = (bf16[2,2,256,512]{3,2,1,0:T(8,128)(2,1)}, bf16[2,2,256,512]{3,2,1,0:T(8,128)(2,1)S(1)}, u32[]{:S(2)}, u32[]{:S(2)}) collective-permute-start(bf16[2,2,256,512]{3,2,1,0:T(8,128)(2,1)} %collective-permute-done.1), channel_id=1, source_target_pairs={{0,15},{1,0},{2,1},{3,2},{4,3},{5,4},{6,5},{7,6},{8,7},{9,8},{10,9... | collective-permute-start | bytes 3145736 | tf_op jit(solution)/shard_map/ppermute | solution.py:12
  54.7 1.6 %copy-start.3 = (f32[2,2,256,512]{3,2,1,0:T(8,128)S(1)}, f32[2,2,256,512]{3,2,1,0:T(8,128)}, u32[]{:S(2)}) copy-start(f32[2,2,256,512]{3,2,1,0:T(8,128)} %reshape.205) | copy-start | bytes 6291460
  54.7 1.6 %copy-start.5 = (bf16[256,256]{1,0:T(8,128)(2,1)S(1)}, bf16[256,256]{1,0:T(8,128)(2,1)}, u32[]{:S(2)}) copy-start(bf16[256,256]{1,0:T(8,128)(2,1)} %param.10) | copy-start | bytes 393220
  57.2 20.6 %copy-start.1 = (f32[2,2,256,512]{3,2,1,0:T(8,128)}, f32[2,2,256,512]{3,2,1,0:T(8,128)S(1)}, u32[]{:S(2)}) copy-start(f32[2,2,256,512]{3,2,1,0:T(8,128)S(1)} %fusion.2.image_ref) | copy-start | bytes 6291460
  59.6 24.5 %all-to-all-start = ((f32[16,1,10]{2,1,0:T(1,128)}), f32[16,1,10]{2,1,0:T(1,128)S(1)}, u32[]{:S(2)}, u32[]{:S(2)}) async-start(f32[16,1,10]{2,1,0:T(1,128)} %bitcast.43), calls=%async_computation | async-start | bytes 16384 | tf_op jit(solution)/shard_map/all_to_all | solution.py:20
  84.1 0.6 copy-start.6

commit v17 on v13

--- a/solution.py
+++ b/solution.py
@@ -40,24 +40,31 @@
     along_x = jnp.einsum("ab,cvbf->cvaf", masked, block, preferred_element_type=jnp.float32)
     centered = (position - harmonics // 2).astype(jnp.float32) + detuning[0]
     lam = -(centered * centered) / (4.0 * harmonics)
-    image = along_y + along_x + lam * block.astype(jnp.float32)
+    qfull = block.astype(jnp.float32)
+    qr = qfull[0]
+    qi = qfull[1]
+    image = along_y + along_x + lam * qfull
+    num_re = jnp.sum(qr[:, None] * image[0][None, :] + qi[:, None] * image[1][None, :], axis=(2, 3))
+    num_im = jnp.sum(qr[:, None] * image[1][None, :] - qi[:, None] * image[0][None, :], axis=(2, 3))
+    flat = block.reshape(2, vecs * width_x, width_fy)
     sources = (above_two, above_one, below_one, below_two)
     counter = jnp.arange(4, dtype=jnp.int32)
     for place in range(4):
         slot = jnp.sum(jnp.where(slot_offsets == place, counter, 0))
         matrix = lax.dynamic_index_in_dim(coupling, slot, 0, keepdims=False)
-        other = sources[place].reshape(2, vecs * width_x, width_fy)
+        back = jnp.einsum("cro,kio->ckri", flat, matrix, preferred_element_type=jnp.float32)
+        pull_a = (back[0, 0] + back[1, 1]).reshape(vecs, width_x, width_fy)
+        pull_b = (back[1, 0] - back[0, 1]).reshape(vecs, width_x, width_fy)
+        source = sources[place]
+        s_re = source[0].astype(jnp.float32)
+        s_im = source[1].astype(jnp.float32)
+        num_re = num_re + jnp.sum(pull_a[:, None] * s_re[None, :] + pull_b[:, None] * s_im[None, :], axis=(2, 3))
+        num_im = num_im + jnp.sum(pull_a[:, None] * s_im[None, :] - pull_b[:, None] * s_re[None, :], axis=(2, 3))
+        other = source.reshape(2, vecs * width_x, width_fy)
         prod = jnp.einsum("cri,kio->ckro", other, matrix, preferred_element_type=jnp.float32)
         real_part = prod[0, 0] - prod[1, 1]
         imag_part = prod[0, 1] + prod[1, 0]
         image = image + jnp.stack([real_part, imag_part]).reshape(block.shape)
-    qfull = block.astype(jnp.float32)
-    qr = qfull[0]
-    qi = qfull[1]
-    wr = image[0]
-    wi = image[1]
-    num_re = jnp.sum(qr[:, None] * wr[None, :] + qi[:, None] * wi[None, :], axis=(2, 3))
-    num_im = jnp.sum(qr[:, None] * wi[None, :] - qi[:, None] * wr[None, :], axis=(2, 3))
     norms = jnp.sum(qr * qr + qi * qi, axis=(1, 2))
     gathered = exchanged(("harm",), num_re, num_im, norms)
     projected = removed_projections(gathered, image, perturbation)

time: 77.9 us -> 105 us (1.35)
  other arithmetic: 6.38 us -> 26.4 us
  matrix products: 8.81 us -> 23.8 us
  waiting for transfers between devices: 16.1 us -> 6.93 us
  local copies, waits for them, and re-layouts: 6.03 us -> 12.8 us
  starting transfers between devices: 28.1 us -> 22.1 us
    dot_general x0 -> x4, matrix products: none -> 10 us  [body(): jnp.einsum('cro,kio->ckri', flat, matrix, preferred_element_type=jnp.floa...]
    add x0 -> x5, other arithmetic: none -> 7.26 us  [the longest x4 7.25 us: body(): pull_a = (back[0, 0] + back[1, 1]).reshape(vecs, width_x, width_fy)]
    all_to_all x1, waiting for transfers between devices: 5.22 us -> 0.01 us  [exchanged(): return lax.all_to_all(spread, axes, 0, 0, tiled=True)]
    reduce_sum x1 -> x5, other arithmetic: 1.32 us -> 6.31 us  [the longest x4 5.03 us: body(): jnp.sum(pull_a[:, None] * s_re[None, :] + pull_b[:, None] * s_im[None, :]...]
    unnamed x16 -> x42, local copies, waits for them, and re-layouts: 1.36 us -> 6.12 us
    ppermute x4, waiting for transfers between devices: 10.9 us -> 6.92 us  [passed_along(): return lax.ppermute(value, axis, pairs)]
    all_to_all x1, starting transfers between devices: 15.7 us -> 12.1 us  [exchanged(): return lax.all_to_all(spread, axes, 0, 0, tiled=True)]
    mul x0 -> x4, other arithmetic: none -> 3.64 us  [body(): pull_a[:, None] * s_re[None, :] + pull_b[:, None] * s_im[None, :]]
  transfers between devices with their start and end apart: 5 -> 5, of which waited for: 3 -> 1; matrix products, arithmetic and copies ran while one was open for 19% -> 48% of each run, Pallas kernels for 0% -> 0%
where the time goes in v17:
time: 105 us; the launch traced here: 104 us
  other arithmetic  26.4 us (25%)
  matrix products  23.8 us (23%)
  starting transfers between devices  22.1 us (21%)
  local copies, waits for them, and re-layouts  12.8 us (12%)
  between operations  9.14 us (9%)
  waiting for transfers between devices  6.93 us (7%)
  Pallas kernels  3.02 us (3%)
    all_to_all x1, starting transfers between devices, exchanged(): return lax.all_to_all(spread, axes, 0, 0, tiled=True)  12.1 us
    dot_general x4, matrix products, body(): jnp.einsum('cro,kio->ckri', flat, matrix, preferred_element_type=jnp.floa...  10 us
    dot_general x4, matrix products, body(): jnp.einsum('cri,kio->ckro', other, matrix, preferred_element_type=jnp.flo...  10 us
    ppermute x4, starting transfers between devices, passed_along(): return lax.ppermute(value, axis, pairs)  10 us
    add x4, other arithmetic, body(): pull_a = (back[0, 0] + back[1, 1]).reshape(vecs, width_x, width_fy)  7.25 us
    ppermute x4, waiting for transfers between devices, passed_along(): return lax.ppermute(value, axis, pairs)  6.92 us
    unnamed x42, local copies, waits for them, and re-layouts  6.12 us
    reduce_sum x4, other arithmetic, body(): jnp.sum(pull_a[:, None] * s_re[None, :] + pull_b[:, None] * s_im[None, :]...  5.03 us
  transfers between devices with their start and end apart: 5, of which 1 were waited for; matrix products, arithmetic and copies ran while one was open for 48% of the time, Pallas kernels for 0%

profile of v17, /device:TPU:0, one launch (start us, length us, event | category | flops | bytes accessed | tf_op | source)
XLA Modules:
  0.0 104.2 jit_solution(15703274266287272100)
XLA Ops:
  0.6 0.0 copy-start
  0.6 0.0 copy-start.2
  0.7 0.5 collective-permute-start.2
  1.2 5.1 %collective-permute-start = (bf16[2,2,256,512]{3,2,1,0:T(8,128)(2,1)}, bf16[2,2,256,512]{3,2,1,0:T(8,128)(2,1)}, u32[]{:S(2)}, u32[]{:S(2)}) collective-permute-start(bf16[2,2,256,512]{3,2,1,0:T(8,128)(2,1)} %bitcast.170), channel_id=1, source_target_pairs={{0,15},{1,0},{2,1},{3,2},{4,3},{5,4},{6,5},{7,6},{8,7},{9,8},{10,9... | collective-permute-start | bytes 3145736 | tf_op jit(solution)/shard_map/ppermute | solution.py:12
  6.2 1.4 %fusion.42 = (s32[]{:T(128)}, s32[]{:T(128)}, s32[]{:T(128)}, s32[]{:T(128)}) fusion(s32[4]{0:T(128)} %param.12), kind=kLoop, calls=%fused_computation.98 | loop fusion | flops 44 | bytes 32 | tf_op jit(solution)/shard_map/reduce_sum | solution.py:53
  12.7 2.5 %reshape_squeeze.6 = bf16[4096,128]{1,0:T(8,128)(2,1)} reshape(bf16[1,2,2,256,512]{4,3,2,1,0:T(8,128)(2,1)} %block_ref.1) | data formatting | bytes 2097152 | tf_op jit(solution)/shard_map/reshape;squeeze | solution.py:36
  15.2 0.3 bitcast_convert_fusion
  16.1 2.5 %convolution_bitcast_fusion = f32[2,2,512,512]{3,2,0,1:T(8,128)S(1)} fusion(bf16[2,512,512,1]{2,1,0,3:T(8,128)(2,1)S(1)} %bitcast.171, bf16[4,2,512,512]{3,2,1,0:T(8,128)(2,1)} %param.8, s32[]{:T(128)S(6)} %select_n.33), kind=kOutput, calls=%fused_computation | convolution fusion | flops 1073741824 | bytes 6291460 | tf_op jit(solution)/shard_map/cro,kio->ckri/dot_general | solution.py:55
  18.6 1.8 %slice_add_fusion = (f32[1,1,512,512]{3,2,0,1:T(8,128)}, f32[1,1,512,512]{3,2,0,1:T(8,128)}) fusion(f32[2,2,512,512]{3,2,0,1:T(8,128)S(1)} %convolution_bitcast_fusion), kind=kLoop, calls=%fused_computation.25 | loop fusion | flops 524288 | bytes 6291456 | tf_op jit(solution)/shard_map/add | solution.py:56
  21.1 2.5 %convolution_bitcast_fusion.3 = f32[2,2,512,512]{3,2,0,1:T(8,128)S(1)} fusion(bf16[2,512,512,1]{2,1,0,3:T(8,128)(2,1)S(1)} %bitcast.172, bf16[4,2,512,512]{3,2,1,0:T(8,128)(2,1)} %param.8, s32[]{:T(128)S(6)} %select_n.27), kind=kOutput, calls=%fused_computation.3 | convolution fusion | flops 1073741824 | bytes 6291460 | tf_op jit(solution)/shard_map/cro,kio->ckri/dot_general | solution.py:55
  23.6 1.8 %slice_add_fusion.3 = (f32[1,1,512,512]{3,2,0,1:T(8,128)}, f32[1,1,512,512]{3,2,0,1:T(8,128)}) fusion(f32[2,2,512,512]{3,2,0,1:T(8,128)S(1)} %convolution_bitcast_fusion.3), kind=kLoop, calls=%fused_computation.31 | loop fusion | flops 524288 | bytes 6291456 | tf_op jit(solution)/shard_map/add | solution.py:56
  26.0 2.5 %convolution_bitcast_fusion.2 = f32[2,2,512,512]{3,2,0,1:T(8,128)S(1)} fusion(bf16[2,512,512,1]{2,1,0,3:T(8,128)(2,1)S(1)} %bitcast.173, bf16[4,2,512,512]{3,2,1,0:T(8,128)(2,1)} %param.8, s32[]{:T(128)S(6)} %select_n.29), kind=kOutput, calls=%fused_computation.2 | convolution fusion | flops 1073741824 | bytes 6291460 | tf_op jit(solution)/shard_map/cro,kio->ckri/dot_general | solution.py:55
  28.5 1.8 %slice_add_fusion.2 = (f32[1,1,512,512]{3,2,0,1:T(8,128)}, f32[1,1,512,512]{3,2,0,1:T(8,128)}) fusion(f32[2,2,512,512]{3,2,0,1:T(8,128)S(1)} %convolution_bitcast_fusion.2), kind=kLoop, calls=%fused_computation.29 | loop fusion | flops 524288 | bytes 6291456 | tf_op jit(solution)/shard_map/add | solution.py:56
  30.9 2.5 %convolution_bitcast_fusion.1 = f32[2,2,512,512]{3,2,0,1:T(8,128)S(1)} fusion(bf16[2,512,512,1]{2,1,0,3:T(8,128)(2,1)S(1)} %bitcast.174, bf16[4,2,512,512]{3,2,1,0:T(8,128)(2,1)} %param.8, s32[]{:T(128)S(6)} %select_n.31), kind=kOutput, calls=%fused_computation.1 | convolution fusion | flops 1073741824 | bytes 6291460 | tf_op jit(solution)/shard_map/cro,kio->ckri/dot_general | solution.py:55
  33.5 0.0 copy-start.6
  33.5 1.8 %slice_add_fusion.1 = (f32[1,1,512,512]{3,2,0,1:T(8,128)}, f32[1,1,512,512]{3,2,0,1:T(8,128)}) fusion(f32[2,2,512,512]{3,2,0,1:T(8,128)S(1)} %convolution_bitcast_fusion.1), kind=kLoop, calls=%fused_computation.27 | loop fusion | flops 524288 | bytes 6291456 | tf_op jit(solution)/shard_map/add | solution.py:56
  35.3 1.7 %fusion.45 = f32[4096,128]{1,0:T(8,128)} fusion(bf16[4096,128]{1,0:T(8,128)(2,1)S(1)} %copy-done.6, bf16[128,128]{1,0:T(8,128)(2,1)S(1)} %copy-done), kind=kOutput, calls=%fused_computation.102 | convolution fusion | flops 134217728 | bytes 3178496 | tf_op jit(solution)/shard_map/dot_general | solution.py:37
  37.1 2.7 %reshape.339 = f32[2,2,256,512]{3,2,1,0:T(8,128)} reshape(f32[4096,128]{1,0:T(8,128)} %fusion.45) | data formatting | bytes 4194304 | tf_op jit(solution)/shard_map/reshape | solution.py:37
  40.5 0.3 broadcast_in_dim.18
  40.8 2.0 %fusion.3 = f32[2,2,256,512]{3,2,1,0:T(8,128)S(1)} fusion(f32[2,2,256,512]{3,2,1,0:T(8,128)} %reshape.339, f32[]{:T(128)S(6)} %div.3, bf16[256,256]{1,0:T(8,128)(2,1)S(1)} %copy-done.18, bf16[32,8,2,128]{3,2,1,0:T(2,128)(2,1)S(1)} %bitcast.193, bf16[1,2,2,256,512]{4,3,2,1,0:T(8,128)(2,1)S(1)} %copy-done.2), kind=kOutput, calls=%fused_computation.13 | convolution fusion | flops 270794752 | bytes 5505028 | tf_op jit(solution)/shard_map/ab,cvbf->cvaf/dot_general | solution.py:40
  42.9 0.2 slice_bitcast_fusion.2
  43.1 1.1 %copy-done.3 = f32[2,2,256,512]{3,2,1,0:T(8,128)} copy-done((f32[2,2,256,512]{3,2,1,0:T(8,128)}, f32[2,2,256,512]{3,2,1,0:T(8,128)S(1)}, u32[]{:S(2)}) %copy-start.3) | copy-done | bytes 2097176
  44.2 0.2 slice_bitcast_fusion.3
  44.4 0.3 add_reduce_fusion.5
  44.7 1.3 %add_reduce_fusion.4 = (f32[2,2]{1,0:T(2,128)S(1)}, f32[2,2]{1,0:T(2,128)S(1)}) fusion(f32[2,256,512]{2,1,0:T(8,128)S(1)} %get-tuple-element.37, f32[2,256,512]{2,1,0:T(8,128)S(1)} %get-tuple-element.35, f32[2,256,512]{2,1,0:T(8,128)S(1)} %get-tuple-element.36, f32[2,256,512]{2,1,0:T(8,128)S(1)} %get-tuple-element.34), kind=kLoop, calls=%fused_computation.23 | loop fusion | flops 4194296 | bytes 4194336 | tf_op jit(solution)/shard_map/reduce_sum | solution.py:47
  45.9 0.0 collective-permute-done
  45.9 0.9 copy-done.5
  46.9 2.5 %convolution_bitcast_fusion.6 = f32[2,2,512,512]{3,2,0,1:T(8,128)S(1)} fusion(bf16[2,512,512,1]{2,1,0,3:T(8,128)(2,1)} %bitcast.18, bf16[4,2,512,512]{3,2,1,0:T(8,128)(2,1)S(1)} %copy-done.5, s32[]{:T(128)S(6)} %select_n.29), kind=kOutput, calls=%fused_computation.6 | convolution fusion | flops 1073741824 | bytes 6291460 | tf_op jit(solution)/shard_map/cri,kio->ckro/dot_general | solution.py:64
  49.4 1.5 %slice_subtract_fusion.6 = (f32[1,1,512,512]{3,2,0,1:T(8,128)S(1)}, f32[1,1,512,512]{3,2,0,1:T(8,128)}) fusion(f32[2,2,512,512]{3,2,0,1:T(8,128)S(1)} %convolution_bitcast_fusion.6), kind=kLoop, calls=%fused_computation.41 | loop fusion | flops 524288 | bytes 6291456 | tf_op jit(solution)/shard_map/sub | solution.py:65
  50.8 2.5 %convolution_bitcast_fusion.5 = f32[2,2,512,512]{3,2,0,1:T(8,128)S(1)} fusion(bf16[2,512,512,1]{2,1,0,3:T(8,128)(2,1)} %bitcast.26, bf16[4,2,512,512]{3,2,1,0:T(8,128)(2,1)S(1)} %copy-done.5, s32[]{:T(128)S(6)} %select_n.31), kind=kOutput, calls=%fused_computation.5 | convolution fusion | flops 1073741824 | bytes 6291460 | tf_op jit(solution)/shard_map/cri,kio->ckro/dot_general | solution.py:64
  53.3 1.8 %slice_subtract_fusion.5 = (f32[1,1,512,512]{3,2,0,1:T(8,128)}, f32[1,1,512,512]{3,2,0,1:T(8,128)}) fusion(f32[2,2,512,512]{3,2,0,1:T(8,128)S(1)} %convolution_bitcast_fusion.5), kind=kLoop, calls=%fused_computation.39 | loop fusion | flops 524288 | bytes 6291456 | tf_op jit(solution)/shard_map/sub | solution.py:65
  55.1 4.4 %collective-permute-start.1 = (bf16[2,2,256,512]{3,2,1,0:T(8,128)(2,1)}, bf16[2,2,256,512]{3,2,1,0:T(8,128)(2,1)S(1)}, u32[]{:S(2)}, u32[]{:S(2)}) collective-permute-start(bf16[2,2,256,512]{3,2,1,0:T(8,128)(2,1)} %collective-permute-done), channel_id=1, source_target_pairs={{0,15},{1,0},{2,1},{3,2},{4,3},{5,4},{6,5},{7,6},{8,7},{9,8},{10,9... | collective-permute-start | bytes 3145736 | tf_op jit(solution)/shard_map/ppermute | solution.py:12
  59.6 1.5 %fusion.25 = (f32[2,256,512]{2,1,0:T(8,128)S(1)}, f32[2,256,512]{2,1,0:T(8,128)S(1)}) fusion(bf16[2,2,256,512]{3,2,1,0:T(8,128)(2,1)} %collective-permute-done), kind=kLoop, calls=%fused_computation.73 | loop fusion | flops 524288 | bytes 3145728 | tf_op jit(solution)/shard_map/mul | solution.py:61
  61.1 1.3 %add_reduce_fusion.2 = (f32[2,2]{1,0:T(2,128)S(1)}, f32[2,2]{1,0:T(2,128)S(1)}) fusion(f32[2,256,512]{2,1,0:T(8,128)S(1)} %get-tuple-element.41, f32[2,256,512]{2,1,0:T(8,128)S(1)} %bitcast.184, f32[2,256,512]{2,1,0:T(8,128)S(1)} %get-tuple-element.40, f32[2,256,512]{2,1,0:T(8,128)S(1)} %bitcast.183), kind=kLoop, calls=%fused_computation.21 | loop fusion | flops 4194296 | bytes 4194336 | tf_op jit(solution)/shard_map/reduce_sum | solution.py:61
  62.3 1.6 %fusion.23 = (f32[2,256,512]{2,1,0:T(8,128)S(1)}, f32[2,256,512]{2,1,0:T(8,128)S(1)}) fusion(bf16[2,2,256,512]{3,2,1,0:T(8,128)(2,1)} %collective-permute-done.2), kind=kLoop, calls=%fused_computation.69 | loop fusion | flops 524288 | bytes 3145728 | tf_op jit(solution)/shard_map/mul | solution.py:61
  64.0 0.2 copy-done.12
  64.2 1.3 %add_reduce_fusion.1 = (f32[2,2]{1,0:T(2,128)S(1)}, f32[2,2]{1,0:T(2,128)S(1)}) fusion(f32[2,256,512]{2,1,0:T(8,128)S(1)} %get-tuple-element.43, f32[2,256,512]{2,1,0:T(8,128)S(1)} %bitcast.182, f32[2,256,512]{2,1,0:T(8,128)S(1)} %get-tuple-element.42, f32[2,256,512]{2,1,0:T(8,128)S(1)} %bitcast.181), kind=kLoop, calls=%fused_computation.20 | loop fusion | flops 4194296 | bytes 4194336 | tf_op jit(solution)/shard_map/reduce_sum | solution.py:61
  65.5 6.9 %collective-permute-done.3 = bf16[2,2,256,512]{3,2,1,0:T(8,128)(2,1)S(1)} collective-permute-done((bf16[2,2,256,512]{3,2,1,0:T(8,128)(2,1)}, bf16[2,2,256,512]{3,2,1,0:T(8,128)(2,1)S(1)}, u32[]{:S(2)}, u32[]{:S(2)}) %collective-permute-start.3) | collective-permute-done | bytes 1048608 | tf_op jit(solution)/shard_map/ppermute | solution.py:12
  72.4 0.3 fusion.21
  72.7 1.3 %add_reduce_fusion = (f32[2,2]{1,0:T(2,128)S(1)}, f32[2,2]{1,0:T(2,128)S(1)}) fusion(f32[2,256,512]{2,1,0:T(8,128)S(1)} %get-tuple-element.45, f32[2,256,512]{2,1,0:T(8,128)S(1)} %bitcast.180, f32[2,256,512]{2,1,0:T(8,128)S(1)} %get-tuple-element.44, f32[2,256,512]{2,1,0:T(8,128)S(1)} %bitcast.179), kind=kLoop, calls=%fused_computation.19 | loop fusion | flops 4194296 | bytes 4194336 | tf_op jit(solution)/shard_map/reduce_sum | solution.py:61
  73.9 0.0 collective-permute-done.1
  73.9 0.3 fusion.27
  74.2 0.9 copy-done.7
  75.2 0.3 copy-done.8
  75.5 1.3 %add_reduce_fusion.3 = (f32[2,2]{1,0:T(2,128)S(1)}, f32[2,2]{1,0:T(2,128)S(1)}) fusion(f32[2,256,512]{2,1,0:T(8,128)S(1)} %get-tuple-element.39, f32[2,256,512]{2,1,0:T(8,128)S(1)} %bitcast.178, f32[2,256,512]{2,1,0:T(8,128)S(1)} %get-tuple-element.38, f32[2,256,512]{2,1,0:T(8,128)S(1)} %bitcast.177), kind=kLoop, calls=%fused_computation.22 | loop fusion | flops 4194296 | bytes 4194336 | tf_op jit(solution)/shard_map/reduce_sum | solution.py:61
  76.7 0.1 reshape.362
  76.8 0.1 reshape.363
  76.9 0.1 maximum_maximum_fusion
  77.0 0.6 broadcast.23
  77.6 12.1 %all-to-all-start = ((f32[16,1,10]{2,1,0:T(1,128)}), f32[16,1,10]{2,1,0:T(1,128)S(1)}, u32[]{:S(2)}, u32[]{:S(2)}) async-start(f32[16,1,10]{2,1,0:T(1,128)} %bitcast.70), calls=%async_computation | async-start | bytes 16384 | tf_op jit(solution)/shard_map/all_to_all | solution.py:20
  89.6 2.5 %convolution_bitcast_fusion.7 = f32[2,2,512,512]{3,2,0,1:T(8,128)S(1)} fusion(bf16[2,512,512,1]{2,1,0,3:T(8,128)(2,1)S(1)} %bitcast.176, bf16[4,2,512,512]{3,2,1,0:T(8,128)(2,1)} %param.8, s32[]{:T(128)S(6)} %select_n.27), kind=kOutput, calls=%fused_computation.7 | convolution fusion | flops 1073741824 | bytes 6291460 | tf_op jit(solution)/shard_map/cri,kio->ckro/dot_general | solution.py:64
  92.1 0.5 slice_subtract_fusion.7
  92.6 2.5 %convolution_bitcast_fusion.4 = f32[2,2,512,512]{3,2,0,1:T(8,128)S(1)} fusion(bf16[2,512,512,1]{2,1,0,3:T(8,128)(2,1)S(1)} %bitcast.175, bf16[4,2,512,512]{3,2,1,0:T(8,128)(2,1)} %param.8, s32[]{:T(128)S(6)} %select_n.33), kind=kOutput, calls=%fused_computation.4 | convolution fusion | flops 1073741824 | bytes 6291460 | tf_op jit(solution)/shard_map/cri,kio->ckro/dot_general | solution.py:64
  95.2 0.0 copy-start.16
  95.2 0.0 copy-start.17
  95.2 0.5 slice_subtract_fusion.4
  95.7 1.1 %copy-done.4 = f32[2,2,256,512]{3,2,1,0:T(8,128)S(1)} copy-done((f32[2,2,256,512]{3,2,1,0:T(8,128)S(1)}, f32[2,2,256,512]{3,2,1,0:T(8,128)}, u32[]{:S(2)}) %copy-start.4) | copy-done | bytes 2097176
  96.7 0.3 copy-done.15
  97.0 0.3 copy-done.16
  97.3 0.3 copy-done.17
  97.6 3.0 %convert_bitcast_fusion = (bf16[1,2,2,256,512]{4,3,2,1,0:T(8,128)(2,1)}, f32[2,2,256,512]{3,2,1,0:T(8,128)}) fusion(f32[1,2,256,512]{3,2,1,0:T(8,128)S(1)} %bitcast.192, f32[1,2,256,512]{3,2,1,0:T(8,128)S(1)} %bitcast.191, f32[1,2,256,512]{3,2,1,0:T(8,128)S(1)} %bitcast.188, f32[1,2,256,512]{3,2,1,0:T(8,128)S(1)} %bitcast.187, ...), kind=kLoop, calls=%fused_computation.53 | loop fusion | flops 4718592 | bytes 13631488 | tf_op jit(solution)/shard_map/broadcast_in_dim | solution.py:71
  100.6 0.0 all-to-all-done
  100.6 0.6 copy-done.19
  101.2 3.0 %shard_map.86 = bf16[1,2,2,256,512]{4,3,2,1,0:T(8,128)(2,1)} custom-call(f32[16,10]{1,0:T(8,128)} %bitcast.195, f32[2,2,256,512]{3,2,1,0:T(8,128)} %get-tuple-element.17.image_ref, bf16[1,2,2,256,512]{4,3,2,1,0:T(8,128)(2,1)} %block_ref.1), custom_call_target="tpu_custom_call" | custom-call | tf_op jit(solution)/shard_map/pallas_call | solution.py:102
  (32 shorter events, 0.1 us)
Async XLA Ops:
  0.6 34.7 %copy-start = (bf16[128,128]{1,0:T(8,128)(2,1)S(1)}, bf16[128,128]{1,0:T(8,128)(2,1)}, u32[]{:S(2)}) copy-start(bf16[128,128]{1,0:T(8,128)(2,1)} %param.9) | copy-start | bytes 98308
  0.6 14.5 %copy-start.2 = (bf16[1,2,2,256,512]{4,3,2,1,0:T(8,128)(2,1)S(1)}, bf16[1,2,2,256,512]{4,3,2,1,0:T(8,128)(2,1)}, u32[]{:S(2)}) copy-start(bf16[1,2,2,256,512]{4,3,2,1,0:T(8,128)(2,1)} %block_ref.1) | copy-start | bytes 3145732
  0.7 50.2 %collective-permute-start.2 = (bf16[2,2,256,512]{3,2,1,0:T(8,128)(2,1)}, bf16[2,2,256,512]{3,2,1,0:T(8,128)(2,1)}, u32[]{:S(2)}, u32[]{:S(2)}) collective-permute-start(bf16[2,2,256,512]{3,2,1,0:T(8,128)(2,1)} %bitcast.169), channel_id=1, source_target_pairs={{0,1},{1,2},{2,3},{3,4},{4,5},{5,6},{6,7},{7,8},{8,9},{9,10},{10,1... | collective-permute-start | bytes 3145736 | tf_op jit(solution)/shard_map/ppermute | solution.py:12
  1.2 44.8 %collective-permute-start = (bf16[2,2,256,512]{3,2,1,0:T(8,128)(2,1)}, bf16[2,2,256,512]{3,2,1,0:T(8,128)(2,1)}, u32[]{:S(2)}, u32[]{:S(2)}) collective-permute-start(bf16[2,2,256,512]{3,2,1,0:T(8,128)(2,1)} %bitcast.170), channel_id=1, source_target_pairs={{0,15},{1,0},{2,1},{3,2},{4,3},{5,4},{6,5},{7,6},{8,7},{9,8},{10,9... | collective-permute-start | bytes 3145736 | tf_op jit(solution)/shard_map/ppermute | solution.py:12
  33.5 1.8 %copy-start.6 = (bf16[4096,128]{1,0:T(8,128)(2,1)S(1)}, bf16[4096,128]{1,0:T(8,128)(2,1)}, u32[]{:S(2)}) copy-start(bf16[4096,128]{1,0:T(8,128)(2,1)} %reshape_squeeze.6) | copy-start | bytes 3145732
  37.1 2.8 %copy-start.20 = (s32[2,2]{1,0:T(2,128)S(1)}, s32[2,2]{1,0:T(2,128)}, u32[]{:S(2)}) copy-start(s32[2,2]{1,0:T(2,128)} %param.11) | copy-start | bytes 52
  37.1 3.8 %copy-start.18 = (bf16[256,256]{1,0:T(8,128)(2,1)S(1)}, bf16[256,256]{1,0:T(8,128)(2,1)}, u32[]{:S(2)}) copy-start(bf16[256,256]{1,0:T(8,128)(2,1)} %param.10) | copy-start | bytes 393220
  42.9 1.3 %copy-start.3 = (f32[2,2,256,512]{3,2,1,0:T(8,128)}, f32[2,2,256,512]{3,2,1,0:T(8,128)S(1)}, u32[]{:S(2)}) copy-start(f32[2,2,256,512]{3,2,1,0:T(8,128)S(1)} %fusion.3) | copy-start | bytes 6291460
  44.7 2.2 %copy-start.5 = (bf16[4,2,512,512]{3,2,1,0:T(8,128)(2,1)S(1)}, bf16[4,2,512,512]{3,2,1,0:T(8,128)(2,1)}, u32[]{:S(2)}) copy-start(bf16[4,2,512,512]{3,2,1,0:T(8,128)(2,1)} %param.8) | copy-start | bytes 12582916
  55.1 5.9 %copy-start.13 = (f32[1,1,512,512]{3,2,0,1:T(8,128)S(1)}, f32[1,1,512,512]{3,2,0,1:T(8,128)}, u32[]{:S(2)}) copy-start(f32[1,1,512,512]{3,2,0,1:T(8,128)} %get-tuple-element.20) | copy-start | bytes 3145732
  55.1 5.9 %copy-start.14 = (f32[1,1,512,512]{3,2,0,1:T(8,128)S(1)}, f32[1,1,512,512]{3,2,0,1:T(8,128)}, u32[]{:S(2)}) copy-start(f32[1,1,512,512]{3,2,0,1:T(8,128)} %get-tuple-element.21) | copy-start | bytes 3145732
  55.1 17.2 %collective-permute-start.3 = (bf16[2,2,256,512]{3,2,1,0:T(8,128)(2,1)}, bf16[2,2,256,512]{3,2,1,0:T(8,128)(2,1)S(1)}, u32[]{:S(2)}, u32[]{:S(2)}) collective-permute-start(bf16[2,2,256,512]{3,2,1,0:T(8,128)(2,1)} %collective-permute-done.2), channel_id=1, source_target_pairs={{0,1},{1,2},{2,3},{3,4},{4,5},{5,6},{6,7},{7,8},{8,9},{9,10},{10,1... | collective-permute-start | bytes 3145736 | tf_op jit(solution)/shard_map/ppermute | solution.py:12
  55.1 18.8 %collective-permute-start.1 = (bf16[2,2,256,512]{3,2,1,0:T(8,128)(2,1)}, bf16[2,2,256,512]{3,2,1,0:T(8,128)(2,1)S(1)}, u32[]{:S(2)}, u32[]{:S(2)}) collective-permute-start(bf16[2,2,256,512]{3,2,1,0:T(8,128)(2,1)} %collective-permute-done), channel_id=1, source_target_pairs={{0,15},{1,0},{2,1},{3,2},{4,3},{5,4},{6,5},{7,6},{8,7},{9,8},{10,9... | collective-permute-start | bytes 3145736 | tf_op jit(solution)/shard_map/ppermute | solution.py:12
  62.3 1.6 %copy-start.11 = (f32[1,1,512,512]{3,2,0,1:T(8,128)S(1)}, f32[1,1,512,512]{3,2,0,1:T(8,128)}, u32[]{:S(2)}) copy-start(f32[1,1,512,512]{3,2,0,1:T(8,128)} %get-tuple-element.22) | copy-start | bytes 3145732
  62.3 1.9 %copy-start.12 = (f32[1,1,512,512]{3,2,0,1:T(8,128)S(1)}, f32[1,1,512,512]{3,2,0,1:T(8,128)}, u32[]{:S(2)}) copy-start(f32[1,1,512,512]{3,2,0,1:T(8,128)} %get-tuple-element.23) | copy-start | bytes 3145732
  65.4 7.2 %copy-start.9 = (f32[1,1,512,512]{3,2,0,1:T(8,128)S(1)}, f32[1,1,512,512]{3,2,0,1:T(8,128)}, u32[]{:S(2)}) copy-start(f32[1,1,512,512]{3,2,0,1:T(8,128)} %get-tuple-element.24) | copy-start | bytes 3145732
  65.4 7.2 %copy-start.10 = (f32[1,1,512,512]{3,2,0,1:T(8,128)S(1)}, f32[1,1,512,512]{3,2,0,1:T(8,128)}, u32[]{:S(2)}) copy-start(f32[1,1,512,512]{3,2,0,1:T(8,128)} %get-tuple-element.25) | copy-start | bytes 3145732
  73.9 1.2 %copy-start.7 = (f32[1,1,512,512]{3,2,0,1:T(8,128)S(1)}, f32[1,1,512,512]{3,2,0,1:T(8,128)}, u32[]{:S(2)}) copy-start(f32[1,1,512,512]{3,2,0,1:T(8,128)} %get-tuple-element.18) | copy-start | bytes 3145732
  73.9 1.5 %copy-start.8 = (f32[1,1,512,512]{3,2,0,1:T(8,128)S(1)}, f32[1,1,512,512]{3,2,0,1:T(8,128)}, u32[]{:S(2)}) copy-start(f32[1,1,512,512]{3,2,0,1:T(8,128)} %get-tuple-element.19) | copy-start | bytes 3145732
  77.6 23.0 %all-to-all-start = ((f32[16,1,10]{2,1,0:T(1,128)}), f32[16,1,10]{2,1,0:T(1,128)S(1)}, u32[]{:S(2)}, u32[]{:S(2)}) async-start(f32[16,1,10]{2,1,0:T(1,128)} %bitcast.70), calls=%async_computation | async-start | bytes 16384 | tf_op jit(solution)/shard_map/all_to_all | solution.py:20
  95.1 1.6 %copy-start.4 = (f32[2,2,256,512]{3,2,1,0:T(8,128)S(1)}, f32[2,2,256,512]{3,2,1,0:T(8,128)}, u32[]{:S(2)}) copy-start(f32[2,2,256,512]{3,2,1,0:T(8,128)} %copy-done.3) | copy-start | bytes 6291460
  95.2 1.8 %copy-start.15 = (f32[1,1,512,512]{3,2,0,1:T(8,128)S(1)}, f32[1,1,512,512]{3,2,0,1:T(8,128)}, u32[]{:S(2)}) copy-start(f32[1,1,512,512]{3,2,0,1:T(8,128)} %get-tuple-element.29) | copy-start | bytes 3145732
  95.2 2.2 %copy-start.16 = (f32[1,1,512,512]{3,2,0,1:T(8,128)S(1)}, f32[1,1,512,512]{3,2,0,1:T(8,128)}, u32[]{:S(2)}) copy-start(f32[1,1,512,512]{3,2,0,1:T(8,128)} %get-tuple-element.30) | copy-start | bytes 3145732
  95.2 2.5 %copy-start.17 = (f32[1,1,512,512]{3,2,0,1:T(8,128)S(1)}, f32[1,1,512,512]{3,2,0,1:T(8,128)}, u32[]{:S(2)}) copy-start(f32[1,1,512,512]{3,2,0,1:T(8,128)} %get-tuple-element.31) | copy-start | bytes 3145732
  100.6 0.6 copy-start.19
  100.6 3.6 %copy-start.1 = (bf16[128,128]{1,0:T(8,128)(2,1)S(1)}, bf16[128,128]{1,0:T(8,128)(2,1)}, u32[]{:S(2)}) copy-start(bf16[128,128]{1,0:T(8,128)(2,1)} %param.9) | copy-start | bytes 98308

commit v18 on v13

--- a/solution.py
+++ b/solution.py
@@ -43,6 +43,7 @@
     image = along_y + along_x + lam * block.astype(jnp.float32)
     sources = (above_two, above_one, below_one, below_two)
     counter = jnp.arange(4, dtype=jnp.int32)
+    terms = []
     for place in range(4):
         slot = jnp.sum(jnp.where(slot_offsets == place, counter, 0))
         matrix = lax.dynamic_index_in_dim(coupling, slot, 0, keepdims=False)
@@ -50,7 +51,10 @@
         prod = jnp.einsum("cri,kio->ckro", other, matrix, preferred_element_type=jnp.float32)
         real_part = prod[0, 0] - prod[1, 1]
         imag_part = prod[0, 1] + prod[1, 0]
-        image = image + jnp.stack([real_part, imag_part]).reshape(block.shape)
+        terms.append((matrix, jnp.stack([real_part, imag_part]).reshape(block.shape)))
+    last_matrix, last_term = terms[0]
+    for _, term in terms[1:]:
+        image = image + term
     qfull = block.astype(jnp.float32)
     qr = qfull[0]
     qi = qfull[1]
@@ -58,6 +62,15 @@
     wi = image[1]
     num_re = jnp.sum(qr[:, None] * wr[None, :] + qi[:, None] * wi[None, :], axis=(2, 3))
     num_im = jnp.sum(qr[:, None] * wi[None, :] - qi[:, None] * wr[None, :], axis=(2, 3))
+    back = jnp.einsum("cro,kio->ckri", block.reshape(2, vecs * width_x, width_fy), last_matrix,
+                      preferred_element_type=jnp.float32)
+    pull_a = (back[0, 0] + back[1, 1]).reshape(vecs, width_x, width_fy)
+    pull_b = (back[1, 0] - back[0, 1]).reshape(vecs, width_x, width_fy)
+    s_re = above_two[0].astype(jnp.float32)
+    s_im = above_two[1].astype(jnp.float32)
+    num_re = num_re + jnp.sum(pull_a[:, None] * s_re[None, :] + pull_b[:, None] * s_im[None, :], axis=(2, 3))
+    num_im = num_im + jnp.sum(pull_a[:, None] * s_im[None, :] - pull_b[:, None] * s_re[None, :], axis=(2, 3))
+    image = image + last_term
     norms = jnp.sum(qr * qr + qi * qi, axis=(1, 2))
     gathered = exchanged(("harm",), num_re, num_im, norms)
     projected = removed_projections(gathered, image, perturbation)

time: 77.9 us -> 79.4 us (1.019)
  waiting for transfers between devices: 16.1 us -> 7.7 us
  local copies, waits for them, and re-layouts: 6.03 us -> 10.5 us
  matrix products: 8.81 us -> 12.9 us
  other arithmetic: 6.38 us -> 8.57 us
  starting transfers between devices: 28.1 us -> 27.3 us
    all_to_all x1, waiting for transfers between devices: 5.22 us -> 0.94 us  [exchanged(): return lax.all_to_all(spread, axes, 0, 0, tiled=True)]
    ppermute x4, waiting for transfers between devices: 10.9 us -> 6.76 us  [passed_along(): return lax.ppermute(value, axis, pairs)]
    dot_general x0 -> x1, matrix products: none -> 2.51 us  [body(): jnp.einsum('cro,kio->ckri', block.reshape(2, vecs * width_x, width_fy), l...]
    unnamed x16 -> x24, local copies, waits for them, and re-layouts: 1.36 us -> 3.73 us
    ppermute x4, starting transfers between devices: 12.3 us -> 10.1 us  [passed_along(): return lax.ppermute(value, axis, pairs)]
    dot_general x4, matrix products: 7.49 us -> 9.03 us  [body(): jnp.einsum('cri,kio->ckro', other, matrix, preferred_element_type=jnp.flo...]
    all_to_all x1, starting transfers between devices: 15.7 us -> 17.1 us  [exchanged(): return lax.all_to_all(spread, axes, 0, 0, tiled=True)]
    mul x2, local copies, waits for them, and re-layouts: 0.34 us -> 1.68 us  [body(): qr[:, None] * wr[None, :] + qi[:, None] * wi[None, :]]
  transfers between devices with their start and end apart: 5 -> 5, of which waited for: 3 -> 2; matrix products, arithmetic and copies ran while one was open for 19% -> 31% of each run, Pallas kernels for 0% -> 0%
where the time goes in v18:
time: 79.4 us; the launch traced here: 78.8 us
  starting transfers between devices  27.3 us (34%)
  matrix products  12.9 us (16%)
  local copies, waits for them, and re-layouts  10.5 us (13%)
  between operations  8.85 us (11%)
  other arithmetic  8.57 us (11%)
  waiting for transfers between devices  7.7 us (10%)
  Pallas kernels  3.02 us (4%)
    all_to_all x1, starting transfers between devices, exchanged(): return lax.all_to_all(spread, axes, 0, 0, tiled=True)  17.1 us
    ppermute x4, starting transfers between devices, passed_along(): return lax.ppermute(value, axis, pairs)  10.1 us
    dot_general x4, matrix products, body(): jnp.einsum('cri,kio->ckro', other, matrix, preferred_element_type=jnp.flo...  9.03 us
    ppermute x4, waiting for transfers between devices, passed_along(): return lax.ppermute(value, axis, pairs)  6.76 us
    unnamed x24, local copies, waits for them, and re-layouts  3.73 us
    pallas_call x1, Pallas kernels, removed_projections(): pl.pallas_call(project_kernel, grid=(width_x // rows,), in_specs=[pl.Bloc...  3.02 us
    another operation x1, local copies, waits for them, and re-layouts, body(): rows = block.reshape(-1, ny)  2.51 us
    dot_general x1, matrix products, body(): jnp.einsum('cro,kio->ckri', block.reshape(2, vecs * width_x, width_fy), l...  2.51 us
  transfers between devices with their start and end apart: 5, of which 2 were waited for; matrix products, arithmetic and copies ran while one was open for 31% of the time, Pallas kernels for 0%

profile of v18, /device:TPU:0, one launch (start us, length us, event | category | flops | bytes accessed | tf_op | source)
XLA Modules:
  0.0 78.8 jit_solution(8461426259791651708)
XLA Ops:
  0.6 0.0 copy-start
  0.6 0.0 copy-start.1
  0.7 0.5 collective-permute-start.1
  1.2 5.1 %collective-permute-start = (bf16[2,2,256,512]{3,2,1,0:T(8,128)(2,1)}, bf16[2,2,256,512]{3,2,1,0:T(8,128)(2,1)}, u32[]{:S(2)}, u32[]{:S(2)}) collective-permute-start(bf16[2,2,256,512]{3,2,1,0:T(8,128)(2,1)} %bitcast.121), channel_id=1, source_target_pairs={{0,15},{1,0},{2,1},{3,2},{4,3},{5,4},{6,5},{7,6},{8,7},{9,8},{10,9... | collective-permute-start | bytes 3145736 | tf_op jit(solution)/shard_map/ppermute | solution.py:12
  6.2 2.5 %reshape_squeeze.6 = bf16[4096,128]{1,0:T(8,128)(2,1)} reshape(bf16[1,2,2,256,512]{4,3,2,1,0:T(8,128)(2,1)} %block_ref.1) | data formatting | bytes 2097152 | tf_op jit(solution)/shard_map/reshape;squeeze | solution.py:36
  8.7 0.0 copy-done.1
  8.7 0.0 copy-start.5
  8.7 0.3 bitcast_convert_fusion
  9.0 0.3 add_reduce_fusion.2
  9.3 0.0 copy-done
  9.3 0.7 copy-done.5
  10.0 0.4 fusion.28
  10.4 0.0 copy-start.10
  10.4 1.5 %slice_bitcast_fusion.3 = (f32[2,256,512]{2,1,0:T(8,128)}, f32[2,256,512]{2,1,0:T(8,128)}) fusion(f32[2,2,256,512]{3,2,1,0:T(8,128)S(1)} %bitcast_convert_fusion), kind=kLoop, calls=%fused_computation.20 | loop fusion | bytes 4194304 | tf_op jit(solution)/shard_map/mul | solution.py:63
  11.9 0.0 copy-done.10
  11.9 0.7 fusion.26
  17.5 0.0 copy-start.11
  17.5 1.5 %reshape.243 = f32[2,2,256,512]{3,2,1,0:T(8,128)} reshape(f32[4096,128]{1,0:T(8,128)S(1)} %fusion.28) | data formatting | bytes 4194304 | tf_op jit(solution)/shard_map/reshape | solution.py:37
  19.0 0.0 copy-done.11
  22.1 2.5 %convolution_bitcast_fusion = f32[2,2,512,512]{3,2,0,1:T(8,128)S(1)} fusion(bf16[2,512,512,1]{2,1,0,3:T(8,128)(2,1)S(1)} %bitcast.122, bf16[4,2,512,512]{3,2,1,0:T(8,128)(2,1)} %param.8, s32[]{:T(128)S(6)} %select_n.33), kind=kOutput, calls=%fused_computation | convolution fusion | flops 1073741824 | bytes 6291460 | tf_op jit(solution)/shard_map/cro,kio->ckri/dot_general | solution.py:65
  24.6 0.0 copy-start.3
  24.6 0.5 slice_add_fusion
  25.1 0.0 collective-permute-done.1
  25.1 2.0 %collective-permute-start.2 = (bf16[2,2,256,512]{3,2,1,0:T(8,128)(2,1)}, bf16[2,2,256,512]{3,2,1,0:T(8,128)(2,1)S(1)}, u32[]{:S(2)}, u32[]{:S(2)}) collective-permute-start(bf16[2,2,256,512]{3,2,1,0:T(8,128)(2,1)} %collective-permute-done.1), channel_id=1, source_target_pairs={{0,1},{1,2},{2,3},{3,4},{4,5},{5,6},{6,7},{7,8},{8,9},{9,10},{10,1... | collective-permute-start | bytes 3145736 | tf_op jit(solution)/shard_map/ppermute | solution.py:12
  27.1 0.0 copy-done.3
  27.1 2.5 %convolution_bitcast_fusion.3 = f32[2,2,512,512]{3,2,0,1:T(8,128)S(1)} fusion(bf16[2,512,512,1]{2,1,0,3:T(8,128)(2,1)} %bitcast.18, bf16[4,2,512,512]{3,2,1,0:T(8,128)(2,1)S(1)} %copy-done.3, s32[]{:T(128)S(6)} %select_n.29), kind=kOutput, calls=%fused_computation.3 | convolution fusion | flops 1073741824 | bytes 6291460 | tf_op jit(solution)/shard_map/cri,kio->ckro/dot_general | solution.py:51
  29.6 0.0 collective-permute-done
  29.6 2.6 %collective-permute-start.3 = (bf16[2,2,256,512]{3,2,1,0:T(8,128)(2,1)}, bf16[2,2,256,512]{3,2,1,0:T(8,128)(2,1)S(1)}, u32[]{:S(2)}, u32[]{:S(2)}) collective-permute-start(bf16[2,2,256,512]{3,2,1,0:T(8,128)(2,1)} %collective-permute-done), channel_id=1, source_target_pairs={{0,15},{1,0},{2,1},{3,2},{4,3},{5,4},{6,5},{7,6},{8,7},{9,8},{10,9... | collective-permute-start | bytes 3145736 | tf_op jit(solution)/shard_map/ppermute | solution.py:12
  32.2 0.5 slice_subtract_fusion.3
  32.7 2.5 %convolution_bitcast_fusion.4 = f32[2,2,512,512]{3,2,0,1:T(8,128)S(1)} fusion(bf16[2,512,512,1]{2,1,0,3:T(8,128)(2,1)} %bitcast.10, bf16[4,2,512,512]{3,2,1,0:T(8,128)(2,1)S(1)} %copy-done.3, s32[]{:T(128)S(6)} %select_n.27), kind=kOutput, calls=%fused_computation.4 | convolution fusion | flops 1073741824 | bytes 6291460 | tf_op jit(solution)/shard_map/cri,kio->ckro/dot_general | solution.py:51
  35.2 0.5 slice_subtract_fusion.4
  35.7 6.8 %collective-permute-done.2 = bf16[2,2,256,512]{3,2,1,0:T(8,128)(2,1)S(1)} collective-permute-done((bf16[2,2,256,512]{3,2,1,0:T(8,128)(2,1)}, bf16[2,2,256,512]{3,2,1,0:T(8,128)(2,1)S(1)}, u32[]{:S(2)}, u32[]{:S(2)}) %collective-permute-start.2) | collective-permute-done | bytes 1048608 | tf_op jit(solution)/shard_map/ppermute | solution.py:12
  42.4 1.3 %convolution_bitcast_fusion.2 = f32[2,2,512,512]{3,2,0,1:T(8,128)S(1)} fusion(bf16[2,512,512,1]{2,1,0,3:T(8,128)(2,1)S(1)} %bitcast.134, bf16[4,2,512,512]{3,2,1,0:T(8,128)(2,1)S(1)} %copy-done.3, s32[]{:T(128)S(6)} %select_n.31), kind=kOutput, calls=%fused_computation.2 | convolution fusion | flops 1073741824 | bytes 6291460 | tf_op jit(solution)/shard_map/cri,kio->ckro/dot_general | solution.py:51
  43.7 0.0 copy-start.2
  43.7 0.0 copy-start.8
  43.7 0.5 slice_subtract_fusion.2
  44.2 0.3 broadcast_in_dim.36
  44.5 0.7 copy-done.2
  45.3 0.0 copy-done.8
  45.3 0.9 %fusion.1 = f32[2,2,256,512]{3,2,1,0:T(8,128)S(1)} fusion(f32[1,2,256,512]{3,2,1,0:T(8,128)S(1)} %bitcast.127, f32[1,2,256,512]{3,2,1,0:T(8,128)S(1)} %bitcast.126, f32[1,2,256,512]{3,2,1,0:T(8,128)S(1)} %bitcast.125, f32[1,2,256,512]{3,2,1,0:T(8,128)S(1)} %bitcast.124, f32[1,2,256,512]{3,2,1,0:T(8,128)S(1)} %bitcast.129, ...), kind=kOutput, calls=%fused_computation.7 | convolution fusion | flops 273940480 | bytes 11796484 | tf_op jit(solution)/shard_map/ab,cvbf->cvaf/dot_general | solution.py:40
  46.2 0.2 slice_bitcast_fusion.2
  46.4 0.0 copy-start.6
  46.4 0.0 copy-start.7
  46.4 0.0 collective-permute-done.3
  46.4 0.0 copy-start.4
  46.4 0.2 fusion.14
  46.6 1.4 %copy-done.6 = f32[2,256,512]{2,1,0:T(8,128)S(1)} copy-done((f32[2,256,512]{2,1,0:T(8,128)S(1)}, f32[2,256,512]{2,1,0:T(8,128)}, u32[]{:S(2)}) %copy-start.6) | copy-done | bytes 1048600
  48.0 0.3 copy-done.7
  48.3 2.5 %add_reduce_fusion = (f32[2,2]{1,0:T(2,128)S(1)}, f32[2,2]{1,0:T(2,128)S(1)}, f32[2,2]{1,0:T(2,128)S(1)}, f32[2,2]{1,0:T(2,128)S(1)}) fusion(f32[2,256,512]{2,1,0:T(8,128)S(1)} %get-tuple-element.27, f32[2,256,512]{2,1,0:T(8,128)S(1)} %bitcast.133, f32[2,256,512]{2,1,0:T(8,128)S(1)} %get-tuple-element.26, f32[2,256,512]{2,1,0:T(8,128)S(1)} %bitcast.132, ...), kind=kLoop, calls=%fused_computation.13 | loop fusion | flops 8388592 | bytes 8388672 | tf_op jit(solution)/shard_map/reduce_sum | solution.py:71
  50.8 0.0 copy-done.4
  50.8 0.1 reshape.260
  50.9 0.1 reshape.261
  51.0 0.1 maximum_maximum_fusion
  51.1 0.6 broadcast.20
  51.7 17.1 %all-to-all-start = ((f32[16,1,10]{2,1,0:T(1,128)}), f32[16,1,10]{2,1,0:T(1,128)S(1)}, u32[]{:S(2)}, u32[]{:S(2)}) async-start(f32[16,1,10]{2,1,0:T(1,128)} %bitcast.51), calls=%async_computation | async-start | bytes 16384 | tf_op jit(solution)/shard_map/all_to_all | solution.py:20
  68.8 2.8 %convolution_bitcast_fusion.1 = f32[2,2,512,512]{3,2,0,1:T(8,128)S(1)} fusion(bf16[2,512,512,1]{2,1,0,3:T(8,128)(2,1)} %bitcast.123, bf16[4,2,512,512]{3,2,1,0:T(8,128)(2,1)} %param.8, s32[]{:T(128)S(6)} %select_n.33), kind=kOutput, calls=%fused_computation.1 | convolution fusion | flops 1073741824 | bytes 6291460 | tf_op jit(solution)/shard_map/cri,kio->ckro/dot_general | solution.py:51
  71.6 0.5 slice_subtract_fusion.1
  72.1 2.2 %convert_bitcast_fusion = (bf16[1,2,2,256,512]{4,3,2,1,0:T(8,128)(2,1)}, f32[2,2,256,512]{3,2,1,0:T(8,128)}) fusion(f32[2,2,256,512]{3,2,1,0:T(8,128)S(1)} %fusion.1, f32[1,2,256,512]{3,2,1,0:T(8,128)S(1)} %bitcast.131, f32[1,2,256,512]{3,2,1,0:T(8,128)S(1)} %bitcast.130), kind=kLoop, calls=%fused_computation.35 | loop fusion | flops 1572864 | bytes 7340032 | tf_op jit(solution)/shard_map/broadcast_in_dim | solution.py:77
  74.3 0.9 %all-to-all-done = f32[16,1,10]{2,1,0:T(1,128)S(1)} async-done(((f32[16,1,10]{2,1,0:T(1,128)}), f32[16,1,10]{2,1,0:T(1,128)S(1)}, u32[]{:S(2)}, u32[]{:S(2)}) %all-to-all-start) | async-done | bytes 672 | tf_op jit(solution)/shard_map/all_to_all | solution.py:20
  75.2 0.0 copy-start.9
  75.2 0.6 copy-done.9
  75.8 3.0 %shard_map.86 = bf16[1,2,2,256,512]{4,3,2,1,0:T(8,128)(2,1)} custom-call(f32[16,10]{1,0:T(8,128)} %bitcast.137, f32[2,2,256,512]{3,2,1,0:T(8,128)} %get-tuple-element.11.image_ref, bf16[1,2,2,256,512]{4,3,2,1,0:T(8,128)(2,1)} %block_ref.1), custom_call_target="tpu_custom_call" | custom-call | tf_op jit(solution)/shard_map/pallas_call | solution.py:108
  (4 shorter events, 0.0 us)
Async XLA Ops:
  0.6 8.7 %copy-start = (bf16[128,128]{1,0:T(8,128)(2,1)S(1)}, bf16[128,128]{1,0:T(8,128)(2,1)}, u32[]{:S(2)}) copy-start(bf16[128,128]{1,0:T(8,128)(2,1)} %param.9) | copy-start | bytes 98308
  0.6 8.1 %copy-start.1 = (bf16[1,2,2,256,512]{4,3,2,1,0:T(8,128)(2,1)S(1)}, bf16[1,2,2,256,512]{4,3,2,1,0:T(8,128)(2,1)}, u32[]{:S(2)}) copy-start(bf16[1,2,2,256,512]{4,3,2,1,0:T(8,128)(2,1)} %block_ref.1) | copy-start | bytes 3145732
  0.7 24.5 %collective-permute-start.1 = (bf16[2,2,256,512]{3,2,1,0:T(8,128)(2,1)}, bf16[2,2,256,512]{3,2,1,0:T(8,128)(2,1)}, u32[]{:S(2)}, u32[]{:S(2)}) collective-permute-start(bf16[2,2,256,512]{3,2,1,0:T(8,128)(2,1)} %bitcast.120), channel_id=1, source_target_pairs={{0,1},{1,2},{2,3},{3,4},{4,5},{5,6},{6,7},{7,8},{8,9},{9,10},{10,1... | collective-permute-start | bytes 3145736 | tf_op jit(solution)/shard_map/ppermute | solution.py:12
  1.2 28.4 %collective-permute-start = (bf16[2,2,256,512]{3,2,1,0:T(8,128)(2,1)}, bf16[2,2,256,512]{3,2,1,0:T(8,128)(2,1)}, u32[]{:S(2)}, u32[]{:S(2)}) collective-permute-start(bf16[2,2,256,512]{3,2,1,0:T(8,128)(2,1)} %bitcast.121), channel_id=1, source_target_pairs={{0,15},{1,0},{2,1},{3,2},{4,3},{5,4},{6,5},{7,6},{8,7},{9,8},{10,9... | collective-permute-start | bytes 3145736 | tf_op jit(solution)/shard_map/ppermute | solution.py:12
  8.7 1.2 %copy-start.5 = (bf16[4096,128]{1,0:T(8,128)(2,1)S(1)}, bf16[4096,128]{1,0:T(8,128)(2,1)}, u32[]{:S(2)}) copy-start(bf16[4096,128]{1,0:T(8,128)(2,1)} %reshape_squeeze.6) | copy-start | bytes 3145732
  10.4 1.5 %copy-start.10 = (s32[4]{0:T(128)S(1)}, s32[4]{0:T(128)}, u32[]{:S(2)}) copy-start(s32[4]{0:T(128)} %param.12) | copy-start | bytes 52
  17.5 1.5 %copy-start.11 = (s32[2,2]{1,0:T(2,128)S(1)}, s32[2,2]{1,0:T(2,128)}, u32[]{:S(2)}) copy-start(s32[2,2]{1,0:T(2,128)} %param.11) | copy-start | bytes 52
  24.6 2.5 %copy-start.3 = (bf16[4,2,512,512]{3,2,1,0:T(8,128)(2,1)S(1)}, bf16[4,2,512,512]{3,2,1,0:T(8,128)(2,1)}, u32[]{:S(2)}) copy-start(bf16[4,2,512,512]{3,2,1,0:T(8,128)(2,1)} %param.8) | copy-start | bytes 12582916
  25.1 17.3 %collective-permute-start.2 = (bf16[2,2,256,512]{3,2,1,0:T(8,128)(2,1)}, bf16[2,2,256,512]{3,2,1,0:T(8,128)(2,1)S(1)}, u32[]{:S(2)}, u32[]{:S(2)}) collective-permute-start(bf16[2,2,256,512]{3,2,1,0:T(8,128)(2,1)} %collective-permute-done.1), channel_id=1, source_target_pairs={{0,1},{1,2},{2,3},{3,4},{4,5},{5,6},{6,7},{7,8},{8,9},{9,10},{10,1... | collective-permute-start | bytes 3145736 | tf_op jit(solution)/shard_map/ppermute | solution.py:12
  29.6 16.8 %collective-permute-start.3 = (bf16[2,2,256,512]{3,2,1,0:T(8,128)(2,1)}, bf16[2,2,256,512]{3,2,1,0:T(8,128)(2,1)S(1)}, u32[]{:S(2)}, u32[]{:S(2)}) collective-permute-start(bf16[2,2,256,512]{3,2,1,0:T(8,128)(2,1)} %collective-permute-done), channel_id=1, source_target_pairs={{0,15},{1,0},{2,1},{3,2},{4,3},{5,4},{6,5},{7,6},{8,7},{9,8},{10,9... | collective-permute-start | bytes 3145736 | tf_op jit(solution)/shard_map/ppermute | solution.py:12
  43.7 1.6 %copy-start.2 = (f32[2,2,256,512]{3,2,1,0:T(8,128)S(1)}, f32[2,2,256,512]{3,2,1,0:T(8,128)}, u32[]{:S(2)}) copy-start(f32[2,2,256,512]{3,2,1,0:T(8,128)} %reshape.243) | copy-start | bytes 6291460
  43.7 1.6 %copy-start.8 = (bf16[256,256]{1,0:T(8,128)(2,1)S(1)}, bf16[256,256]{1,0:T(8,128)(2,1)}, u32[]{:S(2)}) copy-start(bf16[256,256]{1,0:T(8,128)(2,1)} %param.10) | copy-start | bytes 393220
  46.4 1.6 %copy-start.6 = (f32[2,256,512]{2,1,0:T(8,128)S(1)}, f32[2,256,512]{2,1,0:T(8,128)}, u32[]{:S(2)}) copy-start(f32[2,256,512]{2,1,0:T(8,128)} %get-tuple-element.22) | copy-start | bytes 3145732
  46.4 1.9 %copy-start.7 = (f32[2,256,512]{2,1,0:T(8,128)S(1)}, f32[2,256,512]{2,1,0:T(8,128)}, u32[]{:S(2)}) copy-start(f32[2,256,512]{2,1,0:T(8,128)} %get-tuple-element.23) | copy-start | bytes 3145732
  46.4 4.4 %copy-start.4 = (bf16[2,2,256,512]{3,2,1,0:T(8,128)(2,1)}, bf16[2,2,256,512]{3,2,1,0:T(8,128)(2,1)S(1)}, u32[]{:S(2)}) copy-start(bf16[2,2,256,512]{3,2,1,0:T(8,128)(2,1)S(1)} %collective-permute-done.3) | copy-start | bytes 3145732
  51.7 23.5 %all-to-all-start = ((f32[16,1,10]{2,1,0:T(1,128)}), f32[16,1,10]{2,1,0:T(1,128)S(1)}, u32[]{:S(2)}, u32[]{:S(2)}) async-start(f32[16,1,10]{2,1,0:T(1,128)} %bitcast.51), calls=%async_computation | async-start | bytes 16384 | tf_op jit(solution)/shard_map/all_to_all | solution.py:20
  75.2 0.6 copy-start.9

commit v19 on v13

--- a/solution.py
+++ b/solution.py
@@ -40,7 +40,7 @@
     along_x = jnp.einsum("ab,cvbf->cvaf", masked, block, preferred_element_type=jnp.float32)
     centered = (position - harmonics // 2).astype(jnp.float32) + detuning[0]
     lam = -(centered * centered) / (4.0 * harmonics)
-    image = along_y + along_x + lam * block.astype(jnp.float32)
+    image = lax.optimization_barrier(along_y + along_x + lam * block.astype(jnp.float32))
     sources = (above_two, above_one, below_one, below_two)
     counter = jnp.arange(4, dtype=jnp.int32)
     for place in range(4):

time: 77.9 us -> 77.4 us (level)
  blocking collectives: 0 us -> 17.5 us
  waiting for transfers between devices: 16.1 us -> 4.92 us
  starting transfers between devices: 28.1 us -> 17.3 us
  matrix products: 8.81 us -> 11.1 us
  other arithmetic: 6.38 us -> 7.45 us
    all_to_all x0 -> x1, blocking collectives: none -> 17.5 us  [exchanged(): return lax.all_to_all(spread, axes, 0, 0, tiled=True)]
    all_to_all x1 -> x0, starting transfers between devices: 15.7 us -> none  [exchanged(): return lax.all_to_all(spread, axes, 0, 0, tiled=True)]
    ppermute x4, waiting for transfers between devices: 10.9 us -> 4.92 us  [passed_along(): return lax.ppermute(value, axis, pairs)]
    all_to_all x1 -> x0, waiting for transfers between devices: 5.22 us -> none  [exchanged(): return lax.all_to_all(spread, axes, 0, 0, tiled=True)]
    ppermute x4, starting transfers between devices: 12.3 us -> 17.3 us  [passed_along(): return lax.ppermute(value, axis, pairs)]
    dot_general x1, matrix products: 0.41 us -> 1.76 us  [body(): jnp.dot(rows, y_operator, preferred_element_type=jnp.float32)]
    broadcast_in_dim x1, other arithmetic: 1.1 us -> 2.28 us  [body(): return (image.astype(jnp.bfloat16)[None], projected)]
    unnamed x16 -> x14, local copies, waits for them, and re-layouts: 1.36 us -> 2.3 us
  transfers between devices with their start and end apart: 5 -> 4, of which waited for: 3 -> 1; matrix products, arithmetic and copies ran while one was open for 19% -> 22% of each run, Pallas kernels for 0% -> 0%
where the time goes in v19:
time: 77.4 us; the launch traced here: 77 us
  blocking collectives  17.5 us (23%)
  starting transfers between devices  17.3 us (22%)
  matrix products  11.1 us (14%)
  between operations  9.04 us (12%)
  other arithmetic  7.45 us (10%)
  local copies, waits for them, and re-layouts  6.68 us (9%)
  waiting for transfers between devices  4.92 us (6%)
  Pallas kernels  3.02 us (4%)
    all_to_all x1, blocking collectives, exchanged(): return lax.all_to_all(spread, axes, 0, 0, tiled=True)  17.5 us
    ppermute x4, starting transfers between devices, passed_along(): return lax.ppermute(value, axis, pairs)  17.3 us
    dot_general x4, matrix products, body(): jnp.einsum('cri,kio->ckro', other, matrix, preferred_element_type=jnp.flo...  7.52 us
    ppermute x4, waiting for transfers between devices, passed_along(): return lax.ppermute(value, axis, pairs)  4.92 us
    pallas_call x1, Pallas kernels, removed_projections(): pl.pallas_call(project_kernel, grid=(width_x // rows,), in_specs=[pl.Bloc...  3.02 us
    unnamed x14, local copies, waits for them, and re-layouts  2.3 us
    broadcast_in_dim x1, other arithmetic, body(): return (image.astype(jnp.bfloat16)[None], projected)  2.28 us
    sub x4, other arithmetic, body(): real_part = prod[0, 0] - prod[1, 1]  1.92 us
  transfers between devices with their start and end apart: 4, of which 1 were waited for; matrix products, arithmetic and copies ran while one was open for 22% of the time, Pallas kernels for 0%

profile of v19, /device:TPU:0, one launch (start us, length us, event | category | flops | bytes accessed | tf_op | source)
XLA Modules:
  0.0 77.0 jit_solution(5627965275278170546)
XLA Ops:
  0.6 0.0 copy-start
  0.6 5.5 %collective-permute-start = (bf16[2,2,256,512]{3,2,1,0:T(8,128)(2,1)}, bf16[2,2,256,512]{3,2,1,0:T(8,128)(2,1)}, u32[]{:S(2)}, u32[]{:S(2)}) collective-permute-start(bf16[2,2,256,512]{3,2,1,0:T(8,128)(2,1)} %bitcast.98), channel_id=1, source_target_pairs={{0,15},{1,0},{2,1},{3,2},{4,3},{5,4},{6,5},{7,6},{8,7},{9,8},{10,9... | collective-permute-start | bytes 3145736 | tf_op jit(solution)/shard_map/ppermute | solution.py:12
  6.1 0.0 collective-permute-start.2
  6.1 1.4 %fusion.22 = (s32[]{:T(128)}, s32[]{:T(128)}, s32[]{:T(128)}, s32[]{:T(128)}) fusion(s32[4]{0:T(128)} %param.12), kind=kLoop, calls=%fused_computation.48 | loop fusion | flops 44 | bytes 32 | tf_op jit(solution)/shard_map/reduce_sum | solution.py:47
  12.6 1.7 %reshape_squeeze.3 = bf16[4096,128]{1,0:T(8,128)(2,1)S(1)} reshape(bf16[1,2,2,256,512]{4,3,2,1,0:T(8,128)(2,1)} %block_ref.1) | data formatting | bytes 2097152 | tf_op jit(solution)/shard_map/reshape;squeeze | solution.py:36
  14.3 0.0 copy-done
  14.3 1.8 %fusion.25 = f32[4096,128]{1,0:T(8,128)} fusion(bf16[4096,128]{1,0:T(8,128)(2,1)S(1)} %reshape_squeeze.3, bf16[128,128]{1,0:T(8,128)(2,1)S(1)} %copy-done), kind=kOutput, calls=%fused_computation.52 | convolution fusion | flops 134217728 | bytes 3178496 | tf_op jit(solution)/shard_map/dot_general | solution.py:37
  16.0 0.0 copy-start.6
  16.0 0.0 copy-start.2
  16.0 0.0 copy-start.5
  16.0 1.8 %reshape.205 = f32[2,2,256,512]{3,2,1,0:T(8,128)S(1)} reshape(f32[4096,128]{1,0:T(8,128)} %fusion.25) | data formatting | bytes 4194304 | tf_op jit(solution)/shard_map/reshape | solution.py:37
  17.9 0.0 copy-done.6
  18.6 0.3 broadcast_in_dim.34
  18.9 0.0 copy-done.2
  18.9 0.0 copy-done.5
  18.9 1.8 %fusion.3 = f32[2,2,256,512]{3,2,1,0:T(8,128)} fusion(f32[2,2,256,512]{3,2,1,0:T(8,128)S(1)} %reshape.205, f32[]{:T(128)S(6)} %div.3, bf16[256,256]{1,0:T(8,128)(2,1)S(1)} %copy-done.5, bf16[32,8,2,128]{3,2,1,0:T(2,128)(2,1)S(1)} %bitcast.110, bf16[1,2,2,256,512]{4,3,2,1,0:T(8,128)(2,1)S(1)} %copy-done.2), kind=kOutput, calls=%fused_computation.9 | convolution fusion | flops 270794752 | bytes 5505028 | tf_op jit(solution)/shard_map/ab,cvbf->cvaf/dot_general | solution.py:40
  23.3 0.3 bitcast_convert_fusion
  23.6 0.3 add_reduce_fusion.1
  23.8 0.0 copy-start.4
  23.8 0.2 slice_bitcast_fusion.3
  24.0 0.0 collective-permute-done
  24.0 4.5 %collective-permute-start.1 = (bf16[2,2,256,512]{3,2,1,0:T(8,128)(2,1)}, bf16[2,2,256,512]{3,2,1,0:T(8,128)(2,1)S(1)}, u32[]{:S(2)}, u32[]{:S(2)}) collective-permute-start(bf16[2,2,256,512]{3,2,1,0:T(8,128)(2,1)} %collective-permute-done), channel_id=1, source_target_pairs={{0,15},{1,0},{2,1},{3,2},{4,3},{5,4},{6,5},{7,6},{8,7},{9,8},{10,9... | collective-permute-start | bytes 3145736 | tf_op jit(solution)/shard_map/ppermute | solution.py:12
  28.5 0.0 copy-done.4
  28.5 2.5 %convolution_bitcast_fusion.2 = f32[2,2,512,512]{3,2,0,1:T(8,128)S(1)} fusion(bf16[2,512,512,1]{2,1,0,3:T(8,128)(2,1)} %bitcast.18, bf16[4,2,512,512]{3,2,1,0:T(8,128)(2,1)S(1)} %copy-done.4, s32[]{:T(128)S(6)} %select_n.29), kind=kOutput, calls=%fused_computation.2 | convolution fusion | flops 1073741824 | bytes 6291460 | tf_op jit(solution)/shard_map/cri,kio->ckro/dot_general | solution.py:50
  31.0 0.0 collective-permute-done.2
  31.0 7.3 %collective-permute-start.3 = (bf16[2,2,256,512]{3,2,1,0:T(8,128)(2,1)}, bf16[2,2,256,512]{3,2,1,0:T(8,128)(2,1)S(1)}, u32[]{:S(2)}, u32[]{:S(2)}) collective-permute-start(bf16[2,2,256,512]{3,2,1,0:T(8,128)(2,1)} %collective-permute-done.2), channel_id=1, source_target_pairs={{0,1},{1,2},{2,3},{3,4},{4,5},{5,6},{6,7},{7,8},{8,9},{9,10},{10,1... | collective-permute-start | bytes 3145736 | tf_op jit(solution)/shard_map/ppermute | solution.py:12
  38.4 2.5 %convolution_bitcast_fusion.1 = f32[2,2,512,512]{3,2,0,1:T(8,128)S(1)} fusion(bf16[2,512,512,1]{2,1,0,3:T(8,128)(2,1)} %bitcast.26, bf16[4,2,512,512]{3,2,1,0:T(8,128)(2,1)S(1)} %copy-done.4, s32[]{:T(128)S(6)} %select_n.31), kind=kOutput, calls=%fused_computation.1 | convolution fusion | flops 1073741824 | bytes 6291460 | tf_op jit(solution)/shard_map/cri,kio->ckro/dot_general | solution.py:50
  40.9 0.5 slice_subtract_fusion.2
  41.4 0.5 slice_subtract_fusion.1
  41.8 0.0 collective-permute-done.1
  41.8 1.3 %convolution_bitcast_fusion.3 = f32[2,2,512,512]{3,2,0,1:T(8,128)S(1)} fusion(bf16[2,512,512,1]{2,1,0,3:T(8,128)(2,1)S(1)} %bitcast.109, bf16[4,2,512,512]{3,2,1,0:T(8,128)(2,1)S(1)} %copy-done.4, s32[]{:T(128)S(6)} %select_n.27), kind=kOutput, calls=%fused_computation.3 | convolution fusion | flops 1073741824 | bytes 6291460 | tf_op jit(solution)/shard_map/cri,kio->ckro/dot_general | solution.py:50
  43.1 0.5 slice_subtract_fusion.3
  43.6 4.9 %collective-permute-done.3 = bf16[2,2,256,512]{3,2,1,0:T(8,128)(2,1)S(1)} collective-permute-done((bf16[2,2,256,512]{3,2,1,0:T(8,128)(2,1)}, bf16[2,2,256,512]{3,2,1,0:T(8,128)(2,1)S(1)}, u32[]{:S(2)}, u32[]{:S(2)}) %collective-permute-start.3) | collective-permute-done | bytes 1048608 | tf_op jit(solution)/shard_map/ppermute | solution.py:12
  48.5 1.3 %convolution_bitcast_fusion = f32[2,2,512,512]{3,2,0,1:T(8,128)S(1)} fusion(bf16[2,512,512,1]{2,1,0,3:T(8,128)(2,1)S(1)} %bitcast.108, bf16[4,2,512,512]{3,2,1,0:T(8,128)(2,1)S(1)} %copy-done.4, s32[]{:T(128)S(6)} %select_n.33), kind=kOutput, calls=%fused_computation | convolution fusion | flops 1073741824 | bytes 6291460 | tf_op jit(solution)/shard_map/cri,kio->ckro/dot_general | solution.py:50
  49.8 0.0 copy-start.3
  49.8 0.5 slice_subtract_fusion
  50.3 1.1 %copy-done.3 = f32[2,2,256,512]{3,2,1,0:T(8,128)S(1)} copy-done((f32[2,2,256,512]{3,2,1,0:T(8,128)S(1)}, f32[2,2,256,512]{3,2,1,0:T(8,128)}, u32[]{:S(2)}) %copy-start.3) | copy-done | bytes 2097176
  51.4 2.3 %convert_bitcast_fusion = (bf16[1,2,2,256,512]{4,3,2,1,0:T(8,128)(2,1)}, f32[2,2,256,512]{3,2,1,0:T(8,128)S(1)}) fusion(f32[1,2,256,512]{3,2,1,0:T(8,128)S(1)} %bitcast.107, f32[1,2,256,512]{3,2,1,0:T(8,128)S(1)} %bitcast.106, f32[1,2,256,512]{3,2,1,0:T(8,128)S(1)} %bitcast.103, f32[1,2,256,512]{3,2,1,0:T(8,128)S(1)} %bitcast.102, ...), kind=kLoop, calls=%fused_computation.29 | loop fusion | flops 4718592 | bytes 13631488 | tf_op jit(solution)/shard_map/broadcast_in_dim | solution.py:64
  53.7 0.0 copy-start.1
  53.7 0.2 slice_bitcast_fusion.2
  53.8 1.2 %copy-done.1 = f32[2,2,256,512]{3,2,1,0:T(8,128)} copy-done((f32[2,2,256,512]{3,2,1,0:T(8,128)}, f32[2,2,256,512]{3,2,1,0:T(8,128)S(1)}, u32[]{:S(2)}) %copy-start.1) | copy-done | bytes 2097176
  55.0 1.3 %add_reduce_fusion = (f32[2,2]{1,0:T(2,128)S(1)}, f32[2,2]{1,0:T(2,128)S(1)}) fusion(f32[2,256,512]{2,1,0:T(8,128)S(1)} %get-tuple-element.21, f32[2,256,512]{2,1,0:T(8,128)S(1)} %get-tuple-element.19, f32[2,256,512]{2,1,0:T(8,128)S(1)} %get-tuple-element.20, f32[2,256,512]{2,1,0:T(8,128)S(1)} %get-tuple-element.18), kind=kLoop, calls=%fused_computation.11 | loop fusion | flops 4194296 | bytes 4194336 | tf_op jit(solution)/shard_map/reduce_sum | solution.py:59
  56.3 0.1 reshape.219
  56.3 0.1 reshape.220
  56.4 0.1 maximum_maximum_fusion
  56.5 17.5 %all_to_all.11 = f32[16,1,10]{2,1,0:T(1,128)} all-to-all(f32[16,1,10]{2,1,0:T(1,128)S(1)} %bitcast.113), channel_id=1, replica_groups=mesh['det'=2,'harm'=16] {'harm'}, dimensions={0} | all-to-all | bytes 1280 | tf_op jit(solution)/shard_map/all_to_all | solution.py:20
  74.0 3.0 %shard_map.86 = bf16[1,2,2,256,512]{4,3,2,1,0:T(8,128)(2,1)} custom-call(f32[16,10]{1,0:T(8,128)} %bitcast.112, f32[2,2,256,512]{3,2,1,0:T(8,128)} %copy-done.1, bf16[1,2,2,256,512]{4,3,2,1,0:T(8,128)(2,1)} %block_ref.1), custom_call_target="tpu_custom_call" | custom-call | tf_op jit(solution)/shard_map/pallas_call | solution.py:95
  (3 shorter events, 0.0 us)
Async XLA Ops:
  0.6 13.6 %copy-start = (bf16[128,128]{1,0:T(8,128)(2,1)S(1)}, bf16[128,128]{1,0:T(8,128)(2,1)}, u32[]{:S(2)}) copy-start(bf16[128,128]{1,0:T(8,128)(2,1)} %param.9) | copy-start | bytes 98308
  0.6 23.4 %collective-permute-start = (bf16[2,2,256,512]{3,2,1,0:T(8,128)(2,1)}, bf16[2,2,256,512]{3,2,1,0:T(8,128)(2,1)}, u32[]{:S(2)}, u32[]{:S(2)}) collective-permute-start(bf16[2,2,256,512]{3,2,1,0:T(8,128)(2,1)} %bitcast.98), channel_id=1, source_target_pairs={{0,15},{1,0},{2,1},{3,2},{4,3},{5,4},{6,5},{7,6},{8,7},{9,8},{10,9... | collective-permute-start | bytes 3145736 | tf_op jit(solution)/shard_map/ppermute | solution.py:12
  6.1 24.9 %collective-permute-start.2 = (bf16[2,2,256,512]{3,2,1,0:T(8,128)(2,1)}, bf16[2,2,256,512]{3,2,1,0:T(8,128)(2,1)}, u32[]{:S(2)}, u32[]{:S(2)}) collective-permute-start(bf16[2,2,256,512]{3,2,1,0:T(8,128)(2,1)} %bitcast.99), channel_id=1, source_target_pairs={{0,1},{1,2},{2,3},{3,4},{4,5},{5,6},{6,7},{7,8},{8,9},{9,10},{10,1... | collective-permute-start | bytes 3145736 | tf_op jit(solution)/shard_map/ppermute | solution.py:12
  16.0 1.8 %copy-start.6 = (s32[2,2]{1,0:T(2,128)S(1)}, s32[2,2]{1,0:T(2,128)}, u32[]{:S(2)}) copy-start(s32[2,2]{1,0:T(2,128)} %param.11) | copy-start | bytes 52
  16.0 2.9 %copy-start.2 = (bf16[1,2,2,256,512]{4,3,2,1,0:T(8,128)(2,1)S(1)}, bf16[1,2,2,256,512]{4,3,2,1,0:T(8,128)(2,1)}, u32[]{:S(2)}) copy-start(bf16[1,2,2,256,512]{4,3,2,1,0:T(8,128)(2,1)} %block_ref.1) | copy-start | bytes 3145732
  16.0 2.9 %copy-start.5 = (bf16[256,256]{1,0:T(8,128)(2,1)S(1)}, bf16[256,256]{1,0:T(8,128)(2,1)}, u32[]{:S(2)}) copy-start(bf16[256,256]{1,0:T(8,128)(2,1)} %param.10) | copy-start | bytes 393220
  23.8 4.7 %copy-start.4 = (bf16[4,2,512,512]{3,2,1,0:T(8,128)(2,1)S(1)}, bf16[4,2,512,512]{3,2,1,0:T(8,128)(2,1)}, u32[]{:S(2)}) copy-start(bf16[4,2,512,512]{3,2,1,0:T(8,128)(2,1)} %param.8) | copy-start | bytes 12582916
  24.0 17.8 %collective-permute-start.1 = (bf16[2,2,256,512]{3,2,1,0:T(8,128)(2,1)}, bf16[2,2,256,512]{3,2,1,0:T(8,128)(2,1)S(1)}, u32[]{:S(2)}, u32[]{:S(2)}) collective-permute-start(bf16[2,2,256,512]{3,2,1,0:T(8,128)(2,1)} %collective-permute-done), channel_id=1, source_target_pairs={{0,15},{1,0},{2,1},{3,2},{4,3},{5,4},{6,5},{7,6},{8,7},{9,8},{10,9... | collective-permute-start | bytes 3145736 | tf_op jit(solution)/shard_map/ppermute | solution.py:12
  31.0 17.5 %collective-permute-start.3 = (bf16[2,2,256,512]{3,2,1,0:T(8,128)(2,1)}, bf16[2,2,256,512]{3,2,1,0:T(8,128)(2,1)S(1)}, u32[]{:S(2)}, u32[]{:S(2)}) collective-permute-start(bf16[2,2,256,512]{3,2,1,0:T(8,128)(2,1)} %collective-permute-done.2), channel_id=1, source_target_pairs={{0,1},{1,2},{2,3},{3,4},{4,5},{5,6},{6,7},{7,8},{8,9},{9,10},{10,1... | collective-permute-start | bytes 3145736 | tf_op jit(solution)/shard_map/ppermute | solution.py:12
  49.8 1.6 %copy-start.3 = (f32[2,2,256,512]{3,2,1,0:T(8,128)S(1)}, f32[2,2,256,512]{3,2,1,0:T(8,128)}, u32[]{:S(2)}) copy-start(f32[2,2,256,512]{3,2,1,0:T(8,128)} %fusion.3) | copy-start | bytes 6291460
  53.7 1.4 %copy-start.1 = (f32[2,2,256,512]{3,2,1,0:T(8,128)}, f32[2,2,256,512]{3,2,1,0:T(8,128)S(1)}, u32[]{:S(2)}) copy-start(f32[2,2,256,512]{3,2,1,0:T(8,128)S(1)} %get-tuple-element.9.image_ref) | copy-start | bytes 6291460

commit v20 on v19

--- a/solution.py
+++ b/solution.py
@@ -60,11 +60,11 @@
     num_im = jnp.sum(qr[:, None] * wi[None, :] - qi[:, None] * wr[None, :], axis=(2, 3))
     norms = jnp.sum(qr * qr + qi * qi, axis=(1, 2))
     gathered = exchanged(("harm",), num_re, num_im, norms)
-    projected = removed_projections(gathered, image, perturbation)
-    return (image.astype(jnp.bfloat16)[None], projected)
+    rounded, projected = removed_projections(gathered, image, perturbation)
+    return (rounded, projected)
 
 
-def project_kernel(gathered_ref, image_ref, block_ref, out_ref):
+def project_kernel(gathered_ref, image_ref, block_ref, rounded_ref, out_ref):
     vecs = image_ref.shape[1]
     count, values = gathered_ref.shape
     totals = []
@@ -77,6 +77,8 @@
     for u in range(vecs):
         out_re = image_ref[0, u]
         out_im = image_ref[1, u]
+        rounded_ref[0, 0, u] = out_re.astype(rounded_ref.dtype)
+        rounded_ref[0, 1, u] = out_im.astype(rounded_ref.dtype)
         for v in range(vecs):
             scale = jnp.full((1, 1), totals[2 * vecs * vecs + v] + 1e-06, jnp.float32)
             a = jnp.full((1, 1), totals[v * vecs + u], jnp.float32) / scale
@@ -100,8 +102,14 @@
             pl.BlockSpec((parts, vecs, rows, width_fy), lambda i: (0, 0, i, 0)),
             pl.BlockSpec((1, parts, vecs, rows, width_fy), lambda i: (0, 0, 0, i, 0)),
         ],
-        out_specs=pl.BlockSpec((1, parts, vecs, rows, width_fy), lambda i: (0, 0, 0, i, 0)),
-        out_shape=jax.ShapeDtypeStruct(perturbation.shape, jnp.bfloat16),
+        out_specs=[
+            pl.BlockSpec((1, parts, vecs, rows, width_fy), lambda i: (0, 0, 0, i, 0)),
+            pl.BlockSpec((1, parts, vecs, rows, width_fy), lambda i: (0, 0, 0, i, 0)),
+        ],
+        out_shape=[
+            jax.ShapeDtypeStruct(perturbation.shape, jnp.bfloat16),
+            jax.ShapeDtypeStruct(perturbation.shape, jnp.bfloat16),
+        ],
     )(gathered, image, perturbation)
 
 

time: 77.4 us -> 76.7 us (level)
  other arithmetic: 7.45 us -> 6.57 us
    broadcast_in_dim x1 -> x0, other arithmetic: 2.28 us -> none  [body(): return (image.astype(jnp.bfloat16)[None], projected)]
    add x0 -> x1, other arithmetic: none -> 1.29 us  [body(): image = image + jnp.stack([real_part, imag_part]).reshape(block.shape)]
  transfers between devices with their start and end apart: 4 -> 4, of which waited for: 1 -> 1; matrix products, arithmetic and copies ran while one was open for 22% -> 23% of each run, Pallas kernels for 0% -> 0%
where the time goes in v20:
time: 76.7 us; the launch traced here: 76.3 us
  blocking collectives  17.3 us (23%)
  starting transfers between devices  17.1 us (22%)
  matrix products  11.1 us (14%)
  between operations  9.19 us (12%)
  local copies, waits for them, and re-layouts  6.72 us (9%)
  other arithmetic  6.57 us (9%)
  waiting for transfers between devices  5.14 us (7%)
  Pallas kernels  3.22 us (4%)
    all_to_all x1, blocking collectives, exchanged(): return lax.all_to_all(spread, axes, 0, 0, tiled=True)  17.3 us
    ppermute x4, starting transfers between devices, passed_along(): return lax.ppermute(value, axis, pairs)  17.1 us
    dot_general x4, matrix products, body(): jnp.einsum('cri,kio->ckro', other, matrix, preferred_element_type=jnp.flo...  7.52 us
    ppermute x4, waiting for transfers between devices, passed_along(): return lax.ppermute(value, axis, pairs)  5.14 us
    pallas_call x1, Pallas kernels, removed_projections(): pl.pallas_call(project_kernel, grid=(width_x // rows,), in_specs=[pl.Bloc...  3.22 us
    unnamed x14, local copies, waits for them, and re-layouts  2.24 us
    sub x4, other arithmetic, body(): real_part = prod[0, 0] - prod[1, 1]  1.92 us
    reshape x1, local copies, waits for them, and re-layouts, body(): jnp.dot(rows, y_operator, preferred_element_type=jnp.float32)  1.83 us
  transfers between devices with their start and end apart: 4, of which 1 were waited for; matrix products, arithmetic and copies ran while one was open for 23% of the time, Pallas kernels for 0%

profile of v20, /device:TPU:0, one launch (start us, length us, event | category | flops | bytes accessed | tf_op | source)
XLA Modules:
  0.0 76.3 jit_solution(13030766901493002825)
XLA Ops:
  0.6 0.0 copy-start
  0.6 5.5 %collective-permute-start = (bf16[2,2,256,512]{3,2,1,0:T(8,128)(2,1)}, bf16[2,2,256,512]{3,2,1,0:T(8,128)(2,1)}, u32[]{:S(2)}, u32[]{:S(2)}) collective-permute-start(bf16[2,2,256,512]{3,2,1,0:T(8,128)(2,1)} %bitcast.96), channel_id=1, source_target_pairs={{0,15},{1,0},{2,1},{3,2},{4,3},{5,4},{6,5},{7,6},{8,7},{9,8},{10,9... | collective-permute-start | bytes 3145736 | tf_op jit(solution)/shard_map/ppermute | solution.py:12
  6.1 0.0 collective-permute-start.2
  6.1 1.4 %fusion.22 = (s32[]{:T(128)}, s32[]{:T(128)}, s32[]{:T(128)}, s32[]{:T(128)}) fusion(s32[4]{0:T(128)} %param.12), kind=kLoop, calls=%fused_computation.47 | loop fusion | flops 44 | bytes 32 | tf_op jit(solution)/shard_map/reduce_sum | solution.py:47
  12.7 1.7 %reshape_squeeze.3 = bf16[4096,128]{1,0:T(8,128)(2,1)S(1)} reshape(bf16[1,2,2,256,512]{4,3,2,1,0:T(8,128)(2,1)} %block_ref.1) | data formatting | bytes 2097152 | tf_op jit(solution)/shard_map/reshape;squeeze | solution.py:36
  14.4 0.0 copy-done
  14.4 1.8 %fusion.24 = f32[4096,128]{1,0:T(8,128)} fusion(bf16[4096,128]{1,0:T(8,128)(2,1)S(1)} %reshape_squeeze.3, bf16[128,128]{1,0:T(8,128)(2,1)S(1)} %copy-done), kind=kOutput, calls=%fused_computation.51 | convolution fusion | flops 134217728 | bytes 3178496 | tf_op jit(solution)/shard_map/dot_general | solution.py:37
  16.2 0.0 copy-start.6
  16.2 0.0 copy-start.2
  16.2 0.0 copy-start.5
  16.2 1.8 %reshape.205 = f32[2,2,256,512]{3,2,1,0:T(8,128)S(1)} reshape(f32[4096,128]{1,0:T(8,128)} %fusion.24) | data formatting | bytes 4194304 | tf_op jit(solution)/shard_map/reshape | solution.py:37
  18.0 0.0 copy-done.6
  18.7 0.3 broadcast_in_dim.31
  19.1 0.0 copy-done.2
  19.1 0.0 copy-done.5
  19.1 1.8 %fusion.3 = f32[2,2,256,512]{3,2,1,0:T(8,128)} fusion(f32[2,2,256,512]{3,2,1,0:T(8,128)S(1)} %reshape.205, f32[]{:T(128)S(6)} %div.3, bf16[256,256]{1,0:T(8,128)(2,1)S(1)} %copy-done.5, bf16[32,8,2,128]{3,2,1,0:T(2,128)(2,1)S(1)} %bitcast.108, bf16[1,2,2,256,512]{4,3,2,1,0:T(8,128)(2,1)S(1)} %copy-done.2), kind=kOutput, calls=%fused_computation.9 | convolution fusion | flops 270794752 | bytes 5505028 | tf_op jit(solution)/shard_map/ab,cvbf->cvaf/dot_general | solution.py:40
  23.5 0.3 bitcast_convert_fusion
  23.7 0.3 add_reduce_fusion.1
  24.0 0.0 copy-start.4
  24.0 0.2 slice_bitcast_fusion.3
  24.2 0.0 collective-permute-done
  24.3 4.5 %collective-permute-start.1 = (bf16[2,2,256,512]{3,2,1,0:T(8,128)(2,1)}, bf16[2,2,256,512]{3,2,1,0:T(8,128)(2,1)S(1)}, u32[]{:S(2)}, u32[]{:S(2)}) collective-permute-start(bf16[2,2,256,512]{3,2,1,0:T(8,128)(2,1)} %collective-permute-done), channel_id=1, source_target_pairs={{0,15},{1,0},{2,1},{3,2},{4,3},{5,4},{6,5},{7,6},{8,7},{9,8},{10,9... | collective-permute-start | bytes 3145736 | tf_op jit(solution)/shard_map/ppermute | solution.py:12
  28.7 0.0 copy-done.4
  28.7 2.5 %convolution_bitcast_fusion.2 = f32[2,2,512,512]{3,2,0,1:T(8,128)S(1)} fusion(bf16[2,512,512,1]{2,1,0,3:T(8,128)(2,1)} %bitcast.19, bf16[4,2,512,512]{3,2,1,0:T(8,128)(2,1)S(1)} %copy-done.4, s32[]{:T(128)S(6)} %select_n.29), kind=kOutput, calls=%fused_computation.2 | convolution fusion | flops 1073741824 | bytes 6291460 | tf_op jit(solution)/shard_map/cri,kio->ckro/dot_general | solution.py:50
  31.3 0.0 collective-permute-done.2
  31.3 7.1 %collective-permute-start.3 = (bf16[2,2,256,512]{3,2,1,0:T(8,128)(2,1)}, bf16[2,2,256,512]{3,2,1,0:T(8,128)(2,1)S(1)}, u32[]{:S(2)}, u32[]{:S(2)}) collective-permute-start(bf16[2,2,256,512]{3,2,1,0:T(8,128)(2,1)} %collective-permute-done.2), channel_id=1, source_target_pairs={{0,1},{1,2},{2,3},{3,4},{4,5},{5,6},{6,7},{7,8},{8,9},{9,10},{10,1... | collective-permute-start | bytes 3145736 | tf_op jit(solution)/shard_map/ppermute | solution.py:12
  38.4 2.5 %convolution_bitcast_fusion.1 = f32[2,2,512,512]{3,2,0,1:T(8,128)S(1)} fusion(bf16[2,512,512,1]{2,1,0,3:T(8,128)(2,1)} %bitcast.27, bf16[4,2,512,512]{3,2,1,0:T(8,128)(2,1)S(1)} %copy-done.4, s32[]{:T(128)S(6)} %select_n.31), kind=kOutput, calls=%fused_computation.1 | convolution fusion | flops 1073741824 | bytes 6291460 | tf_op jit(solution)/shard_map/cri,kio->ckro/dot_general | solution.py:50
  40.9 0.5 slice_subtract_fusion.2
  41.4 0.5 slice_subtract_fusion.1
  41.8 0.0 collective-permute-done.1
  41.8 1.3 %convolution_bitcast_fusion.3 = f32[2,2,512,512]{3,2,0,1:T(8,128)S(1)} fusion(bf16[2,512,512,1]{2,1,0,3:T(8,128)(2,1)S(1)} %bitcast.107, bf16[4,2,512,512]{3,2,1,0:T(8,128)(2,1)S(1)} %copy-done.4, s32[]{:T(128)S(6)} %select_n.27), kind=kOutput, calls=%fused_computation.3 | convolution fusion | flops 1073741824 | bytes 6291460 | tf_op jit(solution)/shard_map/cri,kio->ckro/dot_general | solution.py:50
  43.1 0.5 slice_subtract_fusion.3
  43.6 5.1 %collective-permute-done.3 = bf16[2,2,256,512]{3,2,1,0:T(8,128)(2,1)S(1)} collective-permute-done((bf16[2,2,256,512]{3,2,1,0:T(8,128)(2,1)}, bf16[2,2,256,512]{3,2,1,0:T(8,128)(2,1)S(1)}, u32[]{:S(2)}, u32[]{:S(2)}) %collective-permute-start.3) | collective-permute-done | bytes 1048608 | tf_op jit(solution)/shard_map/ppermute | solution.py:12
  48.7 1.3 %convolution_bitcast_fusion = f32[2,2,512,512]{3,2,0,1:T(8,128)S(1)} fusion(bf16[2,512,512,1]{2,1,0,3:T(8,128)(2,1)S(1)} %bitcast.106, bf16[4,2,512,512]{3,2,1,0:T(8,128)(2,1)S(1)} %copy-done.4, s32[]{:T(128)S(6)} %select_n.33), kind=kOutput, calls=%fused_computation | convolution fusion | flops 1073741824 | bytes 6291460 | tf_op jit(solution)/shard_map/cri,kio->ckro/dot_general | solution.py:50
  50.0 0.0 copy-start.3
  50.0 0.5 slice_subtract_fusion
  50.5 1.1 %copy-done.3 = f32[2,2,256,512]{3,2,1,0:T(8,128)S(1)} copy-done((f32[2,2,256,512]{3,2,1,0:T(8,128)S(1)}, f32[2,2,256,512]{3,2,1,0:T(8,128)}, u32[]{:S(2)}) %copy-start.3) | copy-done | bytes 2097176
  51.6 1.3 %fusion.2.image_ref = f32[2,2,256,512]{3,2,1,0:T(8,128)S(1)} fusion(f32[2,2,256,512]{3,2,1,0:T(8,128)S(1)} %copy-done.3, f32[1,2,256,512]{3,2,1,0:T(8,128)S(1)} %bitcast.103, f32[1,2,256,512]{3,2,1,0:T(8,128)S(1)} %bitcast.102, f32[1,2,256,512]{3,2,1,0:T(8,128)S(1)} %bitcast.99, f32[1,2,256,512]{3,2,1,0:T(8,128)S(1)} %bitcast.98, ...), kind=kLoop, calls=%fused_computation.7 | loop fusion | flops 4194304 | bytes 12582912 | tf_op jit(solution)/shard_map/add | solution.py:53
  52.9 0.0 copy-start.1
  52.9 0.2 slice_bitcast_fusion.2
  53.1 1.1 %copy-done.1 = f32[2,2,256,512]{3,2,1,0:T(8,128)} copy-done((f32[2,2,256,512]{3,2,1,0:T(8,128)}, f32[2,2,256,512]{3,2,1,0:T(8,128)S(1)}, u32[]{:S(2)}) %copy-start.1) | copy-done | bytes 2097176
  54.2 1.3 %add_reduce_fusion = (f32[2,2]{1,0:T(2,128)S(1)}, f32[2,2]{1,0:T(2,128)S(1)}) fusion(f32[2,256,512]{2,1,0:T(8,128)S(1)} %get-tuple-element.19, f32[2,256,512]{2,1,0:T(8,128)S(1)} %get-tuple-element.17, f32[2,256,512]{2,1,0:T(8,128)S(1)} %get-tuple-element.18, f32[2,256,512]{2,1,0:T(8,128)S(1)} %get-tuple-element.16), kind=kLoop, calls=%fused_computation.11 | loop fusion | flops 4194296 | bytes 4194336 | tf_op jit(solution)/shard_map/reduce_sum | solution.py:59
  55.6 0.1 reshape.219
  55.6 0.1 reshape.220
  55.7 0.1 maximum_maximum_fusion
  55.8 17.3 %all_to_all.11 = f32[16,1,10]{2,1,0:T(1,128)} all-to-all(f32[16,1,10]{2,1,0:T(1,128)S(1)} %bitcast.111), channel_id=1, replica_groups=mesh['det'=2,'harm'=16] {'harm'}, dimensions={0} | all-to-all | bytes 1280 | tf_op jit(solution)/shard_map/all_to_all | solution.py:20
  73.1 3.2 %shard_map.86 = (bf16[1,2,2,256,512]{4,3,2,1,0:T(8,128)(2,1)}, bf16[1,2,2,256,512]{4,3,2,1,0:T(8,128)(2,1)}) custom-call(f32[16,10]{1,0:T(8,128)} %bitcast.110, f32[2,2,256,512]{3,2,1,0:T(8,128)} %copy-done.1, bf16[1,2,2,256,512]{4,3,2,1,0:T(8,128)(2,1)} %block_ref.1), custom_call_target="tpu_custom_call" | custom-call | tf_op jit(solution)/shard_map/pallas_call | solution.py:97
  (3 shorter events, 0.0 us)
Async XLA Ops:
  0.6 13.8 %copy-start = (bf16[128,128]{1,0:T(8,128)(2,1)S(1)}, bf16[128,128]{1,0:T(8,128)(2,1)}, u32[]{:S(2)}) copy-start(bf16[128,128]{1,0:T(8,128)(2,1)} %param.9) | copy-start | bytes 98308
  0.6 23.6 %collective-permute-start = (bf16[2,2,256,512]{3,2,1,0:T(8,128)(2,1)}, bf16[2,2,256,512]{3,2,1,0:T(8,128)(2,1)}, u32[]{:S(2)}, u32[]{:S(2)}) collective-permute-start(bf16[2,2,256,512]{3,2,1,0:T(8,128)(2,1)} %bitcast.96), channel_id=1, source_target_pairs={{0,15},{1,0},{2,1},{3,2},{4,3},{5,4},{6,5},{7,6},{8,7},{9,8},{10,9... | collective-permute-start | bytes 3145736 | tf_op jit(solution)/shard_map/ppermute | solution.py:12
  6.1 25.1 %collective-permute-start.2 = (bf16[2,2,256,512]{3,2,1,0:T(8,128)(2,1)}, bf16[2,2,256,512]{3,2,1,0:T(8,128)(2,1)}, u32[]{:S(2)}, u32[]{:S(2)}) collective-permute-start(bf16[2,2,256,512]{3,2,1,0:T(8,128)(2,1)} %bitcast.97), channel_id=1, source_target_pairs={{0,1},{1,2},{2,3},{3,4},{4,5},{5,6},{6,7},{7,8},{8,9},{9,10},{10,1... | collective-permute-start | bytes 3145736 | tf_op jit(solution)/shard_map/ppermute | solution.py:12
  16.2 1.8 %copy-start.6 = (s32[2,2]{1,0:T(2,128)S(1)}, s32[2,2]{1,0:T(2,128)}, u32[]{:S(2)}) copy-start(s32[2,2]{1,0:T(2,128)} %param.11) | copy-start | bytes 52
  16.2 2.9 %copy-start.2 = (bf16[1,2,2,256,512]{4,3,2,1,0:T(8,128)(2,1)S(1)}, bf16[1,2,2,256,512]{4,3,2,1,0:T(8,128)(2,1)}, u32[]{:S(2)}) copy-start(bf16[1,2,2,256,512]{4,3,2,1,0:T(8,128)(2,1)} %block_ref.1) | copy-start | bytes 3145732
  16.2 2.9 %copy-start.5 = (bf16[256,256]{1,0:T(8,128)(2,1)S(1)}, bf16[256,256]{1,0:T(8,128)(2,1)}, u32[]{:S(2)}) copy-start(bf16[256,256]{1,0:T(8,128)(2,1)} %param.10) | copy-start | bytes 393220
  24.0 4.7 %copy-start.4 = (bf16[4,2,512,512]{3,2,1,0:T(8,128)(2,1)S(1)}, bf16[4,2,512,512]{3,2,1,0:T(8,128)(2,1)}, u32[]{:S(2)}) copy-start(bf16[4,2,512,512]{3,2,1,0:T(8,128)(2,1)} %param.8) | copy-start | bytes 12582916
  24.3 17.6 %collective-permute-start.1 = (bf16[2,2,256,512]{3,2,1,0:T(8,128)(2,1)}, bf16[2,2,256,512]{3,2,1,0:T(8,128)(2,1)S(1)}, u32[]{:S(2)}, u32[]{:S(2)}) collective-permute-start(bf16[2,2,256,512]{3,2,1,0:T(8,128)(2,1)} %collective-permute-done), channel_id=1, source_target_pairs={{0,15},{1,0},{2,1},{3,2},{4,3},{5,4},{6,5},{7,6},{8,7},{9,8},{10,9... | collective-permute-start | bytes 3145736 | tf_op jit(solution)/shard_map/ppermute | solution.py:12
  31.3 17.5 %collective-permute-start.3 = (bf16[2,2,256,512]{3,2,1,0:T(8,128)(2,1)}, bf16[2,2,256,512]{3,2,1,0:T(8,128)(2,1)S(1)}, u32[]{:S(2)}, u32[]{:S(2)}) collective-permute-start(bf16[2,2,256,512]{3,2,1,0:T(8,128)(2,1)} %collective-permute-done.2), channel_id=1, source_target_pairs={{0,1},{1,2},{2,3},{3,4},{4,5},{5,6},{6,7},{7,8},{8,9},{9,10},{10,1... | collective-permute-start | bytes 3145736 | tf_op jit(solution)/shard_map/ppermute | solution.py:12
  50.0 1.6 %copy-start.3 = (f32[2,2,256,512]{3,2,1,0:T(8,128)S(1)}, f32[2,2,256,512]{3,2,1,0:T(8,128)}, u32[]{:S(2)}) copy-start(f32[2,2,256,512]{3,2,1,0:T(8,128)} %fusion.3) | copy-start | bytes 6291460
  52.9 1.4 %copy-start.1 = (f32[2,2,256,512]{3,2,1,0:T(8,128)}, f32[2,2,256,512]{3,2,1,0:T(8,128)S(1)}, u32[]{:S(2)}) copy-start(f32[2,2,256,512]{3,2,1,0:T(8,128)S(1)} %fusion.2.image_ref) | copy-start | bytes 6291460

commit v21 on v19

--- a/solution.py
+++ b/solution.py
@@ -60,8 +60,9 @@
     num_im = jnp.sum(qr[:, None] * wi[None, :] - qi[:, None] * wr[None, :], axis=(2, 3))
     norms = jnp.sum(qr * qr + qi * qi, axis=(1, 2))
     gathered = exchanged(("harm",), num_re, num_im, norms)
+    rounded = rounded_image(image)
     projected = removed_projections(gathered, image, perturbation)
-    return (image.astype(jnp.bfloat16)[None], projected)
+    return (rounded, projected)
 
 
 def project_kernel(gathered_ref, image_ref, block_ref, out_ref):
@@ -105,6 +106,22 @@
     )(gathered, image, perturbation)
 
 
+def round_kernel(image_ref, out_ref):
+    out_ref[0] = image_ref[...].astype(out_ref.dtype)
+
+
+def rounded_image(image):
+    parts, vecs, width_x, width_fy = image.shape
+    rows = 128 if width_x % 128 == 0 else width_x
+    return pl.pallas_call(
+        round_kernel,
+        grid=(width_x // rows,),
+        in_specs=[pl.BlockSpec((parts, vecs, rows, width_fy), lambda i: (0, 0, i, 0))],
+        out_specs=pl.BlockSpec((1, parts, vecs, rows, width_fy), lambda i: (0, 0, 0, i, 0)),
+        out_shape=jax.ShapeDtypeStruct((1,) + image.shape, jnp.bfloat16),
+    )(image)
+
+
 def solution(mesh):
     in_specs = (P(("det", "harm"), None, None, None, None), P(), P(), P(), P(), P(), P("det"))
     out_specs = (

time: 77.4 us -> 77.9 us (level)
  blocking collectives: 17.5 us -> 0 us
  starting transfers between devices: 17.3 us -> 28.9 us
  waiting for transfers between devices: 4.92 us -> 8.72 us
  Pallas kernels: 3.02 us -> 5.42 us
  local copies, waits for them, and re-layouts: 6.68 us -> 7.9 us
  other arithmetic: 7.45 us -> 6.53 us
    all_to_all x1 -> x0, blocking collectives: 17.5 us -> none  [exchanged(): return lax.all_to_all(spread, axes, 0, 0, tiled=True)]
    all_to_all x0 -> x1, starting transfers between devices: none -> 11.5 us  [exchanged(): return lax.all_to_all(spread, axes, 0, 0, tiled=True)]
    all_to_all x0 -> x1, waiting for transfers between devices: none -> 3.92 us  [exchanged(): return lax.all_to_all(spread, axes, 0, 0, tiled=True)]
    pallas_call x0 -> x1, Pallas kernels: none -> 2.41 us  [rounded_image(): pl.pallas_call(round_kernel, grid=(width_x // rows,), in_specs=[pl.BlockS...]
    broadcast_in_dim x1 -> x0, other arithmetic: 2.28 us -> none  [body(): return (image.astype(jnp.bfloat16)[None], projected)]
    add x0 -> x1, other arithmetic: none -> 1.29 us  [body(): image = image + jnp.stack([real_part, imag_part]).reshape(block.shape)]
    unnamed x14 -> x16, local copies, waits for them, and re-layouts: 2.3 us -> 2.82 us
  transfers between devices with their start and end apart: 4 -> 5, of which waited for: 1 -> 2; matrix products, arithmetic and copies ran while one was open for 22% -> 22% of each run, Pallas kernels for 0% -> 3%
where the time goes in v21:
time: 77.9 us; the launch traced here: 77.5 us
  starting transfers between devices  28.9 us (37%)
  matrix products  11.1 us (14%)
  between operations  8.9 us (11%)
  waiting for transfers between devices  8.72 us (11%)
  local copies, waits for them, and re-layouts  7.9 us (10%)
  other arithmetic  6.53 us (8%)
  Pallas kernels  5.42 us (7%)
    ppermute x4, starting transfers between devices, passed_along(): return lax.ppermute(value, axis, pairs)  17.5 us
    all_to_all x1, starting transfers between devices, exchanged(): return lax.all_to_all(spread, axes, 0, 0, tiled=True)  11.5 us
    dot_general x4, matrix products, body(): jnp.einsum('cri,kio->ckro', other, matrix, preferred_element_type=jnp.flo...  7.52 us
    ppermute x4, waiting for transfers between devices, passed_along(): return lax.ppermute(value, axis, pairs)  4.79 us
    all_to_all x1, waiting for transfers between devices, exchanged(): return lax.all_to_all(spread, axes, 0, 0, tiled=True)  3.92 us
    pallas_call x1, Pallas kernels, removed_projections(): pl.pallas_call(project_kernel, grid=(width_x // rows,), in_specs=[pl.Bloc...  3.02 us
    unnamed x16, local copies, waits for them, and re-layouts  2.82 us
    pallas_call x1, Pallas kernels, rounded_image(): pl.pallas_call(round_kernel, grid=(width_x // rows,), in_specs=[pl.BlockS...  2.41 us
  transfers between devices with their start and end apart: 5, of which 2 were waited for; matrix products, arithmetic and copies ran while one was open for 22% of the time, Pallas kernels for 3%

profile of v21, /device:TPU:0, one launch (start us, length us, event | category | flops | bytes accessed | tf_op | source)
XLA Modules:
  0.0 77.5 jit_solution(14022930206530870352)
XLA Ops:
  0.6 0.0 copy-start
  0.6 5.5 %collective-permute-start = (bf16[2,2,256,512]{3,2,1,0:T(8,128)(2,1)}, bf16[2,2,256,512]{3,2,1,0:T(8,128)(2,1)}, u32[]{:S(2)}, u32[]{:S(2)}) collective-permute-start(bf16[2,2,256,512]{3,2,1,0:T(8,128)(2,1)} %bitcast.96), channel_id=1, source_target_pairs={{0,15},{1,0},{2,1},{3,2},{4,3},{5,4},{6,5},{7,6},{8,7},{9,8},{10,9... | collective-permute-start | bytes 3145736 | tf_op jit(solution)/shard_map/ppermute | solution.py:12
  6.1 0.0 collective-permute-start.2
  6.1 1.4 %fusion.22 = (s32[]{:T(128)}, s32[]{:T(128)}, s32[]{:T(128)}, s32[]{:T(128)}) fusion(s32[4]{0:T(128)} %param.12), kind=kLoop, calls=%fused_computation.47 | loop fusion | flops 44 | bytes 32 | tf_op jit(solution)/shard_map/reduce_sum | solution.py:47
  12.4 1.7 %reshape_squeeze.3 = bf16[4096,128]{1,0:T(8,128)(2,1)S(1)} reshape(bf16[1,2,2,256,512]{4,3,2,1,0:T(8,128)(2,1)} %block_ref.1) | data formatting | bytes 2097152 | tf_op jit(solution)/shard_map/reshape;squeeze | solution.py:36
  14.2 0.0 copy-done
  14.2 1.8 %fusion.24 = f32[4096,128]{1,0:T(8,128)} fusion(bf16[4096,128]{1,0:T(8,128)(2,1)S(1)} %reshape_squeeze.3, bf16[128,128]{1,0:T(8,128)(2,1)S(1)} %copy-done), kind=kOutput, calls=%fused_computation.51 | convolution fusion | flops 134217728 | bytes 3178496 | tf_op jit(solution)/shard_map/dot_general | solution.py:37
  15.9 0.0 copy-start.7
  15.9 0.0 copy-start.2
  15.9 0.0 copy-start.5
  15.9 1.8 %reshape.205 = f32[2,2,256,512]{3,2,1,0:T(8,128)S(1)} reshape(f32[4096,128]{1,0:T(8,128)} %fusion.24) | data formatting | bytes 4194304 | tf_op jit(solution)/shard_map/reshape | solution.py:37
  17.8 0.0 copy-done.7
  18.5 0.3 broadcast_in_dim.31
  18.8 0.0 copy-done.2
  18.8 0.0 copy-done.5
  18.8 1.8 %fusion.3 = f32[2,2,256,512]{3,2,1,0:T(8,128)} fusion(f32[2,2,256,512]{3,2,1,0:T(8,128)S(1)} %reshape.205, f32[]{:T(128)S(6)} %div.3, bf16[256,256]{1,0:T(8,128)(2,1)S(1)} %copy-done.5, bf16[32,8,2,128]{3,2,1,0:T(2,128)(2,1)S(1)} %bitcast.108, bf16[1,2,2,256,512]{4,3,2,1,0:T(8,128)(2,1)S(1)} %copy-done.2), kind=kOutput, calls=%fused_computation.9 | convolution fusion | flops 270794752 | bytes 5505028 | tf_op jit(solution)/shard_map/ab,cvbf->cvaf/dot_general | solution.py:40
  23.1 0.3 bitcast_convert_fusion
  23.4 0.3 add_reduce_fusion.1
  23.7 0.0 copy-start.4
  23.7 0.2 slice_bitcast_fusion.3
  23.9 0.0 collective-permute-done
  23.9 4.5 %collective-permute-start.1 = (bf16[2,2,256,512]{3,2,1,0:T(8,128)(2,1)}, bf16[2,2,256,512]{3,2,1,0:T(8,128)(2,1)S(1)}, u32[]{:S(2)}, u32[]{:S(2)}) collective-permute-start(bf16[2,2,256,512]{3,2,1,0:T(8,128)(2,1)} %collective-permute-done), channel_id=1, source_target_pairs={{0,15},{1,0},{2,1},{3,2},{4,3},{5,4},{6,5},{7,6},{8,7},{9,8},{10,9... | collective-permute-start | bytes 3145736 | tf_op jit(solution)/shard_map/ppermute | solution.py:12
  28.4 0.0 copy-done.4
  28.4 2.5 %convolution_bitcast_fusion.2 = f32[2,2,512,512]{3,2,0,1:T(8,128)S(1)} fusion(bf16[2,512,512,1]{2,1,0,3:T(8,128)(2,1)} %bitcast.18, bf16[4,2,512,512]{3,2,1,0:T(8,128)(2,1)S(1)} %copy-done.4, s32[]{:T(128)S(6)} %select_n.29), kind=kOutput, calls=%fused_computation.2 | convolution fusion | flops 1073741824 | bytes 6291460 | tf_op jit(solution)/shard_map/cri,kio->ckro/dot_general | solution.py:50
  30.9 0.0 collective-permute-done.2
  30.9 7.5 %collective-permute-start.3 = (bf16[2,2,256,512]{3,2,1,0:T(8,128)(2,1)}, bf16[2,2,256,512]{3,2,1,0:T(8,128)(2,1)S(1)}, u32[]{:S(2)}, u32[]{:S(2)}) collective-permute-start(bf16[2,2,256,512]{3,2,1,0:T(8,128)(2,1)} %collective-permute-done.2), channel_id=1, source_target_pairs={{0,1},{1,2},{2,3},{3,4},{4,5},{5,6},{6,7},{7,8},{8,9},{9,10},{10,1... | collective-permute-start | bytes 3145736 | tf_op jit(solution)/shard_map/ppermute | solution.py:12
  38.4 2.5 %convolution_bitcast_fusion.1 = f32[2,2,512,512]{3,2,0,1:T(8,128)S(1)} fusion(bf16[2,512,512,1]{2,1,0,3:T(8,128)(2,1)} %bitcast.26, bf16[4,2,512,512]{3,2,1,0:T(8,128)(2,1)S(1)} %copy-done.4, s32[]{:T(128)S(6)} %select_n.31), kind=kOutput, calls=%fused_computation.1 | convolution fusion | flops 1073741824 | bytes 6291460 | tf_op jit(solution)/shard_map/cri,kio->ckro/dot_general | solution.py:50
  40.9 0.5 slice_subtract_fusion.2
  41.4 0.5 slice_subtract_fusion.1
  41.8 0.0 collective-permute-done.1
  41.8 1.3 %convolution_bitcast_fusion.3 = f32[2,2,512,512]{3,2,0,1:T(8,128)S(1)} fusion(bf16[2,512,512,1]{2,1,0,3:T(8,128)(2,1)S(1)} %bitcast.107, bf16[4,2,512,512]{3,2,1,0:T(8,128)(2,1)S(1)} %copy-done.4, s32[]{:T(128)S(6)} %select_n.27), kind=kOutput, calls=%fused_computation.3 | convolution fusion | flops 1073741824 | bytes 6291460 | tf_op jit(solution)/shard_map/cri,kio->ckro/dot_general | solution.py:50
  43.1 0.5 slice_subtract_fusion.3
  43.6 4.8 %collective-permute-done.3 = bf16[2,2,256,512]{3,2,1,0:T(8,128)(2,1)S(1)} collective-permute-done((bf16[2,2,256,512]{3,2,1,0:T(8,128)(2,1)}, bf16[2,2,256,512]{3,2,1,0:T(8,128)(2,1)S(1)}, u32[]{:S(2)}, u32[]{:S(2)}) %collective-permute-start.3) | collective-permute-done | bytes 1048608 | tf_op jit(solution)/shard_map/ppermute | solution.py:12
  48.4 1.3 %convolution_bitcast_fusion = f32[2,2,512,512]{3,2,0,1:T(8,128)S(1)} fusion(bf16[2,512,512,1]{2,1,0,3:T(8,128)(2,1)S(1)} %bitcast.106, bf16[4,2,512,512]{3,2,1,0:T(8,128)(2,1)S(1)} %copy-done.4, s32[]{:T(128)S(6)} %select_n.33), kind=kOutput, calls=%fused_computation | convolution fusion | flops 1073741824 | bytes 6291460 | tf_op jit(solution)/shard_map/cri,kio->ckro/dot_general | solution.py:50
  49.7 0.0 copy-start.3
  49.7 0.5 slice_subtract_fusion
  50.2 1.1 %copy-done.3 = f32[2,2,256,512]{3,2,1,0:T(8,128)S(1)} copy-done((f32[2,2,256,512]{3,2,1,0:T(8,128)S(1)}, f32[2,2,256,512]{3,2,1,0:T(8,128)}, u32[]{:S(2)}) %copy-start.3) | copy-done | bytes 2097176
  51.2 1.3 %fusion.2.image_ref = f32[2,2,256,512]{3,2,1,0:T(8,128)S(1)} fusion(f32[2,2,256,512]{3,2,1,0:T(8,128)S(1)} %copy-done.3, f32[1,2,256,512]{3,2,1,0:T(8,128)S(1)} %bitcast.103, f32[1,2,256,512]{3,2,1,0:T(8,128)S(1)} %bitcast.102, f32[1,2,256,512]{3,2,1,0:T(8,128)S(1)} %bitcast.99, f32[1,2,256,512]{3,2,1,0:T(8,128)S(1)} %bitcast.98, ...), kind=kLoop, calls=%fused_computation.7 | loop fusion | flops 4194304 | bytes 12582912 | tf_op jit(solution)/shard_map/add | solution.py:53
  52.5 0.0 copy-start.1
  52.6 0.2 slice_bitcast_fusion.2
  52.8 1.1 %copy-done.1 = f32[2,2,256,512]{3,2,1,0:T(8,128)} copy-done((f32[2,2,256,512]{3,2,1,0:T(8,128)}, f32[2,2,256,512]{3,2,1,0:T(8,128)S(1)}, u32[]{:S(2)}) %copy-start.1) | copy-done | bytes 2097176
  53.9 1.3 %add_reduce_fusion = (f32[2,2]{1,0:T(2,128)S(1)}, f32[2,2]{1,0:T(2,128)S(1)}) fusion(f32[2,256,512]{2,1,0:T(8,128)S(1)} %get-tuple-element.19, f32[2,256,512]{2,1,0:T(8,128)S(1)} %get-tuple-element.17, f32[2,256,512]{2,1,0:T(8,128)S(1)} %get-tuple-element.18, f32[2,256,512]{2,1,0:T(8,128)S(1)} %get-tuple-element.16), kind=kLoop, calls=%fused_computation.11 | loop fusion | flops 4194296 | bytes 4194336 | tf_op jit(solution)/shard_map/reduce_sum | solution.py:59
  55.2 0.1 reshape.219
  55.3 0.1 reshape.220
  55.4 0.1 maximum_maximum_fusion
  55.4 0.6 broadcast.23
  56.1 11.5 %all-to-all-start = ((f32[16,1,10]{2,1,0:T(1,128)}), f32[16,1,10]{2,1,0:T(1,128)S(1)}, u32[]{:S(2)}, u32[]{:S(2)}) async-start(f32[16,1,10]{2,1,0:T(1,128)} %bitcast.42), calls=%async_computation | async-start | bytes 16384 | tf_op jit(solution)/shard_map/all_to_all | solution.py:20
  67.5 2.4 %shard_map.86 = bf16[1,2,2,256,512]{4,3,2,1,0:T(8,128)(2,1)} custom-call(f32[2,2,256,512]{3,2,1,0:T(8,128)} %copy-done.1), custom_call_target="tpu_custom_call" | custom-call | tf_op jit(solution)/shard_map/pallas_call | solution.py:116
  69.9 3.9 %all-to-all-done = f32[16,1,10]{2,1,0:T(1,128)S(1)} async-done(((f32[16,1,10]{2,1,0:T(1,128)}), f32[16,1,10]{2,1,0:T(1,128)S(1)}, u32[]{:S(2)}, u32[]{:S(2)}) %all-to-all-start) | async-done | bytes 672 | tf_op jit(solution)/shard_map/all_to_all | solution.py:20
  73.8 0.0 copy-start.6
  73.8 0.6 copy-done.6
  74.4 3.0 %shard_map.87 = bf16[1,2,2,256,512]{4,3,2,1,0:T(8,128)(2,1)} custom-call(f32[16,10]{1,0:T(8,128)} %bitcast.110, f32[2,2,256,512]{3,2,1,0:T(8,128)} %copy-done.1, bf16[1,2,2,256,512]{4,3,2,1,0:T(8,128)(2,1)} %block_ref.1), custom_call_target="tpu_custom_call" | custom-call | tf_op jit(solution)/shard_map/pallas_call | solution.py:96
  (2 shorter events, 0.0 us)
Async XLA Ops:
  0.6 13.5 %copy-start = (bf16[128,128]{1,0:T(8,128)(2,1)S(1)}, bf16[128,128]{1,0:T(8,128)(2,1)}, u32[]{:S(2)}) copy-start(bf16[128,128]{1,0:T(8,128)(2,1)} %param.9) | copy-start | bytes 98308
  0.6 23.2 %collective-permute-start = (bf16[2,2,256,512]{3,2,1,0:T(8,128)(2,1)}, bf16[2,2,256,512]{3,2,1,0:T(8,128)(2,1)}, u32[]{:S(2)}, u32[]{:S(2)}) collective-permute-start(bf16[2,2,256,512]{3,2,1,0:T(8,128)(2,1)} %bitcast.96), channel_id=1, source_target_pairs={{0,15},{1,0},{2,1},{3,2},{4,3},{5,4},{6,5},{7,6},{8,7},{9,8},{10,9... | collective-permute-start | bytes 3145736 | tf_op jit(solution)/shard_map/ppermute | solution.py:12
  6.1 24.8 %collective-permute-start.2 = (bf16[2,2,256,512]{3,2,1,0:T(8,128)(2,1)}, bf16[2,2,256,512]{3,2,1,0:T(8,128)(2,1)}, u32[]{:S(2)}, u32[]{:S(2)}) collective-permute-start(bf16[2,2,256,512]{3,2,1,0:T(8,128)(2,1)} %bitcast.97), channel_id=1, source_target_pairs={{0,1},{1,2},{2,3},{3,4},{4,5},{5,6},{6,7},{7,8},{8,9},{9,10},{10,1... | collective-permute-start | bytes 3145736 | tf_op jit(solution)/shard_map/ppermute | solution.py:12
  15.9 1.8 %copy-start.7 = (s32[2,2]{1,0:T(2,128)S(1)}, s32[2,2]{1,0:T(2,128)}, u32[]{:S(2)}) copy-start(s32[2,2]{1,0:T(2,128)} %param.11) | copy-start | bytes 52
  15.9 2.9 %copy-start.2 = (bf16[1,2,2,256,512]{4,3,2,1,0:T(8,128)(2,1)S(1)}, bf16[1,2,2,256,512]{4,3,2,1,0:T(8,128)(2,1)}, u32[]{:S(2)}) copy-start(bf16[1,2,2,256,512]{4,3,2,1,0:T(8,128)(2,1)} %block_ref.1) | copy-start | bytes 3145732
  15.9 2.9 %copy-start.5 = (bf16[256,256]{1,0:T(8,128)(2,1)S(1)}, bf16[256,256]{1,0:T(8,128)(2,1)}, u32[]{:S(2)}) copy-start(bf16[256,256]{1,0:T(8,128)(2,1)} %param.10) | copy-start | bytes 393220
  23.7 4.7 %copy-start.4 = (bf16[4,2,512,512]{3,2,1,0:T(8,128)(2,1)S(1)}, bf16[4,2,512,512]{3,2,1,0:T(8,128)(2,1)}, u32[]{:S(2)}) copy-start(bf16[4,2,512,512]{3,2,1,0:T(8,128)(2,1)} %param.8) | copy-start | bytes 12582916
  23.9 17.9 %collective-permute-start.1 = (bf16[2,2,256,512]{3,2,1,0:T(8,128)(2,1)}, bf16[2,2,256,512]{3,2,1,0:T(8,128)(2,1)S(1)}, u32[]{:S(2)}, u32[]{:S(2)}) collective-permute-start(bf16[2,2,256,512]{3,2,1,0:T(8,128)(2,1)} %collective-permute-done), channel_id=1, source_target_pairs={{0,15},{1,0},{2,1},{3,2},{4,3},{5,4},{6,5},{7,6},{8,7},{9,8},{10,9... | collective-permute-start | bytes 3145736 | tf_op jit(solution)/shard_map/ppermute | solution.py:12
  30.9 17.5 %collective-permute-start.3 = (bf16[2,2,256,512]{3,2,1,0:T(8,128)(2,1)}, bf16[2,2,256,512]{3,2,1,0:T(8,128)(2,1)S(1)}, u32[]{:S(2)}, u32[]{:S(2)}) collective-permute-start(bf16[2,2,256,512]{3,2,1,0:T(8,128)(2,1)} %collective-permute-done.2), channel_id=1, source_target_pairs={{0,1},{1,2},{2,3},{3,4},{4,5},{5,6},{6,7},{7,8},{8,9},{9,10},{10,1... | collective-permute-start | bytes 3145736 | tf_op jit(solution)/shard_map/ppermute | solution.py:12
  49.7 1.6 %copy-start.3 = (f32[2,2,256,512]{3,2,1,0:T(8,128)S(1)}, f32[2,2,256,512]{3,2,1,0:T(8,128)}, u32[]{:S(2)}) copy-start(f32[2,2,256,512]{3,2,1,0:T(8,128)} %fusion.3) | copy-start | bytes 6291460
  52.5 1.3 %copy-start.1 = (f32[2,2,256,512]{3,2,1,0:T(8,128)}, f32[2,2,256,512]{3,2,1,0:T(8,128)S(1)}, u32[]{:S(2)}) copy-start(f32[2,2,256,512]{3,2,1,0:T(8,128)S(1)} %fusion.2.image_ref) | copy-start | bytes 6291460
  56.1 17.8 %all-to-all-start = ((f32[16,1,10]{2,1,0:T(1,128)}), f32[16,1,10]{2,1,0:T(1,128)S(1)}, u32[]{:S(2)}, u32[]{:S(2)}) async-start(f32[16,1,10]{2,1,0:T(1,128)} %bitcast.42), calls=%async_computation | async-start | bytes 16384 | tf_op jit(solution)/shard_map/all_to_all | solution.py:20
  73.8 0.6 copy-start.6

commit v22 on v20

--- a/solution.py
+++ b/solution.py
@@ -56,8 +56,13 @@
     qi = qfull[1]
     wr = image[0]
     wi = image[1]
-    num_re = jnp.sum(qr[:, None] * wr[None, :] + qi[:, None] * wi[None, :], axis=(2, 3))
-    num_im = jnp.sum(qr[:, None] * wi[None, :] - qi[:, None] * wr[None, :], axis=(2, 3))
+    groups = 8 if width_x % 8 == 0 else 1
+    split = (vecs, vecs, groups, width_x // groups, width_fy)
+    part_re = jnp.sum((qr[:, None] * wr[None, :] + qi[:, None] * wi[None, :]).reshape(split), axis=(3, 4))
+    part_im = jnp.sum((qr[:, None] * wi[None, :] - qi[:, None] * wr[None, :]).reshape(split), axis=(3, 4))
+    part_re, part_im = lax.optimization_barrier((part_re, part_im))
+    num_re = jnp.sum(part_re, axis=2)
+    num_im = jnp.sum(part_im, axis=2)
     norms = jnp.sum(qr * qr + qi * qi, axis=(1, 2))
     gathered = exchanged(("harm",), num_re, num_im, norms)
     rounded, projected = removed_projections(gathered, image, perturbation)

time: 76.7 us -> 76.4 us (level)
  waiting for transfers between devices: 5.14 us -> 4.13 us
  blocking collectives: 17.3 us -> 18.3 us
  other arithmetic: 6.57 us -> 5.74 us
  starting transfers between devices: 17.1 us -> 17.9 us
    all_to_all x1, blocking collectives: 17.3 us -> 18.3 us  [exchanged(): return lax.all_to_all(spread, axes, 0, 0, tiled=True)]
    ppermute x4, waiting for transfers between devices: 5.14 us -> 4.13 us  [passed_along(): return lax.ppermute(value, axis, pairs)]
    ppermute x4, starting transfers between devices: 17.1 us -> 17.9 us  [passed_along(): return lax.ppermute(value, axis, pairs)]
    reduce_sum x2 -> x3, other arithmetic: 1.59 us -> 1.02 us  [the longest x1 0.84 us: body(): jnp.sum((qr[:, None] * wi[None, :] - qi[:, None] * wr[None, :]).reshape(s...]
    unnamed x14 -> x16, local copies, waits for them, and re-layouts: 2.24 us -> 2.29 us
  transfers between devices with their start and end apart: 4 -> 4, of which waited for: 1 -> 1; matrix products, arithmetic and copies ran while one was open for 23% -> 22% of each run, Pallas kernels for 0% -> 0%
where the time goes in v22:
time: 76.4 us; the launch traced here: 76 us
  blocking collectives  18.3 us (24%)
  starting transfers between devices  17.9 us (23%)
  matrix products  11.1 us (15%)
  between operations  9.05 us (12%)
  local copies, waits for them, and re-layouts  6.54 us (9%)
  other arithmetic  5.74 us (8%)
  waiting for transfers between devices  4.13 us (5%)
  Pallas kernels  3.22 us (4%)
    all_to_all x1, blocking collectives, exchanged(): return lax.all_to_all(spread, axes, 0, 0, tiled=True)  18.3 us
    ppermute x4, starting transfers between devices, passed_along(): return lax.ppermute(value, axis, pairs)  17.9 us
    dot_general x4, matrix products, body(): jnp.einsum('cri,kio->ckro', other, matrix, preferred_element_type=jnp.flo...  7.52 us
    ppermute x4, waiting for transfers between devices, passed_along(): return lax.ppermute(value, axis, pairs)  4.13 us
    pallas_call x1, Pallas kernels, removed_projections(): pl.pallas_call(project_kernel, grid=(width_x // rows,), in_specs=[pl.Bloc...  3.22 us
    unnamed x16, local copies, waits for them, and re-layouts  2.29 us
    sub x4, other arithmetic, body(): real_part = prod[0, 0] - prod[1, 1]  1.92 us
    reshape x1, local copies, waits for them, and re-layouts, body(): jnp.dot(rows, y_operator, preferred_element_type=jnp.float32)  1.83 us
  transfers between devices with their start and end apart: 4, of which 1 were waited for; matrix products, arithmetic and copies ran while one was open for 22% of the time, Pallas kernels for 0%

profile of v22, /device:TPU:0, one launch (start us, length us, event | category | flops | bytes accessed | tf_op | source)
XLA Modules:
  0.0 76.0 jit_solution(16458610241629940976)
XLA Ops:
  0.6 0.0 copy-start
  0.6 5.5 %collective-permute-start = (bf16[2,2,256,512]{3,2,1,0:T(8,128)(2,1)}, bf16[2,2,256,512]{3,2,1,0:T(8,128)(2,1)}, u32[]{:S(2)}, u32[]{:S(2)}) collective-permute-start(bf16[2,2,256,512]{3,2,1,0:T(8,128)(2,1)} %bitcast.88), channel_id=1, source_target_pairs={{0,15},{1,0},{2,1},{3,2},{4,3},{5,4},{6,5},{7,6},{8,7},{9,8},{10,9... | collective-permute-start | bytes 3145736 | tf_op jit(solution)/shard_map/ppermute | solution.py:12
  6.1 0.0 collective-permute-start.2
  6.1 1.7 %reshape_squeeze.3 = bf16[4096,128]{1,0:T(8,128)(2,1)S(1)} reshape(bf16[1,2,2,256,512]{4,3,2,1,0:T(8,128)(2,1)} %block_ref.1) | data formatting | bytes 2097152 | tf_op jit(solution)/shard_map/reshape;squeeze | solution.py:36
  7.9 0.0 copy-done
  7.9 1.8 %fusion.26 = f32[4096,128]{1,0:T(8,128)} fusion(bf16[4096,128]{1,0:T(8,128)(2,1)S(1)} %reshape_squeeze.3, bf16[128,128]{1,0:T(8,128)(2,1)S(1)} %copy-done), kind=kOutput, calls=%fused_computation.49 | convolution fusion | flops 134217728 | bytes 3178496 | tf_op jit(solution)/shard_map/dot_general | solution.py:37
  9.7 0.0 copy-start.7
  9.7 0.0 copy-start.2
  9.7 0.0 copy-start.5
  9.7 1.8 %reshape.226 = f32[2,2,256,512]{3,2,1,0:T(8,128)S(1)} reshape(f32[4096,128]{1,0:T(8,128)} %fusion.26) | data formatting | bytes 4194304 | tf_op jit(solution)/shard_map/reshape | solution.py:37
  11.5 0.0 copy-done.7
  12.2 0.3 broadcast_in_dim.31
  12.5 0.0 copy-done.2
  12.5 0.0 copy-done.5
  12.6 0.0 copy-start.6
  12.6 1.8 %fusion.3 = f32[2,2,256,512]{3,2,1,0:T(8,128)} fusion(f32[2,2,256,512]{3,2,1,0:T(8,128)S(1)} %reshape.226, f32[]{:T(128)S(6)} %div.3, bf16[256,256]{1,0:T(8,128)(2,1)S(1)} %copy-done.5, bf16[32,8,2,128]{3,2,1,0:T(2,128)(2,1)S(1)} %bitcast.104, bf16[1,2,2,256,512]{4,3,2,1,0:T(8,128)(2,1)S(1)} %copy-done.2), kind=kOutput, calls=%fused_computation.9 | convolution fusion | flops 270794752 | bytes 5505028 | tf_op jit(solution)/shard_map/ab,cvbf->cvaf/dot_general | solution.py:40
  14.4 0.0 copy-done.6
  14.4 0.7 fusion.22
  22.6 0.3 bitcast_convert_fusion
  22.9 0.0 copy-start.4
  22.9 0.5 fusion.24
  23.4 0.0 collective-permute-done
  23.4 4.5 %collective-permute-start.1 = (bf16[2,2,256,512]{3,2,1,0:T(8,128)(2,1)}, bf16[2,2,256,512]{3,2,1,0:T(8,128)(2,1)S(1)}, u32[]{:S(2)}, u32[]{:S(2)}) collective-permute-start(bf16[2,2,256,512]{3,2,1,0:T(8,128)(2,1)} %collective-permute-done), channel_id=1, source_target_pairs={{0,15},{1,0},{2,1},{3,2},{4,3},{5,4},{6,5},{7,6},{8,7},{9,8},{10,9... | collective-permute-start | bytes 3145736 | tf_op jit(solution)/shard_map/ppermute | solution.py:12
  27.9 0.0 copy-done.4
  27.9 2.5 %convolution_bitcast_fusion.2 = f32[2,2,512,512]{3,2,0,1:T(8,128)S(1)} fusion(bf16[2,512,512,1]{2,1,0,3:T(8,128)(2,1)} %bitcast.19, bf16[4,2,512,512]{3,2,1,0:T(8,128)(2,1)S(1)} %copy-done.4, s32[]{:T(128)S(6)} %select_n.29), kind=kOutput, calls=%fused_computation.2 | convolution fusion | flops 1073741824 | bytes 6291460 | tf_op jit(solution)/shard_map/cri,kio->ckro/dot_general | solution.py:50
  30.4 0.0 collective-permute-done.2
  30.4 7.9 %collective-permute-start.3 = (bf16[2,2,256,512]{3,2,1,0:T(8,128)(2,1)}, bf16[2,2,256,512]{3,2,1,0:T(8,128)(2,1)S(1)}, u32[]{:S(2)}, u32[]{:S(2)}) collective-permute-start(bf16[2,2,256,512]{3,2,1,0:T(8,128)(2,1)} %collective-permute-done.2), channel_id=1, source_target_pairs={{0,1},{1,2},{2,3},{3,4},{4,5},{5,6},{6,7},{7,8},{8,9},{9,10},{10,1... | collective-permute-start | bytes 3145736 | tf_op jit(solution)/shard_map/ppermute | solution.py:12
  38.4 2.5 %convolution_bitcast_fusion.1 = f32[2,2,512,512]{3,2,0,1:T(8,128)S(1)} fusion(bf16[2,512,512,1]{2,1,0,3:T(8,128)(2,1)} %bitcast.27, bf16[4,2,512,512]{3,2,1,0:T(8,128)(2,1)S(1)} %copy-done.4, s32[]{:T(128)S(6)} %select_n.31), kind=kOutput, calls=%fused_computation.1 | convolution fusion | flops 1073741824 | bytes 6291460 | tf_op jit(solution)/shard_map/cri,kio->ckro/dot_general | solution.py:50
  40.9 0.5 slice_subtract_fusion.2
  41.4 0.5 slice_subtract_fusion.1
  41.8 0.0 collective-permute-done.1
  41.8 1.3 %convolution_bitcast_fusion.3 = f32[2,2,512,512]{3,2,0,1:T(8,128)S(1)} fusion(bf16[2,512,512,1]{2,1,0,3:T(8,128)(2,1)S(1)} %bitcast.103, bf16[4,2,512,512]{3,2,1,0:T(8,128)(2,1)S(1)} %copy-done.4, s32[]{:T(128)S(6)} %select_n.27), kind=kOutput, calls=%fused_computation.3 | convolution fusion | flops 1073741824 | bytes 6291460 | tf_op jit(solution)/shard_map/cri,kio->ckro/dot_general | solution.py:50
  43.1 0.5 slice_subtract_fusion.3
  43.6 4.1 %collective-permute-done.3 = bf16[2,2,256,512]{3,2,1,0:T(8,128)(2,1)S(1)} collective-permute-done((bf16[2,2,256,512]{3,2,1,0:T(8,128)(2,1)}, bf16[2,2,256,512]{3,2,1,0:T(8,128)(2,1)S(1)}, u32[]{:S(2)}, u32[]{:S(2)}) %collective-permute-start.3) | collective-permute-done | bytes 1048608 | tf_op jit(solution)/shard_map/ppermute | solution.py:12
  47.7 1.3 %convolution_bitcast_fusion = f32[2,2,512,512]{3,2,0,1:T(8,128)S(1)} fusion(bf16[2,512,512,1]{2,1,0,3:T(8,128)(2,1)S(1)} %bitcast.102, bf16[4,2,512,512]{3,2,1,0:T(8,128)(2,1)S(1)} %copy-done.4, s32[]{:T(128)S(6)} %select_n.33), kind=kOutput, calls=%fused_computation | convolution fusion | flops 1073741824 | bytes 6291460 | tf_op jit(solution)/shard_map/cri,kio->ckro/dot_general | solution.py:50
  49.0 0.0 copy-start.3
  49.0 0.5 slice_subtract_fusion
  49.5 1.1 %copy-done.3 = f32[2,2,256,512]{3,2,1,0:T(8,128)S(1)} copy-done((f32[2,2,256,512]{3,2,1,0:T(8,128)S(1)}, f32[2,2,256,512]{3,2,1,0:T(8,128)}, u32[]{:S(2)}) %copy-start.3) | copy-done | bytes 2097176
  50.6 1.3 %fusion.2.image_ref = f32[2,2,256,512]{3,2,1,0:T(8,128)S(1)} fusion(f32[2,2,256,512]{3,2,1,0:T(8,128)S(1)} %copy-done.3, f32[1,2,256,512]{3,2,1,0:T(8,128)S(1)} %bitcast.97, f32[1,2,256,512]{3,2,1,0:T(8,128)S(1)} %bitcast.96, f32[1,2,256,512]{3,2,1,0:T(8,128)S(1)} %bitcast.93, f32[1,2,256,512]{3,2,1,0:T(8,128)S(1)} %bitcast.92, ...), kind=kLoop, calls=%fused_computation.7 | loop fusion | flops 4194304 | bytes 12582912 | tf_op jit(solution)/shard_map/add | solution.py:53
  51.9 0.0 copy-start.1
  51.9 0.2 fusion.25
  52.1 1.2 %copy-done.1 = f32[2,2,256,512]{3,2,1,0:T(8,128)} copy-done((f32[2,2,256,512]{3,2,1,0:T(8,128)}, f32[2,2,256,512]{3,2,1,0:T(8,128)S(1)}, u32[]{:S(2)}) %copy-start.1) | copy-done | bytes 2097176
  53.2 0.8 %subtract_reduce_fusion = (f32[2,2,8]{2,1,0:T(2,128)S(1)}, f32[2,2,8]{2,1,0:T(2,128)S(1)}) fusion(f32[2,8,32,512]{3,2,1,0:T(8,128)S(1)} %bitcast.101, f32[2,8,32,512]{3,2,1,0:T(8,128)S(1)} %bitcast.91, f32[2,8,32,512]{3,2,1,0:T(8,128)S(1)} %bitcast.100, f32[2,8,32,512]{3,2,1,0:T(8,128)S(1)} %bitcast.90), kind=kLoop, calls=%fused_computation.10 | loop fusion | flops 4194240 | bytes 4194560 | tf_op jit(solution)/shard_map/reduce_sum | solution.py:62
  54.1 0.1 reduce_sum.87
  54.2 0.1 reshape.240
  54.3 0.1 reduce_sum.88
  54.3 0.1 reshape.241
  54.4 0.1 maximum_maximum_fusion
  54.5 18.3 %all_to_all.11 = f32[16,1,10]{2,1,0:T(1,128)} all-to-all(f32[16,1,10]{2,1,0:T(1,128)S(1)} %bitcast.107), channel_id=1, replica_groups=mesh['det'=2,'harm'=16] {'harm'}, dimensions={0} | all-to-all | bytes 1280 | tf_op jit(solution)/shard_map/all_to_all | solution.py:20
  72.8 3.2 %shard_map.86 = (bf16[1,2,2,256,512]{4,3,2,1,0:T(8,128)(2,1)}, bf16[1,2,2,256,512]{4,3,2,1,0:T(8,128)(2,1)}) custom-call(f32[16,10]{1,0:T(8,128)} %bitcast.106, f32[2,2,256,512]{3,2,1,0:T(8,128)} %copy-done.1, bf16[1,2,2,256,512]{4,3,2,1,0:T(8,128)(2,1)} %block_ref.1), custom_call_target="tpu_custom_call" | custom-call | tf_op jit(solution)/shard_map/pallas_call | solution.py:102
  (3 shorter events, 0.0 us)
Async XLA Ops:
  0.6 7.3 %copy-start = (bf16[128,128]{1,0:T(8,128)(2,1)S(1)}, bf16[128,128]{1,0:T(8,128)(2,1)}, u32[]{:S(2)}) copy-start(bf16[128,128]{1,0:T(8,128)(2,1)} %param.9) | copy-start | bytes 98308
  0.6 22.8 %collective-permute-start = (bf16[2,2,256,512]{3,2,1,0:T(8,128)(2,1)}, bf16[2,2,256,512]{3,2,1,0:T(8,128)(2,1)}, u32[]{:S(2)}, u32[]{:S(2)}) collective-permute-start(bf16[2,2,256,512]{3,2,1,0:T(8,128)(2,1)} %bitcast.88), channel_id=1, source_target_pairs={{0,15},{1,0},{2,1},{3,2},{4,3},{5,4},{6,5},{7,6},{8,7},{9,8},{10,9... | collective-permute-start | bytes 3145736 | tf_op jit(solution)/shard_map/ppermute | solution.py:12
  6.1 24.3 %collective-permute-start.2 = (bf16[2,2,256,512]{3,2,1,0:T(8,128)(2,1)}, bf16[2,2,256,512]{3,2,1,0:T(8,128)(2,1)}, u32[]{:S(2)}, u32[]{:S(2)}) collective-permute-start(bf16[2,2,256,512]{3,2,1,0:T(8,128)(2,1)} %bitcast.89), channel_id=1, source_target_pairs={{0,1},{1,2},{2,3},{3,4},{4,5},{5,6},{6,7},{7,8},{8,9},{9,10},{10,1... | collective-permute-start | bytes 3145736 | tf_op jit(solution)/shard_map/ppermute | solution.py:12
  9.7 1.8 %copy-start.7 = (s32[2,2]{1,0:T(2,128)S(1)}, s32[2,2]{1,0:T(2,128)}, u32[]{:S(2)}) copy-start(s32[2,2]{1,0:T(2,128)} %param.11) | copy-start | bytes 52
  9.7 2.9 %copy-start.2 = (bf16[1,2,2,256,512]{4,3,2,1,0:T(8,128)(2,1)S(1)}, bf16[1,2,2,256,512]{4,3,2,1,0:T(8,128)(2,1)}, u32[]{:S(2)}) copy-start(bf16[1,2,2,256,512]{4,3,2,1,0:T(8,128)(2,1)} %block_ref.1) | copy-start | bytes 3145732
  9.7 2.9 %copy-start.5 = (bf16[256,256]{1,0:T(8,128)(2,1)S(1)}, bf16[256,256]{1,0:T(8,128)(2,1)}, u32[]{:S(2)}) copy-start(bf16[256,256]{1,0:T(8,128)(2,1)} %param.10) | copy-start | bytes 393220
  12.6 1.8 %copy-start.6 = (s32[4]{0:T(128)S(1)}, s32[4]{0:T(128)}, u32[]{:S(2)}) copy-start(s32[4]{0:T(128)} %param.12) | copy-start | bytes 52
  22.9 5.0 %copy-start.4 = (bf16[4,2,512,512]{3,2,1,0:T(8,128)(2,1)S(1)}, bf16[4,2,512,512]{3,2,1,0:T(8,128)(2,1)}, u32[]{:S(2)}) copy-start(bf16[4,2,512,512]{3,2,1,0:T(8,128)(2,1)} %param.8) | copy-start | bytes 12582916
  23.4 18.4 %collective-permute-start.1 = (bf16[2,2,256,512]{3,2,1,0:T(8,128)(2,1)}, bf16[2,2,256,512]{3,2,1,0:T(8,128)(2,1)S(1)}, u32[]{:S(2)}, u32[]{:S(2)}) collective-permute-start(bf16[2,2,256,512]{3,2,1,0:T(8,128)(2,1)} %collective-permute-done), channel_id=1, source_target_pairs={{0,15},{1,0},{2,1},{3,2},{4,3},{5,4},{6,5},{7,6},{8,7},{9,8},{10,9... | collective-permute-start | bytes 3145736 | tf_op jit(solution)/shard_map/ppermute | solution.py:12
  30.4 17.3 %collective-permute-start.3 = (bf16[2,2,256,512]{3,2,1,0:T(8,128)(2,1)}, bf16[2,2,256,512]{3,2,1,0:T(8,128)(2,1)S(1)}, u32[]{:S(2)}, u32[]{:S(2)}) collective-permute-start(bf16[2,2,256,512]{3,2,1,0:T(8,128)(2,1)} %collective-permute-done.2), channel_id=1, source_target_pairs={{0,1},{1,2},{2,3},{3,4},{4,5},{5,6},{6,7},{7,8},{8,9},{9,10},{10,1... | collective-permute-start | bytes 3145736 | tf_op jit(solution)/shard_map/ppermute | solution.py:12
  49.0 1.6 %copy-start.3 = (f32[2,2,256,512]{3,2,1,0:T(8,128)S(1)}, f32[2,2,256,512]{3,2,1,0:T(8,128)}, u32[]{:S(2)}) copy-start(f32[2,2,256,512]{3,2,1,0:T(8,128)} %fusion.3) | copy-start | bytes 6291460
  51.9 1.4 %copy-start.1 = (f32[2,2,256,512]{3,2,1,0:T(8,128)}, f32[2,2,256,512]{3,2,1,0:T(8,128)S(1)}, u32[]{:S(2)}) copy-start(f32[2,2,256,512]{3,2,1,0:T(8,128)S(1)} %fusion.2.image_ref) | copy-start | bytes 6291460

commit v23 on v22

--- a/solution.py
+++ b/solution.py
@@ -65,8 +65,16 @@
     num_im = jnp.sum(part_im, axis=2)
     norms = jnp.sum(qr * qr + qi * qi, axis=(1, 2))
     gathered = exchanged(("harm",), num_re, num_im, norms)
-    rounded, projected = removed_projections(gathered, image, perturbation)
-    return (rounded, projected)
+    totals = jnp.sum(gathered, axis=0)
+    square = vecs * vecs
+    h_re = (totals[:square].reshape(vecs, vecs) / (totals[2 * square:] + 1e-06)[:, None])
+    h_im = (totals[square:2 * square].reshape(vecs, vecs) / (totals[2 * square:] + 1e-06)[:, None])
+    turned = jnp.stack([-qi, qr])
+    projected = image
+    for vec in range(vecs):
+        projected = projected - (h_re[vec, :, None, None] * qfull[:, vec][:, None]
+                                 + h_im[vec, :, None, None] * turned[:, vec][:, None])
+    return (image.astype(jnp.bfloat16)[None], projected.astype(jnp.bfloat16)[None])
 
 
 def project_kernel(gathered_ref, image_ref, block_ref, rounded_ref, out_ref):

time: 76.4 us -> 79.5 us (1.041)
  blocking collectives: 18.3 us -> 0 us
  waiting for transfers between devices: 4.13 us -> 15.6 us
  other arithmetic: 5.74 us -> 14.7 us
  Pallas kernels: 3.22 us -> 0 us
  starting transfers between devices: 17.9 us -> 20.5 us
  local copies, waits for them, and re-layouts: 6.54 us -> 8.08 us
    all_to_all x1 -> x0, blocking collectives: 18.3 us -> none  [exchanged(): return lax.all_to_all(spread, axes, 0, 0, tiled=True)]
    all_to_all x0 -> x1, starting transfers between devices: none -> 10.5 us  [exchanged(): return lax.all_to_all(spread, axes, 0, 0, tiled=True)]
    ppermute x4, starting transfers between devices: 17.9 us -> 10 us  [passed_along(): return lax.ppermute(value, axis, pairs)]
    ppermute x4, waiting for transfers between devices: 4.13 us -> 12 us  [passed_along(): return lax.ppermute(value, axis, pairs)]
    broadcast_in_dim x0 -> x2, other arithmetic: none -> 6.29 us  [the longest x1 4.03 us: body(): projected.astype(jnp.bfloat16)[None]]
    all_to_all x0 -> x1, waiting for transfers between devices: none -> 3.61 us  [exchanged(): return lax.all_to_all(spread, axes, 0, 0, tiled=True)]
    pallas_call x1 -> x0, Pallas kernels: 3.22 us -> none  [removed_projections(): pl.pallas_call(project_kernel, grid=(width_x // rows,), in_specs=[pl.Bloc...]
    mul x0 -> x1, other arithmetic: none -> 2.78 us  [body(): h_im[vec, :, None, None] * turned[:, vec][:, None]]
  transfers between devices with their start and end apart: 4 -> 5, of which waited for: 1 -> 3; matrix products, arithmetic and copies ran while one was open for 22% -> 28% of each run, Pallas kernels for 0% -> 0%
where the time goes in v23:
time: 79.5 us; the launch traced here: 79 us
  starting transfers between devices  20.5 us (26%)
  waiting for transfers between devices  15.6 us (20%)
  other arithmetic  14.7 us (18%)
  matrix products  11.1 us (14%)
  between operations  9.03 us (11%)
  local copies, waits for them, and re-layouts  8.08 us (10%)
    ppermute x4, waiting for transfers between devices, passed_along(): return lax.ppermute(value, axis, pairs)  12 us
    all_to_all x1, starting transfers between devices, exchanged(): return lax.all_to_all(spread, axes, 0, 0, tiled=True)  10.5 us
    ppermute x4, starting transfers between devices, passed_along(): return lax.ppermute(value, axis, pairs)  10 us
    dot_general x4, matrix products, body(): jnp.einsum('cri,kio->ckro', other, matrix, preferred_element_type=jnp.flo...  7.52 us
    broadcast_in_dim x1, other arithmetic, body(): projected.astype(jnp.bfloat16)[None]  4.03 us
    all_to_all x1, waiting for transfers between devices, exchanged(): return lax.all_to_all(spread, axes, 0, 0, tiled=True)  3.61 us
    mul x1, other arithmetic, body(): h_im[vec, :, None, None] * turned[:, vec][:, None]  2.78 us
    broadcast_in_dim x1, other arithmetic, body(): image.astype(jnp.bfloat16)[None]  2.27 us
  transfers between devices with their start and end apart: 5, of which 3 were waited for; matrix products, arithmetic and copies ran while one was open for 28% of the time, Pallas kernels for 0%

profile of v23, /device:TPU:0, one launch (start us, length us, event | category | flops | bytes accessed | tf_op | source)
XLA Modules:
  0.0 79.0 jit_solution(8047154834653821016)
XLA Ops:
  0.6 0.0 copy-start
  0.6 5.5 %collective-permute-start = (bf16[2,2,256,512]{3,2,1,0:T(8,128)(2,1)}, bf16[2,2,256,512]{3,2,1,0:T(8,128)(2,1)}, u32[]{:S(2)}, u32[]{:S(2)}) collective-permute-start(bf16[2,2,256,512]{3,2,1,0:T(8,128)(2,1)} %bitcast.107), channel_id=1, source_target_pairs={{0,15},{1,0},{2,1},{3,2},{4,3},{5,4},{6,5},{7,6},{8,7},{9,8},{10,9... | collective-permute-start | bytes 3145736 | tf_op jit(solution)/shard_map/ppermute | solution.py:12
  6.1 0.0 collective-permute-start.2
  6.1 1.7 %reshape_squeeze.3 = bf16[4096,128]{1,0:T(8,128)(2,1)S(1)} reshape(bf16[1,2,2,256,512]{4,3,2,1,0:T(8,128)(2,1)} %param.7) | data formatting | bytes 2097152 | tf_op jit(solution)/shard_map/reshape;squeeze | solution.py:36
  7.9 0.0 copy-done
  7.9 1.8 %fusion.32 = f32[4096,128]{1,0:T(8,128)} fusion(bf16[4096,128]{1,0:T(8,128)(2,1)S(1)} %reshape_squeeze.3, bf16[128,128]{1,0:T(8,128)(2,1)S(1)} %copy-done), kind=kOutput, calls=%fused_computation.69 | convolution fusion | flops 134217728 | bytes 3178496 | tf_op jit(solution)/shard_map/dot_general | solution.py:37
  9.7 0.0 copy-start.6
  9.7 0.0 copy-start.1
  9.7 0.0 copy-start.4
  9.7 1.8 %reshape.253 = f32[2,2,256,512]{3,2,1,0:T(8,128)S(1)} reshape(f32[4096,128]{1,0:T(8,128)} %fusion.32) | data formatting | bytes 4194304 | tf_op jit(solution)/shard_map/reshape | solution.py:37
  11.5 0.0 copy-done.6
  12.2 0.3 broadcast_in_dim.39
  12.5 0.0 copy-done.1
  12.5 0.0 copy-done.4
  12.6 1.8 %fusion.3 = f32[2,2,256,512]{3,2,1,0:T(8,128)} fusion(f32[2,2,256,512]{3,2,1,0:T(8,128)S(1)} %reshape.253, f32[]{:T(128)S(6)} %div.8, bf16[256,256]{1,0:T(8,128)(2,1)S(1)} %copy-done.4, bf16[32,8,2,128]{3,2,1,0:T(2,128)(2,1)S(1)} %bitcast.123, bf16[1,2,2,256,512]{4,3,2,1,0:T(8,128)(2,1)S(1)} %copy-done.1), kind=kOutput, calls=%fused_computation.11 | convolution fusion | flops 270794752 | bytes 5505028 | tf_op jit(solution)/shard_map/ab,cvbf->cvaf/dot_general | solution.py:40
  14.4 0.0 copy-start.5
  14.4 0.3 bitcast_convert_fusion
  14.7 0.4 copy-done.5
  15.0 0.7 fusion.26
  23.3 1.5 %slice_bitcast_fusion.1 = (f32[2,256,512]{2,1,0:T(8,128)}, f32[2,256,512]{2,1,0:T(8,128)}) fusion(f32[2,2,256,512]{3,2,1,0:T(8,128)S(1)} %bitcast_convert_fusion), kind=kLoop, calls=%fused_computation.21 | loop fusion | bytes 4194304 | tf_op jit(solution)/shard_map/mul | solution.py:75
  24.8 0.0 copy-start.3
  24.8 1.4 %fusion.30 = (f32[1,2,256,512]{3,2,1,0:T(8,128)S(1)}, f32[1,2,256,512]{3,2,1,0:T(8,128)}, f32[2]{0:T(128)S(1)}, f32[1,2,256,512]{3,2,1,0:T(8,128)S(1)}) fusion(f32[2,2,256,512]{3,2,1,0:T(8,128)S(1)} %bitcast_convert_fusion), kind=kLoop, calls=%fused_computation.67 | loop fusion | flops 1310718 | bytes 5242888 | tf_op jit(solution)/shard_map/slice | solution.py:56
  26.2 0.0 collective-permute-done
  26.2 4.5 %collective-permute-start.1 = (bf16[2,2,256,512]{3,2,1,0:T(8,128)(2,1)}, bf16[2,2,256,512]{3,2,1,0:T(8,128)(2,1)S(1)}, u32[]{:S(2)}, u32[]{:S(2)}) collective-permute-start(bf16[2,2,256,512]{3,2,1,0:T(8,128)(2,1)} %collective-permute-done), channel_id=1, source_target_pairs={{0,15},{1,0},{2,1},{3,2},{4,3},{5,4},{6,5},{7,6},{8,7},{9,8},{10,9... | collective-permute-start | bytes 3145736 | tf_op jit(solution)/shard_map/ppermute | solution.py:12
  30.6 0.0 copy-done.3
  30.6 2.5 %convolution_bitcast_fusion.2 = f32[2,2,512,512]{3,2,0,1:T(8,128)S(1)} fusion(bf16[2,512,512,1]{2,1,0,3:T(8,128)(2,1)} %bitcast.18, bf16[4,2,512,512]{3,2,1,0:T(8,128)(2,1)S(1)} %copy-done.3, s32[]{:T(128)S(6)} %select_n.29), kind=kOutput, calls=%fused_computation.2 | convolution fusion | flops 1073741824 | bytes 6291460 | tf_op jit(solution)/shard_map/cri,kio->ckro/dot_general | solution.py:50
  33.2 0.0 collective-permute-done.2
  33.2 0.1 collective-permute-start.3
  33.2 2.5 %convolution_bitcast_fusion.1 = f32[2,2,512,512]{3,2,0,1:T(8,128)S(1)} fusion(bf16[2,512,512,1]{2,1,0,3:T(8,128)(2,1)} %bitcast.26, bf16[4,2,512,512]{3,2,1,0:T(8,128)(2,1)S(1)} %copy-done.3, s32[]{:T(128)S(6)} %select_n.31), kind=kOutput, calls=%fused_computation.1 | convolution fusion | flops 1073741824 | bytes 6291460 | tf_op jit(solution)/shard_map/cri,kio->ckro/dot_general | solution.py:50
  35.7 0.5 slice_subtract_fusion.2
  36.2 0.5 slice_subtract_fusion.1
  36.7 6.6 %collective-permute-done.1 = bf16[2,2,256,512]{3,2,1,0:T(8,128)(2,1)S(1)} collective-permute-done((bf16[2,2,256,512]{3,2,1,0:T(8,128)(2,1)}, bf16[2,2,256,512]{3,2,1,0:T(8,128)(2,1)S(1)}, u32[]{:S(2)}, u32[]{:S(2)}) %collective-permute-start.1) | collective-permute-done | bytes 1048608 | tf_op jit(solution)/shard_map/ppermute | solution.py:12
  43.3 1.3 %convolution_bitcast_fusion.3 = f32[2,2,512,512]{3,2,0,1:T(8,128)S(1)} fusion(bf16[2,512,512,1]{2,1,0,3:T(8,128)(2,1)S(1)} %bitcast.122, bf16[4,2,512,512]{3,2,1,0:T(8,128)(2,1)S(1)} %copy-done.3, s32[]{:T(128)S(6)} %select_n.27), kind=kOutput, calls=%fused_computation.3 | convolution fusion | flops 1073741824 | bytes 6291460 | tf_op jit(solution)/shard_map/cri,kio->ckro/dot_general | solution.py:50
  44.5 0.5 slice_subtract_fusion.3
  45.0 5.4 %collective-permute-done.3 = bf16[2,2,256,512]{3,2,1,0:T(8,128)(2,1)S(1)} collective-permute-done((bf16[2,2,256,512]{3,2,1,0:T(8,128)(2,1)}, bf16[2,2,256,512]{3,2,1,0:T(8,128)(2,1)S(1)}, u32[]{:S(2)}, u32[]{:S(2)}) %collective-permute-start.3) | collective-permute-done | bytes 1048608 | tf_op jit(solution)/shard_map/ppermute | solution.py:12
  50.5 1.3 %convolution_bitcast_fusion = f32[2,2,512,512]{3,2,0,1:T(8,128)S(1)} fusion(bf16[2,512,512,1]{2,1,0,3:T(8,128)(2,1)S(1)} %bitcast.121, bf16[4,2,512,512]{3,2,1,0:T(8,128)(2,1)S(1)} %copy-done.3, s32[]{:T(128)S(6)} %select_n.33), kind=kOutput, calls=%fused_computation | convolution fusion | flops 1073741824 | bytes 6291460 | tf_op jit(solution)/shard_map/cri,kio->ckro/dot_general | solution.py:50
  51.7 0.0 copy-start.2
  51.7 0.5 slice_subtract_fusion
  52.2 1.1 %copy-done.2 = f32[2,2,256,512]{3,2,1,0:T(8,128)S(1)} copy-done((f32[2,2,256,512]{3,2,1,0:T(8,128)S(1)}, f32[2,2,256,512]{3,2,1,0:T(8,128)}, u32[]{:S(2)}) %copy-start.2) | copy-done | bytes 2097176
  53.3 2.3 %convert_bitcast_fusion = (bf16[1,2,2,256,512]{4,3,2,1,0:T(8,128)(2,1)}, f32[2,2,256,512]{3,2,1,0:T(8,128)S(1)}) fusion(f32[1,2,256,512]{3,2,1,0:T(8,128)S(1)} %bitcast.120, f32[1,2,256,512]{3,2,1,0:T(8,128)S(1)} %bitcast.119, f32[1,2,256,512]{3,2,1,0:T(8,128)S(1)} %bitcast.116, f32[1,2,256,512]{3,2,1,0:T(8,128)S(1)} %bitcast.115, ...), kind=kLoop, calls=%fused_computation.35 | loop fusion | flops 4718592 | bytes 13631488 | tf_op jit(solution)/shard_map/broadcast_in_dim | solution.py:77
  55.6 0.2 fusion.29
  55.8 0.9 %subtract_reduce_fusion = (f32[2,2,8]{2,1,0:T(2,128)S(1)}, f32[2,2,8]{2,1,0:T(2,128)S(1)}) fusion(f32[2,8,32,512]{3,2,1,0:T(8,128)S(1)} %bitcast.112, f32[2,8,32,512]{3,2,1,0:T(8,128)S(1)} %bitcast.110, f32[2,8,32,512]{3,2,1,0:T(8,128)S(1)} %bitcast.111, f32[2,8,32,512]{3,2,1,0:T(8,128)S(1)} %bitcast.109), kind=kLoop, calls=%fused_computation.13 | loop fusion | flops 4194240 | bytes 4194560 | tf_op jit(solution)/shard_map/reduce_sum | solution.py:62
  56.6 0.1 reduce_sum.96
  56.7 0.1 reshape.269
  56.8 0.1 reduce_sum.97
  56.9 0.1 reshape.270
  57.0 0.1 maximum_maximum_fusion
  57.0 0.6 broadcast.36
  57.7 10.5 %all-to-all-start = ((f32[16,1,10]{2,1,0:T(1,128)}), f32[16,1,10]{2,1,0:T(1,128)S(1)}, u32[]{:S(2)}, u32[]{:S(2)}) async-start(f32[16,1,10]{2,1,0:T(1,128)} %bitcast.43), calls=%async_computation | async-start | bytes 16384 | tf_op jit(solution)/shard_map/all_to_all | solution.py:20
  68.2 2.8 %fusion.6 = (f32[2,256,512]{2,1,0:T(8,128)}, f32[2,256,512]{2,1,0:T(8,128)}) fusion(f32[1,2,256,512]{3,2,1,0:T(8,128)} %get-tuple-element.29, f32[1,2,256,512]{3,2,1,0:T(8,128)S(1)} %get-tuple-element.31), kind=kLoop, calls=%fused_computation.17 | loop fusion | flops 524288 | bytes 4194304 | tf_op jit(solution)/shard_map/mul | solution.py:76
  71.0 3.6 %all-to-all-done = f32[16,1,10]{2,1,0:T(1,128)S(1)} async-done(((f32[16,1,10]{2,1,0:T(1,128)}), f32[16,1,10]{2,1,0:T(1,128)S(1)}, u32[]{:S(2)}, u32[]{:S(2)}) %all-to-all-start) | async-done | bytes 672 | tf_op jit(solution)/shard_map/all_to_all | solution.py:20
  74.6 0.1 fusion.31
  74.7 0.1 slice_add_fusion.4
  74.7 0.1 reshape.258
  74.8 0.1 reshape.259
  74.9 0.1 broadcast_divide_fusion.1
  75.0 4.0 %fusion.4 = bf16[1,2,2,256,512]{4,3,2,1,0:T(8,128)(2,1)} fusion(f32[2,2,256,512]{3,2,1,0:T(8,128)S(1)} %get-tuple-element.13, f32[2,256,512]{2,1,0:T(8,128)} %get-tuple-element.25, f32[2]{0:T(128)S(1)} %get-tuple-element.35, f32[2,256,512]{2,1,0:T(8,128)} %get-tuple-element.23, f32[2]{0:T(128)S(1)} %get-tuple-element.40, ...), kind=kLoop, calls=%fused_computation.15 | loop fusion | flops 4718592 | bytes 7340064 | tf_op jit(solution)/shard_map/broadcast_in_dim | solution.py:77
  (4 shorter events, 0.1 us)
Async XLA Ops:
  0.6 7.3 %copy-start = (bf16[128,128]{1,0:T(8,128)(2,1)S(1)}, bf16[128,128]{1,0:T(8,128)(2,1)}, u32[]{:S(2)}) copy-start(bf16[128,128]{1,0:T(8,128)(2,1)} %param.9) | copy-start | bytes 98308
  0.6 25.5 %collective-permute-start = (bf16[2,2,256,512]{3,2,1,0:T(8,128)(2,1)}, bf16[2,2,256,512]{3,2,1,0:T(8,128)(2,1)}, u32[]{:S(2)}, u32[]{:S(2)}) collective-permute-start(bf16[2,2,256,512]{3,2,1,0:T(8,128)(2,1)} %bitcast.107), channel_id=1, source_target_pairs={{0,15},{1,0},{2,1},{3,2},{4,3},{5,4},{6,5},{7,6},{8,7},{9,8},{10,9... | collective-permute-start | bytes 3145736 | tf_op jit(solution)/shard_map/ppermute | solution.py:12
  6.1 27.0 %collective-permute-start.2 = (bf16[2,2,256,512]{3,2,1,0:T(8,128)(2,1)}, bf16[2,2,256,512]{3,2,1,0:T(8,128)(2,1)}, u32[]{:S(2)}, u32[]{:S(2)}) collective-permute-start(bf16[2,2,256,512]{3,2,1,0:T(8,128)(2,1)} %bitcast.108), channel_id=1, source_target_pairs={{0,1},{1,2},{2,3},{3,4},{4,5},{5,6},{6,7},{7,8},{8,9},{9,10},{10,1... | collective-permute-start | bytes 3145736 | tf_op jit(solution)/shard_map/ppermute | solution.py:12
  9.7 1.8 %copy-start.6 = (s32[2,2]{1,0:T(2,128)S(1)}, s32[2,2]{1,0:T(2,128)}, u32[]{:S(2)}) copy-start(s32[2,2]{1,0:T(2,128)} %param.11) | copy-start | bytes 52
  9.7 2.9 %copy-start.1 = (bf16[1,2,2,256,512]{4,3,2,1,0:T(8,128)(2,1)S(1)}, bf16[1,2,2,256,512]{4,3,2,1,0:T(8,128)(2,1)}, u32[]{:S(2)}) copy-start(bf16[1,2,2,256,512]{4,3,2,1,0:T(8,128)(2,1)} %param.7) | copy-start | bytes 3145732
  9.7 2.9 %copy-start.4 = (bf16[256,256]{1,0:T(8,128)(2,1)S(1)}, bf16[256,256]{1,0:T(8,128)(2,1)}, u32[]{:S(2)}) copy-start(bf16[256,256]{1,0:T(8,128)(2,1)} %param.10) | copy-start | bytes 393220
  14.4 0.7 copy-start.5
  24.8 5.9 %copy-start.3 = (bf16[4,2,512,512]{3,2,1,0:T(8,128)(2,1)S(1)}, bf16[4,2,512,512]{3,2,1,0:T(8,128)(2,1)}, u32[]{:S(2)}) copy-start(bf16[4,2,512,512]{3,2,1,0:T(8,128)(2,1)} %param.8) | copy-start | bytes 12582916
  26.2 17.1 %collective-permute-start.1 = (bf16[2,2,256,512]{3,2,1,0:T(8,128)(2,1)}, bf16[2,2,256,512]{3,2,1,0:T(8,128)(2,1)S(1)}, u32[]{:S(2)}, u32[]{:S(2)}) collective-permute-start(bf16[2,2,256,512]{3,2,1,0:T(8,128)(2,1)} %collective-permute-done), channel_id=1, source_target_pairs={{0,15},{1,0},{2,1},{3,2},{4,3},{5,4},{6,5},{7,6},{8,7},{9,8},{10,9... | collective-permute-start | bytes 3145736 | tf_op jit(solution)/shard_map/ppermute | solution.py:12
  33.2 17.3 %collective-permute-start.3 = (bf16[2,2,256,512]{3,2,1,0:T(8,128)(2,1)}, bf16[2,2,256,512]{3,2,1,0:T(8,128)(2,1)S(1)}, u32[]{:S(2)}, u32[]{:S(2)}) collective-permute-start(bf16[2,2,256,512]{3,2,1,0:T(8,128)(2,1)} %collective-permute-done.2), channel_id=1, source_target_pairs={{0,1},{1,2},{2,3},{3,4},{4,5},{5,6},{6,7},{7,8},{8,9},{9,10},{10,1... | collective-permute-start | bytes 3145736 | tf_op jit(solution)/shard_map/ppermute | solution.py:12
  51.7 1.6 %copy-start.2 = (f32[2,2,256,512]{3,2,1,0:T(8,128)S(1)}, f32[2,2,256,512]{3,2,1,0:T(8,128)}, u32[]{:S(2)}) copy-start(f32[2,2,256,512]{3,2,1,0:T(8,128)} %fusion.3) | copy-start | bytes 6291460
  57.7 16.9 %all-to-all-start = ((f32[16,1,10]{2,1,0:T(1,128)}), f32[16,1,10]{2,1,0:T(1,128)S(1)}, u32[]{:S(2)}, u32[]{:S(2)}) async-start(f32[16,1,10]{2,1,0:T(1,128)} %bitcast.43), calls=%async_computation | async-start | bytes 16384 | tf_op jit(solution)/shard_map/all_to_all | solution.py:20

commit v24 on v22

--- a/solution.py
+++ b/solution.py
@@ -56,7 +56,7 @@
     qi = qfull[1]
     wr = image[0]
     wi = image[1]
-    groups = 8 if width_x % 8 == 0 else 1
+    groups = 32 if width_x % 32 == 0 else 1
     split = (vecs, vecs, groups, width_x // groups, width_fy)
     part_re = jnp.sum((qr[:, None] * wr[None, :] + qi[:, None] * wi[None, :]).reshape(split), axis=(3, 4))
     part_im = jnp.sum((qr[:, None] * wi[None, :] - qi[:, None] * wr[None, :]).reshape(split), axis=(3, 4))

time: 76.4 us -> 76.5 us (level)
  no operation moved by 1% of the time
where the time goes in v24:
time: 76.5 us; the launch traced here: 76.1 us
  blocking collectives  18.3 us (24%)
  starting transfers between devices  17.9 us (23%)
  matrix products  11.1 us (15%)
  between operations  9.05 us (12%)
  local copies, waits for them, and re-layouts  6.54 us (9%)
  other arithmetic  5.86 us (8%)
  waiting for transfers between devices  4.13 us (5%)
  Pallas kernels  3.22 us (4%)
    all_to_all x1, blocking collectives, exchanged(): return lax.all_to_all(spread, axes, 0, 0, tiled=True)  18.3 us
    ppermute x4, starting transfers between devices, passed_along(): return lax.ppermute(value, axis, pairs)  17.9 us
    dot_general x4, matrix products, body(): jnp.einsum('cri,kio->ckro', other, matrix, preferred_element_type=jnp.flo...  7.52 us
    ppermute x4, waiting for transfers between devices, passed_along(): return lax.ppermute(value, axis, pairs)  4.13 us
    pallas_call x1, Pallas kernels, removed_projections(): pl.pallas_call(project_kernel, grid=(width_x // rows,), in_specs=[pl.Bloc...  3.22 us
    unnamed x16, local copies, waits for them, and re-layouts  2.29 us
    sub x4, other arithmetic, body(): real_part = prod[0, 0] - prod[1, 1]  1.92 us
    reshape x1, local copies, waits for them, and re-layouts, body(): jnp.dot(rows, y_operator, preferred_element_type=jnp.float32)  1.83 us
  transfers between devices with their start and end apart: 4, of which 1 were waited for; matrix products, arithmetic and copies ran while one was open for 22% of the time, Pallas kernels for 0%

profile of v24, /device:TPU:0, one launch (start us, length us, event | category | flops | bytes accessed | tf_op | source)
XLA Modules:
  0.0 76.1 jit_solution(2098635623731390545)
XLA Ops:
  0.6 0.0 copy-start
  0.6 5.5 %collective-permute-start = (bf16[2,2,256,512]{3,2,1,0:T(8,128)(2,1)}, bf16[2,2,256,512]{3,2,1,0:T(8,128)(2,1)}, u32[]{:S(2)}, u32[]{:S(2)}) collective-permute-start(bf16[2,2,256,512]{3,2,1,0:T(8,128)(2,1)} %bitcast.92), channel_id=1, source_target_pairs={{0,15},{1,0},{2,1},{3,2},{4,3},{5,4},{6,5},{7,6},{8,7},{9,8},{10,9... | collective-permute-start | bytes 3145736 | tf_op jit(solution)/shard_map/ppermute | solution.py:12
  6.1 0.0 collective-permute-start.2
  6.1 1.7 %reshape_squeeze.3 = bf16[4096,128]{1,0:T(8,128)(2,1)S(1)} reshape(bf16[1,2,2,256,512]{4,3,2,1,0:T(8,128)(2,1)} %block_ref.1) | data formatting | bytes 2097152 | tf_op jit(solution)/shard_map/reshape;squeeze | solution.py:36
  7.9 0.0 copy-done
  7.9 1.8 %fusion.24 = f32[4096,128]{1,0:T(8,128)} fusion(bf16[4096,128]{1,0:T(8,128)(2,1)S(1)} %reshape_squeeze.3, bf16[128,128]{1,0:T(8,128)(2,1)S(1)} %copy-done), kind=kOutput, calls=%fused_computation.51 | convolution fusion | flops 134217728 | bytes 3178496 | tf_op jit(solution)/shard_map/dot_general | solution.py:37
  9.7 0.0 copy-start.7
  9.7 0.0 copy-start.2
  9.7 0.0 copy-start.5
  9.7 1.8 %reshape.226 = f32[2,2,256,512]{3,2,1,0:T(8,128)S(1)} reshape(f32[4096,128]{1,0:T(8,128)} %fusion.24) | data formatting | bytes 4194304 | tf_op jit(solution)/shard_map/reshape | solution.py:37
  11.5 0.0 copy-done.7
  12.2 0.3 broadcast_in_dim.31
  12.5 0.0 copy-done.2
  12.5 0.0 copy-done.5
  12.6 0.0 copy-start.6
  12.6 1.8 %fusion.3 = f32[2,2,256,512]{3,2,1,0:T(8,128)} fusion(f32[2,2,256,512]{3,2,1,0:T(8,128)S(1)} %reshape.226, f32[]{:T(128)S(6)} %div.3, bf16[256,256]{1,0:T(8,128)(2,1)S(1)} %copy-done.5, bf16[32,8,2,128]{3,2,1,0:T(2,128)(2,1)S(1)} %bitcast.104, bf16[1,2,2,256,512]{4,3,2,1,0:T(8,128)(2,1)S(1)} %copy-done.2), kind=kOutput, calls=%fused_computation.9 | convolution fusion | flops 270794752 | bytes 5505028 | tf_op jit(solution)/shard_map/ab,cvbf->cvaf/dot_general | solution.py:40
  14.4 0.0 copy-done.6
  14.4 0.7 fusion.22
  22.6 0.3 bitcast_convert_fusion
  22.9 0.0 copy-start.4
  22.9 0.5 slice_bitcast_fusion.3
  23.4 0.0 collective-permute-done
  23.4 4.5 %collective-permute-start.1 = (bf16[2,2,256,512]{3,2,1,0:T(8,128)(2,1)}, bf16[2,2,256,512]{3,2,1,0:T(8,128)(2,1)S(1)}, u32[]{:S(2)}, u32[]{:S(2)}) collective-permute-start(bf16[2,2,256,512]{3,2,1,0:T(8,128)(2,1)} %collective-permute-done), channel_id=1, source_target_pairs={{0,15},{1,0},{2,1},{3,2},{4,3},{5,4},{6,5},{7,6},{8,7},{9,8},{10,9... | collective-permute-start | bytes 3145736 | tf_op jit(solution)/shard_map/ppermute | solution.py:12
  27.9 0.0 copy-done.4
  27.9 2.5 %convolution_bitcast_fusion.2 = f32[2,2,512,512]{3,2,0,1:T(8,128)S(1)} fusion(bf16[2,512,512,1]{2,1,0,3:T(8,128)(2,1)} %bitcast.19, bf16[4,2,512,512]{3,2,1,0:T(8,128)(2,1)S(1)} %copy-done.4, s32[]{:T(128)S(6)} %select_n.29), kind=kOutput, calls=%fused_computation.2 | convolution fusion | flops 1073741824 | bytes 6291460 | tf_op jit(solution)/shard_map/cri,kio->ckro/dot_general | solution.py:50
  30.4 0.0 collective-permute-done.2
  30.4 7.9 %collective-permute-start.3 = (bf16[2,2,256,512]{3,2,1,0:T(8,128)(2,1)}, bf16[2,2,256,512]{3,2,1,0:T(8,128)(2,1)S(1)}, u32[]{:S(2)}, u32[]{:S(2)}) collective-permute-start(bf16[2,2,256,512]{3,2,1,0:T(8,128)(2,1)} %collective-permute-done.2), channel_id=1, source_target_pairs={{0,1},{1,2},{2,3},{3,4},{4,5},{5,6},{6,7},{7,8},{8,9},{9,10},{10,1... | collective-permute-start | bytes 3145736 | tf_op jit(solution)/shard_map/ppermute | solution.py:12
  38.4 2.5 %convolution_bitcast_fusion.1 = f32[2,2,512,512]{3,2,0,1:T(8,128)S(1)} fusion(bf16[2,512,512,1]{2,1,0,3:T(8,128)(2,1)} %bitcast.27, bf16[4,2,512,512]{3,2,1,0:T(8,128)(2,1)S(1)} %copy-done.4, s32[]{:T(128)S(6)} %select_n.31), kind=kOutput, calls=%fused_computation.1 | convolution fusion | flops 1073741824 | bytes 6291460 | tf_op jit(solution)/shard_map/cri,kio->ckro/dot_general | solution.py:50
  40.9 0.5 slice_subtract_fusion.2
  41.4 0.5 slice_subtract_fusion.1
  41.8 0.0 collective-permute-done.1
  41.8 1.3 %convolution_bitcast_fusion.3 = f32[2,2,512,512]{3,2,0,1:T(8,128)S(1)} fusion(bf16[2,512,512,1]{2,1,0,3:T(8,128)(2,1)S(1)} %bitcast.103, bf16[4,2,512,512]{3,2,1,0:T(8,128)(2,1)S(1)} %copy-done.4, s32[]{:T(128)S(6)} %select_n.27), kind=kOutput, calls=%fused_computation.3 | convolution fusion | flops 1073741824 | bytes 6291460 | tf_op jit(solution)/shard_map/cri,kio->ckro/dot_general | solution.py:50
  43.1 0.5 slice_subtract_fusion.3
  43.6 4.1 %collective-permute-done.3 = bf16[2,2,256,512]{3,2,1,0:T(8,128)(2,1)S(1)} collective-permute-done((bf16[2,2,256,512]{3,2,1,0:T(8,128)(2,1)}, bf16[2,2,256,512]{3,2,1,0:T(8,128)(2,1)S(1)}, u32[]{:S(2)}, u32[]{:S(2)}) %collective-permute-start.3) | collective-permute-done | bytes 1048608 | tf_op jit(solution)/shard_map/ppermute | solution.py:12
  47.7 1.3 %convolution_bitcast_fusion = f32[2,2,512,512]{3,2,0,1:T(8,128)S(1)} fusion(bf16[2,512,512,1]{2,1,0,3:T(8,128)(2,1)S(1)} %bitcast.102, bf16[4,2,512,512]{3,2,1,0:T(8,128)(2,1)S(1)} %copy-done.4, s32[]{:T(128)S(6)} %select_n.33), kind=kOutput, calls=%fused_computation | convolution fusion | flops 1073741824 | bytes 6291460 | tf_op jit(solution)/shard_map/cri,kio->ckro/dot_general | solution.py:50
  49.0 0.0 copy-start.3
  49.0 0.5 slice_subtract_fusion
  49.5 1.1 %copy-done.3 = f32[2,2,256,512]{3,2,1,0:T(8,128)S(1)} copy-done((f32[2,2,256,512]{3,2,1,0:T(8,128)S(1)}, f32[2,2,256,512]{3,2,1,0:T(8,128)}, u32[]{:S(2)}) %copy-start.3) | copy-done | bytes 2097176
  50.6 1.3 %fusion.2.image_ref = f32[2,2,256,512]{3,2,1,0:T(8,128)S(1)} fusion(f32[2,2,256,512]{3,2,1,0:T(8,128)S(1)} %copy-done.3, f32[1,2,256,512]{3,2,1,0:T(8,128)S(1)} %bitcast.99, f32[1,2,256,512]{3,2,1,0:T(8,128)S(1)} %bitcast.98, f32[1,2,256,512]{3,2,1,0:T(8,128)S(1)} %bitcast.95, f32[1,2,256,512]{3,2,1,0:T(8,128)S(1)} %bitcast.94, ...), kind=kLoop, calls=%fused_computation.7 | loop fusion | flops 4194304 | bytes 12582912 | tf_op jit(solution)/shard_map/add | solution.py:53
  51.9 0.0 copy-start.1
  51.9 0.2 slice_bitcast_fusion.1
  52.1 1.2 %copy-done.1 = f32[2,2,256,512]{3,2,1,0:T(8,128)} copy-done((f32[2,2,256,512]{3,2,1,0:T(8,128)}, f32[2,2,256,512]{3,2,1,0:T(8,128)S(1)}, u32[]{:S(2)}) %copy-start.1) | copy-done | bytes 2097176
  53.2 1.0 %subtract_reduce_fusion = (f32[2,2,32]{2,1,0:T(2,128)S(1)}, f32[2,2,32]{2,1,0:T(2,128)S(1)}) fusion(f32[2,32,8,512]{3,2,1,0:T(8,128)S(1)} %get-tuple-element.24, f32[2,32,8,512]{3,2,1,0:T(8,128)S(1)} %get-tuple-element.21, f32[2,32,8,512]{3,2,1,0:T(8,128)S(1)} %get-tuple-element.23, f32[2,32,8,512]{3,2,1,0:T(8,128)S(1)} %get-tuple-element.20), kind=kLoop, calls=%fused_computation.10 | loop fusion | flops 4194048 | bytes 4195328 | tf_op jit(solution)/shard_map/reduce_sum | solution.py:62
  54.2 0.1 reduce_sum.87
  54.3 0.1 reshape.240
  54.4 0.1 reduce_sum.88
  54.5 0.1 reshape.241
  54.5 0.1 maximum_maximum_fusion
  54.6 18.3 %all_to_all.11 = f32[16,1,10]{2,1,0:T(1,128)} all-to-all(f32[16,1,10]{2,1,0:T(1,128)S(1)} %bitcast.107), channel_id=1, replica_groups=mesh['det'=2,'harm'=16] {'harm'}, dimensions={0} | all-to-all | bytes 1280 | tf_op jit(solution)/shard_map/all_to_all | solution.py:20
  72.9 3.2 %shard_map.86 = (bf16[1,2,2,256,512]{4,3,2,1,0:T(8,128)(2,1)}, bf16[1,2,2,256,512]{4,3,2,1,0:T(8,128)(2,1)}) custom-call(f32[16,10]{1,0:T(8,128)} %bitcast.106, f32[2,2,256,512]{3,2,1,0:T(8,128)} %copy-done.1, bf16[1,2,2,256,512]{4,3,2,1,0:T(8,128)(2,1)} %block_ref.1), custom_call_target="tpu_custom_call" | custom-call | tf_op jit(solution)/shard_map/pallas_call | solution.py:102
  (3 shorter events, 0.0 us)
Async XLA Ops:
  0.6 7.3 %copy-start = (bf16[128,128]{1,0:T(8,128)(2,1)S(1)}, bf16[128,128]{1,0:T(8,128)(2,1)}, u32[]{:S(2)}) copy-start(bf16[128,128]{1,0:T(8,128)(2,1)} %param.9) | copy-start | bytes 98308
  0.6 22.8 %collective-permute-start = (bf16[2,2,256,512]{3,2,1,0:T(8,128)(2,1)}, bf16[2,2,256,512]{3,2,1,0:T(8,128)(2,1)}, u32[]{:S(2)}, u32[]{:S(2)}) collective-permute-start(bf16[2,2,256,512]{3,2,1,0:T(8,128)(2,1)} %bitcast.92), channel_id=1, source_target_pairs={{0,15},{1,0},{2,1},{3,2},{4,3},{5,4},{6,5},{7,6},{8,7},{9,8},{10,9... | collective-permute-start | bytes 3145736 | tf_op jit(solution)/shard_map/ppermute | solution.py:12
  6.1 24.3 %collective-permute-start.2 = (bf16[2,2,256,512]{3,2,1,0:T(8,128)(2,1)}, bf16[2,2,256,512]{3,2,1,0:T(8,128)(2,1)}, u32[]{:S(2)}, u32[]{:S(2)}) collective-permute-start(bf16[2,2,256,512]{3,2,1,0:T(8,128)(2,1)} %bitcast.93), channel_id=1, source_target_pairs={{0,1},{1,2},{2,3},{3,4},{4,5},{5,6},{6,7},{7,8},{8,9},{9,10},{10,1... | collective-permute-start | bytes 3145736 | tf_op jit(solution)/shard_map/ppermute | solution.py:12
  9.7 1.8 %copy-start.7 = (s32[2,2]{1,0:T(2,128)S(1)}, s32[2,2]{1,0:T(2,128)}, u32[]{:S(2)}) copy-start(s32[2,2]{1,0:T(2,128)} %param.11) | copy-start | bytes 52
  9.7 2.9 %copy-start.2 = (bf16[1,2,2,256,512]{4,3,2,1,0:T(8,128)(2,1)S(1)}, bf16[1,2,2,256,512]{4,3,2,1,0:T(8,128)(2,1)}, u32[]{:S(2)}) copy-start(bf16[1,2,2,256,512]{4,3,2,1,0:T(8,128)(2,1)} %block_ref.1) | copy-start | bytes 3145732
  9.7 2.9 %copy-start.5 = (bf16[256,256]{1,0:T(8,128)(2,1)S(1)}, bf16[256,256]{1,0:T(8,128)(2,1)}, u32[]{:S(2)}) copy-start(bf16[256,256]{1,0:T(8,128)(2,1)} %param.10) | copy-start | bytes 393220
  12.6 1.8 %copy-start.6 = (s32[4]{0:T(128)S(1)}, s32[4]{0:T(128)}, u32[]{:S(2)}) copy-start(s32[4]{0:T(128)} %param.12) | copy-start | bytes 52
  22.9 5.0 %copy-start.4 = (bf16[4,2,512,512]{3,2,1,0:T(8,128)(2,1)S(1)}, bf16[4,2,512,512]{3,2,1,0:T(8,128)(2,1)}, u32[]{:S(2)}) copy-start(bf16[4,2,512,512]{3,2,1,0:T(8,128)(2,1)} %param.8) | copy-start | bytes 12582916
  23.4 18.4 %collective-permute-start.1 = (bf16[2,2,256,512]{3,2,1,0:T(8,128)(2,1)}, bf16[2,2,256,512]{3,2,1,0:T(8,128)(2,1)S(1)}, u32[]{:S(2)}, u32[]{:S(2)}) collective-permute-start(bf16[2,2,256,512]{3,2,1,0:T(8,128)(2,1)} %collective-permute-done), channel_id=1, source_target_pairs={{0,15},{1,0},{2,1},{3,2},{4,3},{5,4},{6,5},{7,6},{8,7},{9,8},{10,9... | collective-permute-start | bytes 3145736 | tf_op jit(solution)/shard_map/ppermute | solution.py:12
  30.4 17.3 %collective-permute-start.3 = (bf16[2,2,256,512]{3,2,1,0:T(8,128)(2,1)}, bf16[2,2,256,512]{3,2,1,0:T(8,128)(2,1)S(1)}, u32[]{:S(2)}, u32[]{:S(2)}) collective-permute-start(bf16[2,2,256,512]{3,2,1,0:T(8,128)(2,1)} %collective-permute-done.2), channel_id=1, source_target_pairs={{0,1},{1,2},{2,3},{3,4},{4,5},{5,6},{6,7},{7,8},{8,9},{9,10},{10,1... | collective-permute-start | bytes 3145736 | tf_op jit(solution)/shard_map/ppermute | solution.py:12
  49.0 1.6 %copy-start.3 = (f32[2,2,256,512]{3,2,1,0:T(8,128)S(1)}, f32[2,2,256,512]{3,2,1,0:T(8,128)}, u32[]{:S(2)}) copy-start(f32[2,2,256,512]{3,2,1,0:T(8,128)} %fusion.3) | copy-start | bytes 6291460
  51.9 1.4 %copy-start.1 = (f32[2,2,256,512]{3,2,1,0:T(8,128)}, f32[2,2,256,512]{3,2,1,0:T(8,128)S(1)}, u32[]{:S(2)}) copy-start(f32[2,2,256,512]{3,2,1,0:T(8,128)S(1)} %fusion.2.image_ref) | copy-start | bytes 6291460

commit v25 on v20

--- a/solution.py
+++ b/solution.py
@@ -40,9 +40,20 @@
     along_x = jnp.einsum("ab,cvbf->cvaf", masked, block, preferred_element_type=jnp.float32)
     centered = (position - harmonics // 2).astype(jnp.float32) + detuning[0]
     lam = -(centered * centered) / (4.0 * harmonics)
-    image = lax.optimization_barrier(along_y + along_x + lam * block.astype(jnp.float32))
+    local = lax.optimization_barrier(along_y + along_x + lam * block.astype(jnp.float32))
+    qfull = block.astype(jnp.float32)
+    qr = qfull[0]
+    qi = qfull[1]
+
+    def products(part):
+        part_re = jnp.sum(qr[:, None] * part[0][None, :] + qi[:, None] * part[1][None, :], axis=(2, 3))
+        part_im = jnp.sum(qr[:, None] * part[1][None, :] - qi[:, None] * part[0][None, :], axis=(2, 3))
+        return part_re, part_im
+
+    local_re, local_im = lax.optimization_barrier(products(local))
     sources = (above_two, above_one, below_one, below_two)
     counter = jnp.arange(4, dtype=jnp.int32)
+    coupled = None
     for place in range(4):
         slot = jnp.sum(jnp.where(slot_offsets == place, counter, 0))
         matrix = lax.dynamic_index_in_dim(coupling, slot, 0, keepdims=False)
@@ -50,21 +61,16 @@
         prod = jnp.einsum("cri,kio->ckro", other, matrix, preferred_element_type=jnp.float32)
         real_part = prod[0, 0] - prod[1, 1]
         imag_part = prod[0, 1] + prod[1, 0]
-        image = image + jnp.stack([real_part, imag_part]).reshape(block.shape)
-    qfull = block.astype(jnp.float32)
-    qr = qfull[0]
-    qi = qfull[1]
-    wr = image[0]
-    wi = image[1]
-    num_re = jnp.sum(qr[:, None] * wr[None, :] + qi[:, None] * wi[None, :], axis=(2, 3))
-    num_im = jnp.sum(qr[:, None] * wi[None, :] - qi[:, None] * wr[None, :], axis=(2, 3))
+        term = jnp.stack([real_part, imag_part]).reshape(block.shape)
+        coupled = term if coupled is None else coupled + term
+    coupled_re, coupled_im = products(coupled)
     norms = jnp.sum(qr * qr + qi * qi, axis=(1, 2))
-    gathered = exchanged(("harm",), num_re, num_im, norms)
-    rounded, projected = removed_projections(gathered, image, perturbation)
+    gathered = exchanged(("harm",), local_re + coupled_re, local_im + coupled_im, norms)
+    rounded, projected = removed_projections(gathered, local, coupled, perturbation)
     return (rounded, projected)
 
 
-def project_kernel(gathered_ref, image_ref, block_ref, rounded_ref, out_ref):
+def project_kernel(gathered_ref, image_ref, coupled_ref, block_ref, rounded_ref, out_ref):
     vecs = image_ref.shape[1]
     count, values = gathered_ref.shape
     totals = []
@@ -75,8 +81,8 @@
         totals.append(total)
     block = block_ref[0].astype(jnp.float32)
     for u in range(vecs):
-        out_re = image_ref[0, u]
-        out_im = image_ref[1, u]
+        out_re = image_ref[0, u] + coupled_ref[0, u]
+        out_im = image_ref[1, u] + coupled_ref[1, u]
         rounded_ref[0, 0, u] = out_re.astype(rounded_ref.dtype)
         rounded_ref[0, 1, u] = out_im.astype(rounded_ref.dtype)
         for v in range(vecs):
@@ -91,7 +97,7 @@
         out_ref[0, 1, u] = out_im.astype(out_ref.dtype)
 
 
-def removed_projections(gathered, image, perturbation):
+def removed_projections(gathered, image, coupled, perturbation):
     parts, vecs, width_x, width_fy = image.shape
     rows = 128 if width_x % 128 == 0 else width_x
     return pl.pallas_call(
@@ -99,6 +105,7 @@
         grid=(width_x // rows,),
         in_specs=[
             pl.BlockSpec(memory_space=pltpu.SMEM),
+            pl.BlockSpec((parts, vecs, rows, width_fy), lambda i: (0, 0, i, 0)),
             pl.BlockSpec((parts, vecs, rows, width_fy), lambda i: (0, 0, i, 0)),
             pl.BlockSpec((1, parts, vecs, rows, width_fy), lambda i: (0, 0, 0, i, 0)),
         ],
@@ -110,7 +117,7 @@
             jax.ShapeDtypeStruct(perturbation.shape, jnp.bfloat16),
             jax.ShapeDtypeStruct(perturbation.shape, jnp.bfloat16),
         ],
-    )(gathered, image, perturbation)
+    )(gathered, image, coupled, perturbation)
 
 
 def solution(mesh):

time: 76.7 us -> 77.5 us (1.010)
    unnamed x14, local copies, waits for them, and re-layouts: 2.24 us -> 1.3 us
    reduce_sum x1, other arithmetic: 1.31 us -> 2.24 us  [products(): jnp.sum(qr[:, None] * part[0][None, :] + qi[:, None] * part[1][None, :],...]
  transfers between devices with their start and end apart: 4 -> 4, of which waited for: 1 -> 1; matrix products, arithmetic and copies ran while one was open for 23% -> 22% of each run, Pallas kernels for 0% -> 0%
where the time goes in v25:
time: 77.5 us; the launch traced here: 77 us
  blocking collectives  17.5 us (23%)
  starting transfers between devices  17.3 us (22%)
  matrix products  11.1 us (14%)
  between operations  9.06 us (12%)
  other arithmetic  7.29 us (9%)
  local copies, waits for them, and re-layouts  5.98 us (8%)
  waiting for transfers between devices  4.93 us (6%)
  Pallas kernels  3.9 us (5%)
    all_to_all x1, blocking collectives, exchanged(): return lax.all_to_all(spread, axes, 0, 0, tiled=True)  17.5 us
    ppermute x4, starting transfers between devices, passed_along(): return lax.ppermute(value, axis, pairs)  17.3 us
    dot_general x4, matrix products, body(): jnp.einsum('cri,kio->ckro', other, matrix, preferred_element_type=jnp.flo...  7.52 us
    ppermute x4, waiting for transfers between devices, passed_along(): return lax.ppermute(value, axis, pairs)  4.93 us
    pallas_call x1, Pallas kernels, removed_projections(): pl.pallas_call(project_kernel, grid=(width_x // rows,), in_specs=[pl.Bloc...  3.9 us
    reduce_sum x1, other arithmetic, products(): jnp.sum(qr[:, None] * part[0][None, :] + qi[:, None] * part[1][None, :],...  2.24 us
    sub x4, other arithmetic, body(): real_part = prod[0, 0] - prod[1, 1]  1.91 us
    reshape x1, local copies, waits for them, and re-layouts, body(): jnp.dot(rows, y_operator, preferred_element_type=jnp.float32)  1.83 us
  transfers between devices with their start and end apart: 4, of which 1 were waited for; matrix products, arithmetic and copies ran while one was open for 22% of the time, Pallas kernels for 0%

profile of v25, /device:TPU:0, one launch (start us, length us, event | category | flops | bytes accessed | tf_op | source)
XLA Modules:
  0.0 77.0 jit_solution(11588597545387894653)
XLA Ops:
  0.6 0.0 copy-start
  0.6 5.5 %collective-permute-start = (bf16[2,2,256,512]{3,2,1,0:T(8,128)(2,1)}, bf16[2,2,256,512]{3,2,1,0:T(8,128)(2,1)}, u32[]{:S(2)}, u32[]{:S(2)}) collective-permute-start(bf16[2,2,256,512]{3,2,1,0:T(8,128)(2,1)} %bitcast.100), channel_id=1, source_target_pairs={{0,15},{1,0},{2,1},{3,2},{4,3},{5,4},{6,5},{7,6},{8,7},{9,8},{10,9... | collective-permute-start | bytes 3145736 | tf_op jit(solution)/shard_map/ppermute | solution.py:12
  6.1 0.0 collective-permute-start.2
  6.1 1.4 %fusion.21 = (s32[]{:T(128)}, s32[]{:T(128)}, s32[]{:T(128)}, s32[]{:T(128)}) fusion(s32[4]{0:T(128)} %param.12), kind=kLoop, calls=%fused_computation.50 | loop fusion | flops 44 | bytes 32 | tf_op jit(solution)/shard_map/reduce_sum | solution.py:58
  12.6 1.7 %reshape_squeeze.3 = bf16[4096,128]{1,0:T(8,128)(2,1)S(1)} reshape(bf16[1,2,2,256,512]{4,3,2,1,0:T(8,128)(2,1)} %block_ref.1) | data formatting | bytes 2097152 | tf_op jit(solution)/shard_map/reshape;squeeze | solution.py:36
  14.3 0.0 copy-done
  14.3 1.8 %fusion.23 = f32[4096,128]{1,0:T(8,128)} fusion(bf16[4096,128]{1,0:T(8,128)(2,1)S(1)} %reshape_squeeze.3, bf16[128,128]{1,0:T(8,128)(2,1)S(1)} %copy-done), kind=kOutput, calls=%fused_computation.54 | convolution fusion | flops 134217728 | bytes 3178496 | tf_op jit(solution)/shard_map/dot_general | solution.py:37
  16.0 0.0 copy-start.6
  16.0 0.0 copy-start.3
  16.0 0.0 copy-start.5
  16.0 1.8 %reshape.205 = f32[2,2,256,512]{3,2,1,0:T(8,128)S(1)} reshape(f32[4096,128]{1,0:T(8,128)} %fusion.23) | data formatting | bytes 4194304 | tf_op jit(solution)/shard_map/reshape | solution.py:37
  17.9 0.0 copy-done.6
  18.6 0.3 broadcast_in_dim.31
  18.9 0.0 copy-done.3
  18.9 0.0 copy-done.5
  18.9 1.8 %fusion.2.image_ref = f32[2,2,256,512]{3,2,1,0:T(8,128)} fusion(f32[2,2,256,512]{3,2,1,0:T(8,128)S(1)} %reshape.205, f32[]{:T(128)S(6)} %div.3, bf16[256,256]{1,0:T(8,128)(2,1)S(1)} %copy-done.5, bf16[32,8,2,128]{3,2,1,0:T(2,128)(2,1)S(1)} %bitcast.112, bf16[1,2,2,256,512]{4,3,2,1,0:T(8,128)(2,1)S(1)} %copy-done.3), kind=kOutput, calls=%fused_computation.8 | convolution fusion | flops 270794752 | bytes 5505028 | tf_op jit(solution)/shard_map/ab,cvbf->cvaf/dot_general | solution.py:40
  23.3 0.3 bitcast_convert_fusion
  23.6 0.3 add_reduce_fusion.2
  23.8 0.0 copy-start.4
  23.8 0.2 slice_bitcast_fusion.5
  24.0 0.0 collective-permute-done
  24.0 4.5 %collective-permute-start.1 = (bf16[2,2,256,512]{3,2,1,0:T(8,128)(2,1)}, bf16[2,2,256,512]{3,2,1,0:T(8,128)(2,1)S(1)}, u32[]{:S(2)}, u32[]{:S(2)}) collective-permute-start(bf16[2,2,256,512]{3,2,1,0:T(8,128)(2,1)} %collective-permute-done), channel_id=1, source_target_pairs={{0,15},{1,0},{2,1},{3,2},{4,3},{5,4},{6,5},{7,6},{8,7},{9,8},{10,9... | collective-permute-start | bytes 3145736 | tf_op jit(solution)/shard_map/ppermute | solution.py:12
  28.5 0.0 copy-done.4
  28.5 2.5 %convolution_bitcast_fusion.2 = f32[2,2,512,512]{3,2,0,1:T(8,128)S(1)} fusion(bf16[2,512,512,1]{2,1,0,3:T(8,128)(2,1)} %bitcast.22, bf16[4,2,512,512]{3,2,1,0:T(8,128)(2,1)S(1)} %copy-done.4, s32[]{:T(128)S(6)} %select_n.29), kind=kOutput, calls=%fused_computation.2 | convolution fusion | flops 1073741824 | bytes 6291460 | tf_op jit(solution)/shard_map/cri,kio->ckro/dot_general | solution.py:61
  31.0 0.0 collective-permute-done.2
  31.0 7.3 %collective-permute-start.3 = (bf16[2,2,256,512]{3,2,1,0:T(8,128)(2,1)}, bf16[2,2,256,512]{3,2,1,0:T(8,128)(2,1)S(1)}, u32[]{:S(2)}, u32[]{:S(2)}) collective-permute-start(bf16[2,2,256,512]{3,2,1,0:T(8,128)(2,1)} %collective-permute-done.2), channel_id=1, source_target_pairs={{0,1},{1,2},{2,3},{3,4},{4,5},{5,6},{6,7},{7,8},{8,9},{9,10},{10,1... | collective-permute-start | bytes 3145736 | tf_op jit(solution)/shard_map/ppermute | solution.py:12
  38.4 2.5 %convolution_bitcast_fusion.1 = f32[2,2,512,512]{3,2,0,1:T(8,128)S(1)} fusion(bf16[2,512,512,1]{2,1,0,3:T(8,128)(2,1)} %bitcast.30, bf16[4,2,512,512]{3,2,1,0:T(8,128)(2,1)S(1)} %copy-done.4, s32[]{:T(128)S(6)} %select_n.31), kind=kOutput, calls=%fused_computation.1 | convolution fusion | flops 1073741824 | bytes 6291460 | tf_op jit(solution)/shard_map/cri,kio->ckro/dot_general | solution.py:61
  40.9 0.5 slice_subtract_fusion.2
  41.4 0.5 slice_subtract_fusion.1
  41.8 0.0 collective-permute-done.1
  41.8 1.3 %convolution_bitcast_fusion.3 = f32[2,2,512,512]{3,2,0,1:T(8,128)S(1)} fusion(bf16[2,512,512,1]{2,1,0,3:T(8,128)(2,1)S(1)} %bitcast.111, bf16[4,2,512,512]{3,2,1,0:T(8,128)(2,1)S(1)} %copy-done.4, s32[]{:T(128)S(6)} %select_n.27), kind=kOutput, calls=%fused_computation.3 | convolution fusion | flops 1073741824 | bytes 6291460 | tf_op jit(solution)/shard_map/cri,kio->ckro/dot_general | solution.py:61
  43.1 0.5 slice_subtract_fusion.3
  43.6 4.9 %collective-permute-done.3 = bf16[2,2,256,512]{3,2,1,0:T(8,128)(2,1)S(1)} collective-permute-done((bf16[2,2,256,512]{3,2,1,0:T(8,128)(2,1)}, bf16[2,2,256,512]{3,2,1,0:T(8,128)(2,1)S(1)}, u32[]{:S(2)}, u32[]{:S(2)}) %collective-permute-start.3) | collective-permute-done | bytes 1048608 | tf_op jit(solution)/shard_map/ppermute | solution.py:12
  48.5 1.3 %convolution_bitcast_fusion = f32[2,2,512,512]{3,2,0,1:T(8,128)S(1)} fusion(bf16[2,512,512,1]{2,1,0,3:T(8,128)(2,1)S(1)} %bitcast.110, bf16[4,2,512,512]{3,2,1,0:T(8,128)(2,1)S(1)} %copy-done.4, s32[]{:T(128)S(6)} %select_n.33), kind=kOutput, calls=%fused_computation | convolution fusion | flops 1073741824 | bytes 6291460 | tf_op jit(solution)/shard_map/cri,kio->ckro/dot_general | solution.py:61
  49.8 0.5 slice_subtract_fusion
  50.3 0.0 copy-start.2
  50.3 1.1 %fusion.1.coupled_ref = f32[2,2,256,512]{3,2,1,0:T(8,128)S(1)} fusion(f32[1,2,256,512]{3,2,1,0:T(8,128)S(1)} %bitcast.107, f32[1,2,256,512]{3,2,1,0:T(8,128)S(1)} %bitcast.106, f32[1,2,256,512]{3,2,1,0:T(8,128)S(1)} %bitcast.103, f32[1,2,256,512]{3,2,1,0:T(8,128)S(1)} %bitcast.102, f32[1,2,256,512]{3,2,1,0:T(8,128)S(1)} %bitcast.105, ...), kind=kLoop, calls=%fused_computation.6 | loop fusion | flops 3670016 | bytes 10485760 | tf_op jit(solution)/shard_map/add | solution.py:65
  51.4 0.4 copy-done.2
  51.9 0.0 copy-start.1
  51.9 0.5 slice_bitcast_fusion.1
  52.3 0.8 %copy-done.1 = f32[2,2,256,512]{3,2,1,0:T(8,128)} copy-done((f32[2,2,256,512]{3,2,1,0:T(8,128)}, f32[2,2,256,512]{3,2,1,0:T(8,128)S(1)}, u32[]{:S(2)}) %copy-start.1) | copy-done | bytes 2097176
  53.2 2.2 %add_reduce_fusion = (f32[2,2]{1,0:T(2,128)S(1)}, f32[2,2]{1,0:T(2,128)S(1)}, f32[2,2]{1,0:T(2,128)S(1)}, f32[2,2]{1,0:T(2,128)S(1)}) fusion(f32[2,256,512]{2,1,0:T(8,128)S(1)} %get-tuple-element.29, f32[2,256,512]{2,1,0:T(8,128)S(1)} %get-tuple-element.28, f32[2,256,512]{2,1,0:T(8,128)S(1)} %get-tuple-element.27, f32[2,256,512]{2,1,0:T(8,128)S(1)} %get-tuple-element.26, ...), kind=kLoop, calls=%fused_computation.10 | loop fusion | flops 8388592 | bytes 6291520 | tf_op jit(solution)/shard_map/reduce_sum | solution.py:49
  55.4 0.1 reshape.219
  55.5 0.1 reshape.220
  55.6 0.1 maximum_maximum_fusion
  55.7 17.5 %all_to_all.11 = f32[16,1,10]{2,1,0:T(1,128)} all-to-all(f32[16,1,10]{2,1,0:T(1,128)S(1)} %bitcast.115), channel_id=1, replica_groups=mesh['det'=2,'harm'=16] {'harm'}, dimensions={0} | all-to-all | bytes 1280 | tf_op jit(solution)/shard_map/all_to_all | solution.py:20
  73.1 3.9 %shard_map.86 = (bf16[1,2,2,256,512]{4,3,2,1,0:T(8,128)(2,1)}, bf16[1,2,2,256,512]{4,3,2,1,0:T(8,128)(2,1)}) custom-call(f32[16,10]{1,0:T(8,128)} %bitcast.114, f32[2,2,256,512]{3,2,1,0:T(8,128)} %fusion.2.image_ref, f32[2,2,256,512]{3,2,1,0:T(8,128)} %copy-done.1, bf16[1,2,2,256,512]{4,3,2,1,0:T(8,128)(2,1)} %block_ref.1), custom_call_target="tpu_custom_call" | custom-call | tf_op jit(solution)/shard_map/pallas_call | solution.py:103
  (5 shorter events, 0.0 us)
Async XLA Ops:
  0.6 13.6 %copy-start = (bf16[128,128]{1,0:T(8,128)(2,1)S(1)}, bf16[128,128]{1,0:T(8,128)(2,1)}, u32[]{:S(2)}) copy-start(bf16[128,128]{1,0:T(8,128)(2,1)} %param.9) | copy-start | bytes 98308
  0.6 23.4 %collective-permute-start = (bf16[2,2,256,512]{3,2,1,0:T(8,128)(2,1)}, bf16[2,2,256,512]{3,2,1,0:T(8,128)(2,1)}, u32[]{:S(2)}, u32[]{:S(2)}) collective-permute-start(bf16[2,2,256,512]{3,2,1,0:T(8,128)(2,1)} %bitcast.100), channel_id=1, source_target_pairs={{0,15},{1,0},{2,1},{3,2},{4,3},{5,4},{6,5},{7,6},{8,7},{9,8},{10,9... | collective-permute-start | bytes 3145736 | tf_op jit(solution)/shard_map/ppermute | solution.py:12
  6.1 24.9 %collective-permute-start.2 = (bf16[2,2,256,512]{3,2,1,0:T(8,128)(2,1)}, bf16[2,2,256,512]{3,2,1,0:T(8,128)(2,1)}, u32[]{:S(2)}, u32[]{:S(2)}) collective-permute-start(bf16[2,2,256,512]{3,2,1,0:T(8,128)(2,1)} %bitcast.101), channel_id=1, source_target_pairs={{0,1},{1,2},{2,3},{3,4},{4,5},{5,6},{6,7},{7,8},{8,9},{9,10},{10,1... | collective-permute-start | bytes 3145736 | tf_op jit(solution)/shard_map/ppermute | solution.py:12
  16.0 1.8 %copy-start.6 = (s32[2,2]{1,0:T(2,128)S(1)}, s32[2,2]{1,0:T(2,128)}, u32[]{:S(2)}) copy-start(s32[2,2]{1,0:T(2,128)} %param.11) | copy-start | bytes 52
  16.0 2.9 %copy-start.3 = (bf16[1,2,2,256,512]{4,3,2,1,0:T(8,128)(2,1)S(1)}, bf16[1,2,2,256,512]{4,3,2,1,0:T(8,128)(2,1)}, u32[]{:S(2)}) copy-start(bf16[1,2,2,256,512]{4,3,2,1,0:T(8,128)(2,1)} %block_ref.1) | copy-start | bytes 3145732
  16.0 2.9 %copy-start.5 = (bf16[256,256]{1,0:T(8,128)(2,1)S(1)}, bf16[256,256]{1,0:T(8,128)(2,1)}, u32[]{:S(2)}) copy-start(bf16[256,256]{1,0:T(8,128)(2,1)} %param.10) | copy-start | bytes 393220
  23.8 4.7 %copy-start.4 = (bf16[4,2,512,512]{3,2,1,0:T(8,128)(2,1)S(1)}, bf16[4,2,512,512]{3,2,1,0:T(8,128)(2,1)}, u32[]{:S(2)}) copy-start(bf16[4,2,512,512]{3,2,1,0:T(8,128)(2,1)} %param.8) | copy-start | bytes 12582916
  24.0 17.8 %collective-permute-start.1 = (bf16[2,2,256,512]{3,2,1,0:T(8,128)(2,1)}, bf16[2,2,256,512]{3,2,1,0:T(8,128)(2,1)S(1)}, u32[]{:S(2)}, u32[]{:S(2)}) collective-permute-start(bf16[2,2,256,512]{3,2,1,0:T(8,128)(2,1)} %collective-permute-done), channel_id=1, source_target_pairs={{0,15},{1,0},{2,1},{3,2},{4,3},{5,4},{6,5},{7,6},{8,7},{9,8},{10,9... | collective-permute-start | bytes 3145736 | tf_op jit(solution)/shard_map/ppermute | solution.py:12
  31.0 17.5 %collective-permute-start.3 = (bf16[2,2,256,512]{3,2,1,0:T(8,128)(2,1)}, bf16[2,2,256,512]{3,2,1,0:T(8,128)(2,1)S(1)}, u32[]{:S(2)}, u32[]{:S(2)}) collective-permute-start(bf16[2,2,256,512]{3,2,1,0:T(8,128)(2,1)} %collective-permute-done.2), channel_id=1, source_target_pairs={{0,1},{1,2},{2,3},{3,4},{4,5},{5,6},{6,7},{7,8},{8,9},{9,10},{10,1... | collective-permute-start | bytes 3145736 | tf_op jit(solution)/shard_map/ppermute | solution.py:12
  50.3 1.6 %copy-start.2 = (f32[2,2,256,512]{3,2,1,0:T(8,128)S(1)}, f32[2,2,256,512]{3,2,1,0:T(8,128)}, u32[]{:S(2)}) copy-start(f32[2,2,256,512]{3,2,1,0:T(8,128)} %fusion.2.image_ref) | copy-start | bytes 6291460
  51.9 1.3 %copy-start.1 = (f32[2,2,256,512]{3,2,1,0:T(8,128)}, f32[2,2,256,512]{3,2,1,0:T(8,128)S(1)}, u32[]{:S(2)}) copy-start(f32[2,2,256,512]{3,2,1,0:T(8,128)S(1)} %fusion.1.coupled_ref) | copy-start | bytes 6291460
